TPU v7x, 128 devices: a whole 4x4x4 slice. The times are simulated.
128 devices in a mesh: seq: 16 (over z_lo, x, core), zero: 8 (over y, z_hi).
Axes of the slice: x: 4, y: 4, z: 4 (z_hi: 2, z_lo: 2; z = z_hi * 2 + z_lo), core: 2. Of those that a mesh axis runs over, the one named last changes fastest.
Arguments:
- tokens: bfloat16 [16384, 1024], P(('seq', 'zero')), may hold values from -18 to 18
- projection: bfloat16 [1024, 3072], P('zero'), may hold values from -0.1875 to 0.1875
- pattern: int32 [128, 8], replicated, may hold values from 0 to 127, as said below
- upstream: bfloat16 [16384, 1024], P(('seq', 'zero')), may hold values from -6 to 6
Outputs:
- attended: bfloat16 [16384, 1024], P(('seq', 'zero'))
- token_gradient: bfloat16 [16384, 1024], P(('seq', 'zero'))
- weight_gradient: float32 [1024, 3072], P('zero')
Inputs may be any that keep to these rules, and one draw needn't show every extreme that they name: `pattern`: each row names 8 different key blocks, block 0 and the row's own block among them.
All inputs are finite; a program needn't handle non-finite values.
Results may differ from a plain program's by a relative error of at most 0.01.
The roundings to bfloat16 on the way count: a program that leaves them out, or rounds other values in their place, can miss the bound.
Values may be sent and summed in bfloat16 or wider, within the bound.
No kernel may reach another device: no remote copies, remote signals or barrier semaphores. Data moves between devices by JAX's collectives and lax.ppermute only.
A program may use at most 128 MiB of HBM per device.

v0:
```python
import jax
import jax.numpy as jnp
from jax import lax
from jax.sharding import PartitionSpec as P

HEADS = 16
HEAD = 64
BLOCK = 128
NBK = 8


def on_device(tokens, projection, pattern, upstream):
    seq_count = lax.axis_size("seq")
    zero_count = lax.axis_size("zero")
    zero_index = lax.axis_index("zero")
    tok_rows = tokens.shape[0]
    model_width = tokens.shape[1]
    heads_here = HEADS // seq_count
    head_cols = heads_here * HEAD
    per_shard = tok_rows // BLOCK
    local_blocks = seq_count * per_shard
    group_size = 4
    step_count = local_blocks // group_size
    score_scale = HEAD ** (-0.5)
    weights = lax.all_gather(projection, "zero", axis=0, tiled=True)
    projected = jnp.dot(tokens, weights, preferred_element_type=jnp.float32).astype(jnp.bfloat16)
    projected = projected.reshape(tok_rows, 3, seq_count, head_cols)
    by_head = lax.all_to_all(projected, "seq", split_axis=2, concat_axis=0, tiled=True)
    by_head = by_head.reshape(local_blocks * BLOCK, 3, head_cols)
    key_all, value_all = (
        lax.all_gather(by_head[:, 1], "zero", axis=0, tiled=True),
        lax.all_gather(by_head[:, 2], "zero", axis=0, tiled=True),
    )
    key_all = key_all.reshape(zero_count * local_blocks, BLOCK, heads_here, HEAD)
    value_all = value_all.reshape(zero_count * local_blocks, BLOCK, heads_here, HEAD)
    queries = by_head[:, 0].reshape(step_count, group_size, BLOCK, heads_here, HEAD)
    incoming = lax.all_to_all(
        upstream.reshape(tok_rows, seq_count, head_cols),
        "seq",
        split_axis=1,
        concat_axis=0,
        tiled=True,
    )
    incoming = incoming.reshape(step_count, group_size, BLOCK, heads_here, HEAD)
    local_ids = jnp.arange(local_blocks, dtype=jnp.int32)
    row_ids = (local_ids // per_shard * zero_count + zero_index) * per_shard + local_ids % per_shard
    row_lists = pattern[row_ids]
    shard_ids = row_lists // per_shard
    key_slots = (
        shard_ids % zero_count * local_blocks
        + shard_ids // zero_count * per_shard
        + row_lists % per_shard
    )
    key_slots = key_slots.reshape(step_count, group_size, NBK)

    def attend(carried, inputs):
        key_grad, value_grad = carried
        query_block, up_block, slot_block = inputs
        key_chosen = key_all[slot_block].reshape(group_size, NBK * BLOCK, heads_here, HEAD)
        value_chosen = value_all[slot_block].reshape(group_size, NBK * BLOCK, heads_here, HEAD)
        scores = (
            jnp.einsum(
                "rqhe,rkhe->rhqk", query_block, key_chosen, preferred_element_type=jnp.float32
            )
            * score_scale
        )
        row_max = jnp.max(scores, axis=-1, keepdims=True)
        exponent = jnp.exp(scores - row_max)
        prob_full = exponent / jnp.sum(exponent, axis=-1, keepdims=True)
        prob_low = prob_full.astype(jnp.bfloat16)
        out_block = jnp.einsum(
            "rhqk,rkhe->rqhe", prob_low, value_chosen, preferred_element_type=jnp.float32
        ).astype(jnp.bfloat16)
        prob_grad = jnp.einsum(
            "rqhe,rkhe->rhqk", up_block, value_chosen, preferred_element_type=jnp.float32
        )
        row_delta = jnp.sum(prob_full * prob_grad, axis=-1, keepdims=True)
        score_grad = (prob_full * (prob_grad - row_delta) * score_scale).astype(jnp.bfloat16)
        query_grad = jnp.einsum(
            "rhqk,rkhe->rqhe", score_grad, key_chosen, preferred_element_type=jnp.float32
        ).astype(jnp.bfloat16)
        key_terms = jnp.einsum(
            "rhqk,rqhe->rkhe", score_grad, query_block, preferred_element_type=jnp.float32
        )
        value_terms = jnp.einsum(
            "rhqk,rqhe->rkhe", prob_low, up_block, preferred_element_type=jnp.float32
        )
        key_grad = key_grad.at[slot_block].add(
            key_terms.reshape(group_size, NBK, BLOCK, heads_here, HEAD)
        )
        value_grad = value_grad.at[slot_block].add(
            value_terms.reshape(group_size, NBK, BLOCK, heads_here, HEAD)
        )
        return ((key_grad, value_grad), (out_block, query_grad))

    zero_start = jnp.zeros((zero_count * local_blocks, BLOCK, heads_here, HEAD), jnp.float32)
    (key_grad, value_grad), (out_blocks, query_grads) = lax.scan(
        attend, (zero_start, zero_start), (queries, incoming, key_slots)
    )
    attended = lax.all_to_all(
        out_blocks.reshape(local_blocks * BLOCK, 1, head_cols),
        "seq",
        split_axis=0,
        concat_axis=1,
        tiled=True,
    )
    attended = attended.reshape(tok_rows, seq_count * head_cols)
    key_sum, value_sum = (
        lax.psum_scatter(
            key_grad.astype(jnp.bfloat16), "zero", scatter_dimension=0, tiled=True
        ).astype(jnp.float32),
        lax.psum_scatter(
            value_grad.astype(jnp.bfloat16), "zero", scatter_dimension=0, tiled=True
        ).astype(jnp.float32),
    )
    local_grads = jnp.stack(
        [
            query_grads.reshape(-1, head_cols),
            key_sum.astype(jnp.bfloat16).reshape(-1, head_cols),
            value_sum.astype(jnp.bfloat16).reshape(-1, head_cols),
        ],
        axis=1,
    )
    local_grads = local_grads.reshape(local_blocks * BLOCK, 3, 1, head_cols)
    token_grads = lax.all_to_all(local_grads, "seq", split_axis=0, concat_axis=2, tiled=True)
    flat_grads = token_grads.reshape(tok_rows, 3 * seq_count * head_cols)
    token_gradient = jnp.einsum(
        "tc,dc->td", flat_grads, weights, preferred_element_type=jnp.float32
    ).astype(jnp.bfloat16)
    part_rows = model_width // (zero_count * seq_count)
    reordered = (
        tokens.reshape(tok_rows, zero_count, seq_count, part_rows)
        .transpose(0, 2, 1, 3)
        .reshape(tok_rows, model_width)
    )
    own_rows = lax.psum_scatter(
        jnp.einsum("td,tc->dc", reordered, flat_grads, preferred_element_type=jnp.float32),
        ("seq", "zero"),
        scatter_dimension=0,
        tiled=True,
    )
    weight_gradient = lax.all_gather(own_rows, "seq", axis=0, tiled=True)
    return (attended, token_gradient, weight_gradient)


def solution(mesh):
    return jax.shard_map(
        on_device,
        mesh=mesh,
        in_specs=(P(("seq", "zero"), None), P("zero", None), P(), P(("seq", "zero"), None)),
        out_specs=(P(("seq", "zero"), None), P(("seq", "zero"), None), P("zero", None)),
        check_vma=False,
    )
```

profile of v0, /device:TPU:1, one launch (start us, length us, event | category | flops | bytes accessed | tf_op | source)
XLA Modules:
  0.0 1301.3 jit_solution(15439516012232887688)
XLA Ops:
  7.9 94.1 %all-gather.7.cloned.1.call-done = bf16[1024,3072]{1,0:T(8,128)(2,1)} async-done(((bf16[128,3072]{1,0:T(8,128)(2,1)}), bf16[1024,3072]{1,0:T(8,128)(2,1)}) %all-gather.7.cloned.1.call-update) | async-done | bytes 6291472 | tf_op jit(solution)/shard_map/all_gather | solution.py:25
  102.0 3.9 convolution_convert_fusion.1
  106.3 18.4 %all_to_all.60 = bf16[128,3,16,64]{0,3,1,2:T(8,128)(2,1)S(1)} all-to-all(bf16[128,3,16,64]{0,3,1,2:T(8,128)(2,1)S(1)} %copy.107), channel_id=1, replica_groups=mesh['seq'=16,'zero'=8] {'seq'}, dimensions={2} | all-to-all | bytes 1572864 | tf_op jit(solution)/shard_map/all_to_all | solution.py:28
  128.0 4.1 all-to-all-start.1
  133.8 42.9 %all-gather.13.cloned.1.call-done = bf16[16384,1,64]{0,2,1:T(8,128)(2,1)} async-done(((bf16[2048,1,64]{0,2,1:T(8,128)(2,1)}), bf16[16384,1,64]{0,2,1:T(8,128)(2,1)}) %all-gather.13.cloned.1.call-update) | async-done | bytes 2097168 | tf_op jit(solution)/shard_map/all_gather | solution.py:32
  176.6 2.2 copy_bitcast_fusion.7
  178.8 53.9 %all-gather.11.cloned.1.call-done = bf16[16384,1,64]{0,2,1:T(8,128)(2,1)} async-done(((bf16[2048,1,64]{0,2,1:T(8,128)(2,1)}), bf16[16384,1,64]{0,2,1:T(8,128)(2,1)}) %all-gather.11.cloned.1.call-update) | async-done | bytes 2097168 | tf_op jit(solution)/shard_map/all_gather | solution.py:31
  232.7 3.5 copy_bitcast_fusion.8
  236.3 2.5 broadcast_in_dim.8.clone
  238.8 2.5 broadcast_in_dim.8
  241.3 146.4 %while.16 = (s32[]{:T(128)}, f32[128,128,1,64]{1,3,0,2:T(8,128)}, f32[128,128,1,64]{1,3,0,2:T(8,128)}, bf16[4,4,128,1,64]{2,4,1,3,0:T(8,128)(2,1)}, bf16[4,4,128...) while((s32[]{:T(128)}, f32[128,128,1,64]{1,3,0,2:T(8,128)}, ...), condition=%wide.region_6.7_spmd, body=%wide.region_0.6_spmd.sunk | while | flops 414258272 | bytes 78265752 | solution.py:97
  241.4 0.9 constant_dynamic-slice_fusion.2
  242.3 2.2 gather_fusion.1
  244.9 0.9 reshape.274
  247.9 2.2 fusion.96
  250.0 4.7 fusion.99
  254.7 5.8 fusion.97
  260.6 2.9 fusion.98
  268.2 4.8 scatter_fusion
  273.0 4.9 scatter_fusion.1
  278.0 0.9 constant_dynamic-slice_fusion.2
  278.9 2.2 gather_fusion.1
  284.5 2.2 fusion.96
  286.7 4.7 fusion.99
  291.4 5.8 fusion.97
  297.2 2.9 fusion.98
  304.9 4.8 scatter_fusion
  309.6 4.9 scatter_fusion.1
  314.6 0.9 constant_dynamic-slice_fusion.2
  315.6 2.2 gather_fusion.1
  321.1 2.2 fusion.96
  323.3 4.7 fusion.99
  328.0 5.8 fusion.97
  333.8 2.9 fusion.98
  341.5 4.8 scatter_fusion
  346.2 4.9 scatter_fusion.1
  351.2 0.9 constant_dynamic-slice_fusion.2
  352.2 2.2 gather_fusion.1
  357.7 2.2 fusion.96
  359.9 4.7 fusion.99
  364.6 5.8 fusion.97
  370.4 2.9 fusion.98
  378.1 4.8 scatter_fusion
  382.8 4.8 scatter_fusion.1
  387.6 4.0 convert_element_type.43
  391.8 4.0 convert_element_type.44
  395.8 1.1 stack_reshape.9
  397.0 70.3 %reduce-scatter.6.cloned.1.call-done = bf16[16,128,1,64]{1,3,0,2:T(8,128)(2,1)} async-done(((bf16[128,128,1,64]{1,3,0,2:T(8,128)(2,1)}), bf16[16,128,1,64]{1,3,0,2:T(8,128)(2,1)}) %reduce-scatter.6.cloned.1.call-update) | async-done | bytes 262160 | tf_op jit(solution)/shard_map/reduce_scatter | solution.py:109
  467.2 1.0 copy_bitcast_fusion.10
  468.2 77.9 %reduce-scatter.8.cloned.1.call-done = bf16[16,128,1,64]{1,3,0,2:T(8,128)(2,1)} async-done(((bf16[128,128,1,64]{1,3,0,2:T(8,128)(2,1)}), bf16[16,128,1,64]{1,3,0,2:T(8,128)(2,1)}) %reduce-scatter.8.cloned.1.call-update) | async-done | bytes 262160 | tf_op jit(solution)/shard_map/reduce_scatter | solution.py:112
  546.1 1.0 copy_bitcast_fusion.9
  547.2 1.6 copy.121
  548.8 2.5 reshape.249
  551.3 6.5 all-to-all-start.3
  558.1 12.4 all-to-all-done.3
  570.5 1.3 reshape.250
  571.8 1.2 copy.130
  573.0 6.3 convolution_bitcast_fusion.1
  579.3 12.6 copy.131
  592.0 658.6 %reduce-scatter.10.cloned.1.call-done = f32[8,3072]{1,0:T(8,128)} async-done(((f32[1024,3072]{1,0:T(8,128)}), f32[8,3072]{1,0:T(8,128)}) %reduce-scatter.10.cloned.1.call-update) | async-done | bytes 98320 | tf_op jit(solution)/shard_map/reduce_scatter | solution.py:136
  1251.7 11.5 reduce.6
  1263.6 20.2 %all_to_all.61 = bf16[16,2,4096]{2,1,0:T(2,128)(2,1)S(1)} all-to-all(bf16[16,2,4096]{2,1,0:T(2,128)(2,1)S(1)} %reshape.247), channel_id=1, replica_groups=mesh['seq'=16,'zero'=8] {'seq'}, dimensions={0} | all-to-all | bytes 524288 | tf_op jit(solution)/shard_map/all_to_all | solution.py:100
  1286.1 5.7 convolution_convert_fusion.2
  1291.8 2.7 copy.220
  (157 shorter events, 41.5 us)
Async XLA Ops:
  7.2 94.9 %all-gather.7.cloned.1.call-start = ((), (), s32[]{:S(2)}) async-start(), calls=%async_computation.7 | async-start | bytes 7077888 | tf_op jit(solution)/shard_map/all_gather | solution.py:25
  7.9 168.7 %all-gather.13.cloned.1.call-start = ((), (), s32[]{:S(2)}) async-start(), calls=%async_computation.12 | async-start | bytes 2359296 | tf_op jit(solution)/shard_map/all_gather | solution.py:32
  125.2 2.0 copy-start.6
  125.2 6.9 copy-start.7
  126.4 106.3 %all-gather.11.cloned.1.call-start = ((), (), s32[]{:S(2)}) async-start(), calls=%async_computation.11 | async-start | bytes 2359296 | tf_op jit(solution)/shard_map/all_gather | solution.py:31
  128.0 108.2 %all-to-all-start.1 = ((bf16[128,16,64]{0,2,1:T(8,128)(2,1)}), bf16[128,16,64]{0,2,1:T(8,128)(2,1)S(1)}, u32[]{:S(2)}, u32[]{:S(2)}) async-start(bf16[128,16,64]{0,2,1:T(8,128)(2,1)} %bitcast.24), calls=%async_computation.1 | async-start | bytes 524288 | tf_op jit(solution)/shard_map/all_to_all | solution.py:37
  132.1 335.1 %reduce-scatter.6.cloned.1.call-start = ((), (), s32[]{:S(2)}) async-start(), calls=%async_computation.8 | async-start | bytes 2359296 | tf_op jit(solution)/shard_map/reduce_scatter | solution.py:109
  241.3 4.6 copy-start.1
  246.8 1.0 copy-start.3
  260.6 2.9 copy-start.8
  264.6 1.2 copy-start
  273.0 4.9 copy-start.2
  277.9 4.6 copy-start.1
  283.5 1.0 copy-start.3
  297.2 2.9 copy-start.8
  301.2 1.2 copy-start
  309.6 4.9 copy-start.2
  314.5 4.6 copy-start.1
  320.1 1.0 copy-start.3
  333.8 2.9 copy-start.8
  337.8 1.2 copy-start
  346.2 4.9 copy-start.2
  351.1 4.6 copy-start.1
  356.7 1.0 copy-start.3
  370.4 2.9 copy-start.8
  374.4 1.2 copy-start
  382.8 4.8 copy-start.2
  391.7 154.4 %reduce-scatter.8.cloned.1.call-start = ((), (), s32[]{:S(2)}) async-start(), calls=%async_computation.9 | async-start | bytes 2359296 | tf_op jit(solution)/shard_map/reduce_scatter | solution.py:112
  548.8 9.0 copy-start.4
  551.3 19.2 %all-to-all-start.3 = ((bf16[16,2,12288]{2,1,0:T(2,128)(2,1)}), bf16[16,2,12288]{2,1,0:T(2,128)(2,1)S(1)}, u32[]{:S(2)}, u32[]{:S(2)}) async-start(bf16[16,2,12288]{2,1,0:T(2,128)(2,1)} %reshape.249), calls=%async_computation.5 | async-start | bytes 1572864 | tf_op jit(solution)/shard_map/all_to_all | solution.py:125
  557.8 692.7 %reduce-scatter.10.cloned.1.call-start = ((), (), s32[]{:S(2)}) async-start(), calls=%async_computation.13 | async-start | bytes 12681216 | tf_op jit(solution)/shard_map/reduce_scatter | solution.py:136
  591.9 658.7 %copy-start.5 = (bf16[4,4,128,1,64]{2,4,1,3,0:T(8,128)(2,1)S(1)}, bf16[4,4,128,1,64]{2,4,1,3,0:T(8,128)(2,1)}, u32[]{:S(2)}) copy-start(bf16[4,4,128,1,64]{2,4,1,3,0:T(8,128)(2,1)} %get-tuple-element.58) | copy-start | bytes 786436
  591.9 699.8 %all-gather.9.cloned.1.call-start = ((), (), s32[]{:S(2)}) async-start(), calls=%async_computation.10 | async-start | bytes 1671168 | tf_op jit(solution)/shard_map/all_gather | solution.py:142
Sparse Core Ops, SparseCore 0:
  10.3 91.6 all-gather.6
  126.6 50.0 all-gather.12
  179.0 53.6 all-gather.10
  391.8 75.3 reduce-scatter.5
  470.9 75.2 reduce-scatter.7
  592.0 658.4 reduce-scatter.9
  1252.3 37.7 all-gather.8
where the time goes:
time: 1300 us
  waiting for transfers between devices  1010 us (78%)
  local copies, waits for them, and re-layouts  85.3 us (7%)
  matrix products  81.9 us (6%)
  other arithmetic  58.3 us (4%)
  blocking collectives  38.6 us (3%)
  between operations  14.4 us (1%)
    reduce_scatter x1, waiting for transfers between devices, on_device(): lax.psum_scatter(jnp.einsum('td,tc->dc', reordered, flat_grads, preferred...  659 us
    all_gather x1, waiting for transfers between devices, on_device(): weights = lax.all_gather(projection, 'zero', axis=0, tiled=True)  94.1 us
    reduce_scatter x1, waiting for transfers between devices, on_device(): lax.psum_scatter(value_grad.astype(jnp.bfloat16), 'zero', scatter_dimensi...  77.9 us
    reduce_scatter x1, waiting for transfers between devices, on_device(): lax.psum_scatter(key_grad.astype(jnp.bfloat16), 'zero', scatter_dimension...  70.3 us
    all_gather x1, waiting for transfers between devices, on_device(): lax.all_gather(by_head[:, 1], 'zero', axis=0, tiled=True)  53.9 us
    all_gather x1, waiting for transfers between devices, on_device(): lax.all_gather(by_head[:, 2], 'zero', axis=0, tiled=True)  42.9 us
  transfers between devices with their start and end apart: 9, of which 7 were waited for; matrix products, arithmetic and copies ran while one was open for 3% of the time, Pallas kernels for 0%

commit v1 on v0

--- a/solution.py
+++ b/solution.py
@@ -127,19 +127,15 @@
     token_gradient = jnp.einsum(
         "tc,dc->td", flat_grads, weights, preferred_element_type=jnp.float32
     ).astype(jnp.bfloat16)
-    part_rows = model_width // (zero_count * seq_count)
-    reordered = (
-        tokens.reshape(tok_rows, zero_count, seq_count, part_rows)
-        .transpose(0, 2, 1, 3)
-        .reshape(tok_rows, model_width)
+    group_tokens = lax.all_gather(tokens, "seq", axis=0, tiled=True)
+    head_grads = local_grads.reshape(local_blocks * BLOCK, 3 * head_cols)
+    head_part = jnp.einsum(
+        "td,tc->dc", group_tokens, head_grads, preferred_element_type=jnp.float32
     )
-    own_rows = lax.psum_scatter(
-        jnp.einsum("td,tc->dc", reordered, flat_grads, preferred_element_type=jnp.float32),
-        ("seq", "zero"),
-        scatter_dimension=0,
-        tiled=True,
-    )
-    weight_gradient = lax.all_gather(own_rows, "seq", axis=0, tiled=True)
+    own_rows = lax.psum_scatter(head_part, "zero", scatter_dimension=0, tiled=True)
+    own_rows = own_rows.reshape(1, -1, 3, head_cols)
+    gathered = lax.all_gather(own_rows, "seq", axis=0, tiled=True)
+    weight_gradient = gathered.transpose(1, 2, 0, 3).reshape(-1, 3 * seq_count * head_cols)
     return (attended, token_gradient, weight_gradient)
 
 

time: 1300 us -> 697 us (0.54)
  waiting for transfers between devices: 1010 us -> 429 us
  blocking collectives: 38.6 us -> 18.4 us
    reduce_scatter x1, waiting for transfers between devices: 659 us -> 70.9 us  [on_device(): lax.psum_scatter(head_part, 'zero', scatter_dimension=0, tiled=True)]
    all_to_all x1 -> x0, blocking collectives: 20.2 us -> none  [on_device(): lax.all_to_all(out_blocks.reshape(local_blocks * BLOCK, 1, head_cols), 's...]
    while x40 -> x72, local copies, waits for them, and re-layouts: 2.34 us -> 15.6 us
  transfers between devices with their start and end apart: 9 -> 11, of which waited for: 7 -> 8; matrix products, arithmetic and copies ran while one was open for 3% -> 6% of each run, Pallas kernels for 0% -> 0%
where the time goes in v1:
time: 697 us; the launch traced here: 695 us
  waiting for transfers between devices  429 us (62%)
  matrix products  79.9 us (11%)
  local copies, waits for them, and re-layouts  76.9 us (11%)
  other arithmetic  58.6 us (8%)
  blocking collectives  18.4 us (3%)
  between operations  15.8 us (2%)
  starting transfers between devices  15.2 us (2%)
    all_gather x1, waiting for transfers between devices, on_device(): weights = lax.all_gather(projection, 'zero', axis=0, tiled=True)  94.1 us
    reduce_scatter x1, waiting for transfers between devices, on_device(): lax.psum_scatter(value_grad.astype(jnp.bfloat16), 'zero', scatter_dimensi...  78 us
    reduce_scatter x1, waiting for transfers between devices, on_device(): lax.psum_scatter(key_grad.astype(jnp.bfloat16), 'zero', scatter_dimension...  73.4 us
    reduce_scatter x1, waiting for transfers between devices, on_device(): lax.psum_scatter(head_part, 'zero', scatter_dimension=0, tiled=True)  70.9 us
    all_gather x1, waiting for transfers between devices, on_device(): lax.all_gather(by_head[:, 1], 'zero', axis=0, tiled=True)  52.6 us
    all_gather x1, waiting for transfers between devices, on_device(): lax.all_gather(by_head[:, 2], 'zero', axis=0, tiled=True)  43.6 us
    dot_general x4, matrix products, attend(): jnp.einsum('rhqk,rkhe->rqhe', score_grad, key_chosen, preferred_element_t...  23.9 us
    dot_general x4, matrix products, attend(): jnp.einsum('rhqk,rqhe->rkhe', score_grad, query_block, preferred_element_...  23.3 us
  transfers between devices with their start and end apart: 11, of which 8 were waited for; matrix products, arithmetic and copies ran while one was open for 6% of the time, Pallas kernels for 0%

profile of v1, /device:TPU:1, one launch (start us, length us, event | category | flops | bytes accessed | tf_op | source)
XLA Modules:
  0.0 694.7 jit_solution(11486207154974319977)
XLA Ops:
  8.8 94.1 %all-gather.8.cloned.1.call-done = bf16[1024,3072]{1,0:T(8,128)(2,1)} async-done(((bf16[128,3072]{1,0:T(8,128)(2,1)}), bf16[1024,3072]{1,0:T(8,128)(2,1)}) %all-gather.8.cloned.1.call-update) | async-done | bytes 6291472 | tf_op jit(solution)/shard_map/all_gather | solution.py:25
  102.9 3.9 convolution_convert_fusion.1
  107.2 18.4 %all_to_all.60 = bf16[128,3,16,64]{0,3,1,2:T(8,128)(2,1)S(1)} all-to-all(bf16[128,3,16,64]{0,3,1,2:T(8,128)(2,1)S(1)} %copy.104), channel_id=1, replica_groups=mesh['seq'=16,'zero'=8] {'seq'}, dimensions={2} | all-to-all | bytes 1572864 | tf_op jit(solution)/shard_map/all_to_all | solution.py:28
  128.9 4.1 all-to-all-start.1
  134.0 43.6 %all-gather.16.cloned.1.call-done = bf16[16384,1,64]{0,2,1:T(8,128)(2,1)} async-done(((bf16[2048,1,64]{0,2,1:T(8,128)(2,1)}), bf16[16384,1,64]{0,2,1:T(8,128)(2,1)}) %all-gather.16.cloned.1.call-update) | async-done | bytes 2097168 | tf_op jit(solution)/shard_map/all_gather | solution.py:32
  177.5 3.5 copy_bitcast_fusion.7
  181.0 52.6 %all-gather.14.cloned.1.call-done = bf16[16384,1,64]{0,2,1:T(8,128)(2,1)} async-done(((bf16[2048,1,64]{0,2,1:T(8,128)(2,1)}), bf16[16384,1,64]{0,2,1:T(8,128)(2,1)}) %all-gather.14.cloned.1.call-update) | async-done | bytes 2097168 | tf_op jit(solution)/shard_map/all_gather | solution.py:31
  233.6 2.2 copy_bitcast_fusion.8
  235.8 2.6 broadcast_in_dim.8
  238.4 2.6 broadcast_in_dim.8.clone
  241.0 152.2 %while.16 = (s32[]{:T(128)}, f32[128,128,1,64]{1,3,0,2:T(8,128)}, f32[128,128,1,64]{1,3,0,2:T(8,128)}, bf16[4,4,128,1,64]{2,4,1,3,0:T(8,128)(2,1)}, bf16[4,4,128...) while((s32[]{:T(128)}, f32[128,128,1,64]{1,3,0,2:T(8,128)}, ...), condition=%wide.region_6.7_spmd, body=%wide.region_0.6_spmd.sunk | while | flops 414258272 | bytes 95044104 | solution.py:97
  241.1 1.2 copy-done.2
  244.4 1.3 copy-done.12
  247.9 4.9 scatter_fusion.1
  254.4 1.3 copy-done
  255.8 5.8 fusion.97
  261.6 1.9 copy.188
  264.6 4.9 scatter_fusion
  269.4 6.0 fusion.99
  276.1 2.9 fusion.98
  279.2 1.2 copy-done.2
  282.5 1.3 copy-done.12
  286.0 4.9 scatter_fusion.1
  292.5 1.3 copy-done
  293.8 5.8 fusion.97
  299.7 1.9 copy.188
  302.6 4.8 scatter_fusion
  307.5 6.0 fusion.99
  314.2 2.9 fusion.98
  317.2 1.2 copy-done.2
  320.6 1.3 copy-done.12
  324.0 4.9 scatter_fusion.1
  330.5 1.3 copy-done
  331.9 5.8 fusion.97
  337.7 1.9 copy.188
  340.7 4.9 scatter_fusion
  345.5 6.0 fusion.99
  352.2 2.9 fusion.98
  355.3 1.2 copy-done.2
  358.6 1.3 copy-done.12
  362.1 4.9 scatter_fusion.1
  368.6 1.3 copy-done
  370.0 5.8 fusion.97
  375.8 1.9 copy.188
  378.8 4.8 scatter_fusion
  383.6 6.0 fusion.99
  390.3 2.9 fusion.98
  393.2 4.0 convert_element_type.43
  397.3 4.0 convert_element_type.44
  402.5 73.4 %reduce-scatter.4.cloned.1.call-done = bf16[16,128,1,64]{1,3,0,2:T(8,128)(2,1)} async-done(((bf16[128,128,1,64]{1,3,0,2:T(8,128)(2,1)}), bf16[16,128,1,64]{1,3,0,2:T(8,128)(2,1)}) %reduce-scatter.4.cloned.1.call-update) | async-done | bytes 262160 | tf_op jit(solution)/shard_map/reduce_scatter | solution.py:109
  476.9 78.0 %reduce-scatter.6.cloned.1.call-done = bf16[16,128,1,64]{1,3,0,2:T(8,128)(2,1)} async-done(((bf16[128,128,1,64]{1,3,0,2:T(8,128)(2,1)}), bf16[16,128,1,64]{1,3,0,2:T(8,128)(2,1)}) %reduce-scatter.6.cloned.1.call-update) | async-done | bytes 262160 | tf_op jit(solution)/shard_map/reduce_scatter | solution.py:112
  555.9 4.1 convolution_bitcast_fusion.1
  560.0 70.9 %reduce-scatter.8.cloned.1.call-done = f32[128,192]{0,1:T(8,128)} async-done(((f32[1024,192]{0,1:T(8,128)}), f32[128,192]{0,1:T(8,128)}) %reduce-scatter.8.cloned.1.call-update) | async-done | bytes 98320 | tf_op jit(solution)/shard_map/reduce_scatter | solution.py:135
  632.1 11.5 %reduce.6 = bf16[2048,64]{1,0:T(8,128)(2,1)S(1)} reduce(bf16[2048,1,64]{2,1,0:T(2,128)(2,1)S(1)} %reshape.244, bf16[]{:T(256)} %broadcast.200), dimensions={1}, to_apply=%reshape.244.reduce_sub_computation | reduce | bytes 524290 | tf_op jit(solution)/shard_map/reshape | solution.py:101
  644.7 7.1 %all-to-all-start.2 = ((bf16[16,2,4096]{2,1,0:T(2,128)(2,1)}), bf16[16,2,4096]{2,1,0:T(2,128)(2,1)S(1)}, u32[]{:S(2)}, u32[]{:S(2)}) async-start(bf16[16,2,4096]{2,1,0:T(2,128)(2,1)} %reshape.245), calls=%async_computation.2 | async-start | bytes 524288 | tf_op jit(solution)/shard_map/all_to_all | solution.py:100
  651.8 1.4 copy.118
  653.2 2.5 reshape.247
  655.6 4.4 all-to-all-done.2
  660.0 3.5 all-to-all-start.3
  665.8 10.3 %all-to-all-done.3 = bf16[16,2,12288]{2,1,0:T(2,128)(2,1)S(1)} async-done(((bf16[16,2,12288]{2,1,0:T(2,128)(2,1)}), bf16[16,2,12288]{2,1,0:T(2,128)(2,1)S(1)}, u32[]{:S(2)}, u32[]{:S(2)}) %all-to-all-start.3) | async-done | bytes 786464 | tf_op jit(solution)/shard_map/all_to_all | solution.py:125
  676.1 1.3 reshape.248
  677.4 1.2 copy.126
  678.6 5.7 convolution_convert_fusion.2
  684.3 3.0 copy.123
  (190 shorter events, 43.5 us)
Async XLA Ops:
  8.0 94.9 %all-gather.8.cloned.1.call-start = ((), (), s32[]{:S(2)}) async-start(), calls=%async_computation.7 | async-start | bytes 7077888 | tf_op jit(solution)/shard_map/all_gather | solution.py:25
  8.7 168.8 %all-gather.16.cloned.1.call-start = ((), (), s32[]{:S(2)}) async-start(), calls=%async_computation.14 | async-start | bytes 2359296 | tf_op jit(solution)/shard_map/all_gather | solution.py:32
  126.1 2.0 copy-start.9
  126.1 7.0 %copy-start.11 = (s32[128,8]{0,1:T(8,128)S(1)}, s32[128,8]{0,1:T(8,128)}, u32[]{:S(2)}) copy-start(s32[128,8]{0,1:T(8,128)} %param.8) | copy-start | bytes 12292
  127.3 106.3 %all-gather.14.cloned.1.call-start = ((), (), s32[]{:S(2)}) async-start(), calls=%async_computation.13 | async-start | bytes 2359296 | tf_op jit(solution)/shard_map/all_gather | solution.py:31
  128.9 106.9 %all-to-all-start.1 = ((bf16[128,16,64]{0,2,1:T(8,128)(2,1)}), bf16[128,16,64]{0,2,1:T(8,128)(2,1)S(1)}, u32[]{:S(2)}, u32[]{:S(2)}) async-start(bf16[128,16,64]{0,2,1:T(8,128)(2,1)} %bitcast.24), calls=%async_computation.1 | async-start | bytes 524288 | tf_op jit(solution)/shard_map/all_to_all | solution.py:37
  133.0 342.9 %reduce-scatter.4.cloned.1.call-start = ((), (), s32[]{:S(2)}) async-start(), calls=%async_computation.8 | async-start | bytes 2359296 | tf_op jit(solution)/shard_map/reduce_scatter | solution.py:109
  241.0 1.3 copy-start.2
  241.0 2.5 copy-start.6
  243.4 1.0 copy-start.4
  244.4 1.3 copy-start.12
  247.9 4.9 copy-start.1
  254.4 1.4 copy-start
  264.6 4.9 copy-start.5
  276.1 2.9 copy-start.3
  276.1 2.9 copy-start.7
  279.0 1.3 copy-start.2
  279.0 2.5 copy-start.6
  281.5 1.0 copy-start.4
  282.5 1.3 copy-start.12
  285.9 4.9 copy-start.1
  292.5 1.4 copy-start
  302.6 4.8 copy-start.5
  314.2 2.9 copy-start.3
  314.2 2.9 copy-start.7
  317.1 1.3 copy-start.2
  317.1 2.5 copy-start.6
  319.6 1.0 copy-start.4
  320.6 1.3 copy-start.12
  324.0 4.9 copy-start.1
  330.5 1.4 copy-start
  340.7 4.9 copy-start.5
  352.2 2.9 copy-start.3
  352.2 2.9 copy-start.7
  355.2 1.3 copy-start.2
  355.2 2.5 copy-start.6
  357.6 1.0 copy-start.4
  358.6 1.3 copy-start.12
  362.1 4.9 copy-start.1
  368.6 1.4 copy-start
  378.7 4.8 copy-start.5
  390.3 2.9 copy-start.3
  390.3 2.9 copy-start.7
  397.2 157.6 %reduce-scatter.6.cloned.1.call-start = ((), (), s32[]{:S(2)}) async-start(), calls=%async_computation.9 | async-start | bytes 2359296 | tf_op jit(solution)/shard_map/reduce_scatter | solution.py:112
  401.3 0.9 copy-start.10
  401.3 154.5 %all-gather.10.cloned.1.call-start = ((), (), s32[]{:S(2)}) async-start(), calls=%async_computation.10 | async-start | bytes 4456448 | tf_op jit(solution)/shard_map/all_gather | solution.py:130
  401.9 229.1 %reduce-scatter.8.cloned.1.call-start = ((), (), s32[]{:S(2)}) async-start(), calls=%async_computation.11 | async-start | bytes 884736 | tf_op jit(solution)/shard_map/reduce_scatter | solution.py:135
  555.9 75.2 %copy-start.8 = (bf16[4,4,128,1,64]{2,4,1,3,0:T(8,128)(2,1)S(1)}, bf16[4,4,128,1,64]{2,4,1,3,0:T(8,128)(2,1)}, u32[]{:S(2)}) copy-start(bf16[4,4,128,1,64]{2,4,1,3,0:T(8,128)(2,1)} %get-tuple-element.58) | copy-start | bytes 786436
  560.0 124.3 %all-gather.12.cloned.1.call-start = ((), (), s32[]{:S(2)}) async-start(), calls=%async_computation.12 | async-start | bytes 1671168 | tf_op jit(solution)/shard_map/all_gather | solution.py:137
  644.7 15.3 %all-to-all-start.2 = ((bf16[16,2,4096]{2,1,0:T(2,128)(2,1)}), bf16[16,2,4096]{2,1,0:T(2,128)(2,1)S(1)}, u32[]{:S(2)}, u32[]{:S(2)}) async-start(bf16[16,2,4096]{2,1,0:T(2,128)(2,1)} %reshape.245), calls=%async_computation.2 | async-start | bytes 524288 | tf_op jit(solution)/shard_map/all_to_all | solution.py:100
  660.0 16.1 %all-to-all-start.3 = ((bf16[16,2,12288]{2,1,0:T(2,128)(2,1)}), bf16[16,2,12288]{2,1,0:T(2,128)(2,1)S(1)}, u32[]{:S(2)}, u32[]{:S(2)}) async-start(bf16[16,2,12288]{2,1,0:T(2,128)(2,1)} %reshape.247), calls=%async_computation.5 | async-start | bytes 1572864 | tf_op jit(solution)/shard_map/all_to_all | solution.py:125
Sparse Core Ops, SparseCore 0:
  11.1 91.6 all-gather.7
  127.4 50.0 all-gather.15
  179.9 53.6 all-gather.13
  397.4 78.4 reduce-scatter.3
  479.5 75.2 reduce-scatter.5
  560.1 70.8 reduce-scatter.7
Sparse Core Ops, SparseCore 1:
  403.5 39.9 all-gather.9
  631.1 35.8 all-gather.11

commit v2 on v1

--- a/solution.py
+++ b/solution.py
@@ -22,17 +22,18 @@
     group_size = 4
     step_count = local_blocks // group_size
     score_scale = HEAD ** (-0.5)
+    seq_index = lax.axis_index("seq")
     weights = lax.all_gather(projection, "zero", axis=0, tiled=True)
-    projected = jnp.dot(tokens, weights, preferred_element_type=jnp.float32).astype(jnp.bfloat16)
-    projected = projected.reshape(tok_rows, 3, seq_count, head_cols)
-    by_head = lax.all_to_all(projected, "seq", split_axis=2, concat_axis=0, tiled=True)
-    by_head = by_head.reshape(local_blocks * BLOCK, 3, head_cols)
-    key_all, value_all = (
-        lax.all_gather(by_head[:, 1], "zero", axis=0, tiled=True),
-        lax.all_gather(by_head[:, 2], "zero", axis=0, tiled=True),
-    )
-    key_all = key_all.reshape(zero_count * local_blocks, BLOCK, heads_here, HEAD)
-    value_all = value_all.reshape(zero_count * local_blocks, BLOCK, heads_here, HEAD)
+    group_tokens = lax.all_gather(tokens, "seq", axis=0, tiled=True)
+    head_w = projection.reshape(projection.shape[0], 3, seq_count, head_cols)
+    head_w = lax.dynamic_index_in_dim(head_w, seq_index, axis=2, keepdims=False)
+    head_w = lax.all_gather(head_w, "zero", axis=0, tiled=True)
+    by_head = jnp.einsum(
+        "td,dgc->tgc", group_tokens, head_w, preferred_element_type=jnp.float32
+    ).astype(jnp.bfloat16)
+    kv_all = lax.all_gather(by_head[:, 1:], "zero", axis=0, tiled=True)
+    key_all = kv_all[:, 0].reshape(zero_count * local_blocks, BLOCK, heads_here, HEAD)
+    value_all = kv_all[:, 1].reshape(zero_count * local_blocks, BLOCK, heads_here, HEAD)
     queries = by_head[:, 0].reshape(step_count, group_size, BLOCK, heads_here, HEAD)
     incoming = lax.all_to_all(
         upstream.reshape(tok_rows, seq_count, head_cols),
@@ -94,9 +95,18 @@
         return ((key_grad, value_grad), (out_block, query_grad))
 
     zero_start = jnp.zeros((zero_count * local_blocks, BLOCK, heads_here, HEAD), jnp.float32)
-    (key_grad, value_grad), (out_blocks, query_grads) = lax.scan(
-        attend, (zero_start, zero_start), (queries, incoming, key_slots)
+    half = step_count // 2
+    carried, (out_a, query_a) = lax.scan(
+        attend,
+        (zero_start, zero_start),
+        (queries[:half], incoming[:half], key_slots[:half]),
     )
+    weights, carried = lax.optimization_barrier((weights, carried))
+    (key_grad, value_grad), (out_b, query_b) = lax.scan(
+        attend, carried, (queries[half:], incoming[half:], key_slots[half:])
+    )
+    out_blocks = jnp.concatenate([out_a, out_b], axis=0)
+    query_grads = jnp.concatenate([query_a, query_b], axis=0)
     attended = lax.all_to_all(
         out_blocks.reshape(local_blocks * BLOCK, 1, head_cols),
         "seq",
@@ -127,7 +137,6 @@
     token_gradient = jnp.einsum(
         "tc,dc->td", flat_grads, weights, preferred_element_type=jnp.float32
     ).astype(jnp.bfloat16)
-    group_tokens = lax.all_gather(tokens, "seq", axis=0, tiled=True)
     head_grads = local_grads.reshape(local_blocks * BLOCK, 3 * head_cols)
     head_part = jnp.einsum(
         "td,tc->dc", group_tokens, head_grads, preferred_element_type=jnp.float32

time: 697 us -> 592 us (0.85)
  waiting for transfers between devices: 429 us -> 314 us
  blocking collectives: 18.4 us -> 28.7 us
    all_gather x1, waiting for transfers between devices: 94.1 us -> 3.62 us  [on_device(): weights = lax.all_gather(projection, 'zero', axis=0, tiled=True)]
    all_gather x2 -> x1, waiting for transfers between devices: 96.2 us -> 55.4 us  [on_device(): kv_all = lax.all_gather(by_head[:, 1:], 'zero', axis=0, tiled=True)]
    all_gather x0 -> x1, blocking collectives: none -> 28.7 us  [on_device(): head_w = lax.all_gather(head_w, 'zero', axis=0, tiled=True)]
    all_to_all x1 -> x0, blocking collectives: 18.4 us -> none  [on_device(): lax.all_to_all(projected, 'seq', split_axis=2, concat_axis=0, tiled=True)]
    while x74 -> x33, local copies, waits for them, and re-layouts: 21.3 us -> 5 us  [the longest x1 3.22 us: on_device(): lax.scan(attend, (zero_start, zero_start), (queries[:half], incoming[:hal...]
    all_gather x1, waiting for transfers between devices: 0.03 us -> 15.4 us  [on_device(): group_tokens = lax.all_gather(tokens, 'seq', axis=0, tiled=True)]
    unnamed x19 -> x24, local copies, waits for them, and re-layouts: 11.4 us -> 16 us
  transfers between devices with their start and end apart: 11 -> 10, of which waited for: 8 -> 9; matrix products, arithmetic and copies ran while one was open for 6% -> 21% of each run, Pallas kernels for 0% -> 0%
where the time goes in v2:
time: 592 us; the launch traced here: 586 us
  waiting for transfers between devices  314 us (53%)
  matrix products  78.6 us (13%)
  local copies, waits for them, and re-layouts  75.8 us (13%)
  other arithmetic  57.9 us (10%)
  blocking collectives  28.7 us (5%)
  starting transfers between devices  15.4 us (3%)
  between operations  14.8 us (2%)
    reduce_scatter x1, waiting for transfers between devices, on_device(): lax.psum_scatter(value_grad.astype(jnp.bfloat16), 'zero', scatter_dimensi...  78 us
    reduce_scatter x1, waiting for transfers between devices, on_device(): lax.psum_scatter(head_part, 'zero', scatter_dimension=0, tiled=True)  71 us
    reduce_scatter x1, waiting for transfers between devices, on_device(): lax.psum_scatter(key_grad.astype(jnp.bfloat16), 'zero', scatter_dimension...  68.4 us
    all_gather x1, waiting for transfers between devices, on_device(): kv_all = lax.all_gather(by_head[:, 1:], 'zero', axis=0, tiled=True)  55.4 us
    all_gather x1, blocking collectives, on_device(): head_w = lax.all_gather(head_w, 'zero', axis=0, tiled=True)  28.7 us
    dot_general x4, matrix products, attend(): jnp.einsum('rhqk,rqhe->rkhe', score_grad, query_block, preferred_element_...  23.5 us
    dot_general x4, matrix products, attend(): jnp.einsum('rhqk,rkhe->rqhe', score_grad, key_chosen, preferred_element_t...  20.2 us
    scatter-add x4, other arithmetic, attend(): key_grad.at[slot_block]  19.2 us
  transfers between devices with their start and end apart: 10, of which 9 were waited for; matrix products, arithmetic and copies ran while one was open for 21% of the time, Pallas kernels for 0%

profile of v2, /device:TPU:1, one launch (start us, length us, event | category | flops | bytes accessed | tf_op | source)
XLA Modules:
  0.0 586.1 jit_solution(1013069680847403294)
XLA Ops:
  8.0 1.5 copy.158
  9.5 28.7 %all-gather = bf16[1024,3,1,64]{0,3,1,2:T(8,128)(2,1)S(1)} all-gather(bf16[128,3,1,64]{0,3,1,2:T(8,128)(2,1)S(1)} %dynamic-slice_bitcast_fusion), channel_id=2, replica_groups=mesh['seq'=16,'zero'=8] {'zero'}, dimensions={0}, use_global_device_ids=true | all-gather | bytes 442368 | tf_op jit(solution)/shard_map/all_gather | solution.py:30
  38.2 15.4 %all-gather.6.cloned.1.call-done = bf16[2048,1024]{1,0:T(8,128)(2,1)} async-done(((bf16[128,1024]{1,0:T(8,128)(2,1)}), bf16[2048,1024]{1,0:T(8,128)(2,1)}) %all-gather.6.cloned.1.call-update) | async-done | bytes 4194320 | tf_op jit(solution)/shard_map/all_gather | solution.py:27
  53.6 3.7 fusion.113
  59.7 3.6 all-to-all-start
  64.1 6.5 %all-to-all-done = bf16[128,16,64]{0,2,1:T(8,128)(2,1)S(1)} async-done(((bf16[128,16,64]{0,2,1:T(8,128)(2,1)}), bf16[128,16,64]{0,2,1:T(8,128)(2,1)S(1)}, u32[]{:S(2)}, u32[]{:S(2)}) %all-to-all-start) | async-done | bytes 262176 | tf_op jit(solution)/shard_map/all_to_all | solution.py:38
  72.1 55.4 %all-gather.8.cloned.1.call-done = bf16[16384,2,64]{0,2,1:T(8,128)(2,1)} async-done(((bf16[2048,2,64]{0,2,1:T(8,128)(2,1)}), bf16[16384,2,64]{0,2,1:T(8,128)(2,1)}) %all-gather.8.cloned.1.call-update) | async-done | bytes 4194320 | tf_op jit(solution)/shard_map/all_gather | solution.py:34
  127.5 2.5 slice_bitcast_fusion
  130.0 3.2 copy_bitcast_fusion.14
  134.6 2.5 broadcast_in_dim.22.clone
  137.1 2.6 broadcast_in_dim.22
  139.7 73.4 %while.32 = (s32[]{:T(128)}, f32[128,128,1,64]{1,3,0,2:T(8,128)}, f32[128,128,1,64]{1,3,0,2:T(8,128)}, bf16[2,4,128,1,64]{2,4,1,3,0:T(8,128)(2,1)}, bf16[2,4,128...) while((s32[]{:T(128)}, f32[128,128,1,64]{1,3,0,2:T(8,128)}, ...), condition=%wide.region_6.7_spmd, body=%wide.region_0.6_spmd.sunk | while | flops 414258272 | bytes 64505212 | solution.py:99
  140.8 2.2 gather_fusion.1
  143.6 2.3 gather_fusion
  146.8 2.2 fusion.180
  149.0 5.4 fusion.183
  154.4 5.9 %fusion.181 = f32[4,1024,1,64]{1,3,0,2:T(8,128)} fusion(f32[4,128,1024]{2,1,0:T(8,128)S(1)} %fusion.179, bf16[1,4,128,1,64]{2,1,0,4,3:T(4,128)(2,1)S(1)} %constant_dynamic-slice_fusion.4, f32[4,128,1024]{2,1,0:T(8,128)} %get-tuple-element.409, f32[4,128]{1,0:T(4,128)S(1)} %get-tuple-element.410), kind=kOutput, calls=%fused_computation.19.clone.1 | convolution fusion | flops 70780416 | bytes 5310464 | tf_op jit(solution)/shard_map/while/body/eval_jaxpr/rhqk,rqhe->rkhe/dot_general | solution.py:83
  160.3 2.3 fusion.182
  166.9 4.8 scatter_fusion
  171.7 4.8 scatter_fusion.1
  177.4 2.3 gather_fusion.1
  180.2 2.2 gather_fusion
  183.4 2.2 fusion.180
  185.6 5.4 fusion.183
  191.0 5.9 %fusion.181 = f32[4,1024,1,64]{1,3,0,2:T(8,128)} fusion(f32[4,128,1024]{2,1,0:T(8,128)S(1)} %fusion.179, bf16[1,4,128,1,64]{2,1,0,4,3:T(4,128)(2,1)S(1)} %constant_dynamic-slice_fusion.4, f32[4,128,1024]{2,1,0:T(8,128)} %get-tuple-element.409, f32[4,128]{1,0:T(4,128)S(1)} %get-tuple-element.410), kind=kOutput, calls=%fused_computation.19.clone.1 | convolution fusion | flops 70780416 | bytes 5310464 | tf_op jit(solution)/shard_map/while/body/eval_jaxpr/rhqk,rqhe->rkhe/dot_general | solution.py:83
  196.9 2.3 fusion.182
  203.5 4.8 scatter_fusion
  208.3 4.8 scatter_fusion.1
  213.1 3.6 all-gather.10.cloned.1.call-done
  217.4 71.9 %while.33 = (s32[]{:T(128)}, f32[128,128,1,64]{1,3,0,2:T(8,128)}, f32[128,128,1,64]{1,3,0,2:T(8,128)}, bf16[2,4,128,1,64]{2,4,1,3,0:T(8,128)(2,1)}, bf16[2,4,128...) while((s32[]{:T(128)}, f32[128,128,1,64]{1,3,0,2:T(8,128)}, ...), condition=%wide.region_13.14_spmd, body=%wide.region_7.13_spmd.sunk | while | flops 414258272 | bytes 64505212 | solution.py:99
  218.6 2.2 gather_fusion.3
  221.3 2.2 gather_fusion.2
  224.6 2.2 fusion.195
  226.7 4.7 fusion.198
  231.4 5.9 %fusion.196 = f32[4,1024,1,64]{1,3,0,2:T(8,128)} fusion(f32[4,128,1024]{2,1,0:T(8,128)S(1)} %fusion.194, bf16[1,4,128,1,64]{2,1,0,4,3:T(4,128)(2,1)S(1)} %constant_dynamic-slice_fusion.5, f32[4,128,1024]{2,1,0:T(8,128)} %get-tuple-element.421, f32[4,128]{1,0:T(4,128)S(1)} %get-tuple-element.422), kind=kOutput, calls=%fused_computation.64.clone.1 | convolution fusion | flops 70780416 | bytes 5310464 | tf_op jit(solution)/shard_map/while/body/eval_jaxpr/rhqk,rqhe->rkhe/dot_general | solution.py:83
  237.3 2.3 fusion.197
  243.9 4.8 scatter_fusion.2
  248.7 4.8 scatter_fusion.3
  254.5 2.2 gather_fusion.3
  257.2 2.2 gather_fusion.2
  260.4 2.2 fusion.195
  262.6 4.7 fusion.198
  267.3 5.9 %fusion.196 = f32[4,1024,1,64]{1,3,0,2:T(8,128)} fusion(f32[4,128,1024]{2,1,0:T(8,128)S(1)} %fusion.194, bf16[1,4,128,1,64]{2,1,0,4,3:T(4,128)(2,1)S(1)} %constant_dynamic-slice_fusion.5, f32[4,128,1024]{2,1,0:T(8,128)} %get-tuple-element.421, f32[4,128]{1,0:T(4,128)S(1)} %get-tuple-element.422), kind=kOutput, calls=%fused_computation.64.clone.1 | convolution fusion | flops 70780416 | bytes 5310464 | tf_op jit(solution)/shard_map/while/body/eval_jaxpr/rhqk,rqhe->rkhe/dot_general | solution.py:83
  273.2 2.3 fusion.197
  279.8 4.8 scatter_fusion.2
  284.5 4.8 scatter_fusion.3
  289.3 4.0 convert_element_type.73
  293.4 4.0 convert_element_type.74
  298.7 68.4 %reduce-scatter.4.cloned.1.call-done = bf16[16,128,1,64]{1,3,0,2:T(8,128)(2,1)} async-done(((bf16[128,128,1,64]{1,3,0,2:T(8,128)(2,1)}), bf16[16,128,1,64]{1,3,0,2:T(8,128)(2,1)}) %reduce-scatter.4.cloned.1.call-update) | async-done | bytes 262160 | tf_op jit(solution)/shard_map/reduce_scatter | solution.py:119
  368.1 78.0 %reduce-scatter.6.cloned.1.call-done = bf16[16,128,1,64]{1,3,0,2:T(8,128)(2,1)} async-done(((bf16[128,128,1,64]{1,3,0,2:T(8,128)(2,1)}), bf16[16,128,1,64]{1,3,0,2:T(8,128)(2,1)}) %reduce-scatter.6.cloned.1.call-update) | async-done | bytes 262160 | tf_op jit(solution)/shard_map/reduce_scatter | solution.py:122
  447.1 4.1 convolution_bitcast_fusion.2
  451.3 71.0 %reduce-scatter.8.cloned.1.call-done = f32[128,192]{0,1:T(8,128)} async-done(((f32[1024,192]{0,1:T(8,128)}), f32[128,192]{0,1:T(8,128)}) %reduce-scatter.8.cloned.1.call-update) | async-done | bytes 98320 | tf_op jit(solution)/shard_map/reduce_scatter | solution.py:144
  523.4 11.5 %reduce.12 = bf16[2048,64]{1,0:T(8,128)(2,1)S(1)} reduce(bf16[2048,1,64]{2,1,0:T(2,128)(2,1)S(1)} %reshape.384, bf16[]{:T(256)} %broadcast.234), dimensions={1}, to_apply=%reshape.384.reduce_sub_computation | reduce | bytes 524290 | tf_op jit(solution)/shard_map/reshape | solution.py:111
  535.0 1.1 reshape.385
  536.1 7.0 %all-to-all-start.1 = ((bf16[16,2,4096]{2,1,0:T(2,128)(2,1)}), bf16[16,2,4096]{2,1,0:T(2,128)(2,1)S(1)}, u32[]{:S(2)}, u32[]{:S(2)}) async-start(bf16[16,2,4096]{2,1,0:T(2,128)(2,1)} %reshape.385), calls=%async_computation.1 | async-start | bytes 524288 | tf_op jit(solution)/shard_map/all_to_all | solution.py:110
  543.1 1.4 copy.176
  544.5 2.5 reshape.387
  546.9 3.8 all-to-all-done.1
  550.7 4.2 all-to-all-start.2
  557.1 10.5 %all-to-all-done.2 = bf16[16,2,12288]{2,1,0:T(2,128)(2,1)S(1)} async-done(((bf16[16,2,12288]{2,1,0:T(2,128)(2,1)}), bf16[16,2,12288]{2,1,0:T(2,128)(2,1)S(1)}, u32[]{:S(2)}, u32[]{:S(2)}) %all-to-all-start.2) | async-done | bytes 786464 | tf_op jit(solution)/shard_map/all_to_all | solution.py:135
  567.6 1.3 reshape.388
  568.9 1.2 copy.184
  570.1 5.7 convolution_convert_fusion.2
  575.8 3.0 copy.181
  (153 shorter events, 40.7 us)
Async XLA Ops:
  7.2 46.4 %all-gather.6.cloned.1.call-start = ((), (), s32[]{:S(2)}) async-start(), calls=%async_computation.6 | async-start | bytes 4456448 | tf_op jit(solution)/shard_map/all_gather | solution.py:27
  7.9 119.6 %all-gather.8.cloned.1.call-start = ((), (), s32[]{:S(2)}) async-start(), calls=%async_computation.7 | async-start | bytes 4718592 | tf_op jit(solution)/shard_map/all_gather | solution.py:34
  57.3 1.6 copy-start.9
  57.3 6.1 %copy-start.10 = (s32[128,8]{0,1:T(8,128)S(1)}, s32[128,8]{0,1:T(8,128)}, u32[]{:S(2)}) copy-start(s32[128,8]{0,1:T(8,128)} %param.10) | copy-start | bytes 12292
  58.2 158.6 %all-gather.10.cloned.1.call-start = ((), (), s32[]{:S(2)}) async-start(), calls=%async_computation.8 | async-start | bytes 7077888 | tf_op jit(solution)/shard_map/all_gather | solution.py:26
  59.7 10.9 %all-to-all-start = ((bf16[128,16,64]{0,2,1:T(8,128)(2,1)}), bf16[128,16,64]{0,2,1:T(8,128)(2,1)S(1)}, u32[]{:S(2)}, u32[]{:S(2)}) async-start(bf16[128,16,64]{0,2,1:T(8,128)(2,1)} %bitcast.44), calls=%async_computation | async-start | bytes 524288 | tf_op jit(solution)/shard_map/all_to_all | solution.py:38
  63.4 303.8 %reduce-scatter.4.cloned.1.call-start = ((), (), s32[]{:S(2)}) async-start(), calls=%async_computation.9 | async-start | bytes 2359296 | tf_op jit(solution)/shard_map/reduce_scatter | solution.py:119
  154.4 5.9 %copy-start.3 = (bf16[2,4,128,1,64]{2,4,1,3,0:T(8,128)(2,1)S(1)}, bf16[2,4,128,1,64]{2,4,1,3,0:T(8,128)(2,1)}, u32[]{:S(2)}) copy-start(bf16[2,4,128,1,64]{2,4,1,3,0:T(8,128)(2,1)} %get-tuple-element.437) | copy-start | bytes 393220 | tf_op jit(solution)/shard_map/while
  160.3 2.3 copy-start.11
  162.6 0.7 copy-start.4
  163.9 1.2 copy-start
  191.0 5.9 %copy-start.3 = (bf16[2,4,128,1,64]{2,4,1,3,0:T(8,128)(2,1)S(1)}, bf16[2,4,128,1,64]{2,4,1,3,0:T(8,128)(2,1)}, u32[]{:S(2)}) copy-start(bf16[2,4,128,1,64]{2,4,1,3,0:T(8,128)(2,1)} %get-tuple-element.437) | copy-start | bytes 393220 | tf_op jit(solution)/shard_map/while
  196.9 2.3 copy-start.11
  199.2 0.7 copy-start.4
  200.5 1.2 copy-start
  231.4 5.9 %copy-start.6 = (bf16[2,4,128,1,64]{2,4,1,3,0:T(8,128)(2,1)S(1)}, bf16[2,4,128,1,64]{2,4,1,3,0:T(8,128)(2,1)}, u32[]{:S(2)}) copy-start(bf16[2,4,128,1,64]{2,4,1,3,0:T(8,128)(2,1)} %get-tuple-element.470) | copy-start | bytes 393220 | tf_op jit(solution)/shard_map/while
  237.3 2.3 copy-start.12
  239.6 0.7 copy-start.7
  241.0 1.2 copy-start.1
  267.3 5.9 %copy-start.6 = (bf16[2,4,128,1,64]{2,4,1,3,0:T(8,128)(2,1)S(1)}, bf16[2,4,128,1,64]{2,4,1,3,0:T(8,128)(2,1)}, u32[]{:S(2)}) copy-start(bf16[2,4,128,1,64]{2,4,1,3,0:T(8,128)(2,1)} %get-tuple-element.470) | copy-start | bytes 393220 | tf_op jit(solution)/shard_map/while
  273.2 2.3 copy-start.12
  275.5 0.7 copy-start.7
  276.8 1.2 copy-start.1
  293.3 152.8 %reduce-scatter.6.cloned.1.call-start = ((), (), s32[]{:S(2)}) async-start(), calls=%async_computation.10 | async-start | bytes 2359296 | tf_op jit(solution)/shard_map/reduce_scatter | solution.py:122
  297.4 0.9 copy-start.2
  297.4 224.9 %reduce-scatter.8.cloned.1.call-start = ((), (), s32[]{:S(2)}) async-start(), calls=%async_computation.11 | async-start | bytes 884736 | tf_op jit(solution)/shard_map/reduce_scatter | solution.py:144
  447.1 75.2 %copy-start.5 = (bf16[2,4,128,1,64]{2,4,1,3,0:T(8,128)(2,1)S(1)}, bf16[2,4,128,1,64]{2,4,1,3,0:T(8,128)(2,1)}, u32[]{:S(2)}) copy-start(bf16[2,4,128,1,64]{2,4,1,3,0:T(8,128)(2,1)} %get-tuple-element.116) | copy-start | bytes 393220
  447.1 75.2 %copy-start.8 = (bf16[2,4,128,1,64]{2,4,1,3,0:T(8,128)(2,1)S(1)}, bf16[2,4,128,1,64]{2,4,1,3,0:T(8,128)(2,1)}, u32[]{:S(2)}) copy-start(bf16[2,4,128,1,64]{2,4,1,3,0:T(8,128)(2,1)} %get-tuple-element.121) | copy-start | bytes 393220
  451.2 124.6 %all-gather.12.cloned.1.call-start = ((), (), s32[]{:S(2)}) async-start(), calls=%async_computation.12 | async-start | bytes 1671168 | tf_op jit(solution)/shard_map/all_gather | solution.py:146
  536.1 14.7 %all-to-all-start.1 = ((bf16[16,2,4096]{2,1,0:T(2,128)(2,1)}), bf16[16,2,4096]{2,1,0:T(2,128)(2,1)S(1)}, u32[]{:S(2)}, u32[]{:S(2)}) async-start(bf16[16,2,4096]{2,1,0:T(2,128)(2,1)} %reshape.385), calls=%async_computation.1 | async-start | bytes 524288 | tf_op jit(solution)/shard_map/all_to_all | solution.py:110
  550.7 16.9 %all-to-all-start.2 = ((bf16[16,2,12288]{2,1,0:T(2,128)(2,1)}), bf16[16,2,12288]{2,1,0:T(2,128)(2,1)S(1)}, u32[]{:S(2)}, u32[]{:S(2)}) async-start(bf16[16,2,12288]{2,1,0:T(2,128)(2,1)} %reshape.387), calls=%async_computation.4 | async-start | bytes 1572864 | tf_op jit(solution)/shard_map/all_to_all | solution.py:135
Sparse Core Ops, SparseCore 0:
  9.7 43.8 all-gather.5
  58.3 69.1 all-gather.7
  129.8 86.8 all-gather.9
  293.4 73.6 reduce-scatter.3
  370.8 75.2 reduce-scatter.5
  451.4 70.8 reduce-scatter.7
  523.9 35.6 all-gather.11

commit v3 on v2

--- a/solution.py
+++ b/solution.py
@@ -115,14 +115,11 @@
         tiled=True,
     )
     attended = attended.reshape(tok_rows, seq_count * head_cols)
-    key_sum, value_sum = (
-        lax.psum_scatter(
-            key_grad.astype(jnp.bfloat16), "zero", scatter_dimension=0, tiled=True
-        ).astype(jnp.float32),
-        lax.psum_scatter(
-            value_grad.astype(jnp.bfloat16), "zero", scatter_dimension=0, tiled=True
-        ).astype(jnp.float32),
-    )
+    group_sums = jnp.stack([key_grad, value_grad], axis=1).astype(jnp.bfloat16)
+    group_sums = group_sums.reshape(zero_count, local_blocks, 2, BLOCK, head_cols)
+    group_sums = lax.all_to_all(group_sums, "zero", split_axis=0, concat_axis=0, tiled=True)
+    kv_sum = jnp.sum(group_sums.astype(jnp.float32), axis=0)
+    key_sum, value_sum = kv_sum[:, 0], kv_sum[:, 1]
     local_grads = jnp.stack(
         [
             query_grads.reshape(-1, head_cols),
@@ -141,7 +138,9 @@
     head_part = jnp.einsum(
         "td,tc->dc", group_tokens, head_grads, preferred_element_type=jnp.float32
     )
-    own_rows = lax.psum_scatter(head_part, "zero", scatter_dimension=0, tiled=True)
+    head_part = head_part.reshape(zero_count, -1, 3 * head_cols)
+    head_part = lax.all_to_all(head_part, "zero", split_axis=0, concat_axis=0, tiled=True)
+    own_rows = jnp.sum(head_part, axis=0)
     own_rows = own_rows.reshape(1, -1, 3, head_cols)
     gathered = lax.all_gather(own_rows, "seq", axis=0, tiled=True)
     weight_gradient = gathered.transpose(1, 2, 0, 3).reshape(-1, 3 * seq_count * head_cols)

time: 592 us -> 453 us (0.77)
  waiting for transfers between devices: 314 us -> 155 us
  blocking collectives: 28.7 us -> 43.4 us
    reduce_scatter x3 -> x0, waiting for transfers between devices: 217 us -> none  [the longest x1 78 us: on_device(): lax.psum_scatter(value_grad.astype(jnp.bfloat16), 'zero', scatter_dimensi...]
    all_to_all x0 -> x1, waiting for transfers between devices: none -> 57.9 us  [on_device(): lax.all_to_all(group_sums, 'zero', split_axis=0, concat_axis=0, tiled=True)]
    all_to_all x0 -> x1, blocking collectives: none -> 14.6 us  [on_device(): lax.all_to_all(head_part, 'zero', split_axis=0, concat_axis=0, tiled=True)]
    convert_element_type x2 -> x0, other arithmetic: 7.99 us -> none  [the longest x1 4 us: on_device(): value_grad.astype(jnp.bfloat16)]
    unnamed x24 -> x26, local copies, waits for them, and re-layouts: 16 us -> 13.6 us
  transfers between devices with their start and end apart: 10 -> 8, of which waited for: 9 -> 7; matrix products, arithmetic and copies ran while one was open for 21% -> 26% of each run, Pallas kernels for 0% -> 0%
where the time goes in v3:
time: 453 us; the launch traced here: 447 us
  waiting for transfers between devices  155 us (34%)
  matrix products  77.7 us (17%)
  local copies, waits for them, and re-layouts  74.7 us (16%)
  other arithmetic  59.5 us (13%)
  blocking collectives  43.4 us (10%)
  starting transfers between devices  21.2 us (5%)
  between operations  14.6 us (3%)
    all_to_all x1, waiting for transfers between devices, on_device(): lax.all_to_all(group_sums, 'zero', split_axis=0, concat_axis=0, tiled=True)  57.9 us
    all_gather x1, waiting for transfers between devices, on_device(): kv_all = lax.all_gather(by_head[:, 1:], 'zero', axis=0, tiled=True)  55.4 us
    all_gather x1, blocking collectives, on_device(): head_w = lax.all_gather(head_w, 'zero', axis=0, tiled=True)  28.7 us
    dot_general x4, matrix products, attend(): jnp.einsum('rhqk,rqhe->rkhe', score_grad, query_block, preferred_element_...  23.5 us
    dot_general x4, matrix products, attend(): jnp.einsum('rhqk,rkhe->rqhe', score_grad, key_chosen, preferred_element_t...  20.2 us
    scatter-add x4, other arithmetic, attend(): key_grad.at[slot_block]  19.2 us
    scatter-add x4, other arithmetic, attend(): value_grad.at[slot_block]  19.1 us
    all_gather x1, waiting for transfers between devices, on_device(): group_tokens = lax.all_gather(tokens, 'seq', axis=0, tiled=True)  15.4 us
  transfers between devices with their start and end apart: 8, of which 7 were waited for; matrix products, arithmetic and copies ran while one was open for 26% of the time, Pallas kernels for 0%

profile of v3, /device:TPU:1, one launch (start us, length us, event | category | flops | bytes accessed | tf_op | source)
XLA Modules:
  0.0 446.6 jit_solution(8081901964505955074)
XLA Ops:
  8.0 1.5 copy.155
  9.5 28.7 %all-gather = bf16[1024,3,1,64]{0,3,1,2:T(8,128)(2,1)S(1)} all-gather(bf16[128,3,1,64]{0,3,1,2:T(8,128)(2,1)S(1)} %dynamic-slice_bitcast_fusion), channel_id=2, replica_groups=mesh['seq'=16,'zero'=8] {'zero'}, dimensions={0}, use_global_device_ids=true | all-gather | bytes 442368 | tf_op jit(solution)/shard_map/all_gather | solution.py:30
  38.2 15.4 %all-gather.6.cloned.1.call-done = bf16[2048,1024]{1,0:T(8,128)(2,1)} async-done(((bf16[128,1024]{1,0:T(8,128)(2,1)}), bf16[2048,1024]{1,0:T(8,128)(2,1)}) %all-gather.6.cloned.1.call-update) | async-done | bytes 4194320 | tf_op jit(solution)/shard_map/all_gather | solution.py:27
  53.6 3.7 fusion.113
  59.7 3.6 all-to-all-start
  64.1 6.5 %all-to-all-done = bf16[128,16,64]{0,2,1:T(8,128)(2,1)S(1)} async-done(((bf16[128,16,64]{0,2,1:T(8,128)(2,1)}), bf16[128,16,64]{0,2,1:T(8,128)(2,1)S(1)}, u32[]{:S(2)}, u32[]{:S(2)}) %all-to-all-start) | async-done | bytes 262176 | tf_op jit(solution)/shard_map/all_to_all | solution.py:38
  72.1 55.4 %all-gather.8.cloned.1.call-done = bf16[16384,2,64]{0,2,1:T(8,128)(2,1)} async-done(((bf16[2048,2,64]{0,2,1:T(8,128)(2,1)}), bf16[16384,2,64]{0,2,1:T(8,128)(2,1)}) %all-gather.8.cloned.1.call-update) | async-done | bytes 4194320 | tf_op jit(solution)/shard_map/all_gather | solution.py:34
  127.5 2.5 slice_bitcast_fusion
  130.0 3.2 copy_bitcast_fusion.14
  134.6 2.5 broadcast_in_dim.22.clone
  137.1 2.6 broadcast_in_dim.22
  139.7 73.5 %while.32 = (s32[]{:T(128)}, f32[128,128,1,64]{1,3,0,2:T(8,128)}, f32[128,128,1,64]{1,3,0,2:T(8,128)}, bf16[2,4,128,1,64]{2,4,1,3,0:T(8,128)(2,1)}, bf16[2,4,128...) while((s32[]{:T(128)}, f32[128,128,1,64]{1,3,0,2:T(8,128)}, ...), condition=%wide.region_6.7_spmd, body=%wide.region_0.6_spmd.sunk | while | flops 414258272 | bytes 64505212 | solution.py:99
  140.9 2.2 gather_fusion.1
  143.6 2.3 gather_fusion
  146.9 2.2 fusion.179
  149.0 5.4 %fusion.182 = bf16[2,4,128,1,64]{2,4,1,3,0:T(8,128)(2,1)} fusion(bf16[2,4,128,1,64]{2,4,1,3,0:T(8,128)(2,1)} %get-tuple-element.440, s32[]{:T(128)S(6)} %copy.310, f32[4,128,1024]{2,1,0:T(8,128)S(1)} %fusion.178, bf16[4,1024,64]{1,0,2:T(4,128)(2,1)S(1)} %reshape.467, f32[4,128,1024]{2,1,0:T(8,128)} %get-tuple-element.411, ...), kind=kOutput, calls=%fused_computation.26.clone.1 | convolution fusion | flops 70813184 | bytes 8982532 | tf_op jit(solution)/shard_map/while/body/eval_jaxpr/rhqk,rkhe->rqhe/dot_general | solution.py:80
  154.5 5.9 %fusion.180 = f32[4,1024,1,64]{1,3,0,2:T(8,128)} fusion(f32[4,128,1024]{2,1,0:T(8,128)S(1)} %fusion.178, bf16[1,4,128,1,64]{2,1,0,4,3:T(4,128)(2,1)S(1)} %constant_dynamic-slice_fusion.4, f32[4,128,1024]{2,1,0:T(8,128)} %get-tuple-element.411, f32[4,128]{1,0:T(4,128)S(1)} %get-tuple-element.412), kind=kOutput, calls=%fused_computation.19.clone.1 | convolution fusion | flops 70780416 | bytes 5310464 | tf_op jit(solution)/shard_map/while/body/eval_jaxpr/rhqk,rqhe->rkhe/dot_general | solution.py:83
  160.3 2.3 fusion.181
  166.9 4.8 %scatter_fusion = f32[128,128,64]{1,2,0:T(8,128)} fusion(f32[128,128,64]{1,2,0:T(8,128)} %bitcast.267, s32[32]{0:T(128)S(1)} %reshape.465, f32[32,128,64]{1,2,0:T(8,128)S(1)} %copy.282), kind=kCustom, calls=%fused_computation.5.clone.1 | custom fusion | flops 262144 | bytes 3145856 | tf_op jit(solution)/shard_map/while/body/eval_jaxpr/scatter-add | solution.py:89
  171.7 4.8 %scatter_fusion.1 = f32[128,128,64]{1,2,0:T(8,128)} fusion(f32[128,128,64]{1,2,0:T(8,128)} %bitcast.263, s32[32]{0:T(128)S(1)} %reshape.465, f32[32,128,64]{1,2,0:T(8,128)S(1)} %copy.284), kind=kCustom, calls=%fused_computation.6.clone.1 | custom fusion | flops 262144 | bytes 3145856 | tf_op jit(solution)/shard_map/while/body/eval_jaxpr/scatter-add | solution.py:92
  177.5 2.3 gather_fusion.1
  180.2 2.2 gather_fusion
  183.5 2.2 fusion.179
  185.6 5.4 %fusion.182 = bf16[2,4,128,1,64]{2,4,1,3,0:T(8,128)(2,1)} fusion(bf16[2,4,128,1,64]{2,4,1,3,0:T(8,128)(2,1)} %get-tuple-element.440, s32[]{:T(128)S(6)} %copy.310, f32[4,128,1024]{2,1,0:T(8,128)S(1)} %fusion.178, bf16[4,1024,64]{1,0,2:T(4,128)(2,1)S(1)} %reshape.467, f32[4,128,1024]{2,1,0:T(8,128)} %get-tuple-element.411, ...), kind=kOutput, calls=%fused_computation.26.clone.1 | convolution fusion | flops 70813184 | bytes 8982532 | tf_op jit(solution)/shard_map/while/body/eval_jaxpr/rhqk,rkhe->rqhe/dot_general | solution.py:80
  191.1 5.9 %fusion.180 = f32[4,1024,1,64]{1,3,0,2:T(8,128)} fusion(f32[4,128,1024]{2,1,0:T(8,128)S(1)} %fusion.178, bf16[1,4,128,1,64]{2,1,0,4,3:T(4,128)(2,1)S(1)} %constant_dynamic-slice_fusion.4, f32[4,128,1024]{2,1,0:T(8,128)} %get-tuple-element.411, f32[4,128]{1,0:T(4,128)S(1)} %get-tuple-element.412), kind=kOutput, calls=%fused_computation.19.clone.1 | convolution fusion | flops 70780416 | bytes 5310464 | tf_op jit(solution)/shard_map/while/body/eval_jaxpr/rhqk,rqhe->rkhe/dot_general | solution.py:83
  196.9 2.3 fusion.181
  203.5 4.8 %scatter_fusion = f32[128,128,64]{1,2,0:T(8,128)} fusion(f32[128,128,64]{1,2,0:T(8,128)} %bitcast.267, s32[32]{0:T(128)S(1)} %reshape.465, f32[32,128,64]{1,2,0:T(8,128)S(1)} %copy.282), kind=kCustom, calls=%fused_computation.5.clone.1 | custom fusion | flops 262144 | bytes 3145856 | tf_op jit(solution)/shard_map/while/body/eval_jaxpr/scatter-add | solution.py:89
  208.4 4.8 %scatter_fusion.1 = f32[128,128,64]{1,2,0:T(8,128)} fusion(f32[128,128,64]{1,2,0:T(8,128)} %bitcast.263, s32[32]{0:T(128)S(1)} %reshape.465, f32[32,128,64]{1,2,0:T(8,128)S(1)} %copy.284), kind=kCustom, calls=%fused_computation.6.clone.1 | custom fusion | flops 262144 | bytes 3145856 | tf_op jit(solution)/shard_map/while/body/eval_jaxpr/scatter-add | solution.py:92
  213.2 3.6 all-gather.10.cloned.1.call-done
  217.4 71.9 %while.33 = (s32[]{:T(128)}, f32[128,128,1,64]{1,3,0,2:T(8,128)}, f32[128,128,1,64]{1,3,0,2:T(8,128)}, bf16[2,4,128,1,64]{2,4,1,3,0:T(8,128)(2,1)}, bf16[2,4,128...) while((s32[]{:T(128)}, f32[128,128,1,64]{1,3,0,2:T(8,128)}, ...), condition=%wide.region_13.14_spmd, body=%wide.region_7.13_spmd.sunk | while | flops 414258272 | bytes 64505212 | solution.py:99
  218.6 2.2 gather_fusion.3
  221.3 2.2 gather_fusion.2
  224.6 2.2 fusion.194
  226.8 4.7 %fusion.197 = bf16[2,4,128,1,64]{2,4,1,3,0:T(8,128)(2,1)S(1)} fusion(bf16[2,4,128,1,64]{2,4,1,3,0:T(8,128)(2,1)S(1)} %get-tuple-element.473, s32[]{:T(128)S(6)} %copy.325, f32[4,128,1024]{2,1,0:T(8,128)S(1)} %fusion.193, bf16[4,1024,64]{1,0,2:T(4,128)(2,1)S(1)} %reshape.480, f32[4,128,1024]{2,1,0:T(8,128)} %get-tuple-element.423, ...), kind=kOutput, calls=%fused_computation.71.clone.1 | convolution fusion | flops 70813184 | bytes 8982532 | tf_op jit(solution)/shard_map/while/body/eval_jaxpr/rhqk,rkhe->rqhe/dot_general | solution.py:80
  231.5 5.9 %fusion.195 = f32[4,1024,1,64]{1,3,0,2:T(8,128)} fusion(f32[4,128,1024]{2,1,0:T(8,128)S(1)} %fusion.193, bf16[1,4,128,1,64]{2,1,0,4,3:T(4,128)(2,1)S(1)} %constant_dynamic-slice_fusion.5, f32[4,128,1024]{2,1,0:T(8,128)} %get-tuple-element.423, f32[4,128]{1,0:T(4,128)S(1)} %get-tuple-element.424), kind=kOutput, calls=%fused_computation.64.clone.1 | convolution fusion | flops 70780416 | bytes 5310464 | tf_op jit(solution)/shard_map/while/body/eval_jaxpr/rhqk,rqhe->rkhe/dot_general | solution.py:83
  237.3 2.3 fusion.196
  243.9 4.8 %scatter_fusion.2 = f32[128,128,64]{1,2,0:T(8,128)} fusion(f32[128,128,64]{1,2,0:T(8,128)} %bitcast.269, s32[32]{0:T(128)S(1)} %reshape.478, f32[32,128,64]{1,2,0:T(8,128)S(1)} %copy.294), kind=kCustom, calls=%fused_computation.7.clone.1 | custom fusion | flops 262144 | bytes 3145856 | tf_op jit(solution)/shard_map/while/body/eval_jaxpr/scatter-add | solution.py:89
  248.7 4.8 %scatter_fusion.3 = f32[128,128,64]{1,2,0:T(8,128)} fusion(f32[128,128,64]{1,2,0:T(8,128)} %bitcast.265, s32[32]{0:T(128)S(1)} %reshape.478, f32[32,128,64]{1,2,0:T(8,128)S(1)} %copy.296), kind=kCustom, calls=%fused_computation.8.clone.1 | custom fusion | flops 262144 | bytes 3145856 | tf_op jit(solution)/shard_map/while/body/eval_jaxpr/scatter-add | solution.py:92
  254.4 2.2 gather_fusion.3
  257.2 2.2 gather_fusion.2
  260.4 2.2 fusion.194
  262.6 4.7 %fusion.197 = bf16[2,4,128,1,64]{2,4,1,3,0:T(8,128)(2,1)S(1)} fusion(bf16[2,4,128,1,64]{2,4,1,3,0:T(8,128)(2,1)S(1)} %get-tuple-element.473, s32[]{:T(128)S(6)} %copy.325, f32[4,128,1024]{2,1,0:T(8,128)S(1)} %fusion.193, bf16[4,1024,64]{1,0,2:T(4,128)(2,1)S(1)} %reshape.480, f32[4,128,1024]{2,1,0:T(8,128)} %get-tuple-element.423, ...), kind=kOutput, calls=%fused_computation.71.clone.1 | convolution fusion | flops 70813184 | bytes 8982532 | tf_op jit(solution)/shard_map/while/body/eval_jaxpr/rhqk,rkhe->rqhe/dot_general | solution.py:80
  267.3 5.9 %fusion.195 = f32[4,1024,1,64]{1,3,0,2:T(8,128)} fusion(f32[4,128,1024]{2,1,0:T(8,128)S(1)} %fusion.193, bf16[1,4,128,1,64]{2,1,0,4,3:T(4,128)(2,1)S(1)} %constant_dynamic-slice_fusion.5, f32[4,128,1024]{2,1,0:T(8,128)} %get-tuple-element.423, f32[4,128]{1,0:T(4,128)S(1)} %get-tuple-element.424), kind=kOutput, calls=%fused_computation.64.clone.1 | convolution fusion | flops 70780416 | bytes 5310464 | tf_op jit(solution)/shard_map/while/body/eval_jaxpr/rhqk,rqhe->rkhe/dot_general | solution.py:83
  273.2 2.3 fusion.196
  279.8 4.8 %scatter_fusion.2 = f32[128,128,64]{1,2,0:T(8,128)} fusion(f32[128,128,64]{1,2,0:T(8,128)} %bitcast.269, s32[32]{0:T(128)S(1)} %reshape.478, f32[32,128,64]{1,2,0:T(8,128)S(1)} %copy.294), kind=kCustom, calls=%fused_computation.7.clone.1 | custom fusion | flops 262144 | bytes 3145856 | tf_op jit(solution)/shard_map/while/body/eval_jaxpr/scatter-add | solution.py:89
  284.6 4.8 %scatter_fusion.3 = f32[128,128,64]{1,2,0:T(8,128)} fusion(f32[128,128,64]{1,2,0:T(8,128)} %bitcast.265, s32[32]{0:T(128)S(1)} %reshape.478, f32[32,128,64]{1,2,0:T(8,128)S(1)} %copy.296), kind=kCustom, calls=%fused_computation.8.clone.1 | custom fusion | flops 262144 | bytes 3145856 | tf_op jit(solution)/shard_map/while/body/eval_jaxpr/scatter-add | solution.py:92
  289.3 2.8 convert.12
  293.3 2.3 pad_maximum_fusion
  295.6 4.7 %all-to-all-start.2 = ((bf16[8,16,2,128,64]{3,4,1,2,0:T(8,128)(2,1)}), bf16[8,16,2,128,64]{3,4,1,2,0:T(8,128)(2,1)}, u32[]{:S(2)}, u32[]{:S(2)}) async-start(bf16[8,16,2,128,64]{3,4,1,2,0:T(8,128)(2,1)} %pad_maximum_fusion), calls=%async_computation.2 | async-start | bytes 8388608 | tf_op jit(solution)/shard_map/all_to_all | solution.py:120
  301.1 57.9 %all-to-all-done.2 = bf16[8,16,2,128,64]{3,4,1,2,0:T(8,128)(2,1)} async-done(((bf16[8,16,2,128,64]{3,4,1,2,0:T(8,128)(2,1)}), bf16[8,16,2,128,64]{3,4,1,2,0:T(8,128)(2,1)}, u32[]{:S(2)}, u32[]{:S(2)}) %all-to-all-start.2) | async-done | bytes 4194336 | tf_op jit(solution)/shard_map/all_to_all | solution.py:120
  359.1 3.1 reduce.12
  362.9 3.2 convolution_bitcast_fusion.2
  366.1 14.6 %all_to_all.55 = f32[8,128,192]{1,2,0:T(8,128)S(1)} all-to-all(f32[8,128,192]{1,2,0:T(8,128)S(1)} %bitcast.279), channel_id=1, replica_groups=mesh['seq'=16,'zero'=8] {'zero'}, dimensions={0} | all-to-all | bytes 1572864 | tf_op jit(solution)/shard_map/all_to_all | solution.py:142
  382.6 11.5 %reduce.13 = bf16[2048,64]{1,0:T(8,128)(2,1)S(1)} reduce(bf16[2048,1,64]{2,1,0:T(2,128)(2,1)S(1)} %reshape.426, bf16[]{:T(256)} %broadcast.234), dimensions={1}, to_apply=%reshape.426.reduce_sub_computation | reduce | bytes 524290 | tf_op jit(solution)/shard_map/reshape | solution.py:111
  395.2 8.2 %all-to-all-start.1 = ((bf16[16,2,4096]{2,1,0:T(2,128)(2,1)}), bf16[16,2,4096]{2,1,0:T(2,128)(2,1)S(1)}, u32[]{:S(2)}, u32[]{:S(2)}) async-start(bf16[16,2,4096]{2,1,0:T(2,128)(2,1)} %reshape.427), calls=%async_computation.1 | async-start | bytes 524288 | tf_op jit(solution)/shard_map/all_to_all | solution.py:110
  403.4 1.4 copy.174
  404.8 2.5 reshape.429
  407.3 4.0 all-to-all-done.1
  411.3 4.3 all-to-all-start.3
  417.8 10.5 %all-to-all-done.3 = bf16[16,2,12288]{2,1,0:T(2,128)(2,1)S(1)} async-done(((bf16[16,2,12288]{2,1,0:T(2,128)(2,1)}), bf16[16,2,12288]{2,1,0:T(2,128)(2,1)S(1)}, u32[]{:S(2)}, u32[]{:S(2)}) %all-to-all-start.3) | async-done | bytes 786464 | tf_op jit(solution)/shard_map/all_to_all | solution.py:132
  428.3 1.3 reshape.430
  430.8 5.7 %convolution_convert_fusion.2 = bf16[128,1024]{1,0:T(8,128)(2,1)} fusion(bf16[128,3072]{0,1:T(8,128)(2,1)S(1)} %bitcast.278, bf16[1024,3072]{1,0:T(8,128)(2,1)} %all-gather.10.cloned.1.call-done), kind=kOutput, calls=%fused_computation.109 | convolution fusion | flops 805437440 | bytes 7340032 | tf_op jit(solution)/shard_map/tc,dc->td/dot_general | solution.py:134
  436.5 1.5 copy.178
  438.0 1.6 copy.180
  (159 shorter events, 42.7 us)
Async XLA Ops:
  7.2 46.4 %all-gather.6.cloned.1.call-start = ((), (), s32[]{:S(2)}) async-start(), calls=%async_computation.5 | async-start | bytes 4456448 | tf_op jit(solution)/shard_map/all_gather | solution.py:27
  7.9 119.6 %all-gather.8.cloned.1.call-start = ((), (), s32[]{:S(2)}) async-start(), calls=%async_computation.6 | async-start | bytes 4718592 | tf_op jit(solution)/shard_map/all_gather | solution.py:34
  57.3 1.6 copy-start.10
  57.3 6.1 %copy-start.11 = (s32[128,8]{0,1:T(8,128)S(1)}, s32[128,8]{0,1:T(8,128)}, u32[]{:S(2)}) copy-start(s32[128,8]{0,1:T(8,128)} %param.10) | copy-start | bytes 12292
  58.2 158.6 %all-gather.10.cloned.1.call-start = ((), (), s32[]{:S(2)}) async-start(), calls=%async_computation.7 | async-start | bytes 7077888 | tf_op jit(solution)/shard_map/all_gather | solution.py:26
  59.7 10.9 %all-to-all-start = ((bf16[128,16,64]{0,2,1:T(8,128)(2,1)}), bf16[128,16,64]{0,2,1:T(8,128)(2,1)S(1)}, u32[]{:S(2)}, u32[]{:S(2)}) async-start(bf16[128,16,64]{0,2,1:T(8,128)(2,1)} %bitcast.44), calls=%async_computation | async-start | bytes 524288 | tf_op jit(solution)/shard_map/all_to_all | solution.py:38
  154.5 5.9 %copy-start.4 = (bf16[2,4,128,1,64]{2,4,1,3,0:T(8,128)(2,1)S(1)}, bf16[2,4,128,1,64]{2,4,1,3,0:T(8,128)(2,1)}, u32[]{:S(2)}) copy-start(bf16[2,4,128,1,64]{2,4,1,3,0:T(8,128)(2,1)} %get-tuple-element.439) | copy-start | bytes 393220 | tf_op jit(solution)/shard_map/while
  160.3 2.3 copy-start.12
  162.7 0.7 copy-start.5
  164.0 1.2 copy-start.1
  191.1 5.9 %copy-start.4 = (bf16[2,4,128,1,64]{2,4,1,3,0:T(8,128)(2,1)S(1)}, bf16[2,4,128,1,64]{2,4,1,3,0:T(8,128)(2,1)}, u32[]{:S(2)}) copy-start(bf16[2,4,128,1,64]{2,4,1,3,0:T(8,128)(2,1)} %get-tuple-element.439) | copy-start | bytes 393220 | tf_op jit(solution)/shard_map/while
  196.9 2.3 copy-start.12
  199.3 0.7 copy-start.5
  200.6 1.2 copy-start.1
  231.4 5.9 %copy-start.7 = (bf16[2,4,128,1,64]{2,4,1,3,0:T(8,128)(2,1)S(1)}, bf16[2,4,128,1,64]{2,4,1,3,0:T(8,128)(2,1)}, u32[]{:S(2)}) copy-start(bf16[2,4,128,1,64]{2,4,1,3,0:T(8,128)(2,1)} %get-tuple-element.472) | copy-start | bytes 393220 | tf_op jit(solution)/shard_map/while
  237.3 2.3 copy-start.13
  239.7 0.6 copy-start.8
  241.0 1.2 copy-start.2
  267.3 5.9 %copy-start.7 = (bf16[2,4,128,1,64]{2,4,1,3,0:T(8,128)(2,1)S(1)}, bf16[2,4,128,1,64]{2,4,1,3,0:T(8,128)(2,1)}, u32[]{:S(2)}) copy-start(bf16[2,4,128,1,64]{2,4,1,3,0:T(8,128)(2,1)} %get-tuple-element.472) | copy-start | bytes 393220 | tf_op jit(solution)/shard_map/while
  273.2 2.3 copy-start.13
  275.5 0.6 copy-start.8
  276.8 1.2 copy-start.2
  289.3 3.4 copy-start
  295.6 5.0 %copy-start.3 = (bf16[2,4,128,1,64]{2,4,1,3,0:T(8,128)(2,1)S(1)}, bf16[2,4,128,1,64]{2,4,1,3,0:T(8,128)(2,1)}, u32[]{:S(2)}) copy-start(bf16[2,4,128,1,64]{2,4,1,3,0:T(8,128)(2,1)} %get-tuple-element.122) | copy-start | bytes 393220
  295.6 63.4 %all-to-all-start.2 = ((bf16[8,16,2,128,64]{3,4,1,2,0:T(8,128)(2,1)}), bf16[8,16,2,128,64]{3,4,1,2,0:T(8,128)(2,1)}, u32[]{:S(2)}, u32[]{:S(2)}) async-start(bf16[8,16,2,128,64]{3,4,1,2,0:T(8,128)(2,1)} %pad_maximum_fusion), calls=%async_computation.2 | async-start | bytes 8388608 | tf_op jit(solution)/shard_map/all_to_all | solution.py:120
  300.4 136.1 %all-gather.12.cloned.1.call-start = ((), (), s32[]{:S(2)}) async-start(), calls=%async_computation.8 | async-start | bytes 1671168 | tf_op jit(solution)/shard_map/all_gather | solution.py:145
  366.0 15.4 %copy-start.6 = (bf16[2,4,128,1,64]{2,4,1,3,0:T(8,128)(2,1)S(1)}, bf16[2,4,128,1,64]{2,4,1,3,0:T(8,128)(2,1)}, u32[]{:S(2)}) copy-start(bf16[2,4,128,1,64]{2,4,1,3,0:T(8,128)(2,1)} %get-tuple-element.116) | copy-start | bytes 393220
  366.1 15.4 %copy-start.9 = (bf16[2,4,128,1,64]{2,4,1,3,0:T(8,128)(2,1)S(1)}, bf16[2,4,128,1,64]{2,4,1,3,0:T(8,128)(2,1)}, u32[]{:S(2)}) copy-start(bf16[2,4,128,1,64]{2,4,1,3,0:T(8,128)(2,1)} %get-tuple-element.121) | copy-start | bytes 393220
  395.2 16.1 %all-to-all-start.1 = ((bf16[16,2,4096]{2,1,0:T(2,128)(2,1)}), bf16[16,2,4096]{2,1,0:T(2,128)(2,1)S(1)}, u32[]{:S(2)}, u32[]{:S(2)}) async-start(bf16[16,2,4096]{2,1,0:T(2,128)(2,1)} %reshape.427), calls=%async_computation.1 | async-start | bytes 524288 | tf_op jit(solution)/shard_map/all_to_all | solution.py:110
  411.3 17.0 %all-to-all-start.3 = ((bf16[16,2,12288]{2,1,0:T(2,128)(2,1)}), bf16[16,2,12288]{2,1,0:T(2,128)(2,1)S(1)}, u32[]{:S(2)}, u32[]{:S(2)}) async-start(bf16[16,2,12288]{2,1,0:T(2,128)(2,1)} %reshape.429), calls=%async_computation.3 | async-start | bytes 1572864 | tf_op jit(solution)/shard_map/all_to_all | solution.py:132
Sparse Core Ops, SparseCore 0:
  9.7 43.8 all-gather.5
  58.3 69.1 all-gather.7
  129.8 86.8 all-gather.9
  381.6 35.8 all-gather.11

commit v4 on v3

--- a/solution.py
+++ b/solution.py
@@ -1,12 +1,72 @@
+import functools
 import jax
 import jax.numpy as jnp
 from jax import lax
 from jax.sharding import PartitionSpec as P
+from jax.experimental import pallas as pl
+from jax.experimental.pallas import tpu as pltpu
 
 HEADS = 16
 HEAD = 64
 BLOCK = 128
 NBK = 8
+
+
+def _attn_kernel(slots_ref, q_ref, up_ref, k_ref, v_ref, out_ref, qg_ref, kg_ref, vg_ref, *, scale):
+    i = pl.program_id(0)
+
+    @pl.when(i == 0)
+    def _():
+        kg_ref[...] = jnp.zeros(kg_ref.shape, kg_ref.dtype)
+        vg_ref[...] = jnp.zeros(vg_ref.shape, vg_ref.dtype)
+
+    q = q_ref[0]
+    up = up_ref[0]
+    ids = [slots_ref[i, j] for j in range(NBK)]
+    keys = jnp.concatenate([k_ref[ids[j]] for j in range(NBK)], axis=0)
+    vals = jnp.concatenate([v_ref[ids[j]] for j in range(NBK)], axis=0)
+    nt = (((1,), (1,)), ((), ()))
+    tn = (((0,), (0,)), ((), ()))
+    scores = lax.dot_general(q, keys, nt, preferred_element_type=jnp.float32) * scale
+    row_max = jnp.max(scores, axis=-1, keepdims=True)
+    exponent = jnp.exp(scores - row_max)
+    prob_full = exponent / jnp.sum(exponent, axis=-1, keepdims=True)
+    prob_low = prob_full.astype(jnp.bfloat16)
+    out_ref[0] = jnp.dot(prob_low, vals, preferred_element_type=jnp.float32).astype(out_ref.dtype)
+    prob_grad = lax.dot_general(up, vals, nt, preferred_element_type=jnp.float32)
+    row_delta = jnp.sum(prob_full * prob_grad, axis=-1, keepdims=True)
+    score_grad = (prob_full * (prob_grad - row_delta) * scale).astype(jnp.bfloat16)
+    qg_ref[0] = jnp.dot(score_grad, keys, preferred_element_type=jnp.float32).astype(qg_ref.dtype)
+    key_terms = lax.dot_general(score_grad, q, tn, preferred_element_type=jnp.float32)
+    value_terms = lax.dot_general(prob_low, up, tn, preferred_element_type=jnp.float32)
+    for j in range(NBK):
+        kg_ref[ids[j]] += key_terms[j * BLOCK:(j + 1) * BLOCK]
+        vg_ref[ids[j]] += value_terms[j * BLOCK:(j + 1) * BLOCK]
+
+
+def block_attention(slots, queries, upstream, keys, values, scale):
+    rows = queries.shape[0]
+    slot_count = keys.shape[0]
+    row_spec = pl.BlockSpec((1, BLOCK, HEAD), lambda i, s: (i, 0, 0))
+    full_spec = pl.BlockSpec((slot_count, BLOCK, HEAD), lambda i, s: (0, 0, 0))
+    grid_spec = pltpu.PrefetchScalarGridSpec(
+        num_scalar_prefetch=1,
+        grid=(rows,),
+        in_specs=[row_spec, row_spec, full_spec, full_spec],
+        out_specs=[row_spec, row_spec, full_spec, full_spec],
+    )
+    out_shape = [
+        jax.ShapeDtypeStruct((rows, BLOCK, HEAD), jnp.bfloat16),
+        jax.ShapeDtypeStruct((rows, BLOCK, HEAD), jnp.bfloat16),
+        jax.ShapeDtypeStruct((slot_count, BLOCK, HEAD), jnp.float32),
+        jax.ShapeDtypeStruct((slot_count, BLOCK, HEAD), jnp.float32),
+    ]
+    return pl.pallas_call(
+        functools.partial(_attn_kernel, scale=scale),
+        grid_spec=grid_spec,
+        out_shape=out_shape,
+        compiler_params=pltpu.CompilerParams(dimension_semantics=("arbitrary",), vmem_limit_bytes=48 * 1024 * 1024),
+    )(slots, queries, upstream, keys, values)
 
 
 def on_device(tokens, projection, pattern, upstream):
@@ -54,59 +114,14 @@
     )
     key_slots = key_slots.reshape(step_count, group_size, NBK)
 
-    def attend(carried, inputs):
-        key_grad, value_grad = carried
-        query_block, up_block, slot_block = inputs
-        key_chosen = key_all[slot_block].reshape(group_size, NBK * BLOCK, heads_here, HEAD)
-        value_chosen = value_all[slot_block].reshape(group_size, NBK * BLOCK, heads_here, HEAD)
-        scores = (
-            jnp.einsum(
-                "rqhe,rkhe->rhqk", query_block, key_chosen, preferred_element_type=jnp.float32
-            )
-            * score_scale
-        )
-        row_max = jnp.max(scores, axis=-1, keepdims=True)
-        exponent = jnp.exp(scores - row_max)
-        prob_full = exponent / jnp.sum(exponent, axis=-1, keepdims=True)
-        prob_low = prob_full.astype(jnp.bfloat16)
-        out_block = jnp.einsum(
-            "rhqk,rkhe->rqhe", prob_low, value_chosen, preferred_element_type=jnp.float32
-        ).astype(jnp.bfloat16)
-        prob_grad = jnp.einsum(
-            "rqhe,rkhe->rhqk", up_block, value_chosen, preferred_element_type=jnp.float32
-        )
-        row_delta = jnp.sum(prob_full * prob_grad, axis=-1, keepdims=True)
-        score_grad = (prob_full * (prob_grad - row_delta) * score_scale).astype(jnp.bfloat16)
-        query_grad = jnp.einsum(
-            "rhqk,rkhe->rqhe", score_grad, key_chosen, preferred_element_type=jnp.float32
-        ).astype(jnp.bfloat16)
-        key_terms = jnp.einsum(
-            "rhqk,rqhe->rkhe", score_grad, query_block, preferred_element_type=jnp.float32
-        )
-        value_terms = jnp.einsum(
-            "rhqk,rqhe->rkhe", prob_low, up_block, preferred_element_type=jnp.float32
-        )
-        key_grad = key_grad.at[slot_block].add(
-            key_terms.reshape(group_size, NBK, BLOCK, heads_here, HEAD)
-        )
-        value_grad = value_grad.at[slot_block].add(
-            value_terms.reshape(group_size, NBK, BLOCK, heads_here, HEAD)
-        )
-        return ((key_grad, value_grad), (out_block, query_grad))
-
-    zero_start = jnp.zeros((zero_count * local_blocks, BLOCK, heads_here, HEAD), jnp.float32)
-    half = step_count // 2
-    carried, (out_a, query_a) = lax.scan(
-        attend,
-        (zero_start, zero_start),
-        (queries[:half], incoming[:half], key_slots[:half]),
+    out_blocks, query_grads, key_grad, value_grad = block_attention(
+        key_slots.reshape(local_blocks, NBK),
+        queries.reshape(local_blocks, BLOCK, head_cols),
+        incoming.reshape(local_blocks, BLOCK, head_cols),
+        key_all.reshape(-1, BLOCK, head_cols),
+        value_all.reshape(-1, BLOCK, head_cols),
+        score_scale,
     )
-    weights, carried = lax.optimization_barrier((weights, carried))
-    (key_grad, value_grad), (out_b, query_b) = lax.scan(
-        attend, carried, (queries[half:], incoming[half:], key_slots[half:])
-    )
-    out_blocks = jnp.concatenate([out_a, out_b], axis=0)
-    query_grads = jnp.concatenate([query_a, query_b], axis=0)
     attended = lax.all_to_all(
         out_blocks.reshape(local_blocks * BLOCK, 1, head_cols),
         "seq",

time: 453 us -> 350 us (0.77); the launches traced: 447 us -> 349 us
  matrix products: 77.7 us -> 12.6 us
  other arithmetic: 59.5 us -> 21.7 us
  local copies, waits for them, and re-layouts: 74.7 us -> 41.5 us
  Pallas kernels: 0 us -> 29.4 us
  blocking collectives: 43.4 us -> 55.2 us
    dot_general x20 -> x0, matrix products: 56.4 us -> none  [the longest x4 23.5 us: attend(): jnp.einsum('rhqk,rqhe->rkhe', score_grad, query_block, preferred_element_...]
    scatter-add x8 -> x0, other arithmetic: 38.3 us -> none  [the longest x4 19.2 us: attend(): key_grad.at[slot_block]]
    pallas_call x0 -> x1, Pallas kernels: none -> 29.4 us  [block_attention(): pl.pallas_call(functools.partial(_attn_kernel, scale=scale), grid_spec=gr...]
    gather x16 -> x0, local copies, waits for them, and re-layouts: 20.7 us -> none  [the longest x8 10.4 us: attend(): value_all[slot_block].reshape(group_size, NBK * BLOCK, heads_here, HEAD)]
    slice x5, local copies, waits for them, and re-layouts: 1.48 us -> 14.4 us  [the longest x2 9.4 us: on_device(): kv_all[:, 1].reshape(zero_count * local_blocks, BLOCK, heads_here, HEAD)]
    all_to_all x1, blocking collectives: 14.6 us -> 26.5 us  [on_device(): lax.all_to_all(head_part, 'zero', split_axis=0, concat_axis=0, tiled=True)]
    reshape x1, other arithmetic: 11.5 us -> 1.11 us  [on_device(): out_blocks.reshape(local_blocks * BLOCK, 1, head_cols)]
    another operation x2 -> x3, other arithmetic: 3.34 us -> 12.9 us
  transfers between devices with their start and end apart: 8 -> 8, of which waited for: 7 -> 6; matrix products, arithmetic and copies ran while one was open for 26% -> 20% of each run, Pallas kernels for 0% -> 8%
where the time goes in v4:
time: 350 us; the launch traced here: 349 us
  waiting for transfers between devices  155 us (44%)
  blocking collectives  55.2 us (16%)
  local copies, waits for them, and re-layouts  41.5 us (12%)
  Pallas kernels  29.4 us (8%)
  other arithmetic  21.7 us (6%)
  starting transfers between devices  19.2 us (5%)
  between operations  14 us (4%)
  matrix products  12.6 us (4%)
    all_to_all x1, waiting for transfers between devices, on_device(): lax.all_to_all(group_sums, 'zero', split_axis=0, concat_axis=0, tiled=True)  59.9 us
    all_gather x1, waiting for transfers between devices, on_device(): kv_all = lax.all_gather(by_head[:, 1:], 'zero', axis=0, tiled=True)  56.3 us
    pallas_call x1, Pallas kernels, block_attention(): pl.pallas_call(functools.partial(_attn_kernel, scale=scale), grid_spec=gr...  29.4 us
    all_gather x1, blocking collectives, on_device(): head_w = lax.all_gather(head_w, 'zero', axis=0, tiled=True)  28.7 us
    all_to_all x1, blocking collectives, on_device(): lax.all_to_all(head_part, 'zero', split_axis=0, concat_axis=0, tiled=True)  26.5 us
    all_gather x1, waiting for transfers between devices, on_device(): group_tokens = lax.all_gather(tokens, 'seq', axis=0, tiled=True)  15.4 us
    another operation x2, other arithmetic  12.8 us
    all_to_all x1, waiting for transfers between devices, on_device(): lax.all_to_all(local_grads, 'seq', split_axis=0, concat_axis=2, tiled=True)  11.7 us
  transfers between devices with their start and end apart: 8, of which 6 were waited for; matrix products, arithmetic and copies ran while one was open for 20% of the time, Pallas kernels for 8%

profile of v4, /device:TPU:1, one launch (start us, length us, event | category | flops | bytes accessed | tf_op | source)
XLA Modules:
  0.0 349.1 jit_solution(86182902953868031)
XLA Ops:
  7.2 0.0 all-gather.6.cloned.1.call-start
  7.2 0.7 all-gather.6.cloned.1.call-update
  7.9 0.0 all-gather.8.cloned.1.call-start
  8.0 1.5 copy.40
  9.5 28.7 %all-gather = bf16[1024,3,1,64]{0,3,1,2:T(8,128)(2,1)S(1)} all-gather(bf16[128,3,1,64]{0,3,1,2:T(8,128)(2,1)S(1)} %dynamic-slice_bitcast_fusion), channel_id=2, replica_groups=mesh['seq'=16,'zero'=8] {'zero'}, dimensions={0}, use_global_device_ids=true | all-gather | bytes 442368 | tf_op jit(solution)/shard_map/all_gather | solution.py:90
  38.2 15.4 %all-gather.6.cloned.1.call-done = bf16[2048,1024]{1,0:T(8,128)(2,1)} async-done(((bf16[128,1024]{1,0:T(8,128)(2,1)}), bf16[2048,1024]{1,0:T(8,128)(2,1)}) %all-gather.6.cloned.1.call-update) | async-done | bytes 4194320 | tf_op jit(solution)/shard_map/all_gather | solution.py:87
  53.6 3.7 %fusion.5 = bf16[2048,3,64]{0,2,1:T(8,128)(2,1)S(1)} fusion(bf16[2048,1024]{1,0:T(8,128)(2,1)} %all-gather.6.cloned.1.call-done, bf16[1024,3,1,64]{0,3,1,2:T(8,128)(2,1)S(1)} %all-gather), kind=kOutput, calls=%fused_computation.5 | convolution fusion | flops 805699584 | bytes 5373952 | tf_op jit(solution)/shard_map/td,dgc->tgc/dot_general | solution.py:91
  57.3 0.8 slice.29
  58.1 0.0 all-gather.8.cloned.1.call-update
  58.1 0.0 all-gather.10.cloned.1.call-start
  58.2 0.7 all-gather.10.cloned.1.call-update
  58.9 0.0 copy-done
  58.9 0.8 copy.43
  59.7 3.6 %all-to-all-start = ((bf16[128,16,64]{0,2,1:T(8,128)(2,1)}), bf16[128,16,64]{0,2,1:T(8,128)(2,1)S(1)}, u32[]{:S(2)}, u32[]{:S(2)}) async-start(bf16[128,16,64]{0,2,1:T(8,128)(2,1)} %bitcast.6), calls=%async_computation | async-start | bytes 524288 | tf_op jit(solution)/shard_map/all_to_all | solution.py:98
  63.4 0.0 copy-done.1
  63.4 0.1 copy.39
  63.5 0.6 gather_fusion
  64.0 6.6 %all-to-all-done = bf16[128,16,64]{0,2,1:T(8,128)(2,1)S(1)} async-done(((bf16[128,16,64]{0,2,1:T(8,128)(2,1)}), bf16[128,16,64]{0,2,1:T(8,128)(2,1)S(1)}, u32[]{:S(2)}, u32[]{:S(2)}) %all-to-all-start) | async-done | bytes 262176 | tf_op jit(solution)/shard_map/all_to_all | solution.py:98
  70.6 0.3 copy.44
  70.9 0.3 copy.42
  71.2 56.3 %all-gather.8.cloned.1.call-done = bf16[16384,2,64]{0,2,1:T(8,128)(2,1)} async-done(((bf16[2048,2,64]{0,2,1:T(8,128)(2,1)}), bf16[16384,2,64]{0,2,1:T(8,128)(2,1)}) %all-gather.8.cloned.1.call-update) | async-done | bytes 4194320 | tf_op jit(solution)/shard_map/all_gather | solution.py:94
  127.5 4.6 %fusion.17 = (bf16[16384,1,64]{0,2,1:T(8,128)(2,1)}, bf16[16384,1,64]{0,2,1:T(8,128)(2,1)}) fusion(bf16[16384,2,64]{0,2,1:T(8,128)(2,1)} %all-gather.8.cloned.1.call-done), kind=kLoop, calls=%fused_computation.28 | loop fusion | bytes 8388608 | tf_op jit(solution)/shard_map/slice | solution.py:96
  132.0 4.7 %copy.45 = bf16[16384,1,64]{2,0,1:T(8,128)(2,1)} copy(bf16[16384,1,64]{0,2,1:T(8,128)(2,1)} %get-tuple-element.21) | data formatting | bytes 4194304 | tf_op jit(solution)/shard_map/slice | solution.py:95
  136.8 4.8 %copy.46 = bf16[16384,1,64]{2,0,1:T(8,128)(2,1)} copy(bf16[16384,1,64]{0,2,1:T(8,128)(2,1)} %get-tuple-element.20) | data formatting | bytes 4194304 | tf_op jit(solution)/shard_map/slice | solution.py:96
  141.6 29.4 %shard_map.67 = (bf16[16,128,64]{2,1,0:T(8,128)(2,1)S(1)}, bf16[16,128,64]{2,1,0:T(8,128)(2,1)S(1)}, f32[128,128,64]{2,1,0:T(8,128)}, f32[128,128,64]{2,1,0:T(8,128)}) custom-call(s32[16,8]{1,0:T(8,128)S(1)} %fusion.10.slots_ref, bf16[16,128,64]{2,1,0:T(8,128)(2,1)S(1)} %bitcast.66, bf16[16,128,64]{2,1,0:T(8,128)(2,1)S(1)} %bitcast.65, ...), custom_call_target="tpu_custom_call" | custom-call | tf_op jit(solution)/shard_map/pallas_call | solution.py:64
  171.0 6.4 %convert.12 = bf16[128,128,64]{2,1,0:T(8,128)(2,1)} convert(f32[128,128,64]{2,1,0:T(8,128)} %get-tuple-element.9) | non-fusion elementwise | flops 1048576 | bytes 6291456 | tf_op jit(solution)/shard_map/convert.5
  177.4 3.7 %copy.50 = bf16[8,16,1,128,64]{3,4,2,1,0:T(8,128)(2,1)S(1)} copy(bf16[8,16,1,128,64]{4,3,1,0,2:T(8,128)(2,1)} %bitcast.69) | data formatting | bytes 4194304 | tf_op jit(solution)/shard_map/stack | solution.py:133
  181.1 6.3 %convert.13 = bf16[128,128,64]{2,1,0:T(8,128)(2,1)} convert(f32[128,128,64]{2,1,0:T(8,128)} %get-tuple-element.10) | non-fusion elementwise | flops 1048576 | bytes 6291456 | tf_op jit(solution)/shard_map/convert.4
  187.5 4.8 %copy.51 = bf16[8,16,1,128,64]{3,4,2,1,0:T(8,128)(2,1)} copy(bf16[8,16,1,128,64]{4,3,1,0,2:T(8,128)(2,1)} %bitcast.70) | data formatting | bytes 4194304 | tf_op jit(solution)/shard_map/stack | solution.py:133
  192.3 3.9 %pad_maximum_fusion = bf16[8,16,2,128,64]{3,4,2,1,0:T(8,128)(2,1)} fusion(bf16[8,16,1,128,64]{3,4,2,1,0:T(8,128)(2,1)} %copy.51, bf16[8,16,1,128,64]{3,4,2,1,0:T(8,128)(2,1)S(1)} %copy.50), kind=kLoop, calls=%fused_computation.1 | loop fusion | flops 2097152 | bytes 8388608 | tf_op jit(solution)/shard_map/stack | solution.py:133
  196.2 4.6 %all-to-all-start.2 = ((bf16[8,16,2,128,64]{3,4,2,1,0:T(8,128)(2,1)}), bf16[8,16,2,128,64]{3,4,2,1,0:T(8,128)(2,1)}, u32[]{:S(2)}, u32[]{:S(2)}) async-start(bf16[8,16,2,128,64]{3,4,2,1,0:T(8,128)(2,1)} %pad_maximum_fusion), calls=%async_computation.2 | async-start | bytes 8388608 | tf_op jit(solution)/shard_map/all_to_all | solution.py:135
  200.8 0.0 all-gather.12.cloned.1.call-start
  200.8 0.2 copy.53
  201.0 59.9 %all-to-all-done.2 = bf16[8,16,2,128,64]{3,4,2,1,0:T(8,128)(2,1)} async-done(((bf16[8,16,2,128,64]{3,4,2,1,0:T(8,128)(2,1)}), bf16[8,16,2,128,64]{3,4,2,1,0:T(8,128)(2,1)}, u32[]{:S(2)}, u32[]{:S(2)}) %all-to-all-start.2) | async-done | bytes 4194336 | tf_op jit(solution)/shard_map/all_to_all | solution.py:135
  260.9 3.1 reduce
  264.1 0.3 copy.67
  264.4 0.2 copy.54
  264.6 0.3 copy.68
  264.9 0.2 copy.55
  265.1 0.1 pad_maximum_fusion.1
  265.2 3.2 convolution_bitcast_fusion
  268.4 0.1 copy.72
  268.4 26.5 %all_to_all.55 = f32[8,128,192]{1,2,0:T(8,128)S(1)} all-to-all(f32[8,128,192]{1,2,0:T(8,128)S(1)} %bitcast.77), channel_id=1, replica_groups=mesh['seq'=16,'zero'=8] {'zero'}, dimensions={0} | all-to-all | bytes 1572864 | tf_op jit(solution)/shard_map/all_to_all | solution.py:157
  294.9 0.7 reduce_sum.19
  295.6 0.0 all-gather.12.cloned.1.call-update
  295.6 0.5 broadcast.116
  296.1 1.1 reduce.1
  297.2 1.1 reshape.103
  298.3 7.4 %all-to-all-start.1 = ((bf16[16,2,4096]{2,1,0:T(2,128)(2,1)}), bf16[16,2,4096]{2,1,0:T(2,128)(2,1)S(1)}, u32[]{:S(2)}, u32[]{:S(2)}) async-start(bf16[16,2,4096]{2,1,0:T(2,128)(2,1)} %reshape.103), calls=%async_computation.1 | async-start | bytes 524288 | tf_op jit(solution)/shard_map/all_to_all | solution.py:125
  305.7 1.4 copy.56
  307.1 2.5 reshape.105
  309.6 4.3 %all-to-all-done.1 = bf16[16,2,4096]{2,1,0:T(2,128)(2,1)S(1)} async-done(((bf16[16,2,4096]{2,1,0:T(2,128)(2,1)}), bf16[16,2,4096]{2,1,0:T(2,128)(2,1)S(1)}, u32[]{:S(2)}, u32[]{:S(2)}) %all-to-all-start.1) | async-done | bytes 262176 | tf_op jit(solution)/shard_map/all_to_all | solution.py:125
  313.8 3.5 %all-to-all-start.3 = ((bf16[16,2,12288]{2,1,0:T(2,128)(2,1)}), bf16[16,2,12288]{2,1,0:T(2,128)(2,1)S(1)}, u32[]{:S(2)}, u32[]{:S(2)}) async-start(bf16[16,2,12288]{2,1,0:T(2,128)(2,1)} %reshape.105), calls=%async_computation.3 | async-start | bytes 1572864 | tf_op jit(solution)/shard_map/all_to_all | solution.py:147
  317.3 0.6 reshape.104
  318.0 0.6 copy.48
  318.6 0.1 copy.49
  318.7 0.9 copy.61
  319.6 11.7 %all-to-all-done.3 = bf16[16,2,12288]{2,1,0:T(2,128)(2,1)S(1)} async-done(((bf16[16,2,12288]{2,1,0:T(2,128)(2,1)}), bf16[16,2,12288]{2,1,0:T(2,128)(2,1)S(1)}, u32[]{:S(2)}, u32[]{:S(2)}) %all-to-all-start.3) | async-done | bytes 786464 | tf_op jit(solution)/shard_map/all_to_all | solution.py:147
  331.3 1.3 reshape.106
  332.5 1.2 copy.64
  333.7 0.0 all-gather.10.cloned.1.call-done
  333.7 5.7 %convolution_convert_fusion = bf16[128,1024]{1,0:T(8,128)(2,1)} fusion(bf16[128,3072]{0,1:T(8,128)(2,1)S(1)} %bitcast.76, bf16[1024,3072]{1,0:T(8,128)(2,1)} %all-gather.10.cloned.1.call-done), kind=kOutput, calls=%fused_computation.7 | convolution fusion | flops 805437440 | bytes 7340032 | tf_op jit(solution)/shard_map/tc,dc->td/dot_general | solution.py:149
  339.5 1.5 copy.60
  341.0 1.6 copy.62
  (10 shorter events, 0.1 us)
Async XLA Ops:
  7.2 46.4 %all-gather.6.cloned.1.call-start = ((), (), s32[]{:S(2)}) async-start(), calls=%async_computation.5 | async-start | bytes 4456448 | tf_op jit(solution)/shard_map/all_gather | solution.py:87
  7.9 119.6 %all-gather.8.cloned.1.call-start = ((), (), s32[]{:S(2)}) async-start(), calls=%async_computation.6 | async-start | bytes 4718592 | tf_op jit(solution)/shard_map/all_gather | solution.py:94
  38.2 20.7 %copy-start = (bf16[128,1024]{1,0:T(8,128)(2,1)S(1)}, bf16[128,1024]{1,0:T(8,128)(2,1)}, u32[]{:S(2)}) copy-start(bf16[128,1024]{1,0:T(8,128)(2,1)} %param.7) | copy-start | bytes 786436
  38.2 25.2 %copy-start.1 = (s32[128,8]{0,1:T(8,128)S(1)}, s32[128,8]{0,1:T(8,128)}, u32[]{:S(2)}) copy-start(s32[128,8]{0,1:T(8,128)} %param.6) | copy-start | bytes 12292
  58.1 275.6 %all-gather.10.cloned.1.call-start = ((), (), s32[]{:S(2)}) async-start(), calls=%async_computation.7 | async-start | bytes 7077888 | tf_op jit(solution)/shard_map/all_gather | solution.py:86
  59.7 10.9 %all-to-all-start = ((bf16[128,16,64]{0,2,1:T(8,128)(2,1)}), bf16[128,16,64]{0,2,1:T(8,128)(2,1)S(1)}, u32[]{:S(2)}, u32[]{:S(2)}) async-start(bf16[128,16,64]{0,2,1:T(8,128)(2,1)} %bitcast.6), calls=%async_computation | async-start | bytes 524288 | tf_op jit(solution)/shard_map/all_to_all | solution.py:98
  196.2 64.7 %all-to-all-start.2 = ((bf16[8,16,2,128,64]{3,4,2,1,0:T(8,128)(2,1)}), bf16[8,16,2,128,64]{3,4,2,1,0:T(8,128)(2,1)}, u32[]{:S(2)}, u32[]{:S(2)}) async-start(bf16[8,16,2,128,64]{3,4,2,1,0:T(8,128)(2,1)} %pad_maximum_fusion), calls=%async_computation.2 | async-start | bytes 8388608 | tf_op jit(solution)/shard_map/all_to_all | solution.py:135
  200.8 138.7 %all-gather.12.cloned.1.call-start = ((), (), s32[]{:S(2)}) async-start(), calls=%async_computation.8 | async-start | bytes 1671168 | tf_op jit(solution)/shard_map/all_gather | solution.py:160
  298.3 15.5 %all-to-all-start.1 = ((bf16[16,2,4096]{2,1,0:T(2,128)(2,1)}), bf16[16,2,4096]{2,1,0:T(2,128)(2,1)S(1)}, u32[]{:S(2)}, u32[]{:S(2)}) async-start(bf16[16,2,4096]{2,1,0:T(2,128)(2,1)} %reshape.103), calls=%async_computation.1 | async-start | bytes 524288 | tf_op jit(solution)/shard_map/all_to_all | solution.py:125
  313.8 17.4 %all-to-all-start.3 = ((bf16[16,2,12288]{2,1,0:T(2,128)(2,1)}), bf16[16,2,12288]{2,1,0:T(2,128)(2,1)S(1)}, u32[]{:S(2)}, u32[]{:S(2)}) async-start(bf16[16,2,12288]{2,1,0:T(2,128)(2,1)} %reshape.105), calls=%async_computation.3 | async-start | bytes 1572864 | tf_op jit(solution)/shard_map/all_to_all | solution.py:147
Sparse Core Ops, SparseCore 0:
  9.7 43.8 all-gather.5
  58.3 69.1 all-gather.7
  129.8 98.0 all-gather.9
  295.7 37.1 all-gather.11

commit v5 on v4

v5 whole, which is shorter than its diff:
```python
import functools
import jax
import jax.numpy as jnp
from jax import lax
from jax.sharding import PartitionSpec as P
from jax.experimental import pallas as pl
from jax.experimental.pallas import tpu as pltpu

HEADS = 16
HEAD = 64
BLOCK = 128
NBK = 8


def _attn_kernel(slots_ref, q_ref, up_ref, kv_ref, out_ref, qg_ref, kvg_ref, acc_ref, *, scale):
    i = pl.program_id(0)

    @pl.when(i == 0)
    def _():
        acc_ref[...] = jnp.zeros(acc_ref.shape, acc_ref.dtype)

    q = q_ref[0]
    up = up_ref[0]
    ids = [slots_ref[i, j] for j in range(NBK)]
    blocks = [kv_ref[ids[j]] for j in range(NBK)]
    keys = jnp.concatenate([b[:, :HEAD] for b in blocks], axis=0)
    vals = jnp.concatenate([b[:, HEAD:] for b in blocks], axis=0)
    nt = (((1,), (1,)), ((), ()))
    tn = (((0,), (0,)), ((), ()))
    scores = lax.dot_general(q, keys, nt, preferred_element_type=jnp.float32) * scale
    row_max = jnp.max(scores, axis=-1, keepdims=True)
    exponent = jnp.exp(scores - row_max)
    prob_full = exponent / jnp.sum(exponent, axis=-1, keepdims=True)
    prob_low = prob_full.astype(jnp.bfloat16)
    out_ref[0] = jnp.dot(prob_low, vals, preferred_element_type=jnp.float32).astype(out_ref.dtype)
    prob_grad = lax.dot_general(up, vals, nt, preferred_element_type=jnp.float32)
    row_delta = jnp.sum(prob_full * prob_grad, axis=-1, keepdims=True)
    score_grad = (prob_full * (prob_grad - row_delta) * scale).astype(jnp.bfloat16)
    qg_ref[0] = jnp.dot(score_grad, keys, preferred_element_type=jnp.float32).astype(qg_ref.dtype)
    key_terms = lax.dot_general(score_grad, q, tn, preferred_element_type=jnp.float32)
    value_terms = lax.dot_general(prob_low, up, tn, preferred_element_type=jnp.float32)
    terms = jnp.concatenate([key_terms, value_terms], axis=1)
    for j in range(NBK):
        acc_ref[ids[j]] += terms[j * BLOCK:(j + 1) * BLOCK]

    @pl.when(i == pl.num_programs(0) - 1)
    def _():
        kvg_ref[...] = acc_ref[...].astype(kvg_ref.dtype)


def block_attention(slots, queries, upstream, kv, scale):
    rows = queries.shape[0]
    slot_count = kv.shape[0]
    row_spec = pl.BlockSpec((1, BLOCK, HEAD), lambda i, s: (i, 0, 0))
    full_spec = pl.BlockSpec((slot_count, BLOCK, 2 * HEAD), lambda i, s: (0, 0, 0))
    grid_spec = pltpu.PrefetchScalarGridSpec(
        num_scalar_prefetch=1,
        grid=(rows,),
        in_specs=[row_spec, row_spec, full_spec],
        out_specs=[row_spec, row_spec, full_spec],
        scratch_shapes=[pltpu.VMEM((slot_count, BLOCK, 2 * HEAD), jnp.float32)],
    )
    out_shape = [
        jax.ShapeDtypeStruct((rows, BLOCK, HEAD), jnp.bfloat16),
        jax.ShapeDtypeStruct((rows, BLOCK, HEAD), jnp.bfloat16),
        jax.ShapeDtypeStruct((slot_count, BLOCK, 2 * HEAD), jnp.bfloat16),
    ]
    return pl.pallas_call(
        functools.partial(_attn_kernel, scale=scale),
        grid_spec=grid_spec,
        out_shape=out_shape,
        compiler_params=pltpu.CompilerParams(
            dimension_semantics=("arbitrary",), vmem_limit_bytes=48 * 1024 * 1024
        ),
    )(slots, queries, upstream, kv)


def on_device(tokens, projection, pattern, upstream):
    seq_count = lax.axis_size("seq")
    zero_count = lax.axis_size("zero")
    zero_index = lax.axis_index("zero")
    tok_rows = tokens.shape[0]
    model_width = tokens.shape[1]
    heads_here = HEADS // seq_count
    head_cols = heads_here * HEAD
    per_shard = tok_rows // BLOCK
    local_blocks = seq_count * per_shard
    score_scale = HEAD ** (-0.5)
    seq_index = lax.axis_index("seq")
    weights = lax.all_gather(projection, "zero", axis=0, tiled=True)
    group_tokens = lax.all_gather(tokens, "seq", axis=0, tiled=True)
    head_w = projection.reshape(projection.shape[0], 3, seq_count, head_cols)
    head_w = lax.dynamic_index_in_dim(head_w, seq_index, axis=2, keepdims=False)
    head_w = lax.all_gather(head_w, "zero", axis=0, tiled=True)
    queries = jnp.einsum(
        "td,dc->tc", group_tokens, head_w[:, 0], preferred_element_type=jnp.float32
    ).astype(jnp.bfloat16)
    kv_local = jnp.einsum(
        "td,dc->tc",
        group_tokens,
        head_w[:, 1:].reshape(-1, 2 * head_cols),
        preferred_element_type=jnp.float32,
    ).astype(jnp.bfloat16)
    kv_all = lax.all_gather(kv_local, "zero", axis=0, tiled=True)
    incoming = lax.all_to_all(
        upstream.reshape(tok_rows, seq_count, head_cols),
        "seq",
        split_axis=1,
        concat_axis=0,
        tiled=True,
    )
    local_ids = jnp.arange(local_blocks, dtype=jnp.int32)
    row_ids = (local_ids // per_shard * zero_count + zero_index) * per_shard + local_ids % per_shard
    row_lists = pattern[row_ids]
    shard_ids = row_lists // per_shard
    key_slots = (
        shard_ids % zero_count * local_blocks
        + shard_ids // zero_count * per_shard
        + row_lists % per_shard
    )

    out_blocks, query_grads, group_sums = block_attention(
        key_slots.reshape(local_blocks, NBK),
        queries.reshape(local_blocks, BLOCK, head_cols),
        incoming.reshape(local_blocks, BLOCK, head_cols),
        kv_all.reshape(-1, BLOCK, 2 * head_cols),
        score_scale,
    )
    attended = lax.all_to_all(
        out_blocks.reshape(local_blocks * BLOCK, 1, head_cols),
        "seq",
        split_axis=0,
        concat_axis=1,
        tiled=True,
    )
    attended = attended.reshape(tok_rows, seq_count * head_cols)
    group_sums = group_sums.reshape(zero_count, local_blocks * BLOCK, 2 * head_cols)
    group_sums = lax.all_to_all(group_sums, "zero", split_axis=0, concat_axis=0, tiled=True)
    kv_sum = jnp.sum(group_sums.astype(jnp.float32), axis=0).astype(jnp.bfloat16)
    local_grads = jnp.concatenate([query_grads.reshape(-1, head_cols), kv_sum], axis=1)
    local_grads = local_grads.reshape(local_blocks * BLOCK, 3, 1, head_cols)
    token_grads = lax.all_to_all(local_grads, "seq", split_axis=0, concat_axis=2, tiled=True)
    flat_grads = token_grads.reshape(tok_rows, 3 * seq_count * head_cols)
    token_gradient = jnp.einsum(
        "tc,dc->td", flat_grads, weights, preferred_element_type=jnp.float32
    ).astype(jnp.bfloat16)
    head_grads = local_grads.reshape(local_blocks * BLOCK, 3 * head_cols)
    head_part = jnp.einsum(
        "td,tc->dc", group_tokens, head_grads, preferred_element_type=jnp.float32
    )
    head_part = head_part.reshape(zero_count, -1, 3 * head_cols)
    head_part = lax.all_to_all(head_part, "zero", split_axis=0, concat_axis=0, tiled=True)
    own_rows = jnp.sum(head_part, axis=0)
    own_rows = own_rows.reshape(1, -1, 3, head_cols)
    gathered = lax.all_gather(own_rows, "seq", axis=0, tiled=True)
    weight_gradient = gathered.transpose(1, 2, 0, 3).reshape(-1, 3 * seq_count * head_cols)
    return (attended, token_gradient, weight_gradient)


def solution(mesh):
    return jax.shard_map(
        on_device,
        mesh=mesh,
        in_specs=(P(("seq", "zero"), None), P("zero", None), P(), P(("seq", "zero"), None)),
        out_specs=(P(("seq", "zero"), None), P(("seq", "zero"), None), P("zero", None)),
        check_vma=False,
    )
```

time: 350 us -> 312 us (0.89)
  waiting for transfers between devices: 155 us -> 101 us
  blocking collectives: 55.2 us -> 109 us
  local copies, waits for them, and re-layouts: 41.5 us -> 23.8 us
  other arithmetic: 21.7 us -> 5.38 us
  matrix products: 12.6 us -> 17.1 us
  Pallas kernels: 29.4 us -> 25.1 us
  starting transfers between devices: 19.2 us -> 15.6 us
    all_to_all x0 -> x1, blocking collectives: none -> 63.8 us  [on_device(): lax.all_to_all(group_sums, 'zero', split_axis=0, concat_axis=0, tiled=True)]
    all_to_all x1 -> x0, waiting for transfers between devices: 59.9 us -> none  [on_device(): lax.all_to_all(group_sums, 'zero', split_axis=0, concat_axis=0, tiled=True)]
    another operation x4 -> x0, other arithmetic: 16.8 us -> none
    slice x7 -> x1, local copies, waits for them, and re-layouts: 15.3 us -> 0.02 us  [on_device(): head_w[:, 1:].reshape(-1, 2 * head_cols)]
    all_gather x1, waiting for transfers between devices: 0.01 us -> 12.2 us  [on_device(): gathered = lax.all_gather(own_rows, 'seq', axis=0, tiled=True)]
    all_to_all x1, blocking collectives: 26.5 us -> 16.7 us  [on_device(): lax.all_to_all(head_part, 'zero', split_axis=0, concat_axis=0, tiled=True)]
    another operation x3 -> x0, local copies, waits for them, and re-layouts: 8.67 us -> none  [the longest x2 8.47 us: on_device(): group_sums = jnp.stack([key_grad, value_grad], axis=1).astype(jnp.bfloat16)]
    all_gather x0 -> x1, local copies, waits for them, and re-layouts: none -> 6.4 us  [on_device(): kv_all = lax.all_gather(kv_local, 'zero', axis=0, tiled=True)]
  transfers between devices with their start and end apart: 8 -> 7, of which waited for: 6 -> 6; matrix products, arithmetic and copies ran while one was open for 20% -> 12% of each run, Pallas kernels for 8% -> 8%
where the time goes in v5:
time: 312 us; the launch traced here: 311 us
  blocking collectives  109 us (35%)
  waiting for transfers between devices  101 us (32%)
  Pallas kernels  25.1 us (8%)
  local copies, waits for them, and re-layouts  23.8 us (8%)
  matrix products  17.1 us (5%)
  starting transfers between devices  15.6 us (5%)
  between operations  14 us (4%)
  other arithmetic  5.38 us (2%)
    all_to_all x1, blocking collectives, on_device(): lax.all_to_all(group_sums, 'zero', split_axis=0, concat_axis=0, tiled=True)  63.8 us
    all_gather x1, waiting for transfers between devices, on_device(): kv_all = lax.all_gather(kv_local, 'zero', axis=0, tiled=True)  52.8 us
    all_gather x1, blocking collectives, on_device(): head_w = lax.all_gather(head_w, 'zero', axis=0, tiled=True)  28.7 us
    pallas_call x1, Pallas kernels, block_attention(): pl.pallas_call(functools.partial(_attn_kernel, scale=scale), grid_spec=gr...  25.1 us
    all_to_all x1, blocking collectives, on_device(): lax.all_to_all(head_part, 'zero', split_axis=0, concat_axis=0, tiled=True)  16.7 us
    all_gather x1, waiting for transfers between devices, on_device(): group_tokens = lax.all_gather(tokens, 'seq', axis=0, tiled=True)  15.3 us
    all_gather x1, waiting for transfers between devices, on_device(): gathered = lax.all_gather(own_rows, 'seq', axis=0, tiled=True)  12.2 us
    all_to_all x1, waiting for transfers between devices, on_device(): lax.all_to_all(local_grads, 'seq', split_axis=0, concat_axis=2, tiled=True)  10.7 us
  transfers between devices with their start and end apart: 7, of which 6 were waited for; matrix products, arithmetic and copies ran while one was open for 12% of the time, Pallas kernels for 8%

profile of v5, /device:TPU:1, one launch (start us, length us, event | category | flops | bytes accessed | tf_op | source)
XLA Modules:
  0.0 311.4 jit_solution(12422322035967888587)
XLA Ops:
  7.2 0.0 all-gather.6.cloned.1.call-start
  7.2 0.7 all-gather.6.cloned.1.call-update
  7.9 0.0 all-gather.8.cloned.1.call-start
  8.0 0.0 copy-start
  8.0 1.5 copy.51
  9.5 0.0 copy-start.1
  9.5 28.7 %all-gather = bf16[1024,3,1,64]{0,3,2,1:T(8,128)(2,1)S(1)} all-gather(bf16[128,3,1,64]{0,3,2,1:T(8,128)(2,1)S(1)} %constant_dynamic-slice_fusion), channel_id=2, replica_groups=mesh['seq'=16,'zero'=8] {'zero'}, dimensions={0}, use_global_device_ids=true | all-gather | bytes 442368 | tf_op jit(solution)/shard_map/all_gather | solution.py:94
  38.3 15.3 %all-gather.6.cloned.1.call-done = bf16[2048,1024]{1,0:T(8,128)(2,1)} async-done(((bf16[128,1024]{1,0:T(8,128)(2,1)}), bf16[2048,1024]{1,0:T(8,128)(2,1)}) %all-gather.6.cloned.1.call-update) | async-done | bytes 4194320 | tf_op jit(solution)/shard_map/all_gather | solution.py:91
  53.6 4.5 %fusion = bf16[2048,128]{0,1:T(8,128)(2,1)} fusion(bf16[1024,128]{0,1:T(8,128)(2,1)S(1)} %bitcast.71, bf16[2048,1024]{1,0:T(8,128)(2,1)} %all-gather.6.cloned.1.call-done), kind=kOutput, calls=%fused_computation.2 | convolution fusion | flops 537133056 | bytes 4980736 | tf_op jit(solution)/shard_map/td,dc->tc/dot_general | solution.py:98
  58.1 0.0 all-gather.8.cloned.1.call-update
  58.1 0.0 all-gather.10.cloned.1.call-start
  58.1 0.7 all-gather.10.cloned.1.call-update
  58.8 0.0 copy-done
  58.8 0.8 copy.53
  59.7 3.6 %all-to-all-start = ((bf16[128,16,64]{0,2,1:T(8,128)(2,1)}), bf16[128,16,64]{0,2,1:T(8,128)(2,1)S(1)}, u32[]{:S(2)}, u32[]{:S(2)}) async-start(bf16[128,16,64]{0,2,1:T(8,128)(2,1)} %bitcast.6), calls=%async_computation | async-start | bytes 524288 | tf_op jit(solution)/shard_map/all_to_all | solution.py:105
  63.3 0.0 all-gather.12.cloned.1.call-start
  63.4 0.0 copy-done.1
  63.4 0.1 copy.50
  63.5 0.6 gather_fusion
  64.0 6.5 %all-to-all-done = bf16[128,16,64]{0,2,1:T(8,128)(2,1)S(1)} async-done(((bf16[128,16,64]{0,2,1:T(8,128)(2,1)}), bf16[128,16,64]{0,2,1:T(8,128)(2,1)S(1)}, u32[]{:S(2)}, u32[]{:S(2)}) %all-to-all-start) | async-done | bytes 262176 | tf_op jit(solution)/shard_map/all_to_all | solution.py:105
  70.5 0.3 copy.54
  70.8 3.6 %fusion.1 = bf16[2048,64]{0,1:T(8,128)(2,1)S(1)} fusion(bf16[2048,1024]{1,0:T(8,128)(2,1)} %all-gather.6.cloned.1.call-done, bf16[1024,3,64]{0,2,1:T(8,128)(2,1)S(1)} %bitcast.70), kind=kOutput, calls=%fused_computation.4 | convolution fusion | flops 268566528 | bytes 4587520 | tf_op jit(solution)/shard_map/td,dc->tc/dot_general | solution.py:95
  74.4 0.3 copy.52
  74.7 52.8 %all-gather.8.cloned.1.call-done = bf16[16384,128]{0,1:T(8,128)(2,1)} async-done(((bf16[2048,128]{0,1:T(8,128)(2,1)}), bf16[16384,128]{0,1:T(8,128)(2,1)}) %all-gather.8.cloned.1.call-update) | async-done | bytes 4194320 | tf_op jit(solution)/shard_map/all_gather | solution.py:104
  127.5 6.4 %copy.55 = bf16[16384,128]{1,0:T(8,128)(2,1)} copy(bf16[16384,128]{0,1:T(8,128)(2,1)} %all-gather.8.cloned.1.call-done) | data formatting | bytes 8388608 | tf_op jit(solution)/shard_map/all_gather | solution.py:104
  133.9 25.1 %shard_map.67 = (bf16[16,128,64]{2,1,0:T(8,128)(2,1)S(1)}, bf16[16,128,64]{2,1,0:T(8,128)(2,1)S(1)}, bf16[128,128,128]{2,1,0:T(8,128)(2,1)}) custom-call(s32[16,8]{1,0:T(8,128)S(1)} %fusion.3.slots_ref, bf16[16,128,64]{2,1,0:T(8,128)(2,1)S(1)} %bitcast.57, bf16[16,128,64]{2,1,0:T(8,128)(2,1)S(1)} %bitcast.56, bf16[128,128,128]{2,1,0:T(8,128)(2,1)} %bitcast.61), custom_call_target="tpu_custom_call" | custom-call | tf_op jit(solution)/shard_map/pallas_call | solution.py:68
  158.9 63.8 %all_to_all.55 = bf16[8,2048,128]{2,1,0:T(8,128)(2,1)} all-to-all(bf16[8,2048,128]{2,1,0:T(8,128)(2,1)} %bitcast.65), channel_id=1, replica_groups=mesh['seq'=16,'zero'=8] {'zero'}, dimensions={0} | all-to-all | bytes 8388608 | tf_op jit(solution)/shard_map/all_to_all | solution.py:138
  222.7 3.1 reduce_sum.21
  225.8 3.3 %convolution_bitcast_fusion = f32[24,8,8,128]{3,2,1,0:T(8,128)S(1)} fusion(bf16[2048,1024]{1,0:T(8,128)(2,1)} %all-gather.6.cloned.1.call-done, bf16[2048,128]{1,0:T(8,128)(2,1)S(1)} %reduce_sum.21, bf16[2048,64]{1,0:T(8,128)(2,1)S(1)} %bitcast.59), kind=kOutput, calls=%fused_computation.5 | convolution fusion | flops 806879232 | bytes 5767168 | tf_op jit(solution)/shard_map/td,tc->dc/dot_general | solution.py:148
  229.1 0.1 copy.72
  229.2 16.7 %all_to_all.56 = f32[8,128,192]{1,2,0:T(8,128)S(1)} all-to-all(f32[8,128,192]{1,2,0:T(8,128)S(1)} %bitcast.67), channel_id=1, replica_groups=mesh['seq'=16,'zero'=8] {'zero'}, dimensions={0} | all-to-all | bytes 1572864 | tf_op jit(solution)/shard_map/all_to_all | solution.py:152
  245.9 0.7 reduce_sum.22
  246.6 0.0 all-gather.12.cloned.1.call-update
  246.6 0.5 broadcast.116
  247.1 1.1 reduce.1
  248.2 1.1 reshape.97
  249.3 7.7 %all-to-all-start.1 = ((bf16[16,2,4096]{2,1,0:T(2,128)(2,1)}), bf16[16,2,4096]{2,1,0:T(2,128)(2,1)S(1)}, u32[]{:S(2)}, u32[]{:S(2)}) async-start(bf16[16,2,4096]{2,1,0:T(2,128)(2,1)} %reshape.97), calls=%async_computation.1 | async-start | bytes 524288 | tf_op jit(solution)/shard_map/all_to_all | solution.py:129
  257.1 0.5 pad_maximum_fusion
  257.6 0.5 copy.59
  258.1 1.4 copy.60
  259.5 2.5 reshape.99
  261.9 2.3 all-to-all-done.1
  264.3 4.1 %all-to-all-start.3 = ((bf16[16,2,12288]{2,1,0:T(2,128)(2,1)}), bf16[16,2,12288]{2,1,0:T(2,128)(2,1)S(1)}, u32[]{:S(2)}, u32[]{:S(2)}) async-start(bf16[16,2,12288]{2,1,0:T(2,128)(2,1)} %reshape.99), calls=%async_computation.3 | async-start | bytes 1572864 | tf_op jit(solution)/shard_map/all_to_all | solution.py:142
  268.4 0.6 reshape.98
  269.1 0.6 copy.57
  269.7 0.1 copy.58
  269.8 0.9 copy.65
  270.6 10.7 %all-to-all-done.3 = bf16[16,2,12288]{2,1,0:T(2,128)(2,1)S(1)} async-done(((bf16[16,2,12288]{2,1,0:T(2,128)(2,1)}), bf16[16,2,12288]{2,1,0:T(2,128)(2,1)S(1)}, u32[]{:S(2)}, u32[]{:S(2)}) %all-to-all-start.3) | async-done | bytes 786464 | tf_op jit(solution)/shard_map/all_to_all | solution.py:142
  281.3 1.3 reshape.100
  282.6 1.2 copy.68
  283.8 0.0 all-gather.10.cloned.1.call-done
  283.8 5.7 %convolution_convert_fusion.2 = bf16[128,1024]{1,0:T(8,128)(2,1)} fusion(bf16[128,3072]{0,1:T(8,128)(2,1)S(1)} %bitcast.66, bf16[1024,3072]{1,0:T(8,128)(2,1)} %all-gather.10.cloned.1.call-done), kind=kOutput, calls=%fused_computation.6 | convolution fusion | flops 805437440 | bytes 7340032 | tf_op jit(solution)/shard_map/tc,dc->td/dot_general | solution.py:144
  289.5 12.2 %all-gather.12.cloned.1.call-done = f32[16,128,3,64]{1,3,2,0:T(8,128)} async-done(((f32[1,128,3,64]{1,3,2,0:T(8,128)}), f32[16,128,3,64]{1,3,2,0:T(8,128)}) %all-gather.12.cloned.1.call-update) | async-done | bytes 1572880 | tf_op jit(solution)/shard_map/all_gather | solution.py:155
  301.7 1.5 copy.64
  303.2 1.6 copy.66
  (6 shorter events, 0.1 us)
Async XLA Ops:
  7.2 46.4 %all-gather.6.cloned.1.call-start = ((), (), s32[]{:S(2)}) async-start(), calls=%async_computation.5 | async-start | bytes 4456448 | tf_op jit(solution)/shard_map/all_gather | solution.py:91
  7.9 119.6 %all-gather.8.cloned.1.call-start = ((), (), s32[]{:S(2)}) async-start(), calls=%async_computation.6 | async-start | bytes 4718592 | tf_op jit(solution)/shard_map/all_gather | solution.py:104
  8.0 50.9 %copy-start = (bf16[128,1024]{1,0:T(8,128)(2,1)S(1)}, bf16[128,1024]{1,0:T(8,128)(2,1)}, u32[]{:S(2)}) copy-start(bf16[128,1024]{1,0:T(8,128)(2,1)} %param.7) | copy-start | bytes 786436
  9.5 53.8 %copy-start.1 = (s32[128,8]{0,1:T(8,128)S(1)}, s32[128,8]{0,1:T(8,128)}, u32[]{:S(2)}) copy-start(s32[128,8]{0,1:T(8,128)} %param.6) | copy-start | bytes 12292
  58.1 225.7 %all-gather.10.cloned.1.call-start = ((), (), s32[]{:S(2)}) async-start(), calls=%async_computation.7 | async-start | bytes 7077888 | tf_op jit(solution)/shard_map/all_gather | solution.py:90
  59.7 10.9 %all-to-all-start = ((bf16[128,16,64]{0,2,1:T(8,128)(2,1)}), bf16[128,16,64]{0,2,1:T(8,128)(2,1)S(1)}, u32[]{:S(2)}, u32[]{:S(2)}) async-start(bf16[128,16,64]{0,2,1:T(8,128)(2,1)} %bitcast.6), calls=%async_computation | async-start | bytes 524288 | tf_op jit(solution)/shard_map/all_to_all | solution.py:105
  63.3 238.5 %all-gather.12.cloned.1.call-start = ((), (), s32[]{:S(2)}) async-start(), calls=%async_computation.8 | async-start | bytes 1671168 | tf_op jit(solution)/shard_map/all_gather | solution.py:155
  249.3 14.9 %all-to-all-start.1 = ((bf16[16,2,4096]{2,1,0:T(2,128)(2,1)}), bf16[16,2,4096]{2,1,0:T(2,128)(2,1)S(1)}, u32[]{:S(2)}, u32[]{:S(2)}) async-start(bf16[16,2,4096]{2,1,0:T(2,128)(2,1)} %reshape.97), calls=%async_computation.1 | async-start | bytes 524288 | tf_op jit(solution)/shard_map/all_to_all | solution.py:129
  264.3 17.0 %all-to-all-start.3 = ((bf16[16,2,12288]{2,1,0:T(2,128)(2,1)}), bf16[16,2,12288]{2,1,0:T(2,128)(2,1)S(1)}, u32[]{:S(2)}, u32[]{:S(2)}) async-start(bf16[16,2,12288]{2,1,0:T(2,128)(2,1)} %reshape.99), calls=%async_computation.3 | async-start | bytes 1572864 | tf_op jit(solution)/shard_map/all_to_all | solution.py:142
Sparse Core Ops, SparseCore 0:
  9.7 43.8 all-gather.5
  58.2 69.2 all-gather.7
  129.8 139.3 all-gather.9
  270.7 30.9 all-gather.11

commit v6 on v5

--- a/solution.py
+++ b/solution.py
@@ -87,8 +87,22 @@
     local_blocks = seq_count * per_shard
     score_scale = HEAD ** (-0.5)
     seq_index = lax.axis_index("seq")
-    weights = lax.all_gather(projection, "zero", axis=0, tiled=True)
-    group_tokens = lax.all_gather(tokens, "seq", axis=0, tiled=True)
+    core = seq_index % 2
+    first = core == 0
+    pair = [(i, i ^ 1) for i in range(seq_count)]
+    width = projection.shape[1] // 2
+    w_mine = lax.dynamic_slice_in_dim(projection, core * width, width, axis=1)
+    w_mine = lax.all_gather(w_mine, "zero", axis=0, tiled=True)
+    w_other = lax.ppermute(w_mine, "seq", pair)
+    half_d = model_width // 2
+    t_halves = tokens.reshape(tok_rows, 2, half_d).transpose(1, 0, 2)
+    t_send = jnp.tile(t_halves, (seq_count // 2, 1, 1))
+    t_mine = lax.all_to_all(t_send, "seq", split_axis=0, concat_axis=0, tiled=True)
+    t_mine = t_mine.reshape(seq_count * tok_rows, half_d)
+    t_other = lax.ppermute(t_mine, "seq", pair)
+    group_tokens = jnp.concatenate(
+        [jnp.where(first, t_mine, t_other), jnp.where(first, t_other, t_mine)], axis=1
+    )
     head_w = projection.reshape(projection.shape[0], 3, seq_count, head_cols)
     head_w = lax.dynamic_index_in_dim(head_w, seq_index, axis=2, keepdims=False)
     head_w = lax.all_gather(head_w, "zero", axis=0, tiled=True)
@@ -141,8 +155,11 @@
     local_grads = local_grads.reshape(local_blocks * BLOCK, 3, 1, head_cols)
     token_grads = lax.all_to_all(local_grads, "seq", split_axis=0, concat_axis=2, tiled=True)
     flat_grads = token_grads.reshape(tok_rows, 3 * seq_count * head_cols)
-    token_gradient = jnp.einsum(
-        "tc,dc->td", flat_grads, weights, preferred_element_type=jnp.float32
+    g_mine = lax.dynamic_slice_in_dim(flat_grads, core * width, width, axis=1)
+    g_other = lax.dynamic_slice_in_dim(flat_grads, (1 - core) * width, width, axis=1)
+    token_gradient = (
+        jnp.einsum("tc,dc->td", g_mine, w_mine, preferred_element_type=jnp.float32)
+        + jnp.einsum("tc,dc->td", g_other, w_other, preferred_element_type=jnp.float32)
     ).astype(jnp.bfloat16)
     head_grads = local_grads.reshape(local_blocks * BLOCK, 3 * head_cols)
     head_part = jnp.einsum(

time: 312 us -> 322 us (1.032)
  waiting for transfers between devices: 101 us -> 83.9 us
  starting transfers between devices: 15.6 us -> 29.9 us
  blocking collectives: 109 us -> 120 us
    all_to_all x1, blocking collectives: 16.7 us -> 33.4 us  [on_device(): lax.all_to_all(t_send, 'seq', split_axis=0, concat_axis=0, tiled=True)]
    all_gather x1, waiting for transfers between devices: 12.2 us -> 0.01 us  [on_device(): gathered = lax.all_gather(own_rows, 'seq', axis=0, tiled=True)]
    all_gather x2 -> x1, waiting for transfers between devices: 15.3 us -> 4.48 us  [on_device(): w_mine = lax.all_gather(w_mine, 'zero', axis=0, tiled=True)]
    all_to_all x0 -> x1, starting transfers between devices: none -> 8.71 us  [on_device(): lax.all_to_all(head_part, 'zero', split_axis=0, concat_axis=0, tiled=True)]
    all_gather x1 -> x0, local copies, waits for them, and re-layouts: 6.4 us -> none  [on_device(): kv_all = lax.all_gather(kv_local, 'zero', axis=0, tiled=True)]
    all_to_all x0 -> x1, waiting for transfers between devices: none -> 5.83 us  [on_device(): lax.all_to_all(head_part, 'zero', split_axis=0, concat_axis=0, tiled=True)]
    all_to_all x1, blocking collectives: 63.8 us -> 58.8 us  [on_device(): lax.all_to_all(group_sums, 'zero', split_axis=0, concat_axis=0, tiled=True)]
    unnamed x14 -> x20, local copies, waits for them, and re-layouts: 10.5 us -> 13.8 us
  transfers between devices with their start and end apart: 7 -> 9, of which waited for: 6 -> 6; matrix products, arithmetic and copies ran while one was open for 12% -> 12% of each run, Pallas kernels for 8% -> 8%
where the time goes in v6:
time: 322 us; the launch traced here: 321 us
  blocking collectives  120 us (37%)
  waiting for transfers between devices  83.9 us (26%)
  starting transfers between devices  29.9 us (9%)
  Pallas kernels  24.9 us (8%)
  local copies, waits for them, and re-layouts  24.6 us (8%)
  matrix products  16.1 us (5%)
  between operations  14 us (4%)
  other arithmetic  7.23 us (2%)
    all_to_all x1, blocking collectives, on_device(): lax.all_to_all(group_sums, 'zero', split_axis=0, concat_axis=0, tiled=True)  58.8 us
    all_gather x1, waiting for transfers between devices, on_device(): kv_all = lax.all_gather(kv_local, 'zero', axis=0, tiled=True)  52.5 us
    all_to_all x1, blocking collectives, on_device(): lax.all_to_all(t_send, 'seq', split_axis=0, concat_axis=0, tiled=True)  33.4 us
    all_gather x1, blocking collectives, on_device(): head_w = lax.all_gather(head_w, 'zero', axis=0, tiled=True)  27.7 us
    pallas_call x1, Pallas kernels, block_attention(): pl.pallas_call(functools.partial(_attn_kernel, scale=scale), grid_spec=gr...  24.9 us
    unnamed x20, local copies, waits for them, and re-layouts  13.8 us
    all_to_all x1, waiting for transfers between devices, on_device(): lax.all_to_all(local_grads, 'seq', split_axis=0, concat_axis=2, tiled=True)  11.6 us
    all_to_all x1, starting transfers between devices, on_device(): lax.all_to_all(head_part, 'zero', split_axis=0, concat_axis=0, tiled=True)  8.71 us
  transfers between devices with their start and end apart: 9, of which 6 were waited for; matrix products, arithmetic and copies ran while one was open for 12% of the time, Pallas kernels for 8%

profile of v6, /device:TPU:1, one launch (start us, length us, event | category | flops | bytes accessed | tf_op | source)
XLA Modules:
  0.0 320.6 jit_solution(17110742814545425810)
XLA Ops:
  7.2 0.0 all-gather.5.cloned.1.call-start
  7.2 1.1 reshape.83
  8.4 0.0 copy-start.2
  8.4 0.2 tile.4
  8.6 33.4 %all_to_all.60 = bf16[16,128,512]{2,1,0:T(8,128)(2,1)S(1)} all-to-all(bf16[16,128,512]{2,1,0:T(8,128)(2,1)S(1)} %bitcast.58), channel_id=1, replica_groups=mesh['seq'=16,'zero'=8] {'seq'}, dimensions={0} | all-to-all | bytes 4194304 | tf_op jit(solution)/shard_map/all_to_all | solution.py:100
  42.0 1.4 collective-permute-start
  43.5 0.0 copy-done.2
  43.5 1.2 copy.52
  44.6 0.8 constant_dynamic-slice_fusion.1
  45.4 27.7 %all-gather = bf16[1024,3,1,64]{0,3,2,1:T(8,128)(2,1)S(1)} all-gather(bf16[128,3,1,64]{0,3,2,1:T(8,128)(2,1)S(1)} %constant_dynamic-slice_fusion.1), channel_id=2, replica_groups=mesh['seq'=16,'zero'=8] {'zero'}, dimensions={0}, use_global_device_ids=true | all-gather | bytes 442368 | tf_op jit(solution)/shard_map/all_gather | solution.py:108
  73.2 0.0 collective-permute-done
  73.2 1.9 broadcast_select_fusion.1
  75.0 0.0 copy-start
  75.1 1.3 copy-done
  76.4 0.8 copy-done.1
  77.1 2.0 convolution_convert_fusion
  79.2 0.0 all-gather.5.cloned.1.call-update
  79.2 0.0 all-gather.7.cloned.1.call-start
  79.3 0.8 constant_dynamic-slice_fusion
  80.1 0.0 all-gather.7.cloned.1.call-update
  80.1 0.0 copy-done.3
  80.1 0.8 copy.54
  80.9 6.8 %all-to-all-start.1 = ((bf16[128,16,64]{0,2,1:T(8,128)(2,1)}), bf16[128,16,64]{0,2,1:T(8,128)(2,1)S(1)}, u32[]{:S(2)}, u32[]{:S(2)}) async-start(bf16[128,16,64]{0,2,1:T(8,128)(2,1)} %bitcast.8), calls=%async_computation.1 | async-start | bytes 524288 | tf_op jit(solution)/shard_map/all_to_all | solution.py:119
  87.8 0.1 copy.50
  87.9 0.6 gather_fusion
  88.5 6.6 %all-to-all-done.1 = bf16[128,16,64]{0,2,1:T(8,128)(2,1)S(1)} async-done(((bf16[128,16,64]{0,2,1:T(8,128)(2,1)}), bf16[128,16,64]{0,2,1:T(8,128)(2,1)S(1)}, u32[]{:S(2)}, u32[]{:S(2)}) %all-to-all-start.1) | async-done | bytes 262176 | tf_op jit(solution)/shard_map/all_to_all | solution.py:119
  95.0 0.3 copy.55
  95.3 3.6 %convolution_convert_fusion.1 = bf16[2048,64]{0,1:T(8,128)(2,1)S(1)} fusion(bf16[2048,512]{1,0:T(8,128)(2,1)} %copy-done.1, bf16[2048,512]{1,0:T(8,128)(2,1)} %copy-done, bf16[1024,3,64]{0,2,1:T(8,128)(2,1)S(1)} %bitcast.69), kind=kOutput, calls=%fused_computation.3 | convolution fusion | flops 276955136 | bytes 4587520 | tf_op jit(solution)/shard_map/td,dc->tc/dot_general | solution.py:109
  99.0 0.3 copy.53
  99.2 52.5 %all-gather.5.cloned.1.call-done = bf16[16384,128]{1,0:T(8,128)(2,1)} async-done(((bf16[2048,128]{1,0:T(8,128)(2,1)}), bf16[16384,128]{1,0:T(8,128)(2,1)}) %all-gather.5.cloned.1.call-update) | async-done | bytes 4194320 | tf_op jit(solution)/shard_map/all_gather | solution.py:118
  151.7 24.9 %shard_map.67 = (bf16[16,128,64]{2,1,0:T(8,128)(2,1)S(1)}, bf16[16,128,64]{2,1,0:T(8,128)(2,1)S(1)}, bf16[128,128,128]{2,1,0:T(8,128)(2,1)}) custom-call(s32[16,8]{1,0:T(8,128)S(1)} %fusion.5.slots_ref, bf16[16,128,64]{2,1,0:T(8,128)(2,1)S(1)} %bitcast.54, bf16[16,128,64]{2,1,0:T(8,128)(2,1)S(1)} %bitcast.53, bf16[128,128,128]{2,1,0:T(8,128)(2,1)} %bitcast.63), custom_call_target="tpu_custom_call" | custom-call | tf_op jit(solution)/shard_map/pallas_call | solution.py:68
  176.6 58.8 %all_to_all.61 = bf16[8,2048,128]{2,1,0:T(8,128)(2,1)} all-to-all(bf16[8,2048,128]{2,1,0:T(8,128)(2,1)} %bitcast.64), channel_id=1, replica_groups=mesh['seq'=16,'zero'=8] {'zero'}, dimensions={0} | all-to-all | bytes 8388608 | tf_op jit(solution)/shard_map/all_to_all | solution.py:152
  235.4 3.1 reduce_sum.21
  238.5 3.6 %convolution_bitcast_fusion = f32[24,8,8,128]{3,2,1,0:T(8,128)S(1)} fusion(bf16[2048,512]{1,0:T(8,128)(2,1)} %copy-done.1, bf16[2048,512]{1,0:T(8,128)(2,1)} %copy-done, bf16[2048,128]{1,0:T(8,128)(2,1)S(1)} %reduce_sum.21, bf16[2048,64]{1,0:T(8,128)(2,1)S(1)} %bitcast.56), kind=kOutput, calls=%fused_computation.6 | convolution fusion | flops 815267840 | bytes 5767168 | tf_op jit(solution)/shard_map/td,tc->dc/dot_general | solution.py:165
  242.1 0.9 copy.72
  243.1 8.7 %all-to-all-start.5 = ((f32[8,128,192]{1,2,0:T(8,128)}), f32[8,128,192]{1,2,0:T(8,128)S(1)}, u32[]{:S(2)}, u32[]{:S(2)}) async-start(f32[8,128,192]{1,2,0:T(8,128)} %bitcast.52), calls=%async_computation.5 | async-start | bytes 1572864 | tf_op jit(solution)/shard_map/all_to_all | solution.py:169
  251.8 0.0 all-gather.9.cloned.1.call-start
  251.8 4.5 %all-gather.7.cloned.1.call-done = bf16[1024,1536]{1,0:T(8,128)(2,1)} async-done(((bf16[128,1536]{1,0:T(8,128)(2,1)}), bf16[1024,1536]{1,0:T(8,128)(2,1)}) %all-gather.7.cloned.1.call-update) | async-done | bytes 3145744 | tf_op jit(solution)/shard_map/all_gather | solution.py:95
  256.3 1.4 collective-permute-start.1
  257.7 5.8 %all-to-all-done.5 = f32[8,128,192]{1,2,0:T(8,128)S(1)} async-done(((f32[8,128,192]{1,2,0:T(8,128)}), f32[8,128,192]{1,2,0:T(8,128)S(1)}, u32[]{:S(2)}, u32[]{:S(2)}) %all-to-all-start.5) | async-done | bytes 786464 | tf_op jit(solution)/shard_map/all_to_all | solution.py:169
  263.6 0.7 reduce_sum.22
  264.2 0.0 all-gather.9.cloned.1.call-update
  264.3 0.5 broadcast.120
  264.8 1.1 reduce.1
  265.9 1.1 reshape.109
  267.0 7.2 %all-to-all-start.2 = ((bf16[16,2,4096]{2,1,0:T(2,128)(2,1)}), bf16[16,2,4096]{2,1,0:T(2,128)(2,1)S(1)}, u32[]{:S(2)}, u32[]{:S(2)}) async-start(bf16[16,2,4096]{2,1,0:T(2,128)(2,1)} %reshape.109), calls=%async_computation.2 | async-start | bytes 524288 | tf_op jit(solution)/shard_map/all_to_all | solution.py:143
  274.2 0.5 pad_maximum_fusion.4
  274.7 0.5 copy.59
  275.2 1.4 copy.60
  276.6 2.5 reshape.111
  279.0 3.0 all-to-all-done.2
  282.0 4.2 %all-to-all-start.4 = ((bf16[16,2,12288]{2,1,0:T(2,128)(2,1)}), bf16[16,2,12288]{2,1,0:T(2,128)(2,1)}, u32[]{:S(2)}, u32[]{:S(2)}) async-start(bf16[16,2,12288]{2,1,0:T(2,128)(2,1)} %reshape.111), calls=%async_computation.4 | async-start | bytes 1572864 | tf_op jit(solution)/shard_map/all_to_all | solution.py:156
  286.2 0.6 reshape.110
  286.9 0.6 copy.57
  287.5 0.1 copy.58
  287.6 0.9 copy.65
  288.4 11.6 %all-to-all-done.4 = bf16[16,2,12288]{2,1,0:T(2,128)(2,1)} async-done(((bf16[16,2,12288]{2,1,0:T(2,128)(2,1)}), bf16[16,2,12288]{2,1,0:T(2,128)(2,1)}, u32[]{:S(2)}, u32[]{:S(2)}) %all-to-all-start.4) | async-done | bytes 786464 | tf_op jit(solution)/shard_map/all_to_all | solution.py:156
  300.0 2.9 reshape.112
  302.9 1.2 copy.68
  304.1 3.1 fusion.2
  307.2 0.0 collective-permute-done.1
  307.2 3.8 %fusion = bf16[128,1024]{1,0:T(8,128)(2,1)} fusion(f32[128,1024]{1,0:T(8,128)S(1)} %fusion.2, bf16[1024,1536]{1,0:T(8,128)(2,1)} %collective-permute-done.1, bf16[128,3072]{0,1:T(8,128)(2,1)S(1)} %bitcast.66, s32[]{:T(128)S(6)} %select_n.77), kind=kOutput, calls=%fused_computation.8 | convolution fusion | flops 402915328 | bytes 4325380 | tf_op jit(solution)/shard_map/tc,dc->td/dot_general | solution.py:162
  311.0 1.5 copy.64
  312.5 1.6 copy.66
  (11 shorter events, 0.1 us)
Async XLA Ops:
  7.2 144.5 %all-gather.5.cloned.1.call-start = ((), (), s32[]{:S(2)}) async-start(), calls=%async_computation.6 | async-start | bytes 4718592 | tf_op jit(solution)/shard_map/all_gather | solution.py:118
  8.4 35.1 %copy-start.2 = (bf16[128,3072]{1,0:T(8,128)(2,1)S(1)}, bf16[128,3072]{1,0:T(8,128)(2,1)}, u32[]{:S(2)}) copy-start(bf16[128,3072]{1,0:T(8,128)(2,1)} %param.5) | copy-start | bytes 2359300
  42.0 31.1 %collective-permute-start = (bf16[2048,512]{1,0:T(8,128)(2,1)S(1)}, bf16[2048,512]{1,0:T(8,128)(2,1)}, u32[]{:S(2)}, u32[]{:S(2)}) collective-permute-start(bf16[2048,512]{1,0:T(8,128)(2,1)S(1)} %bitcast.61), channel_id=1, source_target_pairs={{0,8},{8,0},{16,24},{24,16},{32,40},{40,32},{48,56},{56,48},{64,72... | collective-permute-start | bytes 6291464 | tf_op jit(solution)/shard_map/ppermute | solution.py:102
  75.0 1.3 copy-start
  75.1 2.1 copy-start.1
  77.1 2.9 copy-start.3
  77.1 10.7 %copy-start.4 = (s32[128,8]{0,1:T(8,128)S(1)}, s32[128,8]{0,1:T(8,128)}, u32[]{:S(2)}) copy-start(s32[128,8]{0,1:T(8,128)} %param.6) | copy-start | bytes 12292
  79.2 177.1 %all-gather.7.cloned.1.call-start = ((), (), s32[]{:S(2)}) async-start(), calls=%async_computation.7 | async-start | bytes 3538944 | tf_op jit(solution)/shard_map/all_gather | solution.py:95
  80.9 14.1 %all-to-all-start.1 = ((bf16[128,16,64]{0,2,1:T(8,128)(2,1)}), bf16[128,16,64]{0,2,1:T(8,128)(2,1)S(1)}, u32[]{:S(2)}, u32[]{:S(2)}) async-start(bf16[128,16,64]{0,2,1:T(8,128)(2,1)} %bitcast.8), calls=%async_computation.1 | async-start | bytes 524288 | tf_op jit(solution)/shard_map/all_to_all | solution.py:119
  243.1 20.5 %all-to-all-start.5 = ((f32[8,128,192]{1,2,0:T(8,128)}), f32[8,128,192]{1,2,0:T(8,128)S(1)}, u32[]{:S(2)}, u32[]{:S(2)}) async-start(f32[8,128,192]{1,2,0:T(8,128)} %bitcast.52), calls=%async_computation.5 | async-start | bytes 1572864 | tf_op jit(solution)/shard_map/all_to_all | solution.py:169
  251.8 59.2 %all-gather.9.cloned.1.call-start = ((), (), s32[]{:S(2)}) async-start(), calls=%async_computation.8 | async-start | bytes 1671168 | tf_op jit(solution)/shard_map/all_gather | solution.py:172
  256.3 50.9 %collective-permute-start.1 = (bf16[1024,1536]{1,0:T(8,128)(2,1)}, bf16[1024,1536]{1,0:T(8,128)(2,1)}, u32[]{:S(2)}, u32[]{:S(2)}) collective-permute-start(bf16[1024,1536]{1,0:T(8,128)(2,1)} %all-gather.7.cloned.1.call-done), channel_id=1, source_target_pairs={{0,8},{8,0},{16,24},{24,16},{32,40},{40,32},{48,56},{56,48},{64,72... | collective-permute-start | bytes 9437192 | tf_op jit(solution)/shard_map/ppermute | solution.py:96
  267.0 15.0 %all-to-all-start.2 = ((bf16[16,2,4096]{2,1,0:T(2,128)(2,1)}), bf16[16,2,4096]{2,1,0:T(2,128)(2,1)S(1)}, u32[]{:S(2)}, u32[]{:S(2)}) async-start(bf16[16,2,4096]{2,1,0:T(2,128)(2,1)} %reshape.109), calls=%async_computation.2 | async-start | bytes 524288 | tf_op jit(solution)/shard_map/all_to_all | solution.py:143
  282.0 18.0 %all-to-all-start.4 = ((bf16[16,2,12288]{2,1,0:T(2,128)(2,1)}), bf16[16,2,12288]{2,1,0:T(2,128)(2,1)}, u32[]{:S(2)}, u32[]{:S(2)}) async-start(bf16[16,2,12288]{2,1,0:T(2,128)(2,1)} %reshape.111), calls=%async_computation.4 | async-start | bytes 1572864 | tf_op jit(solution)/shard_map/all_to_all | solution.py:156
Sparse Core Ops, SparseCore 0:
  79.3 72.3 all-gather.4
  154.0 102.2 all-gather.6
  264.4 37.4 all-gather.8

commit v7 on v6

--- a/solution.py
+++ b/solution.py
@@ -88,32 +88,24 @@
     score_scale = HEAD ** (-0.5)
     seq_index = lax.axis_index("seq")
     core = seq_index % 2
-    first = core == 0
     pair = [(i, i ^ 1) for i in range(seq_count)]
     width = projection.shape[1] // 2
     w_mine = lax.dynamic_slice_in_dim(projection, core * width, width, axis=1)
     w_mine = lax.all_gather(w_mine, "zero", axis=0, tiled=True)
     w_other = lax.ppermute(w_mine, "seq", pair)
-    half_d = model_width // 2
-    t_halves = tokens.reshape(tok_rows, 2, half_d).transpose(1, 0, 2)
-    t_send = jnp.tile(t_halves, (seq_count // 2, 1, 1))
-    t_mine = lax.all_to_all(t_send, "seq", split_axis=0, concat_axis=0, tiled=True)
-    t_mine = t_mine.reshape(seq_count * tok_rows, half_d)
-    t_other = lax.ppermute(t_mine, "seq", pair)
-    group_tokens = jnp.concatenate(
-        [jnp.where(first, t_mine, t_other), jnp.where(first, t_other, t_mine)], axis=1
-    )
+    group_tokens = lax.all_gather(tokens, "seq", axis=0, tiled=True)
     head_w = projection.reshape(projection.shape[0], 3, seq_count, head_cols)
     head_w = lax.dynamic_index_in_dim(head_w, seq_index, axis=2, keepdims=False)
     head_w = lax.all_gather(head_w, "zero", axis=0, tiled=True)
-    queries = jnp.einsum(
-        "td,dc->tc", group_tokens, head_w[:, 0], preferred_element_type=jnp.float32
-    ).astype(jnp.bfloat16)
     kv_local = jnp.einsum(
         "td,dc->tc",
         group_tokens,
         head_w[:, 1:].reshape(-1, 2 * head_cols),
         preferred_element_type=jnp.float32,
+    ).astype(jnp.bfloat16)
+    kv_local, group_tokens, upstream = lax.optimization_barrier((kv_local, group_tokens, upstream))
+    queries = jnp.einsum(
+        "td,dc->tc", group_tokens, head_w[:, 0], preferred_element_type=jnp.float32
     ).astype(jnp.bfloat16)
     kv_all = lax.all_gather(kv_local, "zero", axis=0, tiled=True)
     incoming = lax.all_to_all(

time: 322 us -> 305 us (0.947)
  blocking collectives: 120 us -> 93.6 us
  waiting for transfers between devices: 83.9 us -> 99.9 us
  starting transfers between devices: 29.9 us -> 20.5 us
    all_to_all x1 -> x0, blocking collectives: 33.4 us -> none  [on_device(): lax.all_to_all(t_send, 'seq', split_axis=0, concat_axis=0, tiled=True)]
    all_gather x0 -> x1, waiting for transfers between devices: none -> 15.2 us  [on_device(): group_tokens = lax.all_gather(tokens, 'seq', axis=0, tiled=True)]
    all_gather x0 -> x1, local copies, waits for them, and re-layouts: none -> 6.38 us  [on_device(): kv_all = lax.all_gather(kv_local, 'zero', axis=0, tiled=True)]
    all_to_all x1, blocking collectives: 58.8 us -> 64.7 us  [on_device(): lax.all_to_all(group_sums, 'zero', split_axis=0, concat_axis=0, tiled=True)]
    all_to_all x1, starting transfers between devices: 8.71 us -> 4.16 us  [on_device(): lax.all_to_all(head_part, 'zero', split_axis=0, concat_axis=0, tiled=True)]
    all_to_all x1, waiting for transfers between devices: 5.83 us -> 10.4 us  [on_device(): lax.all_to_all(head_part, 'zero', split_axis=0, concat_axis=0, tiled=True)]
    all_gather x1, waiting for transfers between devices: 4.48 us -> 0.02 us  [on_device(): w_mine = lax.all_gather(w_mine, 'zero', axis=0, tiled=True)]
    all_gather x1, waiting for transfers between devices: 52.5 us -> 55.9 us  [on_device(): kv_all = lax.all_gather(kv_local, 'zero', axis=0, tiled=True)]
  transfers between devices with their start and end apart: 9 -> 9, of which waited for: 6 -> 6; matrix products, arithmetic and copies ran while one was open for 12% -> 14% of each run, Pallas kernels for 8% -> 8%
where the time goes in v7:
time: 305 us; the launch traced here: 304 us
  waiting for transfers between devices  99.9 us (33%)
  blocking collectives  93.6 us (31%)
  local copies, waits for them, and re-layouts  27.1 us (9%)
  Pallas kernels  25 us (8%)
  starting transfers between devices  20.5 us (7%)
  matrix products  18.7 us (6%)
  between operations  14 us (5%)
  other arithmetic  5.37 us (2%)
    all_to_all x1, blocking collectives, on_device(): lax.all_to_all(group_sums, 'zero', split_axis=0, concat_axis=0, tiled=True)  64.7 us
    all_gather x1, waiting for transfers between devices, on_device(): kv_all = lax.all_gather(kv_local, 'zero', axis=0, tiled=True)  55.9 us
    all_gather x1, blocking collectives, on_device(): head_w = lax.all_gather(head_w, 'zero', axis=0, tiled=True)  28.9 us
    pallas_call x1, Pallas kernels, block_attention(): pl.pallas_call(functools.partial(_attn_kernel, scale=scale), grid_spec=gr...  25 us
    all_gather x1, waiting for transfers between devices, on_device(): group_tokens = lax.all_gather(tokens, 'seq', axis=0, tiled=True)  15.2 us
    all_to_all x1, waiting for transfers between devices, on_device(): lax.all_to_all(local_grads, 'seq', split_axis=0, concat_axis=2, tiled=True)  11.4 us
    unnamed x15, local copies, waits for them, and re-layouts  11.2 us
    all_to_all x1, waiting for transfers between devices, on_device(): lax.all_to_all(head_part, 'zero', split_axis=0, concat_axis=0, tiled=True)  10.4 us
  transfers between devices with their start and end apart: 9, of which 6 were waited for; matrix products, arithmetic and copies ran while one was open for 14% of the time, Pallas kernels for 8%

profile of v7, /device:TPU:1, one launch (start us, length us, event | category | flops | bytes accessed | tf_op | source)
XLA Modules:
  0.0 304.2 jit_solution(228384311599069465)
XLA Ops:
  7.2 0.0 all-gather.6.cloned.1.call-start
  7.2 0.7 all-gather.6.cloned.1.call-update
  7.9 0.0 all-gather.8.cloned.1.call-start
  7.9 1.5 copy.51
  9.5 0.0 copy-start
  9.5 28.9 %all-gather = bf16[1024,3,1,64]{0,3,2,1:T(8,128)(2,1)S(1)} all-gather(bf16[128,3,1,64]{0,3,2,1:T(8,128)(2,1)S(1)} %constant_dynamic-slice_fusion.1), channel_id=2, replica_groups=mesh['seq'=16,'zero'=8] {'zero'}, dimensions={0}, use_global_device_ids=true | all-gather | bytes 442368 | tf_op jit(solution)/shard_map/all_gather | solution.py:99
  38.4 15.2 %all-gather.6.cloned.1.call-done = bf16[2048,1024]{1,0:T(8,128)(2,1)} async-done(((bf16[128,1024]{1,0:T(8,128)(2,1)}), bf16[2048,1024]{1,0:T(8,128)(2,1)}) %all-gather.6.cloned.1.call-update) | async-done | bytes 4194320 | tf_op jit(solution)/shard_map/all_gather | solution.py:96
  53.6 0.0 copy-start.2
  53.6 0.0 copy-start.1
  53.6 4.5 %fusion = bf16[2048,128]{0,1:T(8,128)(2,1)} fusion(bf16[1024,128]{0,1:T(8,128)(2,1)S(1)} %bitcast.68, bf16[2048,1024]{1,0:T(8,128)(2,1)} %all-gather.6.cloned.1.call-done), kind=kOutput, calls=%fused_computation.2 | convolution fusion | flops 537133056 | bytes 4980736 | tf_op jit(solution)/shard_map/td,dc->tc/dot_general | solution.py:100
  58.1 0.0 all-gather.8.cloned.1.call-update
  58.1 0.0 all-gather.10.cloned.1.call-start
  58.2 0.0 copy-done
  58.2 0.8 constant_dynamic-slice_fusion
  59.0 0.0 all-gather.10.cloned.1.call-update
  59.0 0.0 copy-done.2
  59.0 0.1 copy.50
  59.1 0.6 gather_fusion
  59.7 0.0 copy-done.1
  59.7 0.8 copy.53
  60.6 3.6 %all-to-all-start = ((bf16[128,16,64]{0,2,1:T(8,128)(2,1)}), bf16[128,16,64]{0,2,1:T(8,128)(2,1)S(1)}, u32[]{:S(2)}, u32[]{:S(2)}) async-start(bf16[128,16,64]{0,2,1:T(8,128)(2,1)} %bitcast.7), calls=%async_computation | async-start | bytes 524288 | tf_op jit(solution)/shard_map/all_to_all | solution.py:111
  64.2 3.6 %convolution_convert_fusion.1 = bf16[2048,64]{0,1:T(8,128)(2,1)S(1)} fusion(bf16[2048,1024]{1,0:T(8,128)(2,1)} %all-gather.6.cloned.1.call-done, bf16[1024,3,64]{0,2,1:T(8,128)(2,1)S(1)} %bitcast.67), kind=kOutput, calls=%fused_computation.3 | convolution fusion | flops 268566528 | bytes 4587520 | tf_op jit(solution)/shard_map/td,dc->tc/dot_general | solution.py:107
  67.8 0.3 copy.52
  68.1 3.4 %all-to-all-done = bf16[128,16,64]{0,2,1:T(8,128)(2,1)S(1)} async-done(((bf16[128,16,64]{0,2,1:T(8,128)(2,1)}), bf16[128,16,64]{0,2,1:T(8,128)(2,1)S(1)}, u32[]{:S(2)}, u32[]{:S(2)}) %all-to-all-start) | async-done | bytes 262176 | tf_op jit(solution)/shard_map/all_to_all | solution.py:111
  71.5 0.3 copy.54
  71.7 55.9 %all-gather.8.cloned.1.call-done = bf16[16384,128]{0,1:T(8,128)(2,1)} async-done(((bf16[2048,128]{0,1:T(8,128)(2,1)}), bf16[16384,128]{0,1:T(8,128)(2,1)}) %all-gather.8.cloned.1.call-update) | async-done | bytes 4194320 | tf_op jit(solution)/shard_map/all_gather | solution.py:110
  127.7 6.4 %copy.55 = bf16[16384,128]{1,0:T(8,128)(2,1)} copy(bf16[16384,128]{0,1:T(8,128)(2,1)} %all-gather.8.cloned.1.call-done) | data formatting | bytes 8388608 | tf_op jit(solution)/shard_map/all_gather | solution.py:110
  134.0 25.0 %shard_map.67 = (bf16[16,128,64]{2,1,0:T(8,128)(2,1)S(1)}, bf16[16,128,64]{2,1,0:T(8,128)(2,1)S(1)}, bf16[128,128,128]{2,1,0:T(8,128)(2,1)}) custom-call(s32[16,8]{1,0:T(8,128)S(1)} %fusion.6.slots_ref, bf16[16,128,64]{2,1,0:T(8,128)(2,1)S(1)} %bitcast.53, bf16[16,128,64]{2,1,0:T(8,128)(2,1)S(1)} %bitcast.54, bf16[128,128,128]{2,1,0:T(8,128)(2,1)} %bitcast.58), custom_call_target="tpu_custom_call" | custom-call | tf_op jit(solution)/shard_map/pallas_call | solution.py:68
  159.0 64.7 %all_to_all.55 = bf16[8,2048,128]{2,1,0:T(8,128)(2,1)} all-to-all(bf16[8,2048,128]{2,1,0:T(8,128)(2,1)} %bitcast.62), channel_id=1, replica_groups=mesh['seq'=16,'zero'=8] {'zero'}, dimensions={0} | all-to-all | bytes 8388608 | tf_op jit(solution)/shard_map/all_to_all | solution.py:144
  223.8 3.1 %reduce_sum.21 = bf16[2048,128]{1,0:T(8,128)(2,1)S(1)} reduce(bf16[8,2048,128]{2,1,0:T(8,128)(2,1)} %all_to_all.55, bf16[]{:T(256)} %constant.99.clone.1), dimensions={0}, to_apply=%region_0.1 | reduce | flops 1835008 | bytes 4718594 | tf_op jit(solution)/shard_map/reduce_sum | solution.py:145
  226.9 3.7 %convolution_bitcast_fusion = f32[24,8,8,128]{3,2,1,0:T(8,128)S(1)} fusion(bf16[2048,1024]{1,0:T(8,128)(2,1)} %all-gather.6.cloned.1.call-done, bf16[2048,128]{1,0:T(8,128)(2,1)S(1)} %reduce_sum.21, bf16[2048,64]{1,0:T(8,128)(2,1)S(1)} %bitcast.56), kind=kOutput, calls=%fused_computation.4 | convolution fusion | flops 806879232 | bytes 5767168 | tf_op jit(solution)/shard_map/td,tc->dc/dot_general | solution.py:157
  230.6 0.9 copy.72
  231.5 4.2 %all-to-all-start.4 = ((f32[8,128,192]{1,2,0:T(8,128)}), f32[8,128,192]{1,2,0:T(8,128)S(1)}, u32[]{:S(2)}, u32[]{:S(2)}) async-start(f32[8,128,192]{1,2,0:T(8,128)} %bitcast.52), calls=%async_computation.4 | async-start | bytes 1572864 | tf_op jit(solution)/shard_map/all_to_all | solution.py:161
  235.7 0.0 all-gather.12.cloned.1.call-start
  235.7 0.0 all-gather.10.cloned.1.call-done
  235.7 1.8 collective-permute-start
  237.6 10.4 %all-to-all-done.4 = f32[8,128,192]{1,2,0:T(8,128)S(1)} async-done(((f32[8,128,192]{1,2,0:T(8,128)}), f32[8,128,192]{1,2,0:T(8,128)S(1)}, u32[]{:S(2)}, u32[]{:S(2)}) %all-to-all-start.4) | async-done | bytes 786464 | tf_op jit(solution)/shard_map/all_to_all | solution.py:161
  247.9 0.7 reduce_sum.22
  248.6 0.0 all-gather.12.cloned.1.call-update
  248.6 0.5 broadcast.117
  249.2 1.1 reduce.1
  250.3 1.1 reshape.97
  251.4 6.4 %all-to-all-start.1 = ((bf16[16,2,4096]{2,1,0:T(2,128)(2,1)}), bf16[16,2,4096]{2,1,0:T(2,128)(2,1)S(1)}, u32[]{:S(2)}, u32[]{:S(2)}) async-start(bf16[16,2,4096]{2,1,0:T(2,128)(2,1)} %reshape.97), calls=%async_computation.1 | async-start | bytes 524288 | tf_op jit(solution)/shard_map/all_to_all | solution.py:135
  257.8 0.5 pad_maximum_fusion
  258.3 0.5 copy.59
  258.8 1.4 copy.60
  260.2 2.5 reshape.99
  262.7 3.0 all-to-all-done.1
  265.7 4.4 %all-to-all-start.3 = ((bf16[16,2,12288]{2,1,0:T(2,128)(2,1)}), bf16[16,2,12288]{2,1,0:T(2,128)(2,1)}, u32[]{:S(2)}, u32[]{:S(2)}) async-start(bf16[16,2,12288]{2,1,0:T(2,128)(2,1)} %reshape.99), calls=%async_computation.3 | async-start | bytes 1572864 | tf_op jit(solution)/shard_map/all_to_all | solution.py:148
  270.0 0.6 reshape.98
  270.7 0.6 copy.57
  271.3 0.1 copy.58
  271.4 0.9 copy.65
  272.3 11.4 %all-to-all-done.3 = bf16[16,2,12288]{2,1,0:T(2,128)(2,1)} async-done(((bf16[16,2,12288]{2,1,0:T(2,128)(2,1)}), bf16[16,2,12288]{2,1,0:T(2,128)(2,1)}, u32[]{:S(2)}, u32[]{:S(2)}) %all-to-all-start.3) | async-done | bytes 786464 | tf_op jit(solution)/shard_map/all_to_all | solution.py:148
  283.6 2.9 reshape.100
  286.5 1.2 copy.68
  287.7 3.0 %fusion.3 = f32[128,1024]{1,0:T(8,128)S(1)} fusion(bf16[1024,1536]{1,0:T(8,128)(2,1)} %all-gather.10.cloned.1.call-done, bf16[128,3072]{0,1:T(8,128)(2,1)S(1)} %bitcast.63, s32[]{:T(128)S(6)} %select_n.61), kind=kOutput, calls=%fused_computation.10 | convolution fusion | flops 402653184 | bytes 4063236 | tf_op jit(solution)/shard_map/tc,dc->td/dot_general | solution.py:153
  290.8 0.0 collective-permute-done
  290.8 3.8 %fusion.1 = bf16[128,1024]{1,0:T(8,128)(2,1)} fusion(f32[128,1024]{1,0:T(8,128)S(1)} %fusion.3, bf16[1024,1536]{1,0:T(8,128)(2,1)} %collective-permute-done, bf16[128,3072]{0,1:T(8,128)(2,1)S(1)} %bitcast.64, s32[]{:T(128)S(6)} %select_n.62), kind=kOutput, calls=%fused_computation.6 | convolution fusion | flops 402915328 | bytes 4325380 | tf_op jit(solution)/shard_map/tc,dc->td/dot_general | solution.py:154
  294.6 0.0 all-gather.12.cloned.1.call-done
  294.6 1.5 copy.64
  296.1 1.6 copy.66
  (6 shorter events, 0.1 us)
Async XLA Ops:
  7.2 46.4 %all-gather.6.cloned.1.call-start = ((), (), s32[]{:S(2)}) async-start(), calls=%async_computation.5 | async-start | bytes 4456448 | tf_op jit(solution)/shard_map/all_gather | solution.py:96
  7.9 119.8 %all-gather.8.cloned.1.call-start = ((), (), s32[]{:S(2)}) async-start(), calls=%async_computation.6 | async-start | bytes 4718592 | tf_op jit(solution)/shard_map/all_gather | solution.py:110
  9.5 48.7 %copy-start = (bf16[128,3072]{1,0:T(8,128)(2,1)S(1)}, bf16[128,3072]{1,0:T(8,128)(2,1)}, u32[]{:S(2)}) copy-start(bf16[128,3072]{1,0:T(8,128)(2,1)} %param.5) | copy-start | bytes 2359300
  53.6 5.5 %copy-start.2 = (s32[128,8]{0,1:T(8,128)S(1)}, s32[128,8]{0,1:T(8,128)}, u32[]{:S(2)}) copy-start(s32[128,8]{0,1:T(8,128)} %param.6) | copy-start | bytes 12292
  53.6 6.2 %copy-start.1 = (bf16[128,1024]{1,0:T(8,128)(2,1)S(1)}, bf16[128,1024]{1,0:T(8,128)(2,1)}, u32[]{:S(2)}) copy-start(bf16[128,1024]{1,0:T(8,128)(2,1)} %param.7) | copy-start | bytes 786436
  58.1 177.6 %all-gather.10.cloned.1.call-start = ((), (), s32[]{:S(2)}) async-start(), calls=%async_computation.7 | async-start | bytes 3538944 | tf_op jit(solution)/shard_map/all_gather | solution.py:94
  60.6 10.9 %all-to-all-start = ((bf16[128,16,64]{0,2,1:T(8,128)(2,1)}), bf16[128,16,64]{0,2,1:T(8,128)(2,1)S(1)}, u32[]{:S(2)}, u32[]{:S(2)}) async-start(bf16[128,16,64]{0,2,1:T(8,128)(2,1)} %bitcast.7), calls=%async_computation | async-start | bytes 524288 | tf_op jit(solution)/shard_map/all_to_all | solution.py:111
  231.5 16.4 %all-to-all-start.4 = ((f32[8,128,192]{1,2,0:T(8,128)}), f32[8,128,192]{1,2,0:T(8,128)S(1)}, u32[]{:S(2)}, u32[]{:S(2)}) async-start(f32[8,128,192]{1,2,0:T(8,128)} %bitcast.52), calls=%async_computation.4 | async-start | bytes 1572864 | tf_op jit(solution)/shard_map/all_to_all | solution.py:161
  235.7 58.9 %all-gather.12.cloned.1.call-start = ((), (), s32[]{:S(2)}) async-start(), calls=%async_computation.8 | async-start | bytes 1671168 | tf_op jit(solution)/shard_map/all_gather | solution.py:164
  235.7 55.0 %collective-permute-start = (bf16[1024,1536]{1,0:T(8,128)(2,1)}, bf16[1024,1536]{1,0:T(8,128)(2,1)}, u32[]{:S(2)}, u32[]{:S(2)}) collective-permute-start(bf16[1024,1536]{1,0:T(8,128)(2,1)} %all-gather.10.cloned.1.call-done), channel_id=1, source_target_pairs={{0,8},{8,0},{16,24},{24,16},{32,40},{40,32},{48,56},{56,48},{64,72... | collective-permute-start | bytes 9437192 | tf_op jit(solution)/shard_map/ppermute | solution.py:95
  251.4 14.3 %all-to-all-start.1 = ((bf16[16,2,4096]{2,1,0:T(2,128)(2,1)}), bf16[16,2,4096]{2,1,0:T(2,128)(2,1)S(1)}, u32[]{:S(2)}, u32[]{:S(2)}) async-start(bf16[16,2,4096]{2,1,0:T(2,128)(2,1)} %reshape.97), calls=%async_computation.1 | async-start | bytes 524288 | tf_op jit(solution)/shard_map/all_to_all | solution.py:135
  265.7 18.0 %all-to-all-start.3 = ((bf16[16,2,12288]{2,1,0:T(2,128)(2,1)}), bf16[16,2,12288]{2,1,0:T(2,128)(2,1)}, u32[]{:S(2)}, u32[]{:S(2)}) async-start(bf16[16,2,12288]{2,1,0:T(2,128)(2,1)} %reshape.99), calls=%async_computation.3 | async-start | bytes 1572864 | tf_op jit(solution)/shard_map/all_to_all | solution.py:148
Sparse Core Ops, SparseCore 0:
  9.7 43.8 all-gather.5
  58.2 69.3 all-gather.7
  130.0 105.3 all-gather.9
  248.8 36.5 all-gather.11

commit v8 on v7

--- a/solution.py
+++ b/solution.py
@@ -107,6 +107,7 @@
     queries = jnp.einsum(
         "td,dc->tc", group_tokens, head_w[:, 0], preferred_element_type=jnp.float32
     ).astype(jnp.bfloat16)
+    kv_local = kv_local.reshape(local_blocks, BLOCK, 2 * head_cols)
     kv_all = lax.all_gather(kv_local, "zero", axis=0, tiled=True)
     incoming = lax.all_to_all(
         upstream.reshape(tok_rows, seq_count, head_cols),
@@ -129,7 +130,7 @@
         key_slots.reshape(local_blocks, NBK),
         queries.reshape(local_blocks, BLOCK, head_cols),
         incoming.reshape(local_blocks, BLOCK, head_cols),
-        kv_all.reshape(-1, BLOCK, 2 * head_cols),
+        kv_all,
         score_scale,
     )
     attended = lax.all_to_all(

time: 305 us -> 298 us (0.977)
  blocking collectives: 93.6 us -> 87.5 us
  local copies, waits for them, and re-layouts: 27.1 us -> 21.7 us
  starting transfers between devices: 20.5 us -> 25.5 us
    all_gather x1 -> x0, local copies, waits for them, and re-layouts: 6.38 us -> none  [on_device(): kv_all = lax.all_gather(kv_local, 'zero', axis=0, tiled=True)]
    all_to_all x1, blocking collectives: 64.7 us -> 58.8 us  [on_device(): lax.all_to_all(group_sums, 'zero', split_axis=0, concat_axis=0, tiled=True)]
    all_to_all x1, waiting for transfers between devices: 10.4 us -> 5.79 us  [on_device(): lax.all_to_all(head_part, 'zero', split_axis=0, concat_axis=0, tiled=True)]
    all_to_all x1, starting transfers between devices: 4.16 us -> 8.72 us  [on_device(): lax.all_to_all(head_part, 'zero', split_axis=0, concat_axis=0, tiled=True)]
    all_gather x1, waiting for transfers between devices: 0.02 us -> 4.51 us  [on_device(): w_mine = lax.all_gather(w_mine, 'zero', axis=0, tiled=True)]
  transfers between devices with their start and end apart: 9 -> 9, of which waited for: 6 -> 7; matrix products, arithmetic and copies ran while one was open for 14% -> 12% of each run, Pallas kernels for 8% -> 8%
where the time goes in v8:
time: 298 us; the launch traced here: 297 us
  waiting for transfers between devices  99.9 us (34%)
  blocking collectives  87.5 us (29%)
  starting transfers between devices  25.5 us (9%)
  Pallas kernels  24.9 us (8%)
  local copies, waits for them, and re-layouts  21.7 us (7%)
  matrix products  17.9 us (6%)
  between operations  14 us (5%)
  other arithmetic  5.37 us (2%)
    all_to_all x1, blocking collectives, on_device(): lax.all_to_all(group_sums, 'zero', split_axis=0, concat_axis=0, tiled=True)  58.8 us
    all_gather x1, waiting for transfers between devices, on_device(): kv_all = lax.all_gather(kv_local, 'zero', axis=0, tiled=True)  55.8 us
    all_gather x1, blocking collectives, on_device(): head_w = lax.all_gather(head_w, 'zero', axis=0, tiled=True)  28.7 us
    pallas_call x1, Pallas kernels, block_attention(): pl.pallas_call(functools.partial(_attn_kernel, scale=scale), grid_spec=gr...  24.9 us
    all_gather x1, waiting for transfers between devices, on_device(): group_tokens = lax.all_gather(tokens, 'seq', axis=0, tiled=True)  15.3 us
    all_to_all x1, waiting for transfers between devices, on_device(): lax.all_to_all(local_grads, 'seq', split_axis=0, concat_axis=2, tiled=True)  11.4 us
    unnamed x15, local copies, waits for them, and re-layouts  11.2 us
    all_to_all x1, starting transfers between devices, on_device(): lax.all_to_all(head_part, 'zero', split_axis=0, concat_axis=0, tiled=True)  8.72 us
  transfers between devices with their start and end apart: 9, of which 7 were waited for; matrix products, arithmetic and copies ran while one was open for 12% of the time, Pallas kernels for 8%

profile of v8, /device:TPU:1, one launch (start us, length us, event | category | flops | bytes accessed | tf_op | source)
XLA Modules:
  0.0 296.7 jit_solution(10489643821103681924)
XLA Ops:
  7.2 0.0 all-gather.6.cloned.1.call-start
  7.2 0.7 all-gather.6.cloned.1.call-update
  7.9 0.0 all-gather.8.cloned.1.call-start
  7.9 1.5 copy.51
  9.5 28.7 %all-gather = bf16[1024,3,1,64]{0,3,2,1:T(8,128)(2,1)S(1)} all-gather(bf16[128,3,1,64]{0,3,2,1:T(8,128)(2,1)S(1)} %constant_dynamic-slice_fusion.1), channel_id=2, replica_groups=mesh['seq'=16,'zero'=8] {'zero'}, dimensions={0}, use_global_device_ids=true | all-gather | bytes 442368 | tf_op jit(solution)/shard_map/all_gather | solution.py:99
  38.2 15.3 %all-gather.6.cloned.1.call-done = bf16[2048,1024]{1,0:T(8,128)(2,1)} async-done(((bf16[128,1024]{1,0:T(8,128)(2,1)}), bf16[2048,1024]{1,0:T(8,128)(2,1)}) %all-gather.6.cloned.1.call-update) | async-done | bytes 4194320 | tf_op jit(solution)/shard_map/all_gather | solution.py:96
  53.6 0.0 copy-start
  53.6 0.0 copy-start.2
  53.6 0.0 copy-start.1
  53.6 3.8 %fusion = bf16[2048,128]{0,1:T(8,128)(2,1)S(1)} fusion(bf16[1024,128]{0,1:T(8,128)(2,1)S(1)} %bitcast.68, bf16[2048,1024]{1,0:T(8,128)(2,1)} %all-gather.6.cloned.1.call-done), kind=kOutput, calls=%fused_computation.2 | convolution fusion | flops 537133056 | bytes 4980736 | tf_op jit(solution)/shard_map/td,dc->tc/dot_general | solution.py:100
  57.3 1.0 copy.67
  58.3 0.0 all-gather.8.cloned.1.call-update
  58.4 0.0 all-gather.10.cloned.1.call-start
  58.4 0.0 copy-done
  58.4 0.8 constant_dynamic-slice_fusion
  59.2 0.0 all-gather.10.cloned.1.call-update
  59.3 0.0 copy-done.2
  59.3 0.1 copy.50
  59.4 0.6 gather_fusion
  60.0 0.0 copy-done.1
  60.0 0.8 copy.53
  60.8 3.6 %all-to-all-start = ((bf16[128,16,64]{0,2,1:T(8,128)(2,1)}), bf16[128,16,64]{0,2,1:T(8,128)(2,1)S(1)}, u32[]{:S(2)}, u32[]{:S(2)}) async-start(bf16[128,16,64]{0,2,1:T(8,128)(2,1)} %bitcast.7), calls=%async_computation | async-start | bytes 524288 | tf_op jit(solution)/shard_map/all_to_all | solution.py:112
  64.4 3.7 %convolution_convert_fusion.1 = bf16[2048,64]{0,1:T(8,128)(2,1)S(1)} fusion(bf16[2048,1024]{1,0:T(8,128)(2,1)} %all-gather.6.cloned.1.call-done, bf16[1024,3,64]{0,2,1:T(8,128)(2,1)S(1)} %bitcast.67), kind=kOutput, calls=%fused_computation.3 | convolution fusion | flops 268566528 | bytes 4587520 | tf_op jit(solution)/shard_map/td,dc->tc/dot_general | solution.py:107
  68.1 0.3 copy.52
  68.4 3.3 %all-to-all-done = bf16[128,16,64]{0,2,1:T(8,128)(2,1)S(1)} async-done(((bf16[128,16,64]{0,2,1:T(8,128)(2,1)}), bf16[128,16,64]{0,2,1:T(8,128)(2,1)S(1)}, u32[]{:S(2)}, u32[]{:S(2)}) %all-to-all-start) | async-done | bytes 262176 | tf_op jit(solution)/shard_map/all_to_all | solution.py:112
  71.7 0.3 copy.54
  72.0 55.8 %all-gather.8.cloned.1.call-done.kv_ref = bf16[128,128,128]{2,1,0:T(8,128)(2,1)} async-done(((bf16[16,128,128]{2,1,0:T(8,128)(2,1)}), bf16[128,128,128]{2,1,0:T(8,128)(2,1)}) %all-gather.8.cloned.1.call-update) | async-done | bytes 4194320 | tf_op jit(solution)/shard_map/all_gather | solution.py:111
  127.8 24.9 %shard_map.67 = (bf16[16,128,64]{2,1,0:T(8,128)(2,1)S(1)}, bf16[16,128,64]{2,1,0:T(8,128)(2,1)S(1)}, bf16[128,128,128]{2,1,0:T(8,128)(2,1)}) custom-call(s32[16,8]{1,0:T(8,128)S(1)} %fusion.6.slots_ref, bf16[16,128,64]{2,1,0:T(8,128)(2,1)S(1)} %bitcast.53, bf16[16,128,64]{2,1,0:T(8,128)(2,1)S(1)} %bitcast.54, ...), custom_call_target="tpu_custom_call" | custom-call | tf_op jit(solution)/shard_map/pallas_call | solution.py:68
  152.7 58.8 %all_to_all.55 = bf16[8,2048,128]{2,1,0:T(8,128)(2,1)} all-to-all(bf16[8,2048,128]{2,1,0:T(8,128)(2,1)} %bitcast.61), channel_id=1, replica_groups=mesh['seq'=16,'zero'=8] {'zero'}, dimensions={0} | all-to-all | bytes 8388608 | tf_op jit(solution)/shard_map/all_to_all | solution.py:145
  211.5 3.1 %reduce_sum.21 = bf16[2048,128]{1,0:T(8,128)(2,1)S(1)} reduce(bf16[8,2048,128]{2,1,0:T(8,128)(2,1)} %all_to_all.55, bf16[]{:T(256)} %constant.99.clone.1), dimensions={0}, to_apply=%region_0.1 | reduce | flops 1835008 | bytes 4718594 | tf_op jit(solution)/shard_map/reduce_sum | solution.py:146
  214.6 3.6 %convolution_bitcast_fusion = f32[24,8,8,128]{3,2,1,0:T(8,128)S(1)} fusion(bf16[2048,1024]{1,0:T(8,128)(2,1)} %all-gather.6.cloned.1.call-done, bf16[2048,128]{1,0:T(8,128)(2,1)S(1)} %reduce_sum.21, bf16[2048,64]{1,0:T(8,128)(2,1)S(1)} %bitcast.56), kind=kOutput, calls=%fused_computation.4 | convolution fusion | flops 806879232 | bytes 5767168 | tf_op jit(solution)/shard_map/td,tc->dc/dot_general | solution.py:158
  218.2 0.9 copy.73
  219.1 8.7 %all-to-all-start.4 = ((f32[8,128,192]{1,2,0:T(8,128)}), f32[8,128,192]{1,2,0:T(8,128)S(1)}, u32[]{:S(2)}, u32[]{:S(2)}) async-start(f32[8,128,192]{1,2,0:T(8,128)} %bitcast.52), calls=%async_computation.4 | async-start | bytes 1572864 | tf_op jit(solution)/shard_map/all_to_all | solution.py:162
  227.9 0.0 all-gather.12.cloned.1.call-start
  227.9 4.5 %all-gather.10.cloned.1.call-done = bf16[1024,1536]{1,0:T(8,128)(2,1)} async-done(((bf16[128,1536]{1,0:T(8,128)(2,1)}), bf16[1024,1536]{1,0:T(8,128)(2,1)}) %all-gather.10.cloned.1.call-update) | async-done | bytes 3145744 | tf_op jit(solution)/shard_map/all_gather | solution.py:94
  232.4 1.5 collective-permute-start
  233.9 5.8 %all-to-all-done.4 = f32[8,128,192]{1,2,0:T(8,128)S(1)} async-done(((f32[8,128,192]{1,2,0:T(8,128)}), f32[8,128,192]{1,2,0:T(8,128)S(1)}, u32[]{:S(2)}, u32[]{:S(2)}) %all-to-all-start.4) | async-done | bytes 786464 | tf_op jit(solution)/shard_map/all_to_all | solution.py:162
  239.7 0.7 reduce_sum.22
  240.4 0.0 all-gather.12.cloned.1.call-update
  240.4 0.5 broadcast.117
  240.9 1.1 reduce.1
  242.0 1.1 reshape.97
  243.1 7.2 %all-to-all-start.1 = ((bf16[16,2,4096]{2,1,0:T(2,128)(2,1)}), bf16[16,2,4096]{2,1,0:T(2,128)(2,1)S(1)}, u32[]{:S(2)}, u32[]{:S(2)}) async-start(bf16[16,2,4096]{2,1,0:T(2,128)(2,1)} %reshape.97), calls=%async_computation.1 | async-start | bytes 524288 | tf_op jit(solution)/shard_map/all_to_all | solution.py:136
  250.3 0.5 pad_maximum_fusion
  250.8 0.5 copy.59
  251.3 1.4 copy.60
  252.7 2.5 reshape.99
  255.1 3.0 %all-to-all-done.1 = bf16[16,2,4096]{2,1,0:T(2,128)(2,1)S(1)} async-done(((bf16[16,2,4096]{2,1,0:T(2,128)(2,1)}), bf16[16,2,4096]{2,1,0:T(2,128)(2,1)S(1)}, u32[]{:S(2)}, u32[]{:S(2)}) %all-to-all-start.1) | async-done | bytes 262176 | tf_op jit(solution)/shard_map/all_to_all | solution.py:136
  258.1 4.4 %all-to-all-start.3 = ((bf16[16,2,12288]{2,1,0:T(2,128)(2,1)}), bf16[16,2,12288]{2,1,0:T(2,128)(2,1)}, u32[]{:S(2)}, u32[]{:S(2)}) async-start(bf16[16,2,12288]{2,1,0:T(2,128)(2,1)} %reshape.99), calls=%async_computation.3 | async-start | bytes 1572864 | tf_op jit(solution)/shard_map/all_to_all | solution.py:149
  262.5 0.6 reshape.98
  263.1 0.6 copy.57
  263.8 0.1 copy.58
  263.9 0.9 copy.65
  264.7 11.4 %all-to-all-done.3 = bf16[16,2,12288]{2,1,0:T(2,128)(2,1)} async-done(((bf16[16,2,12288]{2,1,0:T(2,128)(2,1)}), bf16[16,2,12288]{2,1,0:T(2,128)(2,1)}, u32[]{:S(2)}, u32[]{:S(2)}) %all-to-all-start.3) | async-done | bytes 786464 | tf_op jit(solution)/shard_map/all_to_all | solution.py:149
  276.1 2.9 reshape.100
  279.0 1.2 copy.69
  280.2 3.1 %fusion.3 = f32[128,1024]{1,0:T(8,128)S(1)} fusion(bf16[1024,1536]{1,0:T(8,128)(2,1)} %all-gather.10.cloned.1.call-done, bf16[128,3072]{0,1:T(8,128)(2,1)S(1)} %bitcast.62, s32[]{:T(128)S(6)} %select_n.61), kind=kOutput, calls=%fused_computation.10 | convolution fusion | flops 402653184 | bytes 4063236 | tf_op jit(solution)/shard_map/tc,dc->td/dot_general | solution.py:154
  283.3 0.0 collective-permute-done
  283.3 3.8 %fusion.1 = bf16[128,1024]{1,0:T(8,128)(2,1)} fusion(f32[128,1024]{1,0:T(8,128)S(1)} %fusion.3, bf16[1024,1536]{1,0:T(8,128)(2,1)} %collective-permute-done, bf16[128,3072]{0,1:T(8,128)(2,1)S(1)} %bitcast.63, s32[]{:T(128)S(6)} %select_n.62), kind=kOutput, calls=%fused_computation.6 | convolution fusion | flops 402915328 | bytes 4325380 | tf_op jit(solution)/shard_map/tc,dc->td/dot_general | solution.py:155
  287.0 0.0 all-gather.12.cloned.1.call-done
  287.1 1.5 copy.64
  288.6 1.6 copy.66
  (6 shorter events, 0.1 us)
Async XLA Ops:
  7.2 46.4 %all-gather.6.cloned.1.call-start = ((), (), s32[]{:S(2)}) async-start(), calls=%async_computation.5 | async-start | bytes 4456448 | tf_op jit(solution)/shard_map/all_gather | solution.py:96
  7.9 119.9 %all-gather.8.cloned.1.call-start = ((), (), s32[]{:S(2)}) async-start(), calls=%async_computation.6 | async-start | bytes 4718592 | tf_op jit(solution)/shard_map/all_gather | solution.py:111
  53.6 4.9 %copy-start = (bf16[128,3072]{1,0:T(8,128)(2,1)S(1)}, bf16[128,3072]{1,0:T(8,128)(2,1)}, u32[]{:S(2)}) copy-start(bf16[128,3072]{1,0:T(8,128)(2,1)} %param.5) | copy-start | bytes 2359300
  53.6 5.7 %copy-start.2 = (s32[128,8]{0,1:T(8,128)S(1)}, s32[128,8]{0,1:T(8,128)}, u32[]{:S(2)}) copy-start(s32[128,8]{0,1:T(8,128)} %param.6) | copy-start | bytes 12292
  53.6 6.4 %copy-start.1 = (bf16[128,1024]{1,0:T(8,128)(2,1)S(1)}, bf16[128,1024]{1,0:T(8,128)(2,1)}, u32[]{:S(2)}) copy-start(bf16[128,1024]{1,0:T(8,128)(2,1)} %param.7) | copy-start | bytes 786436
  58.4 174.0 %all-gather.10.cloned.1.call-start = ((), (), s32[]{:S(2)}) async-start(), calls=%async_computation.7 | async-start | bytes 3538944 | tf_op jit(solution)/shard_map/all_gather | solution.py:94
  60.8 10.9 %all-to-all-start = ((bf16[128,16,64]{0,2,1:T(8,128)(2,1)}), bf16[128,16,64]{0,2,1:T(8,128)(2,1)S(1)}, u32[]{:S(2)}, u32[]{:S(2)}) async-start(bf16[128,16,64]{0,2,1:T(8,128)(2,1)} %bitcast.7), calls=%async_computation | async-start | bytes 524288 | tf_op jit(solution)/shard_map/all_to_all | solution.py:112
  219.1 20.5 %all-to-all-start.4 = ((f32[8,128,192]{1,2,0:T(8,128)}), f32[8,128,192]{1,2,0:T(8,128)S(1)}, u32[]{:S(2)}, u32[]{:S(2)}) async-start(f32[8,128,192]{1,2,0:T(8,128)} %bitcast.52), calls=%async_computation.4 | async-start | bytes 1572864 | tf_op jit(solution)/shard_map/all_to_all | solution.py:162
  227.9 59.2 %all-gather.12.cloned.1.call-start = ((), (), s32[]{:S(2)}) async-start(), calls=%async_computation.8 | async-start | bytes 1671168 | tf_op jit(solution)/shard_map/all_gather | solution.py:165
  232.4 50.9 %collective-permute-start = (bf16[1024,1536]{1,0:T(8,128)(2,1)}, bf16[1024,1536]{1,0:T(8,128)(2,1)}, u32[]{:S(2)}, u32[]{:S(2)}) collective-permute-start(bf16[1024,1536]{1,0:T(8,128)(2,1)} %all-gather.10.cloned.1.call-done), channel_id=1, source_target_pairs={{0,8},{8,0},{16,24},{24,16},{32,40},{40,32},{48,56},{56,48},{64,72... | collective-permute-start | bytes 9437192 | tf_op jit(solution)/shard_map/ppermute | solution.py:95
  243.1 15.0 %all-to-all-start.1 = ((bf16[16,2,4096]{2,1,0:T(2,128)(2,1)}), bf16[16,2,4096]{2,1,0:T(2,128)(2,1)S(1)}, u32[]{:S(2)}, u32[]{:S(2)}) async-start(bf16[16,2,4096]{2,1,0:T(2,128)(2,1)} %reshape.97), calls=%async_computation.1 | async-start | bytes 524288 | tf_op jit(solution)/shard_map/all_to_all | solution.py:136
  258.1 18.0 %all-to-all-start.3 = ((bf16[16,2,12288]{2,1,0:T(2,128)(2,1)}), bf16[16,2,12288]{2,1,0:T(2,128)(2,1)}, u32[]{:S(2)}, u32[]{:S(2)}) async-start(bf16[16,2,12288]{2,1,0:T(2,128)(2,1)} %reshape.99), calls=%async_computation.3 | async-start | bytes 1572864 | tf_op jit(solution)/shard_map/all_to_all | solution.py:149
Sparse Core Ops, SparseCore 0:
  9.7 43.8 all-gather.5
  58.5 69.2 all-gather.7
  130.1 102.2 all-gather.9
  240.5 37.5 all-gather.11

commit v9 on v8

--- a/solution.py
+++ b/solution.py
@@ -12,7 +12,7 @@
 NBK = 8
 
 
-def _attn_kernel(slots_ref, q_ref, up_ref, kv_ref, out_ref, qg_ref, kvg_ref, acc_ref, *, scale):
+def _attn_kernel(slots_ref, a_ids_ref, b_ids_ref, q_ref, up_ref, ka_ref, kb_ref, out_ref, qg_ref, kvg_ref, acc_ref, *, scale):
     i = pl.program_id(0)
 
     @pl.when(i == 0)
@@ -22,7 +22,10 @@
     q = q_ref[0]
     up = up_ref[0]
     ids = [slots_ref[i, j] for j in range(NBK)]
-    blocks = [kv_ref[ids[j]] for j in range(NBK)]
+    blocks = [
+        jnp.where(a_ids_ref[i, j] >= 0, ka_ref[jnp.maximum(a_ids_ref[i, j], 0)], kb_ref[b_ids_ref[i, j]])
+        for j in range(NBK)
+    ]
     keys = jnp.concatenate([b[:, :HEAD] for b in blocks], axis=0)
     vals = jnp.concatenate([b[:, HEAD:] for b in blocks], axis=0)
     nt = (((1,), (1,)), ((), ()))
@@ -48,15 +51,16 @@
         kvg_ref[...] = acc_ref[...].astype(kvg_ref.dtype)
 
 
-def block_attention(slots, queries, upstream, kv, scale):
+def block_attention(slots, a_ids, b_ids, queries, upstream, kv_a, kv_b, scale):
     rows = queries.shape[0]
-    slot_count = kv.shape[0]
-    row_spec = pl.BlockSpec((1, BLOCK, HEAD), lambda i, s: (i, 0, 0))
-    full_spec = pl.BlockSpec((slot_count, BLOCK, 2 * HEAD), lambda i, s: (0, 0, 0))
+    slot_count = 2 * kv_a.shape[0]
+    row_spec = pl.BlockSpec((1, BLOCK, HEAD), lambda i, s, a, b: (i, 0, 0))
+    half_spec = pl.BlockSpec((slot_count // 2, BLOCK, 2 * HEAD), lambda i, s, a, b: (0, 0, 0))
+    full_spec = pl.BlockSpec((slot_count, BLOCK, 2 * HEAD), lambda i, s, a, b: (0, 0, 0))
     grid_spec = pltpu.PrefetchScalarGridSpec(
-        num_scalar_prefetch=1,
+        num_scalar_prefetch=3,
         grid=(rows,),
-        in_specs=[row_spec, row_spec, full_spec],
+        in_specs=[row_spec, row_spec, half_spec, half_spec],
         out_specs=[row_spec, row_spec, full_spec],
         scratch_shapes=[pltpu.VMEM((slot_count, BLOCK, 2 * HEAD), jnp.float32)],
     )
@@ -72,7 +76,7 @@
         compiler_params=pltpu.CompilerParams(
             dimension_semantics=("arbitrary",), vmem_limit_bytes=48 * 1024 * 1024
         ),
-    )(slots, queries, upstream, kv)
+    )(slots, a_ids, b_ids, queries, upstream, kv_a, kv_b)
 
 
 def on_device(tokens, projection, pattern, upstream):
@@ -108,7 +112,11 @@
         "td,dc->tc", group_tokens, head_w[:, 0], preferred_element_type=jnp.float32
     ).astype(jnp.bfloat16)
     kv_local = kv_local.reshape(local_blocks, BLOCK, 2 * head_cols)
-    kv_all = lax.all_gather(kv_local, "zero", axis=0, tiled=True)
+    split = local_blocks // 2
+    kv_a = lax.all_gather(kv_local[:split], "zero", axis=0, tiled=True)
+    kv_b = jnp.broadcast_to(kv_local[split:], (zero_count,) + kv_local[split:].shape)
+    kv_b = lax.all_to_all(kv_b, "zero", split_axis=0, concat_axis=0, tiled=True)
+    kv_b = kv_b.reshape(-1, BLOCK, 2 * head_cols)
     incoming = lax.all_to_all(
         upstream.reshape(tok_rows, seq_count, head_cols),
         "seq",
@@ -126,11 +134,19 @@
         + row_lists % per_shard
     )
 
+    key_slots = key_slots.reshape(local_blocks, NBK)
+    slot_zero = key_slots // local_blocks
+    slot_local = key_slots % local_blocks
+    a_ids = jnp.where(slot_local < split, slot_zero * split + slot_local, -1)
+    b_ids = slot_zero * (local_blocks - split) + jnp.maximum(slot_local - split, 0)
     out_blocks, query_grads, group_sums = block_attention(
-        key_slots.reshape(local_blocks, NBK),
+        key_slots,
+        a_ids,
+        b_ids,
         queries.reshape(local_blocks, BLOCK, head_cols),
         incoming.reshape(local_blocks, BLOCK, head_cols),
-        kv_all,
+        kv_a,
+        kv_b,
         score_scale,
     )
     attended = lax.all_to_all(

time: 298 us -> 293 us (0.983)
  waiting for transfers between devices: 99.9 us -> 88 us
  local copies, waits for them, and re-layouts: 21.7 us -> 25.2 us
  starting transfers between devices: 25.5 us -> 28.7 us
    all_gather x1, waiting for transfers between devices: 55.8 us -> 12.3 us  [on_device(): kv_a = lax.all_gather(kv_local[:split], 'zero', axis=0, tiled=True)]
    all_to_all x0 -> x1, waiting for transfers between devices: none -> 27.3 us  [on_device(): kv_b = lax.all_to_all(kv_b, 'zero', split_axis=0, concat_axis=0, tiled=True)]
    all_to_all x0 -> x1, starting transfers between devices: none -> 5.43 us  [on_device(): kv_b = lax.all_to_all(kv_b, 'zero', split_axis=0, concat_axis=0, tiled=True)]
    all_to_all x1, waiting for transfers between devices: 3.31 us -> 7.2 us  [on_device(): lax.all_to_all(upstream.reshape(tok_rows, seq_count, head_cols), 'seq', s...]
    unnamed x15 -> x17, local copies, waits for them, and re-layouts: 11.2 us -> 12.8 us
  transfers between devices with their start and end apart: 9 -> 10, of which waited for: 7 -> 8; matrix products, arithmetic and copies ran while one was open for 12% -> 13% of each run, Pallas kernels for 8% -> 9%
where the time goes in v9:
time: 293 us; the launch traced here: 292 us
  blocking collectives  88.4 us (30%)
  waiting for transfers between devices  88 us (30%)
  starting transfers between devices  28.7 us (10%)
  local copies, waits for them, and re-layouts  25.2 us (9%)
  Pallas kernels  24.9 us (8%)
  matrix products  17.7 us (6%)
  between operations  14 us (5%)
  other arithmetic  5.42 us (2%)
    all_to_all x1, blocking collectives, on_device(): lax.all_to_all(group_sums, 'zero', split_axis=0, concat_axis=0, tiled=True)  59.7 us
    all_gather x1, blocking collectives, on_device(): head_w = lax.all_gather(head_w, 'zero', axis=0, tiled=True)  28.7 us
    all_to_all x1, waiting for transfers between devices, on_device(): kv_b = lax.all_to_all(kv_b, 'zero', split_axis=0, concat_axis=0, tiled=True)  27.3 us
    pallas_call x1, Pallas kernels, block_attention(): pl.pallas_call(functools.partial(_attn_kernel, scale=scale), grid_spec=gr...  24.9 us
    all_gather x1, waiting for transfers between devices, on_device(): group_tokens = lax.all_gather(tokens, 'seq', axis=0, tiled=True)  15.3 us
    unnamed x17, local copies, waits for them, and re-layouts  12.8 us
    all_gather x1, waiting for transfers between devices, on_device(): kv_a = lax.all_gather(kv_local[:split], 'zero', axis=0, tiled=True)  12.3 us
    all_to_all x1, waiting for transfers between devices, on_device(): lax.all_to_all(local_grads, 'seq', split_axis=0, concat_axis=2, tiled=True)  10.7 us
  transfers between devices with their start and end apart: 10, of which 8 were waited for; matrix products, arithmetic and copies ran while one was open for 13% of the time, Pallas kernels for 9%

profile of v9, /device:TPU:1, one launch (start us, length us, event | category | flops | bytes accessed | tf_op | source)
XLA Modules:
  0.0 292.4 jit_solution(13933213251896112064)
XLA Ops:
  7.2 0.0 all-gather.6.cloned.1.call-start
  7.2 0.7 all-gather.6.cloned.1.call-update
  7.9 0.0 all-gather.8.cloned.1.call-start
  7.9 1.5 copy.55
  9.5 28.7 %all-gather = bf16[1024,3,1,64]{0,3,2,1:T(8,128)(2,1)S(1)} all-gather(bf16[128,3,1,64]{0,3,2,1:T(8,128)(2,1)S(1)} %constant_dynamic-slice_fusion.1), channel_id=2, replica_groups=mesh['seq'=16,'zero'=8] {'zero'}, dimensions={0}, use_global_device_ids=true | all-gather | bytes 442368 | tf_op jit(solution)/shard_map/all_gather | solution.py:103
  38.2 15.3 %all-gather.6.cloned.1.call-done = bf16[2048,1024]{1,0:T(8,128)(2,1)} async-done(((bf16[128,1024]{1,0:T(8,128)(2,1)}), bf16[2048,1024]{1,0:T(8,128)(2,1)}) %all-gather.6.cloned.1.call-update) | async-done | bytes 4194320 | tf_op jit(solution)/shard_map/all_gather | solution.py:100
  53.6 0.0 copy-start.2
  53.6 3.7 %fusion = bf16[2048,128]{0,1:T(8,128)(2,1)S(1)} fusion(bf16[1024,128]{0,1:T(8,128)(2,1)S(1)} %bitcast.70, bf16[2048,1024]{1,0:T(8,128)(2,1)} %all-gather.6.cloned.1.call-done), kind=kOutput, calls=%fused_computation.2 | convolution fusion | flops 537133056 | bytes 4980736 | tf_op jit(solution)/shard_map/td,dc->tc/dot_general | solution.py:104
  57.3 0.8 copy.72
  58.2 0.0 all-gather.8.cloned.1.call-update
  58.2 0.0 copy-done.2
  58.2 0.8 copy.57
  59.1 3.6 %all-to-all-start = ((bf16[128,16,64]{0,2,1:T(8,128)(2,1)}), bf16[128,16,64]{0,2,1:T(8,128)(2,1)S(1)}, u32[]{:S(2)}, u32[]{:S(2)}) async-start(bf16[128,16,64]{0,2,1:T(8,128)(2,1)} %bitcast.7), calls=%async_computation | async-start | bytes 524288 | tf_op jit(solution)/shard_map/all_to_all | solution.py:120
  62.7 0.2 copy.73
  62.8 7.2 %all-to-all-done = bf16[128,16,64]{0,2,1:T(8,128)(2,1)S(1)} async-done(((bf16[128,16,64]{0,2,1:T(8,128)(2,1)}), bf16[128,16,64]{0,2,1:T(8,128)(2,1)S(1)}, u32[]{:S(2)}, u32[]{:S(2)}) %all-to-all-start) | async-done | bytes 262176 | tf_op jit(solution)/shard_map/all_to_all | solution.py:120
  70.0 1.9 broadcast_in_dim.6
  71.9 5.4 %all-to-all-start.1 = ((bf16[8,8,128,128]{3,2,1,0:T(8,128)(2,1)}), bf16[8,8,128,128]{3,2,1,0:T(8,128)(2,1)}, u32[]{:S(2)}, u32[]{:S(2)}) async-start(bf16[8,8,128,128]{3,2,1,0:T(8,128)(2,1)} %broadcast_in_dim.6), calls=%async_computation.1 | async-start | bytes 4194304 | tf_op jit(solution)/shard_map/all_to_all | solution.py:118
  77.3 0.0 all-gather.10.cloned.1.call-start
  77.4 0.0 copy-done.1
  77.4 0.8 constant_dynamic-slice_fusion
  78.2 0.0 all-gather.10.cloned.1.call-update
  78.2 0.0 copy-done.3
  78.3 0.1 copy.54
  78.4 0.6 gather_fusion
  79.0 3.6 %convolution_convert_fusion.1 = bf16[2048,64]{0,1:T(8,128)(2,1)S(1)} fusion(bf16[2048,1024]{1,0:T(8,128)(2,1)} %all-gather.6.cloned.1.call-done, bf16[1024,3,64]{0,2,1:T(8,128)(2,1)S(1)} %bitcast.68), kind=kOutput, calls=%fused_computation.3 | convolution fusion | flops 268566528 | bytes 4587520 | tf_op jit(solution)/shard_map/td,dc->tc/dot_general | solution.py:111
  82.6 0.3 copy.56
  82.9 0.3 copy.58
  83.2 27.3 %all-to-all-done.1 = bf16[8,8,128,128]{3,2,1,0:T(8,128)(2,1)} async-done(((bf16[8,8,128,128]{3,2,1,0:T(8,128)(2,1)}), bf16[8,8,128,128]{3,2,1,0:T(8,128)(2,1)}, u32[]{:S(2)}, u32[]{:S(2)}) %all-to-all-start.1) | async-done | bytes 2097184 | tf_op jit(solution)/shard_map/all_to_all | solution.py:118
  110.5 12.3 %all-gather.8.cloned.1.call-done.ka_ref = bf16[64,128,128]{2,1,0:T(8,128)(2,1)} async-done(((bf16[8,128,128]{2,1,0:T(8,128)(2,1)}), bf16[64,128,128]{2,1,0:T(8,128)(2,1)}) %all-gather.8.cloned.1.call-update) | async-done | bytes 2097168 | tf_op jit(solution)/shard_map/all_gather | solution.py:116
  122.8 1.6 copy-done
  124.4 24.9 %shard_map.67 = (bf16[16,128,64]{2,1,0:T(8,128)(2,1)S(1)}, bf16[16,128,64]{2,1,0:T(8,128)(2,1)S(1)}, bf16[128,128,128]{2,1,0:T(8,128)(2,1)}) custom-call(s32[16,8]{1,0:T(8,128)S(1)} %get-tuple-element.28.slots_ref, s32[16,8]{1,0:T(8,128)S(1)} %add_select_fusion.4.a_ids_ref, s32[16,8]{1,0:T(8,128)S(1)} %get-tuple-element.27.b_ids_ref, ...), custom_call_target="tpu_custom_call" | custom-call | tf_op jit(solution)/shard_map/pallas_call | solution.py:72
  149.3 59.7 %all_to_all.60 = bf16[8,2048,128]{2,1,0:T(8,128)(2,1)} all-to-all(bf16[8,2048,128]{2,1,0:T(8,128)(2,1)} %bitcast.63), channel_id=1, replica_groups=mesh['seq'=16,'zero'=8] {'zero'}, dimensions={0} | all-to-all | bytes 8388608 | tf_op jit(solution)/shard_map/all_to_all | solution.py:161
  209.0 3.1 %reduce_sum.21 = bf16[2048,128]{1,0:T(8,128)(2,1)S(1)} reduce(bf16[8,2048,128]{2,1,0:T(8,128)(2,1)} %all_to_all.60, bf16[]{:T(256)} %constant.123.clone.1), dimensions={0}, to_apply=%region_0.1 | reduce | flops 1835008 | bytes 4718594 | tf_op jit(solution)/shard_map/reduce_sum | solution.py:162
  212.1 3.6 %convolution_bitcast_fusion = f32[24,8,8,128]{3,2,1,0:T(8,128)S(1)} fusion(bf16[2048,1024]{1,0:T(8,128)(2,1)} %all-gather.6.cloned.1.call-done, bf16[2048,128]{1,0:T(8,128)(2,1)S(1)} %reduce_sum.21, bf16[2048,64]{1,0:T(8,128)(2,1)S(1)} %bitcast.58), kind=kOutput, calls=%fused_computation.4 | convolution fusion | flops 806879232 | bytes 5767168 | tf_op jit(solution)/shard_map/td,tc->dc/dot_general | solution.py:174
  215.7 0.9 copy.79
  216.6 8.2 %all-to-all-start.5 = ((f32[8,128,192]{1,2,0:T(8,128)}), f32[8,128,192]{1,2,0:T(8,128)S(1)}, u32[]{:S(2)}, u32[]{:S(2)}) async-start(f32[8,128,192]{1,2,0:T(8,128)} %bitcast.54), calls=%async_computation.5 | async-start | bytes 1572864 | tf_op jit(solution)/shard_map/all_to_all | solution.py:178
  224.8 0.0 all-gather.12.cloned.1.call-start
  224.8 4.2 %all-gather.10.cloned.1.call-done = bf16[1024,1536]{1,0:T(8,128)(2,1)} async-done(((bf16[128,1536]{1,0:T(8,128)(2,1)}), bf16[1024,1536]{1,0:T(8,128)(2,1)}) %all-gather.10.cloned.1.call-update) | async-done | bytes 3145744 | tf_op jit(solution)/shard_map/all_gather | solution.py:98
  229.0 1.1 collective-permute-start
  230.1 6.7 %all-to-all-done.5 = f32[8,128,192]{1,2,0:T(8,128)S(1)} async-done(((f32[8,128,192]{1,2,0:T(8,128)}), f32[8,128,192]{1,2,0:T(8,128)S(1)}, u32[]{:S(2)}, u32[]{:S(2)}) %all-to-all-start.5) | async-done | bytes 786464 | tf_op jit(solution)/shard_map/all_to_all | solution.py:178
  236.8 0.7 reduce_sum.22
  237.5 0.0 all-gather.12.cloned.1.call-update
  237.5 0.5 broadcast.143
  238.0 1.1 reduce.1
  239.1 1.1 reshape.100
  240.2 5.9 %all-to-all-start.2 = ((bf16[16,2,4096]{2,1,0:T(2,128)(2,1)}), bf16[16,2,4096]{2,1,0:T(2,128)(2,1)S(1)}, u32[]{:S(2)}, u32[]{:S(2)}) async-start(bf16[16,2,4096]{2,1,0:T(2,128)(2,1)} %reshape.100), calls=%async_computation.2 | async-start | bytes 524288 | tf_op jit(solution)/shard_map/all_to_all | solution.py:152
  246.1 0.5 pad_maximum_fusion
  246.6 0.5 copy.64
  247.1 1.4 copy.65
  248.5 2.5 reshape.102
  251.0 3.5 %all-to-all-done.2 = bf16[16,2,4096]{2,1,0:T(2,128)(2,1)S(1)} async-done(((bf16[16,2,4096]{2,1,0:T(2,128)(2,1)}), bf16[16,2,4096]{2,1,0:T(2,128)(2,1)S(1)}, u32[]{:S(2)}, u32[]{:S(2)}) %all-to-all-start.2) | async-done | bytes 262176 | tf_op jit(solution)/shard_map/all_to_all | solution.py:152
  254.5 4.4 %all-to-all-start.4 = ((bf16[16,2,12288]{2,1,0:T(2,128)(2,1)}), bf16[16,2,12288]{2,1,0:T(2,128)(2,1)}, u32[]{:S(2)}, u32[]{:S(2)}) async-start(bf16[16,2,12288]{2,1,0:T(2,128)(2,1)} %reshape.102), calls=%async_computation.4 | async-start | bytes 1572864 | tf_op jit(solution)/shard_map/all_to_all | solution.py:165
  258.8 0.6 reshape.101
  259.5 0.6 copy.62
  260.1 0.1 copy.63
  260.2 0.9 copy.70
  261.1 10.7 %all-to-all-done.4 = bf16[16,2,12288]{2,1,0:T(2,128)(2,1)} async-done(((bf16[16,2,12288]{2,1,0:T(2,128)(2,1)}), bf16[16,2,12288]{2,1,0:T(2,128)(2,1)}, u32[]{:S(2)}, u32[]{:S(2)}) %all-to-all-start.4) | async-done | bytes 786464 | tf_op jit(solution)/shard_map/all_to_all | solution.py:165
  271.8 2.9 reshape.103
  274.7 1.2 copy.75
  275.9 3.1 %fusion.3 = f32[128,1024]{1,0:T(8,128)S(1)} fusion(bf16[1024,1536]{1,0:T(8,128)(2,1)} %all-gather.10.cloned.1.call-done, bf16[128,3072]{0,1:T(8,128)(2,1)S(1)} %bitcast.64, s32[]{:T(128)S(6)} %select_n.75), kind=kOutput, calls=%fused_computation.10 | convolution fusion | flops 402653184 | bytes 4063236 | tf_op jit(solution)/shard_map/tc,dc->td/dot_general | solution.py:170
  278.9 0.0 collective-permute-done
  278.9 3.8 %fusion.1 = bf16[128,1024]{1,0:T(8,128)(2,1)} fusion(f32[128,1024]{1,0:T(8,128)S(1)} %fusion.3, bf16[1024,1536]{1,0:T(8,128)(2,1)} %collective-permute-done, bf16[128,3072]{0,1:T(8,128)(2,1)S(1)} %bitcast.65, s32[]{:T(128)S(6)} %select_n.76), kind=kOutput, calls=%fused_computation.6 | convolution fusion | flops 402915328 | bytes 4325380 | tf_op jit(solution)/shard_map/tc,dc->td/dot_general | solution.py:171
  282.7 1.5 copy.69
  284.2 1.6 copy.71
  (12 shorter events, 0.2 us)
Async XLA Ops:
  7.2 46.4 %all-gather.6.cloned.1.call-start = ((), (), s32[]{:S(2)}) async-start(), calls=%async_computation.6 | async-start | bytes 4456448 | tf_op jit(solution)/shard_map/all_gather | solution.py:100
  7.9 114.9 %all-gather.8.cloned.1.call-start = ((), (), s32[]{:S(2)}) async-start(), calls=%async_computation.7 | async-start | bytes 2359296 | tf_op jit(solution)/shard_map/all_gather | solution.py:116
  53.6 4.7 %copy-start.2 = (bf16[128,1024]{1,0:T(8,128)(2,1)S(1)}, bf16[128,1024]{1,0:T(8,128)(2,1)}, u32[]{:S(2)}) copy-start(bf16[128,1024]{1,0:T(8,128)(2,1)} %param.7) | copy-start | bytes 786436
  59.1 11.0 %all-to-all-start = ((bf16[128,16,64]{0,2,1:T(8,128)(2,1)}), bf16[128,16,64]{0,2,1:T(8,128)(2,1)S(1)}, u32[]{:S(2)}, u32[]{:S(2)}) async-start(bf16[128,16,64]{0,2,1:T(8,128)(2,1)} %bitcast.7), calls=%async_computation | async-start | bytes 524288 | tf_op jit(solution)/shard_map/all_to_all | solution.py:120
  70.0 7.4 %copy-start.1 = (bf16[128,3072]{1,0:T(8,128)(2,1)S(1)}, bf16[128,3072]{1,0:T(8,128)(2,1)}, u32[]{:S(2)}) copy-start(bf16[128,3072]{1,0:T(8,128)(2,1)} %param.5) | copy-start | bytes 2359300
  71.9 6.3 %copy-start.3 = (s32[128,8]{0,1:T(8,128)S(1)}, s32[128,8]{0,1:T(8,128)}, u32[]{:S(2)}) copy-start(s32[128,8]{0,1:T(8,128)} %param.6) | copy-start | bytes 12292
  71.9 38.5 %all-to-all-start.1 = ((bf16[8,8,128,128]{3,2,1,0:T(8,128)(2,1)}), bf16[8,8,128,128]{3,2,1,0:T(8,128)(2,1)}, u32[]{:S(2)}, u32[]{:S(2)}) async-start(bf16[8,8,128,128]{3,2,1,0:T(8,128)(2,1)} %broadcast_in_dim.6), calls=%async_computation.1 | async-start | bytes 4194304 | tf_op jit(solution)/shard_map/all_to_all | solution.py:118
  77.3 151.6 %all-gather.10.cloned.1.call-start = ((), (), s32[]{:S(2)}) async-start(), calls=%async_computation.8 | async-start | bytes 3538944 | tf_op jit(solution)/shard_map/all_gather | solution.py:98
  122.8 1.6 copy-start
  216.6 20.2 %all-to-all-start.5 = ((f32[8,128,192]{1,2,0:T(8,128)}), f32[8,128,192]{1,2,0:T(8,128)S(1)}, u32[]{:S(2)}, u32[]{:S(2)}) async-start(f32[8,128,192]{1,2,0:T(8,128)} %bitcast.54), calls=%async_computation.5 | async-start | bytes 1572864 | tf_op jit(solution)/shard_map/all_to_all | solution.py:178
  224.8 57.9 %all-gather.12.cloned.1.call-start = ((), (), s32[]{:S(2)}) async-start(), calls=%async_computation.9 | async-start | bytes 1671168 | tf_op jit(solution)/shard_map/all_gather | solution.py:181
  229.0 49.9 %collective-permute-start = (bf16[1024,1536]{1,0:T(8,128)(2,1)}, bf16[1024,1536]{1,0:T(8,128)(2,1)}, u32[]{:S(2)}, u32[]{:S(2)}) collective-permute-start(bf16[1024,1536]{1,0:T(8,128)(2,1)} %all-gather.10.cloned.1.call-done), channel_id=1, source_target_pairs={{0,8},{8,0},{16,24},{24,16},{32,40},{40,32},{48,56},{56,48},{64,72... | collective-permute-start | bytes 9437192 | tf_op jit(solution)/shard_map/ppermute | solution.py:99
  240.2 14.2 %all-to-all-start.2 = ((bf16[16,2,4096]{2,1,0:T(2,128)(2,1)}), bf16[16,2,4096]{2,1,0:T(2,128)(2,1)S(1)}, u32[]{:S(2)}, u32[]{:S(2)}) async-start(bf16[16,2,4096]{2,1,0:T(2,128)(2,1)} %reshape.100), calls=%async_computation.2 | async-start | bytes 524288 | tf_op jit(solution)/shard_map/all_to_all | solution.py:152
  254.5 17.3 %all-to-all-start.4 = ((bf16[16,2,12288]{2,1,0:T(2,128)(2,1)}), bf16[16,2,12288]{2,1,0:T(2,128)(2,1)}, u32[]{:S(2)}, u32[]{:S(2)}) async-start(bf16[16,2,12288]{2,1,0:T(2,128)(2,1)} %reshape.102), calls=%async_computation.4 | async-start | bytes 1572864 | tf_op jit(solution)/shard_map/all_to_all | solution.py:165
Sparse Core Ops, SparseCore 0:
  9.7 43.8 all-gather.5
  58.3 64.4 all-gather.7
  125.1 103.8 all-gather.9
  237.6 37.9 all-gather.11

commit v10 on v9

--- a/solution.py
+++ b/solution.py
@@ -53,14 +53,15 @@
 
 def block_attention(slots, a_ids, b_ids, queries, upstream, kv_a, kv_b, scale):
     rows = queries.shape[0]
-    slot_count = 2 * kv_a.shape[0]
+    slot_count = kv_a.shape[0] + kv_b.shape[0]
     row_spec = pl.BlockSpec((1, BLOCK, HEAD), lambda i, s, a, b: (i, 0, 0))
-    half_spec = pl.BlockSpec((slot_count // 2, BLOCK, 2 * HEAD), lambda i, s, a, b: (0, 0, 0))
+    a_spec = pl.BlockSpec((kv_a.shape[0], BLOCK, 2 * HEAD), lambda i, s, a, b: (0, 0, 0))
+    b_spec = pl.BlockSpec((kv_b.shape[0], BLOCK, 2 * HEAD), lambda i, s, a, b: (0, 0, 0))
     full_spec = pl.BlockSpec((slot_count, BLOCK, 2 * HEAD), lambda i, s, a, b: (0, 0, 0))
     grid_spec = pltpu.PrefetchScalarGridSpec(
         num_scalar_prefetch=3,
         grid=(rows,),
-        in_specs=[row_spec, row_spec, half_spec, half_spec],
+        in_specs=[row_spec, row_spec, a_spec, b_spec],
         out_specs=[row_spec, row_spec, full_spec],
         scratch_shapes=[pltpu.VMEM((slot_count, BLOCK, 2 * HEAD), jnp.float32)],
     )
@@ -112,7 +113,7 @@
         "td,dc->tc", group_tokens, head_w[:, 0], preferred_element_type=jnp.float32
     ).astype(jnp.bfloat16)
     kv_local = kv_local.reshape(local_blocks, BLOCK, 2 * head_cols)
-    split = local_blocks // 2
+    split = local_blocks // 4
     kv_a = lax.all_gather(kv_local[:split], "zero", axis=0, tiled=True)
     kv_b = jnp.broadcast_to(kv_local[split:], (zero_count,) + kv_local[split:].shape)
     kv_b = lax.all_to_all(kv_b, "zero", split_axis=0, concat_axis=0, tiled=True)

time: 293 us -> 298 us (1.017)
  waiting for transfers between devices: 88 us -> 92.3 us
    all_gather x1, waiting for transfers between devices: 12.3 us -> 43.5 us  [on_device(): kv_a = lax.all_gather(kv_local[:split], 'zero', axis=0, tiled=True)]
    all_to_all x1, waiting for transfers between devices: 27.3 us -> 0.01 us  [on_device(): kv_b = lax.all_to_all(kv_b, 'zero', split_axis=0, concat_axis=0, tiled=True)]
  transfers between devices with their start and end apart: 10 -> 10, of which waited for: 8 -> 7; matrix products, arithmetic and copies ran while one was open for 13% -> 13% of each run, Pallas kernels for 9% -> 9%
where the time goes in v10:
time: 298 us; the launch traced here: 297 us
  waiting for transfers between devices  92.3 us (31%)
  blocking collectives  87.9 us (29%)
  starting transfers between devices  28.9 us (10%)
  local copies, waits for them, and re-layouts  25.4 us (9%)
  Pallas kernels  25.3 us (8%)
  matrix products  17.7 us (6%)
  between operations  14 us (5%)
  other arithmetic  5.4 us (2%)
    all_to_all x1, blocking collectives, on_device(): lax.all_to_all(group_sums, 'zero', split_axis=0, concat_axis=0, tiled=True)  59.2 us
    all_gather x1, waiting for transfers between devices, on_device(): kv_a = lax.all_gather(kv_local[:split], 'zero', axis=0, tiled=True)  43.5 us
    all_gather x1, blocking collectives, on_device(): head_w = lax.all_gather(head_w, 'zero', axis=0, tiled=True)  28.7 us
    pallas_call x1, Pallas kernels, block_attention(): pl.pallas_call(functools.partial(_attn_kernel, scale=scale), grid_spec=gr...  25.3 us
    all_gather x1, waiting for transfers between devices, on_device(): group_tokens = lax.all_gather(tokens, 'seq', axis=0, tiled=True)  15.3 us
    unnamed x17, local copies, waits for them, and re-layouts  12.5 us
    all_to_all x1, waiting for transfers between devices, on_device(): lax.all_to_all(local_grads, 'seq', split_axis=0, concat_axis=2, tiled=True)  11.3 us
    all_to_all x1, starting transfers between devices, on_device(): lax.all_to_all(head_part, 'zero', split_axis=0, concat_axis=0, tiled=True)  8.85 us
  transfers between devices with their start and end apart: 10, of which 7 were waited for; matrix products, arithmetic and copies ran while one was open for 13% of the time, Pallas kernels for 9%

profile of v10, /device:TPU:1, one launch (start us, length us, event | category | flops | bytes accessed | tf_op | source)
XLA Modules:
  0.0 296.9 jit_solution(15655372443418179997)
XLA Ops:
  7.2 0.0 all-gather.6.cloned.1.call-start
  7.2 0.7 all-gather.6.cloned.1.call-update
  7.9 0.0 all-gather.8.cloned.1.call-start
  7.9 1.5 copy.55
  9.5 28.7 %all-gather = bf16[1024,3,1,64]{0,3,2,1:T(8,128)(2,1)S(1)} all-gather(bf16[128,3,1,64]{0,3,2,1:T(8,128)(2,1)S(1)} %constant_dynamic-slice_fusion.1), channel_id=2, replica_groups=mesh['seq'=16,'zero'=8] {'zero'}, dimensions={0}, use_global_device_ids=true | all-gather | bytes 442368 | tf_op jit(solution)/shard_map/all_gather | solution.py:104
  38.2 0.0 copy-start.2
  38.2 15.3 %all-gather.6.cloned.1.call-done = bf16[2048,1024]{1,0:T(8,128)(2,1)} async-done(((bf16[128,1024]{1,0:T(8,128)(2,1)}), bf16[2048,1024]{1,0:T(8,128)(2,1)}) %all-gather.6.cloned.1.call-update) | async-done | bytes 4194320 | tf_op jit(solution)/shard_map/all_gather | solution.py:101
  53.6 3.7 %fusion = bf16[2048,128]{0,1:T(8,128)(2,1)S(1)} fusion(bf16[1024,128]{0,1:T(8,128)(2,1)S(1)} %bitcast.70, bf16[2048,1024]{1,0:T(8,128)(2,1)} %all-gather.6.cloned.1.call-done), kind=kOutput, calls=%fused_computation.2 | convolution fusion | flops 537133056 | bytes 4980736 | tf_op jit(solution)/shard_map/td,dc->tc/dot_general | solution.py:105
  57.3 0.8 copy.72
  58.0 0.0 all-gather.8.cloned.1.call-update
  58.1 0.0 copy-done.2
  58.1 0.8 copy.57
  58.9 3.6 %all-to-all-start = ((bf16[128,16,64]{0,2,1:T(8,128)(2,1)}), bf16[128,16,64]{0,2,1:T(8,128)(2,1)S(1)}, u32[]{:S(2)}, u32[]{:S(2)}) async-start(bf16[128,16,64]{0,2,1:T(8,128)(2,1)} %bitcast.7), calls=%async_computation | async-start | bytes 524288 | tf_op jit(solution)/shard_map/all_to_all | solution.py:121
  62.5 0.2 copy.60
  62.8 7.1 %all-to-all-done = bf16[128,16,64]{0,2,1:T(8,128)(2,1)S(1)} async-done(((bf16[128,16,64]{0,2,1:T(8,128)(2,1)}), bf16[128,16,64]{0,2,1:T(8,128)(2,1)S(1)}, u32[]{:S(2)}, u32[]{:S(2)}) %all-to-all-start) | async-done | bytes 262176 | tf_op jit(solution)/shard_map/all_to_all | solution.py:121
  69.9 2.5 broadcast_in_dim.6
  72.4 5.4 %all-to-all-start.1 = ((bf16[8,12,128,128]{3,2,1,0:T(8,128)(2,1)}), bf16[8,12,128,128]{3,2,1,0:T(8,128)(2,1)}, u32[]{:S(2)}, u32[]{:S(2)}) async-start(bf16[8,12,128,128]{3,2,1,0:T(8,128)(2,1)} %broadcast_in_dim.6), calls=%async_computation.1 | async-start | bytes 6291456 | tf_op jit(solution)/shard_map/all_to_all | solution.py:119
  77.8 0.0 all-gather.10.cloned.1.call-start
  77.8 0.0 copy-done.1
  77.8 0.8 constant_dynamic-slice_fusion
  78.7 0.0 all-gather.10.cloned.1.call-update
  78.7 0.0 copy-done.3
  78.7 0.1 copy.54
  78.8 0.6 gather_fusion
  79.4 3.6 %convolution_convert_fusion.1 = bf16[2048,64]{0,1:T(8,128)(2,1)S(1)} fusion(bf16[2048,1024]{1,0:T(8,128)(2,1)} %all-gather.6.cloned.1.call-done, bf16[1024,3,64]{0,2,1:T(8,128)(2,1)S(1)} %bitcast.68), kind=kOutput, calls=%fused_computation.3 | convolution fusion | flops 268566528 | bytes 4587520 | tf_op jit(solution)/shard_map/td,dc->tc/dot_general | solution.py:112
  83.0 0.3 copy.56
  83.3 0.3 copy.58
  83.6 43.5 %all-gather.8.cloned.1.call-done.ka_ref = bf16[32,128,128]{2,1,0:T(8,128)(2,1)} async-done(((bf16[4,128,128]{2,1,0:T(8,128)(2,1)}), bf16[32,128,128]{2,1,0:T(8,128)(2,1)}) %all-gather.8.cloned.1.call-update) | async-done | bytes 1048592 | tf_op jit(solution)/shard_map/all_gather | solution.py:117
  127.1 0.0 all-to-all-done.1
  127.1 1.2 copy-done
  128.3 25.3 %shard_map.67 = (bf16[16,128,64]{2,1,0:T(8,128)(2,1)S(1)}, bf16[16,128,64]{2,1,0:T(8,128)(2,1)S(1)}, bf16[128,128,128]{2,1,0:T(8,128)(2,1)}) custom-call(s32[16,8]{1,0:T(8,128)S(1)} %get-tuple-element.28.slots_ref, s32[16,8]{1,0:T(8,128)S(1)} %add_select_fusion.4.a_ids_ref, s32[16,8]{1,0:T(8,128)S(1)} %get-tuple-element.27.b_ids_ref, ...), custom_call_target="tpu_custom_call" | custom-call | tf_op jit(solution)/shard_map/pallas_call | solution.py:73
  153.6 59.2 %all_to_all.60 = bf16[8,2048,128]{2,1,0:T(8,128)(2,1)} all-to-all(bf16[8,2048,128]{2,1,0:T(8,128)(2,1)} %bitcast.63), channel_id=1, replica_groups=mesh['seq'=16,'zero'=8] {'zero'}, dimensions={0} | all-to-all | bytes 8388608 | tf_op jit(solution)/shard_map/all_to_all | solution.py:162
  212.8 3.1 %reduce_sum.21 = bf16[2048,128]{1,0:T(8,128)(2,1)S(1)} reduce(bf16[8,2048,128]{2,1,0:T(8,128)(2,1)} %all_to_all.60, bf16[]{:T(256)} %constant.125.clone.1), dimensions={0}, to_apply=%region_0.1 | reduce | flops 1835008 | bytes 4718594 | tf_op jit(solution)/shard_map/reduce_sum | solution.py:163
  215.8 3.6 %convolution_bitcast_fusion = f32[24,8,8,128]{3,2,1,0:T(8,128)S(1)} fusion(bf16[2048,1024]{1,0:T(8,128)(2,1)} %all-gather.6.cloned.1.call-done, bf16[2048,128]{1,0:T(8,128)(2,1)S(1)} %reduce_sum.21, bf16[2048,64]{1,0:T(8,128)(2,1)S(1)} %bitcast.58), kind=kOutput, calls=%fused_computation.4 | convolution fusion | flops 806879232 | bytes 5767168 | tf_op jit(solution)/shard_map/td,tc->dc/dot_general | solution.py:175
  219.4 0.9 copy.78
  220.4 8.8 %all-to-all-start.5 = ((f32[8,128,192]{1,2,0:T(8,128)}), f32[8,128,192]{1,2,0:T(8,128)S(1)}, u32[]{:S(2)}, u32[]{:S(2)}) async-start(f32[8,128,192]{1,2,0:T(8,128)} %bitcast.54), calls=%async_computation.5 | async-start | bytes 1572864 | tf_op jit(solution)/shard_map/all_to_all | solution.py:179
  229.2 0.0 all-gather.12.cloned.1.call-start
  229.3 4.1 %all-gather.10.cloned.1.call-done = bf16[1024,1536]{1,0:T(8,128)(2,1)} async-done(((bf16[128,1536]{1,0:T(8,128)(2,1)}), bf16[1024,1536]{1,0:T(8,128)(2,1)}) %all-gather.10.cloned.1.call-update) | async-done | bytes 3145744 | tf_op jit(solution)/shard_map/all_gather | solution.py:99
  233.3 1.1 collective-permute-start
  234.4 7.1 %all-to-all-done.5 = f32[8,128,192]{1,2,0:T(8,128)S(1)} async-done(((f32[8,128,192]{1,2,0:T(8,128)}), f32[8,128,192]{1,2,0:T(8,128)S(1)}, u32[]{:S(2)}, u32[]{:S(2)}) %all-to-all-start.5) | async-done | bytes 786464 | tf_op jit(solution)/shard_map/all_to_all | solution.py:179
  241.5 0.7 reduce_sum.22
  242.2 0.0 all-gather.12.cloned.1.call-update
  242.2 0.5 broadcast.152
  242.7 1.1 reduce.1
  243.8 1.1 reshape.100
  244.9 5.4 %all-to-all-start.2 = ((bf16[16,2,4096]{2,1,0:T(2,128)(2,1)}), bf16[16,2,4096]{2,1,0:T(2,128)(2,1)S(1)}, u32[]{:S(2)}, u32[]{:S(2)}) async-start(bf16[16,2,4096]{2,1,0:T(2,128)(2,1)} %reshape.100), calls=%async_computation.2 | async-start | bytes 524288 | tf_op jit(solution)/shard_map/all_to_all | solution.py:153
  250.4 0.5 pad_maximum_fusion
  250.8 0.5 copy.64
  251.4 1.4 copy.65
  252.7 2.5 reshape.102
  255.2 3.2 %all-to-all-done.2 = bf16[16,2,4096]{2,1,0:T(2,128)(2,1)S(1)} async-done(((bf16[16,2,4096]{2,1,0:T(2,128)(2,1)}), bf16[16,2,4096]{2,1,0:T(2,128)(2,1)S(1)}, u32[]{:S(2)}, u32[]{:S(2)}) %all-to-all-start.2) | async-done | bytes 262176 | tf_op jit(solution)/shard_map/all_to_all | solution.py:153
  258.4 4.4 %all-to-all-start.4 = ((bf16[16,2,12288]{2,1,0:T(2,128)(2,1)}), bf16[16,2,12288]{2,1,0:T(2,128)(2,1)}, u32[]{:S(2)}, u32[]{:S(2)}) async-start(bf16[16,2,12288]{2,1,0:T(2,128)(2,1)} %reshape.102), calls=%async_computation.4 | async-start | bytes 1572864 | tf_op jit(solution)/shard_map/all_to_all | solution.py:166
  262.8 0.6 reshape.101
  263.4 0.6 copy.62
  264.1 0.1 copy.63
  264.2 0.9 copy.70
  265.0 11.3 %all-to-all-done.4 = bf16[16,2,12288]{2,1,0:T(2,128)(2,1)} async-done(((bf16[16,2,12288]{2,1,0:T(2,128)(2,1)}), bf16[16,2,12288]{2,1,0:T(2,128)(2,1)}, u32[]{:S(2)}, u32[]{:S(2)}) %all-to-all-start.4) | async-done | bytes 786464 | tf_op jit(solution)/shard_map/all_to_all | solution.py:166
  276.3 2.9 reshape.103
  279.2 1.2 copy.74
  280.4 3.1 %fusion.3 = f32[128,1024]{1,0:T(8,128)S(1)} fusion(bf16[1024,1536]{1,0:T(8,128)(2,1)} %all-gather.10.cloned.1.call-done, bf16[128,3072]{0,1:T(8,128)(2,1)S(1)} %bitcast.64, s32[]{:T(128)S(6)} %select_n.75), kind=kOutput, calls=%fused_computation.10 | convolution fusion | flops 402653184 | bytes 4063236 | tf_op jit(solution)/shard_map/tc,dc->td/dot_general | solution.py:171
  283.4 0.0 collective-permute-done
  283.5 3.8 %fusion.1 = bf16[128,1024]{1,0:T(8,128)(2,1)} fusion(f32[128,1024]{1,0:T(8,128)S(1)} %fusion.3, bf16[1024,1536]{1,0:T(8,128)(2,1)} %collective-permute-done, bf16[128,3072]{0,1:T(8,128)(2,1)S(1)} %bitcast.65, s32[]{:T(128)S(6)} %select_n.76), kind=kOutput, calls=%fused_computation.6 | convolution fusion | flops 402915328 | bytes 4325380 | tf_op jit(solution)/shard_map/tc,dc->td/dot_general | solution.py:172
  287.2 1.5 copy.69
  288.7 1.6 copy.71
  (13 shorter events, 0.2 us)
Async XLA Ops:
  7.2 46.4 %all-gather.6.cloned.1.call-start = ((), (), s32[]{:S(2)}) async-start(), calls=%async_computation.6 | async-start | bytes 4456448 | tf_op jit(solution)/shard_map/all_gather | solution.py:101
  7.9 119.2 %all-gather.8.cloned.1.call-start = ((), (), s32[]{:S(2)}) async-start(), calls=%async_computation.7 | async-start | bytes 1179648 | tf_op jit(solution)/shard_map/all_gather | solution.py:117
  38.2 19.9 %copy-start.2 = (bf16[128,1024]{1,0:T(8,128)(2,1)S(1)}, bf16[128,1024]{1,0:T(8,128)(2,1)}, u32[]{:S(2)}) copy-start(bf16[128,1024]{1,0:T(8,128)(2,1)} %param.7) | copy-start | bytes 786436
  58.9 11.0 %all-to-all-start = ((bf16[128,16,64]{0,2,1:T(8,128)(2,1)}), bf16[128,16,64]{0,2,1:T(8,128)(2,1)S(1)}, u32[]{:S(2)}, u32[]{:S(2)}) async-start(bf16[128,16,64]{0,2,1:T(8,128)(2,1)} %bitcast.7), calls=%async_computation | async-start | bytes 524288 | tf_op jit(solution)/shard_map/all_to_all | solution.py:121
  72.3 5.5 %copy-start.1 = (bf16[128,3072]{1,0:T(8,128)(2,1)S(1)}, bf16[128,3072]{1,0:T(8,128)(2,1)}, u32[]{:S(2)}) copy-start(bf16[128,3072]{1,0:T(8,128)(2,1)} %param.5) | copy-start | bytes 2359300
  72.3 6.3 %copy-start.3 = (s32[128,8]{0,1:T(8,128)S(1)}, s32[128,8]{0,1:T(8,128)}, u32[]{:S(2)}) copy-start(s32[128,8]{0,1:T(8,128)} %param.6) | copy-start | bytes 12292
  72.4 54.7 %all-to-all-start.1 = ((bf16[8,12,128,128]{3,2,1,0:T(8,128)(2,1)}), bf16[8,12,128,128]{3,2,1,0:T(8,128)(2,1)}, u32[]{:S(2)}, u32[]{:S(2)}) async-start(bf16[8,12,128,128]{3,2,1,0:T(8,128)(2,1)} %broadcast_in_dim.6), calls=%async_computation.1 | async-start | bytes 6291456 | tf_op jit(solution)/shard_map/all_to_all | solution.py:119
  77.8 155.5 %all-gather.10.cloned.1.call-start = ((), (), s32[]{:S(2)}) async-start(), calls=%async_computation.8 | async-start | bytes 3538944 | tf_op jit(solution)/shard_map/all_gather | solution.py:99
  127.1 1.2 copy-start
  220.4 21.1 %all-to-all-start.5 = ((f32[8,128,192]{1,2,0:T(8,128)}), f32[8,128,192]{1,2,0:T(8,128)S(1)}, u32[]{:S(2)}, u32[]{:S(2)}) async-start(f32[8,128,192]{1,2,0:T(8,128)} %bitcast.54), calls=%async_computation.5 | async-start | bytes 1572864 | tf_op jit(solution)/shard_map/all_to_all | solution.py:179
  229.2 58.0 %all-gather.12.cloned.1.call-start = ((), (), s32[]{:S(2)}) async-start(), calls=%async_computation.9 | async-start | bytes 1671168 | tf_op jit(solution)/shard_map/all_gather | solution.py:182
  233.3 50.1 %collective-permute-start = (bf16[1024,1536]{1,0:T(8,128)(2,1)}, bf16[1024,1536]{1,0:T(8,128)(2,1)}, u32[]{:S(2)}, u32[]{:S(2)}) collective-permute-start(bf16[1024,1536]{1,0:T(8,128)(2,1)} %all-gather.10.cloned.1.call-done), channel_id=1, source_target_pairs={{0,8},{8,0},{16,24},{24,16},{32,40},{40,32},{48,56},{56,48},{64,72... | collective-permute-start | bytes 9437192 | tf_op jit(solution)/shard_map/ppermute | solution.py:100
  244.9 13.5 %all-to-all-start.2 = ((bf16[16,2,4096]{2,1,0:T(2,128)(2,1)}), bf16[16,2,4096]{2,1,0:T(2,128)(2,1)S(1)}, u32[]{:S(2)}, u32[]{:S(2)}) async-start(bf16[16,2,4096]{2,1,0:T(2,128)(2,1)} %reshape.100), calls=%async_computation.2 | async-start | bytes 524288 | tf_op jit(solution)/shard_map/all_to_all | solution.py:153
  258.4 17.9 %all-to-all-start.4 = ((bf16[16,2,12288]{2,1,0:T(2,128)(2,1)}), bf16[16,2,12288]{2,1,0:T(2,128)(2,1)}, u32[]{:S(2)}, u32[]{:S(2)}) async-start(bf16[16,2,12288]{2,1,0:T(2,128)(2,1)} %reshape.102), calls=%async_computation.4 | async-start | bytes 1572864 | tf_op jit(solution)/shard_map/all_to_all | solution.py:166
Sparse Core Ops, SparseCore 0:
  9.7 43.8 all-gather.5
  58.2 68.8 all-gather.7
  129.4 103.8 all-gather.9
  242.3 35.7 all-gather.11

commit v11 on v9

--- a/solution.py
+++ b/solution.py
@@ -149,28 +149,22 @@
         kv_b,
         score_scale,
     )
-    attended = lax.all_to_all(
-        out_blocks.reshape(local_blocks * BLOCK, 1, head_cols),
-        "seq",
-        split_axis=0,
-        concat_axis=1,
-        tiled=True,
-    )
-    attended = attended.reshape(tok_rows, seq_count * head_cols)
     group_sums = group_sums.reshape(zero_count, local_blocks * BLOCK, 2 * head_cols)
     group_sums = lax.all_to_all(group_sums, "zero", split_axis=0, concat_axis=0, tiled=True)
     kv_sum = jnp.sum(group_sums.astype(jnp.float32), axis=0).astype(jnp.bfloat16)
     local_grads = jnp.concatenate([query_grads.reshape(-1, head_cols), kv_sum], axis=1)
-    local_grads = local_grads.reshape(local_blocks * BLOCK, 3, 1, head_cols)
-    token_grads = lax.all_to_all(local_grads, "seq", split_axis=0, concat_axis=2, tiled=True)
-    flat_grads = token_grads.reshape(tok_rows, 3 * seq_count * head_cols)
+    outgoing = jnp.concatenate([out_blocks.reshape(-1, head_cols), local_grads], axis=1)
+    outgoing = outgoing.reshape(local_blocks * BLOCK, 4, 1, head_cols)
+    token_grads = lax.all_to_all(outgoing, "seq", split_axis=0, concat_axis=2, tiled=True)
+    attended = token_grads[:, 0].reshape(tok_rows, seq_count * head_cols)
+    flat_grads = token_grads[:, 1:].reshape(tok_rows, 3 * seq_count * head_cols)
     g_mine = lax.dynamic_slice_in_dim(flat_grads, core * width, width, axis=1)
     g_other = lax.dynamic_slice_in_dim(flat_grads, (1 - core) * width, width, axis=1)
     token_gradient = (
         jnp.einsum("tc,dc->td", g_mine, w_mine, preferred_element_type=jnp.float32)
         + jnp.einsum("tc,dc->td", g_other, w_other, preferred_element_type=jnp.float32)
     ).astype(jnp.bfloat16)
-    head_grads = local_grads.reshape(local_blocks * BLOCK, 3 * head_cols)
+    head_grads = local_grads
     head_part = jnp.einsum(
         "td,tc->dc", group_tokens, head_grads, preferred_element_type=jnp.float32
     )

time: 293 us -> 287 us (0.980)
  starting transfers between devices: 28.7 us -> 24 us
  local copies, waits for them, and re-layouts: 25.2 us -> 21.2 us
  waiting for transfers between devices: 88 us -> 91.5 us
    all_to_all x2 -> x1, starting transfers between devices: 10.2 us -> 5.77 us  [on_device(): lax.all_to_all(outgoing, 'seq', split_axis=0, concat_axis=2, tiled=True)]
    unnamed x17 -> x14, local copies, waits for them, and re-layouts: 12.8 us -> 9.25 us
    all_to_all x2 -> x1, waiting for transfers between devices: 14.2 us -> 17.5 us  [on_device(): lax.all_to_all(outgoing, 'seq', split_axis=0, concat_axis=2, tiled=True)]
  transfers between devices with their start and end apart: 10 -> 9, of which waited for: 8 -> 7; matrix products, arithmetic and copies ran while one was open for 13% -> 12% of each run, Pallas kernels for 9% -> 9%
where the time goes in v11:
time: 287 us
  waiting for transfers between devices  91.5 us (32%)
  blocking collectives  88.8 us (31%)
  Pallas kernels  25 us (9%)
  starting transfers between devices  24 us (8%)
  local copies, waits for them, and re-layouts  21.2 us (7%)
  matrix products  17.7 us (6%)
  between operations  14 us (5%)
  other arithmetic  4.31 us (2%)
    all_to_all x1, blocking collectives, on_device(): lax.all_to_all(group_sums, 'zero', split_axis=0, concat_axis=0, tiled=True)  60 us
    all_gather x1, blocking collectives, on_device(): head_w = lax.all_gather(head_w, 'zero', axis=0, tiled=True)  28.7 us
    all_to_all x1, waiting for transfers between devices, on_device(): kv_b = lax.all_to_all(kv_b, 'zero', split_axis=0, concat_axis=0, tiled=True)  27.3 us
    pallas_call x1, Pallas kernels, block_attention(): pl.pallas_call(functools.partial(_attn_kernel, scale=scale), grid_spec=gr...  25 us
    all_to_all x1, waiting for transfers between devices, on_device(): lax.all_to_all(outgoing, 'seq', split_axis=0, concat_axis=2, tiled=True)  17.5 us
    all_gather x1, waiting for transfers between devices, on_device(): group_tokens = lax.all_gather(tokens, 'seq', axis=0, tiled=True)  15.3 us
    all_gather x1, waiting for transfers between devices, on_device(): kv_a = lax.all_gather(kv_local[:split], 'zero', axis=0, tiled=True)  12.3 us
    unnamed x14, local copies, waits for them, and re-layouts  9.25 us
  transfers between devices with their start and end apart: 9, of which 7 were waited for; matrix products, arithmetic and copies ran while one was open for 12% of the time, Pallas kernels for 9%

profile of v11, /device:TPU:1, one launch (start us, length us, event | category | flops | bytes accessed | tf_op | source)
XLA Modules:
  0.0 286.6 jit_solution(13918729593314655532)
XLA Ops:
  7.2 0.0 all-gather.6.cloned.1.call-start
  7.2 0.7 all-gather.6.cloned.1.call-update
  7.9 0.0 all-gather.8.cloned.1.call-start
  7.9 1.5 copy.27
  9.5 28.7 %all-gather = bf16[1024,3,1,64]{0,3,2,1:T(8,128)(2,1)S(1)} all-gather(bf16[128,3,1,64]{0,3,2,1:T(8,128)(2,1)S(1)} %constant_dynamic-slice_fusion.1), channel_id=2, replica_groups=mesh['seq'=16,'zero'=8] {'zero'}, dimensions={0}, use_global_device_ids=true | all-gather | bytes 442368 | tf_op jit(solution)/shard_map/all_gather | solution.py:103
  38.2 15.3 %all-gather.6.cloned.1.call-done = bf16[2048,1024]{1,0:T(8,128)(2,1)} async-done(((bf16[128,1024]{1,0:T(8,128)(2,1)}), bf16[2048,1024]{1,0:T(8,128)(2,1)}) %all-gather.6.cloned.1.call-update) | async-done | bytes 4194320 | tf_op jit(solution)/shard_map/all_gather | solution.py:100
  53.6 0.0 copy-start.2
  53.6 3.7 %fusion = bf16[2048,128]{0,1:T(8,128)(2,1)S(1)} fusion(bf16[1024,128]{0,1:T(8,128)(2,1)S(1)} %bitcast.64, bf16[2048,1024]{1,0:T(8,128)(2,1)} %all-gather.6.cloned.1.call-done), kind=kOutput, calls=%fused_computation.2 | convolution fusion | flops 537133056 | bytes 4980736 | tf_op jit(solution)/shard_map/td,dc->tc/dot_general | solution.py:104
  57.3 0.8 copy.42
  58.2 0.0 all-gather.8.cloned.1.call-update
  58.2 0.0 copy-done.2
  58.2 0.8 copy.29
  59.1 3.6 %all-to-all-start = ((bf16[128,16,64]{0,2,1:T(8,128)(2,1)}), bf16[128,16,64]{0,2,1:T(8,128)(2,1)S(1)}, u32[]{:S(2)}, u32[]{:S(2)}) async-start(bf16[128,16,64]{0,2,1:T(8,128)(2,1)} %bitcast.7), calls=%async_computation | async-start | bytes 524288 | tf_op jit(solution)/shard_map/all_to_all | solution.py:120
  62.7 0.2 copy.43
  62.8 7.2 %all-to-all-done = bf16[128,16,64]{0,2,1:T(8,128)(2,1)S(1)} async-done(((bf16[128,16,64]{0,2,1:T(8,128)(2,1)}), bf16[128,16,64]{0,2,1:T(8,128)(2,1)S(1)}, u32[]{:S(2)}, u32[]{:S(2)}) %all-to-all-start) | async-done | bytes 262176 | tf_op jit(solution)/shard_map/all_to_all | solution.py:120
  70.0 0.0 copy-start.1
  70.0 1.9 broadcast_in_dim.6
  71.9 0.0 copy-start.3
  71.9 5.4 %all-to-all-start.1 = ((bf16[8,8,128,128]{3,2,1,0:T(8,128)(2,1)}), bf16[8,8,128,128]{3,2,1,0:T(8,128)(2,1)}, u32[]{:S(2)}, u32[]{:S(2)}) async-start(bf16[8,8,128,128]{3,2,1,0:T(8,128)(2,1)} %broadcast_in_dim.6), calls=%async_computation.1 | async-start | bytes 4194304 | tf_op jit(solution)/shard_map/all_to_all | solution.py:118
  77.3 0.0 all-gather.10.cloned.1.call-start
  77.4 0.0 copy-done.1
  77.4 0.8 constant_dynamic-slice_fusion
  78.2 0.0 all-gather.10.cloned.1.call-update
  78.2 0.0 copy-done.3
  78.2 0.1 copy.26
  78.4 0.6 gather_fusion
  79.0 3.6 %convolution_convert_fusion.1 = bf16[2048,64]{0,1:T(8,128)(2,1)S(1)} fusion(bf16[2048,1024]{1,0:T(8,128)(2,1)} %all-gather.6.cloned.1.call-done, bf16[1024,3,64]{0,2,1:T(8,128)(2,1)S(1)} %bitcast.62), kind=kOutput, calls=%fused_computation.3 | convolution fusion | flops 268566528 | bytes 4587520 | tf_op jit(solution)/shard_map/td,dc->tc/dot_general | solution.py:111
  82.5 0.3 copy.28
  82.8 0.3 copy.30
  83.1 27.3 %all-to-all-done.1 = bf16[8,8,128,128]{3,2,1,0:T(8,128)(2,1)} async-done(((bf16[8,8,128,128]{3,2,1,0:T(8,128)(2,1)}), bf16[8,8,128,128]{3,2,1,0:T(8,128)(2,1)}, u32[]{:S(2)}, u32[]{:S(2)}) %all-to-all-start.1) | async-done | bytes 2097184 | tf_op jit(solution)/shard_map/all_to_all | solution.py:118
  110.5 12.3 %all-gather.8.cloned.1.call-done.ka_ref = bf16[64,128,128]{2,1,0:T(8,128)(2,1)} async-done(((bf16[8,128,128]{2,1,0:T(8,128)(2,1)}), bf16[64,128,128]{2,1,0:T(8,128)(2,1)}) %all-gather.8.cloned.1.call-update) | async-done | bytes 2097168 | tf_op jit(solution)/shard_map/all_gather | solution.py:116
  122.8 0.0 copy-start
  122.8 1.6 copy-done
  124.4 25.0 %shard_map.67 = (bf16[16,128,64]{2,1,0:T(8,128)(2,1)S(1)}, bf16[16,128,64]{2,1,0:T(8,128)(2,1)S(1)}, bf16[128,128,128]{2,1,0:T(8,128)(2,1)}) custom-call(s32[16,8]{1,0:T(8,128)S(1)} %get-tuple-element.22.slots_ref, s32[16,8]{1,0:T(8,128)S(1)} %add_select_fusion.4.a_ids_ref, s32[16,8]{1,0:T(8,128)S(1)} %get-tuple-element.21.b_ids_ref, ...), custom_call_target="tpu_custom_call" | custom-call | tf_op jit(solution)/shard_map/pallas_call | solution.py:72
  149.4 60.0 %all_to_all.48 = bf16[8,2048,128]{2,1,0:T(8,128)(2,1)} all-to-all(bf16[8,2048,128]{2,1,0:T(8,128)(2,1)} %bitcast.58), channel_id=1, replica_groups=mesh['seq'=16,'zero'=8] {'zero'}, dimensions={0} | all-to-all | bytes 8388608 | tf_op jit(solution)/shard_map/all_to_all | solution.py:153
  209.4 3.1 %reduce_sum.21 = bf16[2048,128]{1,0:T(8,128)(2,1)S(1)} reduce(bf16[8,2048,128]{2,1,0:T(8,128)(2,1)} %all_to_all.48, bf16[]{:T(256)} %constant.123.clone.1), dimensions={0}, to_apply=%region_0.1 | reduce | flops 1835008 | bytes 4718594 | tf_op jit(solution)/shard_map/reduce_sum | solution.py:154
  212.5 3.6 %convolution_bitcast_fusion = f32[24,8,8,128]{3,2,1,0:T(8,128)S(1)} fusion(bf16[2048,1024]{1,0:T(8,128)(2,1)} %all-gather.6.cloned.1.call-done, bf16[2048,128]{1,0:T(8,128)(2,1)S(1)} %reduce_sum.21, bf16[2048,64]{1,0:T(8,128)(2,1)S(1)} %bitcast.50), kind=kOutput, calls=%fused_computation.4 | convolution fusion | flops 806879232 | bytes 5767168 | tf_op jit(solution)/shard_map/td,tc->dc/dot_general | solution.py:168
  216.1 0.9 copy.47
  217.0 8.1 %all-to-all-start.4 = ((f32[8,128,192]{1,2,0:T(8,128)}), f32[8,128,192]{1,2,0:T(8,128)S(1)}, u32[]{:S(2)}, u32[]{:S(2)}) async-start(f32[8,128,192]{1,2,0:T(8,128)} %bitcast.46), calls=%async_computation.4 | async-start | bytes 1572864 | tf_op jit(solution)/shard_map/all_to_all | solution.py:172
  225.1 0.0 all-gather.12.cloned.1.call-start
  225.2 3.9 %all-gather.10.cloned.1.call-done = bf16[1024,1536]{1,0:T(8,128)(2,1)} async-done(((bf16[128,1536]{1,0:T(8,128)(2,1)}), bf16[1024,1536]{1,0:T(8,128)(2,1)}) %all-gather.10.cloned.1.call-update) | async-done | bytes 3145744 | tf_op jit(solution)/shard_map/all_gather | solution.py:98
  229.1 1.0 collective-permute-start
  230.1 7.2 %all-to-all-done.4 = f32[8,128,192]{1,2,0:T(8,128)S(1)} async-done(((f32[8,128,192]{1,2,0:T(8,128)}), f32[8,128,192]{1,2,0:T(8,128)S(1)}, u32[]{:S(2)}, u32[]{:S(2)}) %all-to-all-start.4) | async-done | bytes 786464 | tf_op jit(solution)/shard_map/all_to_all | solution.py:172
  237.3 0.7 reduce_sum.22
  238.0 0.0 all-gather.12.cloned.1.call-update
  238.0 0.5 pad_maximum_fusion
  238.5 0.6 copy.33
  239.1 1.4 copy.34
  240.5 2.2 reshape.94
  242.8 5.8 %all-to-all-start.3 = ((bf16[16,2,16384]{2,1,0:T(2,128)(2,1)}), bf16[16,2,16384]{2,1,0:T(2,128)(2,1)S(1)}, u32[]{:S(2)}, u32[]{:S(2)}) async-start(bf16[16,2,16384]{2,1,0:T(2,128)(2,1)} %reshape.94), calls=%async_computation.3 | async-start | bytes 2097152 | tf_op jit(solution)/shard_map/all_to_all | solution.py:158
  248.5 17.5 %all-to-all-done.3 = bf16[16,2,16384]{2,1,0:T(2,128)(2,1)S(1)} async-done(((bf16[16,2,16384]{2,1,0:T(2,128)(2,1)}), bf16[16,2,16384]{2,1,0:T(2,128)(2,1)S(1)}, u32[]{:S(2)}, u32[]{:S(2)}) %all-to-all-start.3) | async-done | bytes 1048608 | tf_op jit(solution)/shard_map/all_to_all | solution.py:158
  266.0 1.3 reshape.95
  267.4 1.4 copy.44
  268.8 0.1 slice.37
  269.0 0.2 copy.37
  269.2 0.1 copy.36
  269.3 0.9 copy.40
  270.1 3.0 %fusion.6 = f32[128,1024]{1,0:T(8,128)S(1)} fusion(bf16[1024,1536]{1,0:T(8,128)(2,1)} %all-gather.10.cloned.1.call-done, bf16[128,3072]{0,1:T(8,128)(2,1)S(1)} %bitcast.59, s32[]{:T(128)S(6)} %select_n.75), kind=kOutput, calls=%fused_computation.13 | convolution fusion | flops 402653184 | bytes 4063236 | tf_op jit(solution)/shard_map/tc,dc->td/dot_general | solution.py:164
  273.2 0.0 collective-permute-done
  273.2 3.8 %fusion.1 = bf16[128,1024]{1,0:T(8,128)(2,1)} fusion(f32[128,1024]{1,0:T(8,128)S(1)} %fusion.6, bf16[1024,1536]{1,0:T(8,128)(2,1)} %collective-permute-done, bf16[128,3072]{0,1:T(8,128)(2,1)S(1)} %bitcast.60, s32[]{:T(128)S(6)} %select_n.76), kind=kOutput, calls=%fused_computation.6 | convolution fusion | flops 402915328 | bytes 4325380 | tf_op jit(solution)/shard_map/tc,dc->td/dot_general | solution.py:165
  276.9 0.0 all-gather.12.cloned.1.call-done
  276.9 1.5 copy.39
  278.5 1.6 copy.41
  (8 shorter events, 0.1 us)
Async XLA Ops:
  7.2 46.4 %all-gather.6.cloned.1.call-start = ((), (), s32[]{:S(2)}) async-start(), calls=%async_computation.5 | async-start | bytes 4456448 | tf_op jit(solution)/shard_map/all_gather | solution.py:100
  7.9 114.9 %all-gather.8.cloned.1.call-start = ((), (), s32[]{:S(2)}) async-start(), calls=%async_computation.6 | async-start | bytes 2359296 | tf_op jit(solution)/shard_map/all_gather | solution.py:116
  53.6 4.7 %copy-start.2 = (bf16[128,1024]{1,0:T(8,128)(2,1)S(1)}, bf16[128,1024]{1,0:T(8,128)(2,1)}, u32[]{:S(2)}) copy-start(bf16[128,1024]{1,0:T(8,128)(2,1)} %param.7) | copy-start | bytes 786436
  59.1 11.0 %all-to-all-start = ((bf16[128,16,64]{0,2,1:T(8,128)(2,1)}), bf16[128,16,64]{0,2,1:T(8,128)(2,1)S(1)}, u32[]{:S(2)}, u32[]{:S(2)}) async-start(bf16[128,16,64]{0,2,1:T(8,128)(2,1)} %bitcast.7), calls=%async_computation | async-start | bytes 524288 | tf_op jit(solution)/shard_map/all_to_all | solution.py:120
  70.0 7.3 %copy-start.1 = (bf16[128,3072]{1,0:T(8,128)(2,1)S(1)}, bf16[128,3072]{1,0:T(8,128)(2,1)}, u32[]{:S(2)}) copy-start(bf16[128,3072]{1,0:T(8,128)(2,1)} %param.5) | copy-start | bytes 2359300
  71.9 6.3 %copy-start.3 = (s32[128,8]{0,1:T(8,128)S(1)}, s32[128,8]{0,1:T(8,128)}, u32[]{:S(2)}) copy-start(s32[128,8]{0,1:T(8,128)} %param.6) | copy-start | bytes 12292
  71.9 38.6 %all-to-all-start.1 = ((bf16[8,8,128,128]{3,2,1,0:T(8,128)(2,1)}), bf16[8,8,128,128]{3,2,1,0:T(8,128)(2,1)}, u32[]{:S(2)}, u32[]{:S(2)}) async-start(bf16[8,8,128,128]{3,2,1,0:T(8,128)(2,1)} %broadcast_in_dim.6), calls=%async_computation.1 | async-start | bytes 4194304 | tf_op jit(solution)/shard_map/all_to_all | solution.py:118
  77.3 151.8 %all-gather.10.cloned.1.call-start = ((), (), s32[]{:S(2)}) async-start(), calls=%async_computation.7 | async-start | bytes 3538944 | tf_op jit(solution)/shard_map/all_gather | solution.py:98
  122.8 1.6 copy-start
  217.0 20.2 %all-to-all-start.4 = ((f32[8,128,192]{1,2,0:T(8,128)}), f32[8,128,192]{1,2,0:T(8,128)S(1)}, u32[]{:S(2)}, u32[]{:S(2)}) async-start(f32[8,128,192]{1,2,0:T(8,128)} %bitcast.46), calls=%async_computation.4 | async-start | bytes 1572864 | tf_op jit(solution)/shard_map/all_to_all | solution.py:172
  225.1 51.8 %all-gather.12.cloned.1.call-start = ((), (), s32[]{:S(2)}) async-start(), calls=%async_computation.8 | async-start | bytes 1671168 | tf_op jit(solution)/shard_map/all_gather | solution.py:175
  229.1 44.0 %collective-permute-start = (bf16[1024,1536]{1,0:T(8,128)(2,1)}, bf16[1024,1536]{1,0:T(8,128)(2,1)}, u32[]{:S(2)}, u32[]{:S(2)}) collective-permute-start(bf16[1024,1536]{1,0:T(8,128)(2,1)} %all-gather.10.cloned.1.call-done), channel_id=1, source_target_pairs={{0,8},{8,0},{16,24},{24,16},{32,40},{40,32},{48,56},{56,48},{64,72... | collective-permute-start | bytes 9437192 | tf_op jit(solution)/shard_map/ppermute | solution.py:99
  242.8 23.3 %all-to-all-start.3 = ((bf16[16,2,16384]{2,1,0:T(2,128)(2,1)}), bf16[16,2,16384]{2,1,0:T(2,128)(2,1)S(1)}, u32[]{:S(2)}, u32[]{:S(2)}) async-start(bf16[16,2,16384]{2,1,0:T(2,128)(2,1)} %reshape.94), calls=%async_computation.3 | async-start | bytes 2097152 | tf_op jit(solution)/shard_map/all_to_all | solution.py:158
Sparse Core Ops, SparseCore 0:
  9.7 43.8 all-gather.5
  58.3 64.4 all-gather.7
  125.1 103.9 all-gather.9
  238.1 38.1 all-gather.11

commit v12 on v11

--- a/solution.py
+++ b/solution.py
@@ -97,10 +97,18 @@
     w_mine = lax.dynamic_slice_in_dim(projection, core * width, width, axis=1)
     w_mine = lax.all_gather(w_mine, "zero", axis=0, tiled=True)
     w_other = lax.ppermute(w_mine, "seq", pair)
-    group_tokens = lax.all_gather(tokens, "seq", axis=0, tiled=True)
+    half_rows = tok_rows // 2
+    t_a = lax.all_gather(tokens[:half_rows], "seq", axis=0, tiled=True)
+    t_b = jnp.broadcast_to(tokens[half_rows:], (seq_count, half_rows, model_width))
+    t_b = lax.all_to_all(t_b, "seq", split_axis=0, concat_axis=0, tiled=True)
+    group_tokens = jnp.concatenate(
+        [t_a.reshape(seq_count, half_rows, model_width), t_b], axis=1
+    ).reshape(seq_count * tok_rows, model_width)
     head_w = projection.reshape(projection.shape[0], 3, seq_count, head_cols)
     head_w = lax.dynamic_index_in_dim(head_w, seq_index, axis=2, keepdims=False)
-    head_w = lax.all_gather(head_w, "zero", axis=0, tiled=True)
+    head_w = jnp.broadcast_to(head_w, (zero_count,) + head_w.shape)
+    head_w = lax.all_to_all(head_w, "zero", split_axis=0, concat_axis=0, tiled=True)
+    head_w = head_w.reshape(-1, 3, head_cols)
     kv_local = jnp.einsum(
         "td,dc->tc",
         group_tokens,

time: 287 us -> 300 us (1.045)
  waiting for transfers between devices: 91.5 us -> 99.2 us
    all_gather x1 -> x0, blocking collectives: 28.7 us -> none  [on_device(): head_w = lax.all_gather(head_w, 'zero', axis=0, tiled=True)]
    all_to_all x0 -> x2, blocking collectives: none -> 28.5 us  [the longest x1 16.9 us: on_device(): lax.all_to_all(head_w, 'zero', split_axis=0, concat_axis=0, tiled=True)]
    all_to_all x1, waiting for transfers between devices: 7.2 us -> 30.5 us  [on_device(): t_b = lax.all_to_all(t_b, 'seq', split_axis=0, concat_axis=0, tiled=True)]
    all_gather x1, waiting for transfers between devices: 15.3 us -> 0.01 us  [on_device(): t_a = lax.all_gather(tokens[:half_rows], 'seq', axis=0, tiled=True)]
    all_to_all x1, starting transfers between devices: 3.61 us -> 6.94 us  [on_device(): t_b = lax.all_to_all(t_b, 'seq', split_axis=0, concat_axis=0, tiled=True)]
    unnamed x14 -> x16, local copies, waits for them, and re-layouts: 9.25 us -> 9.26 us
  transfers between devices with their start and end apart: 9 -> 9, of which waited for: 7 -> 6; matrix products, arithmetic and copies ran while one was open for 12% -> 12% of each run, Pallas kernels for 9% -> 8%
where the time goes in v12:
time: 300 us; the launch traced here: 299 us
  waiting for transfers between devices  99.2 us (33%)
  blocking collectives  88.5 us (30%)
  starting transfers between devices  26.8 us (9%)
  Pallas kernels  25 us (8%)
  local copies, waits for them, and re-layouts  23.7 us (8%)
  matrix products  15.2 us (5%)
  between operations  14 us (5%)
  other arithmetic  6.56 us (2%)
    all_to_all x1, blocking collectives, on_device(): lax.all_to_all(group_sums, 'zero', split_axis=0, concat_axis=0, tiled=True)  60 us
    all_to_all x1, waiting for transfers between devices, on_device(): t_b = lax.all_to_all(t_b, 'seq', split_axis=0, concat_axis=0, tiled=True)  30.5 us
    all_to_all x1, waiting for transfers between devices, on_device(): kv_b = lax.all_to_all(kv_b, 'zero', split_axis=0, concat_axis=0, tiled=True)  27.3 us
    pallas_call x1, Pallas kernels, block_attention(): pl.pallas_call(functools.partial(_attn_kernel, scale=scale), grid_spec=gr...  25 us
    all_to_all x1, waiting for transfers between devices, on_device(): lax.all_to_all(outgoing, 'seq', split_axis=0, concat_axis=2, tiled=True)  18 us
    all_to_all x1, blocking collectives, on_device(): lax.all_to_all(head_w, 'zero', split_axis=0, concat_axis=0, tiled=True)  16.9 us
    all_gather x1, waiting for transfers between devices, on_device(): kv_a = lax.all_gather(kv_local[:split], 'zero', axis=0, tiled=True)  12.4 us
    all_to_all x1, blocking collectives, on_device(): lax.all_to_all(upstream.reshape(tok_rows, seq_count, head_cols), 'seq', s...  11.6 us
  transfers between devices with their start and end apart: 9, of which 6 were waited for; matrix products, arithmetic and copies ran while one was open for 12% of the time, Pallas kernels for 8%

profile of v12, /device:TPU:1, one launch (start us, length us, event | category | flops | bytes accessed | tf_op | source)
XLA Modules:
  0.0 298.9 jit_solution(1542190672803416282)
XLA Ops:
  7.2 0.0 all-gather.5.cloned.1.call-start
  7.2 1.6 fusion.22
  8.8 0.0 all-gather.5.cloned.1.call-update
  8.9 1.5 copy.23
  10.4 0.1 broadcast_in_dim.13
  10.5 16.9 %all_to_all.58 = bf16[8,128,3,64]{1,3,2,0:T(8,128)(2,1)S(1)} all-to-all(bf16[8,128,3,64]{1,3,2,0:T(8,128)(2,1)S(1)} %broadcast_in_dim.13), channel_id=1, replica_groups=mesh['seq'=16,'zero'=8] {'zero'}, dimensions={0} | all-to-all | bytes 786432 | tf_op jit(solution)/shard_map/all_to_all | solution.py:110
  27.4 1.6 broadcast_in_dim.12
  29.0 6.9 %all-to-all-start = ((bf16[16,64,1024]{2,1,0:T(8,128)(2,1)}), bf16[16,64,1024]{2,1,0:T(8,128)(2,1)S(1)}, u32[]{:S(2)}, u32[]{:S(2)}) async-start(bf16[16,64,1024]{2,1,0:T(8,128)(2,1)} %broadcast_in_dim.12), calls=%async_computation | async-start | bytes 4194304 | tf_op jit(solution)/shard_map/all_to_all | solution.py:103
  35.9 0.0 all-gather.7.cloned.1.call-start
  36.0 0.1 copy_bitcast_fusion.1
  36.0 30.5 %all-to-all-done = bf16[16,64,1024]{2,1,0:T(8,128)(2,1)S(1)} async-done(((bf16[16,64,1024]{2,1,0:T(8,128)(2,1)}), bf16[16,64,1024]{2,1,0:T(8,128)(2,1)S(1)}, u32[]{:S(2)}, u32[]{:S(2)}) %all-to-all-start) | async-done | bytes 2097184 | tf_op jit(solution)/shard_map/all_to_all | solution.py:103
  66.6 2.3 pad_maximum_fusion
  68.8 0.0 copy-start.1
  68.8 0.0 copy-start.3
  68.8 1.3 convolution_convert_fusion
  70.1 0.8 fusion.21
  70.9 0.0 all-gather.7.cloned.1.call-update
  70.9 0.0 copy-done.3
  70.9 0.2 copy.26
  71.1 11.6 %all_to_all.59 = bf16[128,16,64]{0,2,1:T(8,128)(2,1)S(1)} all-to-all(bf16[128,16,64]{0,2,1:T(8,128)(2,1)S(1)} %bitcast.73), channel_id=1, replica_groups=mesh['seq'=16,'zero'=8] {'seq'}, dimensions={1} | all-to-all | bytes 524288 | tf_op jit(solution)/shard_map/all_to_all | solution.py:128
  82.7 1.9 broadcast_in_dim.14
  84.6 4.7 %all-to-all-start.3 = ((bf16[8,8,128,128]{3,2,1,0:T(8,128)(2,1)}), bf16[8,8,128,128]{3,2,1,0:T(8,128)(2,1)}, u32[]{:S(2)}, u32[]{:S(2)}) async-start(bf16[8,8,128,128]{3,2,1,0:T(8,128)(2,1)} %broadcast_in_dim.14), calls=%async_computation.3 | async-start | bytes 4194304 | tf_op jit(solution)/shard_map/all_to_all | solution.py:126
  89.3 0.0 all-gather.9.cloned.1.call-start
  89.4 0.0 copy-done.2
  89.4 0.8 constant_dynamic-slice_fusion
  90.2 0.0 all-gather.9.cloned.1.call-update
  90.2 0.0 copy-done.4
  90.2 0.1 copy.22
  90.3 0.6 gather_fusion
  90.9 3.6 %convolution_convert_fusion.1 = bf16[2048,64]{0,1:T(8,128)(2,1)S(1)} fusion(bf16[2048,1024]{1,0:T(8,128)(2,1)} %bitcast.59, bf16[1024,3,64]{0,2,1:T(8,128)(2,1)S(1)} %copy_bitcast_fusion.1), kind=kOutput, calls=%fused_computation.3 | convolution fusion | flops 268566528 | bytes 4587520 | tf_op jit(solution)/shard_map/td,dc->tc/dot_general | solution.py:119
  94.5 0.3 copy.25
  94.8 0.3 copy.27
  95.1 27.3 %all-to-all-done.3 = bf16[8,8,128,128]{3,2,1,0:T(8,128)(2,1)} async-done(((bf16[8,8,128,128]{3,2,1,0:T(8,128)(2,1)}), bf16[8,8,128,128]{3,2,1,0:T(8,128)(2,1)}, u32[]{:S(2)}, u32[]{:S(2)}) %all-to-all-start.3) | async-done | bytes 2097184 | tf_op jit(solution)/shard_map/all_to_all | solution.py:126
  122.4 12.4 %all-gather.7.cloned.1.call-done.ka_ref = bf16[64,128,128]{2,1,0:T(8,128)(2,1)} async-done(((bf16[8,128,128]{2,1,0:T(8,128)(2,1)}), bf16[64,128,128]{2,1,0:T(8,128)(2,1)}) %all-gather.7.cloned.1.call-update) | async-done | bytes 2097168 | tf_op jit(solution)/shard_map/all_gather | solution.py:124
  134.8 1.6 copy-done
  136.4 25.0 %shard_map.67 = (bf16[16,128,64]{2,1,0:T(8,128)(2,1)S(1)}, bf16[16,128,64]{2,1,0:T(8,128)(2,1)S(1)}, bf16[128,128,128]{2,1,0:T(8,128)(2,1)}) custom-call(s32[16,8]{1,0:T(8,128)S(1)} %get-tuple-element.22.slots_ref, s32[16,8]{1,0:T(8,128)S(1)} %add_select_fusion.4.a_ids_ref, s32[16,8]{1,0:T(8,128)S(1)} %get-tuple-element.21.b_ids_ref, ...), custom_call_target="tpu_custom_call" | custom-call | tf_op jit(solution)/shard_map/pallas_call | solution.py:72
  161.3 60.0 %all_to_all.60 = bf16[8,2048,128]{2,1,0:T(8,128)(2,1)} all-to-all(bf16[8,2048,128]{2,1,0:T(8,128)(2,1)} %bitcast.67), channel_id=1, replica_groups=mesh['seq'=16,'zero'=8] {'zero'}, dimensions={0} | all-to-all | bytes 8388608 | tf_op jit(solution)/shard_map/all_to_all | solution.py:161
  221.3 3.1 %reduce_sum.21 = bf16[2048,128]{1,0:T(8,128)(2,1)S(1)} reduce(bf16[8,2048,128]{2,1,0:T(8,128)(2,1)} %all_to_all.60, bf16[]{:T(256)} %constant.123.clone.1), dimensions={0}, to_apply=%region_0.1 | reduce | flops 1835008 | bytes 4718594 | tf_op jit(solution)/shard_map/reduce_sum | solution.py:162
  224.4 3.6 %convolution_bitcast_fusion = f32[24,8,8,128]{3,2,1,0:T(8,128)S(1)} fusion(bf16[2048,1024]{1,0:T(8,128)(2,1)} %bitcast.60, bf16[2048,128]{1,0:T(8,128)(2,1)S(1)} %reduce_sum.21, bf16[2048,64]{1,0:T(8,128)(2,1)S(1)} %bitcast.56), kind=kOutput, calls=%fused_computation.4 | convolution fusion | flops 806879232 | bytes 5767168 | tf_op jit(solution)/shard_map/td,tc->dc/dot_general | solution.py:176
  228.0 0.9 copy.42
  228.9 8.1 %all-to-all-start.6 = ((f32[8,128,192]{1,2,0:T(8,128)}), f32[8,128,192]{1,2,0:T(8,128)S(1)}, u32[]{:S(2)}, u32[]{:S(2)}) async-start(f32[8,128,192]{1,2,0:T(8,128)} %bitcast.52), calls=%async_computation.6 | async-start | bytes 1572864 | tf_op jit(solution)/shard_map/all_to_all | solution.py:180
  237.0 0.0 all-gather.11.cloned.1.call-start
  237.0 4.0 %all-gather.9.cloned.1.call-done = bf16[1024,1536]{1,0:T(8,128)(2,1)} async-done(((bf16[128,1536]{1,0:T(8,128)(2,1)}), bf16[1024,1536]{1,0:T(8,128)(2,1)}) %all-gather.9.cloned.1.call-update) | async-done | bytes 3145744 | tf_op jit(solution)/shard_map/all_gather | solution.py:98
  241.1 1.0 collective-permute-start
  242.1 7.0 %all-to-all-done.6 = f32[8,128,192]{1,2,0:T(8,128)S(1)} async-done(((f32[8,128,192]{1,2,0:T(8,128)}), f32[8,128,192]{1,2,0:T(8,128)S(1)}, u32[]{:S(2)}, u32[]{:S(2)}) %all-to-all-start.6) | async-done | bytes 786464 | tf_op jit(solution)/shard_map/all_to_all | solution.py:180
  249.1 0.7 reduce_sum.22
  249.8 0.0 all-gather.11.cloned.1.call-update
  249.8 0.5 pad_maximum_fusion.1
  250.3 0.6 copy.28
  250.9 1.4 copy.29
  252.3 2.2 reshape.105
  254.6 5.9 %all-to-all-start.5 = ((bf16[16,2,16384]{2,1,0:T(2,128)(2,1)}), bf16[16,2,16384]{2,1,0:T(2,128)(2,1)S(1)}, u32[]{:S(2)}, u32[]{:S(2)}) async-start(bf16[16,2,16384]{2,1,0:T(2,128)(2,1)} %reshape.105), calls=%async_computation.5 | async-start | bytes 2097152 | tf_op jit(solution)/shard_map/all_to_all | solution.py:166
  260.4 18.0 %all-to-all-done.5 = bf16[16,2,16384]{2,1,0:T(2,128)(2,1)S(1)} async-done(((bf16[16,2,16384]{2,1,0:T(2,128)(2,1)}), bf16[16,2,16384]{2,1,0:T(2,128)(2,1)S(1)}, u32[]{:S(2)}, u32[]{:S(2)}) %all-to-all-start.5) | async-done | bytes 1048608 | tf_op jit(solution)/shard_map/all_to_all | solution.py:166
  278.4 1.3 reshape.106
  279.7 1.4 copy.37
  281.1 0.1 slice.45
  281.3 0.2 copy.32
  281.5 0.1 copy.31
  281.6 0.9 copy.35
  282.4 3.1 %fusion.5 = f32[128,1024]{1,0:T(8,128)S(1)} fusion(bf16[1024,1536]{1,0:T(8,128)(2,1)} %all-gather.9.cloned.1.call-done, bf16[128,3072]{0,1:T(8,128)(2,1)S(1)} %bitcast.68, s32[]{:T(128)S(6)} %select_n.75), kind=kOutput, calls=%fused_computation.14 | convolution fusion | flops 402653184 | bytes 4063236 | tf_op jit(solution)/shard_map/tc,dc->td/dot_general | solution.py:172
  285.5 0.0 collective-permute-done
  285.5 3.8 %fusion = bf16[128,1024]{1,0:T(8,128)(2,1)} fusion(f32[128,1024]{1,0:T(8,128)S(1)} %fusion.5, bf16[1024,1536]{1,0:T(8,128)(2,1)} %collective-permute-done, bf16[128,3072]{0,1:T(8,128)(2,1)S(1)} %bitcast.69, s32[]{:T(128)S(6)} %select_n.76), kind=kOutput, calls=%fused_computation.6 | convolution fusion | flops 402915328 | bytes 4325380 | tf_op jit(solution)/shard_map/tc,dc->td/dot_general | solution.py:173
  289.3 1.5 copy.34
  290.8 1.6 copy.36
  (13 shorter events, 0.1 us)
Async XLA Ops:
  7.2 59.4 %all-gather.5.cloned.1.call-start = ((), (), s32[]{:S(2)}) async-start(), calls=%async_computation.7 | async-start | bytes 2228224 | tf_op jit(solution)/shard_map/all_gather | solution.py:101
  29.0 37.6 %all-to-all-start = ((bf16[16,64,1024]{2,1,0:T(8,128)(2,1)}), bf16[16,64,1024]{2,1,0:T(8,128)(2,1)S(1)}, u32[]{:S(2)}, u32[]{:S(2)}) async-start(bf16[16,64,1024]{2,1,0:T(8,128)(2,1)} %broadcast_in_dim.12), calls=%async_computation | async-start | bytes 4194304 | tf_op jit(solution)/shard_map/all_to_all | solution.py:103
  35.9 98.8 %all-gather.7.cloned.1.call-start = ((), (), s32[]{:S(2)}) async-start(), calls=%async_computation.8 | async-start | bytes 2359296 | tf_op jit(solution)/shard_map/all_gather | solution.py:124
  68.8 2.1 copy-start.1
  68.8 2.1 copy-start.3
  82.7 6.7 %copy-start.2 = (bf16[128,3072]{1,0:T(8,128)(2,1)S(1)}, bf16[128,3072]{1,0:T(8,128)(2,1)}, u32[]{:S(2)}) copy-start(bf16[128,3072]{1,0:T(8,128)(2,1)} %param.5) | copy-start | bytes 2359300
  84.6 5.6 %copy-start.4 = (s32[128,8]{0,1:T(8,128)S(1)}, s32[128,8]{0,1:T(8,128)}, u32[]{:S(2)}) copy-start(s32[128,8]{0,1:T(8,128)} %param.6) | copy-start | bytes 12292
  84.6 37.8 %all-to-all-start.3 = ((bf16[8,8,128,128]{3,2,1,0:T(8,128)(2,1)}), bf16[8,8,128,128]{3,2,1,0:T(8,128)(2,1)}, u32[]{:S(2)}, u32[]{:S(2)}) async-start(bf16[8,8,128,128]{3,2,1,0:T(8,128)(2,1)} %broadcast_in_dim.14), calls=%async_computation.3 | async-start | bytes 4194304 | tf_op jit(solution)/shard_map/all_to_all | solution.py:126
  89.3 151.8 %all-gather.9.cloned.1.call-start = ((), (), s32[]{:S(2)}) async-start(), calls=%async_computation.9 | async-start | bytes 3538944 | tf_op jit(solution)/shard_map/all_gather | solution.py:98
  134.8 1.6 copy-start
  228.9 20.2 %all-to-all-start.6 = ((f32[8,128,192]{1,2,0:T(8,128)}), f32[8,128,192]{1,2,0:T(8,128)S(1)}, u32[]{:S(2)}, u32[]{:S(2)}) async-start(f32[8,128,192]{1,2,0:T(8,128)} %bitcast.52), calls=%async_computation.6 | async-start | bytes 1572864 | tf_op jit(solution)/shard_map/all_to_all | solution.py:180
  237.0 52.3 %all-gather.11.cloned.1.call-start = ((), (), s32[]{:S(2)}) async-start(), calls=%async_computation.10 | async-start | bytes 1671168 | tf_op jit(solution)/shard_map/all_gather | solution.py:183
  241.1 44.5 %collective-permute-start = (bf16[1024,1536]{1,0:T(8,128)(2,1)}, bf16[1024,1536]{1,0:T(8,128)(2,1)}, u32[]{:S(2)}, u32[]{:S(2)}) collective-permute-start(bf16[1024,1536]{1,0:T(8,128)(2,1)} %all-gather.9.cloned.1.call-done), channel_id=1, source_target_pairs={{0,8},{8,0},{16,24},{24,16},{32,40},{40,32},{48,56},{56,48},{64,72... | collective-permute-start | bytes 9437192 | tf_op jit(solution)/shard_map/ppermute | solution.py:99
  254.6 23.8 %all-to-all-start.5 = ((bf16[16,2,16384]{2,1,0:T(2,128)(2,1)}), bf16[16,2,16384]{2,1,0:T(2,128)(2,1)S(1)}, u32[]{:S(2)}, u32[]{:S(2)}) async-start(bf16[16,2,16384]{2,1,0:T(2,128)(2,1)} %reshape.105), calls=%async_computation.5 | async-start | bytes 2097152 | tf_op jit(solution)/shard_map/all_to_all | solution.py:166
Sparse Core Ops, SparseCore 0:
  10.2 55.5 all-gather.4
  71.1 63.6 all-gather.6
  137.1 103.9 all-gather.8
  249.9 37.9 all-gather.10

commit v13 on v11

--- a/solution.py
+++ b/solution.py
@@ -149,9 +149,18 @@
         kv_b,
         score_scale,
     )
-    group_sums = group_sums.reshape(zero_count, local_blocks * BLOCK, 2 * head_cols)
-    group_sums = lax.all_to_all(group_sums, "zero", split_axis=0, concat_axis=0, tiled=True)
-    kv_sum = jnp.sum(group_sums.astype(jnp.float32), axis=0).astype(jnp.bfloat16)
+    group_sums = group_sums.reshape(zero_count, local_blocks, BLOCK, 2 * head_cols)
+    part_a = lax.all_to_all(group_sums[:, :split], "zero", split_axis=0, concat_axis=0, tiled=True)
+    sum_a = jnp.sum(part_a.astype(jnp.float32), axis=0)
+    part_b = group_sums[:, split:]
+    sum_b = lax.dynamic_index_in_dim(part_b, zero_index, axis=0, keepdims=False).astype(jnp.float32)
+    for shift in range(1, zero_count):
+        dest = (zero_index + shift) % zero_count
+        piece = lax.dynamic_index_in_dim(part_b, dest, axis=0, keepdims=False)
+        ring = [(i, (i + shift) % zero_count) for i in range(zero_count)]
+        sum_b = sum_b + lax.ppermute(piece, "zero", ring).astype(jnp.float32)
+    kv_sum = jnp.concatenate([sum_a, sum_b], axis=0).astype(jnp.bfloat16)
+    kv_sum = kv_sum.reshape(local_blocks * BLOCK, 2 * head_cols)
     local_grads = jnp.concatenate([query_grads.reshape(-1, head_cols), kv_sum], axis=1)
     outgoing = jnp.concatenate([out_blocks.reshape(-1, head_cols), local_grads], axis=1)
     outgoing = outgoing.reshape(local_blocks * BLOCK, 4, 1, head_cols)

time: 287 us -> 312 us (1.087)
  blocking collectives: 88.8 us -> 28.7 us
  waiting for transfers between devices: 91.5 us -> 148 us
  local copies, waits for them, and re-layouts: 21.2 us -> 36.1 us
  starting transfers between devices: 24 us -> 38.2 us
    all_to_all x1 -> x0, blocking collectives: 60 us -> none  [on_device(): lax.all_to_all(group_sums, 'zero', split_axis=0, concat_axis=0, tiled=True)]
    ppermute x0 -> x7, waiting for transfers between devices: none -> 59.3 us  [on_device(): sum_b = sum_b + lax.ppermute(piece, 'zero', ring).astype(jnp.float32)]
    ppermute x0 -> x7, starting transfers between devices: none -> 9.35 us  [on_device(): sum_b = sum_b + lax.ppermute(piece, 'zero', ring).astype(jnp.float32)]
    slice x0 -> x1, local copies, waits for them, and re-layouts: none -> 4.77 us  [on_device(): group_sums[:, :split]]
    all_to_all x1, starting transfers between devices: 8.09 us -> 3.93 us  [on_device(): lax.all_to_all(head_part, 'zero', split_axis=0, concat_axis=0, tiled=True)]
    all_gather x1, waiting for transfers between devices: 3.93 us -> 0.02 us  [on_device(): w_mine = lax.all_gather(w_mine, 'zero', axis=0, tiled=True)]
    all_to_all x0 -> x1, starting transfers between devices: none -> 3.63 us  [on_device(): lax.all_to_all(group_sums[:, :split], 'zero', split_axis=0, concat_axis=0...]
    unnamed x14, local copies, waits for them, and re-layouts: 9.25 us -> 12.6 us
  transfers between devices with their start and end apart: 9 -> 17, of which waited for: 7 -> 9; matrix products, arithmetic and copies ran while one was open for 12% -> 15% of each run, Pallas kernels for 9% -> 8%
where the time goes in v13:
time: 312 us; the launch traced here: 311 us
  waiting for transfers between devices  148 us (47%)
  starting transfers between devices  38.2 us (12%)
  local copies, waits for them, and re-layouts  36.1 us (12%)
  blocking collectives  28.7 us (9%)
  Pallas kernels  25 us (8%)
  matrix products  17.3 us (6%)
  between operations  14.2 us (5%)
  other arithmetic  4 us (1%)
    ppermute x7, waiting for transfers between devices, on_device(): sum_b = sum_b + lax.ppermute(piece, 'zero', ring).astype(jnp.float32)  59.3 us
    all_gather x1, blocking collectives, on_device(): head_w = lax.all_gather(head_w, 'zero', axis=0, tiled=True)  28.7 us
    all_to_all x1, waiting for transfers between devices, on_device(): kv_b = lax.all_to_all(kv_b, 'zero', split_axis=0, concat_axis=0, tiled=True)  28.6 us
    pallas_call x1, Pallas kernels, block_attention(): pl.pallas_call(functools.partial(_attn_kernel, scale=scale), grid_spec=gr...  25 us
    all_to_all x1, waiting for transfers between devices, on_device(): lax.all_to_all(outgoing, 'seq', split_axis=0, concat_axis=2, tiled=True)  18.1 us
    all_gather x1, waiting for transfers between devices, on_device(): group_tokens = lax.all_gather(tokens, 'seq', axis=0, tiled=True)  15.3 us
    unnamed x14, local copies, waits for them, and re-layouts  12.6 us
    all_gather x1, waiting for transfers between devices, on_device(): kv_a = lax.all_gather(kv_local[:split], 'zero', axis=0, tiled=True)  12 us
  transfers between devices with their start and end apart: 17, of which 9 were waited for; matrix products, arithmetic and copies ran while one was open for 15% of the time, Pallas kernels for 8%

profile of v13, /device:TPU:1, one launch (start us, length us, event | category | flops | bytes accessed | tf_op | source)
XLA Modules:
  0.0 311.3 jit_solution(17830720717472912492)
XLA Ops:
  7.2 0.0 all-gather.6.cloned.1.call-start
  7.2 0.7 all-gather.6.cloned.1.call-update
  7.9 0.0 all-gather.8.cloned.1.call-start
  7.9 1.5 copy.28
  9.5 28.7 %all-gather = bf16[1024,3,1,64]{0,3,2,1:T(8,128)(2,1)S(1)} all-gather(bf16[128,3,1,64]{0,3,2,1:T(8,128)(2,1)S(1)} %constant_dynamic-slice_fusion.1), channel_id=2, replica_groups=mesh['seq'=16,'zero'=8] {'zero'}, dimensions={0}, use_global_device_ids=true | all-gather | bytes 442368 | tf_op jit(solution)/shard_map/all_gather | solution.py:103
  38.2 15.3 %all-gather.6.cloned.1.call-done = bf16[2048,1024]{1,0:T(8,128)(2,1)} async-done(((bf16[128,1024]{1,0:T(8,128)(2,1)}), bf16[2048,1024]{1,0:T(8,128)(2,1)}) %all-gather.6.cloned.1.call-update) | async-done | bytes 4194320 | tf_op jit(solution)/shard_map/all_gather | solution.py:100
  53.6 3.7 %fusion = bf16[2048,128]{0,1:T(8,128)(2,1)S(1)} fusion(bf16[1024,128]{0,1:T(8,128)(2,1)S(1)} %bitcast.82, bf16[2048,1024]{1,0:T(8,128)(2,1)} %all-gather.6.cloned.1.call-done), kind=kOutput, calls=%fused_computation.2 | convolution fusion | flops 537133056 | bytes 4980736 | tf_op jit(solution)/shard_map/td,dc->tc/dot_general | solution.py:104
  57.3 0.8 copy.46
  58.2 0.0 all-gather.10.cloned.1.call-start
  58.3 0.2 copy-done.1
  58.4 0.8 constant_dynamic-slice_fusion
  59.2 0.8 copy.30
  60.1 3.6 %all-to-all-start = ((bf16[128,16,64]{0,2,1:T(8,128)(2,1)}), bf16[128,16,64]{0,2,1:T(8,128)(2,1)S(1)}, u32[]{:S(2)}, u32[]{:S(2)}) async-start(bf16[128,16,64]{0,2,1:T(8,128)(2,1)} %bitcast.7), calls=%async_computation | async-start | bytes 524288 | tf_op jit(solution)/shard_map/all_to_all | solution.py:120
  63.7 0.2 copy.47
  63.9 7.1 %all-to-all-done = bf16[128,16,64]{0,2,1:T(8,128)(2,1)S(1)} async-done(((bf16[128,16,64]{0,2,1:T(8,128)(2,1)}), bf16[128,16,64]{0,2,1:T(8,128)(2,1)S(1)}, u32[]{:S(2)}, u32[]{:S(2)}) %all-to-all-start) | async-done | bytes 262176 | tf_op jit(solution)/shard_map/all_to_all | solution.py:120
  71.0 1.9 broadcast_in_dim.6
  72.9 5.6 %all-to-all-start.1 = ((bf16[8,8,128,128]{3,2,1,0:T(8,128)(2,1)}), bf16[8,8,128,128]{3,2,1,0:T(8,128)(2,1)}, u32[]{:S(2)}, u32[]{:S(2)}) async-start(bf16[8,8,128,128]{3,2,1,0:T(8,128)(2,1)} %broadcast_in_dim.6), calls=%async_computation.1 | async-start | bytes 4194304 | tf_op jit(solution)/shard_map/all_to_all | solution.py:118
  78.5 0.1 copy.27
  78.6 0.6 gather_fusion
  79.2 3.6 %convolution_convert_fusion.1 = bf16[2048,64]{0,1:T(8,128)(2,1)S(1)} fusion(bf16[2048,1024]{1,0:T(8,128)(2,1)} %all-gather.6.cloned.1.call-done, bf16[1024,3,64]{0,2,1:T(8,128)(2,1)S(1)} %bitcast.80), kind=kOutput, calls=%fused_computation.3 | convolution fusion | flops 268566528 | bytes 4587520 | tf_op jit(solution)/shard_map/td,dc->tc/dot_general | solution.py:111
  82.8 0.3 copy.29
  83.1 0.3 copy.31
  83.4 28.6 %all-to-all-done.1 = bf16[8,8,128,128]{3,2,1,0:T(8,128)(2,1)} async-done(((bf16[8,8,128,128]{3,2,1,0:T(8,128)(2,1)}), bf16[8,8,128,128]{3,2,1,0:T(8,128)(2,1)}, u32[]{:S(2)}, u32[]{:S(2)}) %all-to-all-start.1) | async-done | bytes 2097184 | tf_op jit(solution)/shard_map/all_to_all | solution.py:118
  112.0 12.0 %all-gather.8.cloned.1.call-done.ka_ref = bf16[64,128,128]{2,1,0:T(8,128)(2,1)} async-done(((bf16[8,128,128]{2,1,0:T(8,128)(2,1)}), bf16[64,128,128]{2,1,0:T(8,128)(2,1)}) %all-gather.8.cloned.1.call-update) | async-done | bytes 2097168 | tf_op jit(solution)/shard_map/all_gather | solution.py:116
  124.0 1.6 copy-done
  125.5 25.0 %shard_map.67 = (bf16[16,128,64]{2,1,0:T(8,128)(2,1)S(1)}, bf16[16,128,64]{2,1,0:T(8,128)(2,1)S(1)}, bf16[128,128,128]{2,1,0:T(8,128)(2,1)}) custom-call(s32[16,8]{1,0:T(8,128)S(1)} %get-tuple-element.22.slots_ref, s32[16,8]{1,0:T(8,128)S(1)} %add_select_fusion.4.a_ids_ref, s32[16,8]{1,0:T(8,128)S(1)} %get-tuple-element.21.b_ids_ref, ...), custom_call_target="tpu_custom_call" | custom-call | tf_op jit(solution)/shard_map/pallas_call | solution.py:72
  150.5 4.8 %fusion.29 = (bf16[8,8,128,128]{3,2,1,0:T(8,128)(2,1)}, bf16[8,8,128,128]{3,2,1,0:T(8,128)(2,1)}) fusion(bf16[8,16,128,128]{3,2,1,0:T(8,128)(2,1)} %bitcast.75), kind=kLoop, calls=%fused_computation.63 | loop fusion | bytes 8388608 | tf_op jit(solution)/shard_map/slice | solution.py:153
  155.3 3.6 %all-to-all-start.2 = ((bf16[8,8,128,128]{3,2,1,0:T(8,128)(2,1)}), bf16[8,8,128,128]{3,2,1,0:T(8,128)(2,1)S(1)}, u32[]{:S(2)}, u32[]{:S(2)}) async-start(bf16[8,8,128,128]{3,2,1,0:T(8,128)(2,1)} %get-tuple-element.23), calls=%async_computation.2 | async-start | bytes 4194304 | tf_op jit(solution)/shard_map/all_to_all | solution.py:153
  159.0 2.5 dynamic-slice_bitcast_fusion.6
  161.6 4.9 %collective-permute-start.6 = (bf16[8,128,128]{2,1,0:T(8,128)(2,1)S(1)}, bf16[8,128,128]{2,1,0:T(8,128)(2,1)}, u32[]{:S(2)}, u32[]{:S(2)}) collective-permute-start(bf16[8,128,128]{2,1,0:T(8,128)(2,1)S(1)} %get-tuple-element.26), channel_id=1, source_target_pairs={{0,7},{1,0},{2,1},{3,2},{4,3},{5,4},{6,5},{7,6},{8,15},{9,8},{10,9... | collective-permute-start | bytes 786440 | tf_op jit(solution)/shard_map/ppermute | solution.py:161
  166.5 0.6 collective-permute-start.5
  167.0 0.3 collective-permute-start.4
  167.3 2.4 collective-permute-start.3
  169.7 1.2 collective-permute-start.2
  170.9 42.4 %collective-permute-done.6 = bf16[8,128,128]{2,1,0:T(8,128)(2,1)} collective-permute-done((bf16[8,128,128]{2,1,0:T(8,128)(2,1)S(1)}, bf16[8,128,128]{2,1,0:T(8,128)(2,1)}, u32[]{:S(2)}, u32[]{:S(2)}) %collective-permute-start.6) | collective-permute-done | bytes 262176 | tf_op jit(solution)/shard_map/ppermute | solution.py:161
  213.3 0.2 copy.36
  213.5 9.8 %collective-permute-done.1 = bf16[8,128,128]{2,1,0:T(8,128)(2,1)} collective-permute-done((bf16[8,128,128]{2,1,0:T(8,128)(2,1)}, bf16[8,128,128]{2,1,0:T(8,128)(2,1)}, u32[]{:S(2)}, u32[]{:S(2)}) %collective-permute-start.1) | collective-permute-done | bytes 262176 | tf_op jit(solution)/shard_map/ppermute | solution.py:161
  223.3 7.1 %collective-permute-done = bf16[8,128,128]{2,1,0:T(8,128)(2,1)} collective-permute-done((bf16[8,128,128]{2,1,0:T(8,128)(2,1)}, bf16[8,128,128]{2,1,0:T(8,128)(2,1)}, u32[]{:S(2)}, u32[]{:S(2)}) %collective-permute-start) | collective-permute-done | bytes 262176 | tf_op jit(solution)/shard_map/ppermute | solution.py:161
  230.4 1.8 fusion.11
  232.3 0.4 reduce
  232.7 0.2 copy.48
  232.9 3.2 %convolution_bitcast_fusion = f32[24,8,8,128]{3,2,1,0:T(8,128)S(1)} fusion(bf16[2048,1024]{1,0:T(8,128)(2,1)} %all-gather.6.cloned.1.call-done, bf16[2048,128]{0,1:T(8,128)(2,1)S(1)} %copy.48, bf16[2048,64]{0,1:T(8,128)(2,1)S(1)} %copy.36), kind=kOutput, calls=%fused_computation.4 | convolution fusion | flops 806879232 | bytes 5767168 | tf_op jit(solution)/shard_map/td,tc->dc/dot_general | solution.py:177
  236.1 0.9 copy.52
  237.0 3.9 %all-to-all-start.4 = ((f32[8,128,192]{1,2,0:T(8,128)}), f32[8,128,192]{1,2,0:T(8,128)S(1)}, u32[]{:S(2)}, u32[]{:S(2)}) async-start(f32[8,128,192]{1,2,0:T(8,128)} %bitcast.64), calls=%async_computation.4 | async-start | bytes 1572864 | tf_op jit(solution)/shard_map/all_to_all | solution.py:181
  241.0 3.0 collective-permute-start.7
  244.1 6.8 %all-to-all-done.4 = f32[8,128,192]{1,2,0:T(8,128)S(1)} async-done(((f32[8,128,192]{1,2,0:T(8,128)}), f32[8,128,192]{1,2,0:T(8,128)S(1)}, u32[]{:S(2)}, u32[]{:S(2)}) %all-to-all-start.4) | async-done | bytes 786464 | tf_op jit(solution)/shard_map/all_to_all | solution.py:181
  250.8 0.7 reduce_sum.19
  251.5 0.2 copy.35
  251.7 1.0 pad_maximum_fusion
  252.8 2.9 copy.37
  255.7 2.2 reshape.100
  257.9 8.9 %all-to-all-start.3 = ((bf16[16,2,16384]{2,1,0:T(2,128)(2,1)}), bf16[16,2,16384]{2,1,0:T(2,128)(2,1)}, u32[]{:S(2)}, u32[]{:S(2)}) async-start(bf16[16,2,16384]{2,1,0:T(2,128)(2,1)} %reshape.100), calls=%async_computation.3 | async-start | bytes 2097152 | tf_op jit(solution)/shard_map/all_to_all | solution.py:167
  266.8 18.1 %all-to-all-done.3 = bf16[16,2,16384]{2,1,0:T(2,128)(2,1)} async-done(((bf16[16,2,16384]{2,1,0:T(2,128)(2,1)}), bf16[16,2,16384]{2,1,0:T(2,128)(2,1)}, u32[]{:S(2)}, u32[]{:S(2)}) %all-to-all-start.3) | async-done | bytes 1048608 | tf_op jit(solution)/shard_map/all_to_all | solution.py:167
  284.9 4.5 %reshape.101 = bf16[2048,1,4,64]{3,2,1,0:T(4,128)(2,1)S(1)} reshape(bf16[16,2,16384]{2,1,0:T(2,128)(2,1)} %all-to-all-done.3) | data formatting | bytes 2097152
  289.4 2.0 copy.49
  291.4 1.0 slice.46
  292.4 1.3 slice.47
  293.7 0.1 copy.39
  293.8 0.8 copy.44
  294.6 0.2 copy.40
  294.8 3.1 fusion.13
  297.9 3.8 %fusion.1 = bf16[128,1024]{1,0:T(8,128)(2,1)} fusion(f32[128,1024]{1,0:T(8,128)S(1)} %fusion.13, bf16[1024,1536]{1,0:T(8,128)(2,1)} %collective-permute-done.7, bf16[128,3072]{0,1:T(8,128)(2,1)S(1)} %bitcast.77, s32[]{:T(128)S(6)} %select_n.144), kind=kOutput, calls=%fused_computation.6 | convolution fusion | flops 402915328 | bytes 4325380 | tf_op jit(solution)/shard_map/tc,dc->td/dot_general | solution.py:174
  301.7 1.5 copy.43
  303.2 1.6 copy.45
  (28 shorter events, 0.3 us)
Async XLA Ops:
  7.2 46.4 %all-gather.6.cloned.1.call-start = ((), (), s32[]{:S(2)}) async-start(), calls=%async_computation.5 | async-start | bytes 4456448 | tf_op jit(solution)/shard_map/all_gather | solution.py:100
  7.9 116.1 %all-gather.8.cloned.1.call-start = ((), (), s32[]{:S(2)}) async-start(), calls=%async_computation.6 | async-start | bytes 2359296 | tf_op jit(solution)/shard_map/all_gather | solution.py:116
  57.3 1.2 copy-start.1
  57.3 2.0 copy-start.2
  58.2 182.8 %all-gather.10.cloned.1.call-start = ((), (), s32[]{:S(2)}) async-start(), calls=%async_computation.7 | async-start | bytes 3538944 | tf_op jit(solution)/shard_map/all_gather | solution.py:98
  60.1 10.9 %all-to-all-start = ((bf16[128,16,64]{0,2,1:T(8,128)(2,1)}), bf16[128,16,64]{0,2,1:T(8,128)(2,1)S(1)}, u32[]{:S(2)}, u32[]{:S(2)}) async-start(bf16[128,16,64]{0,2,1:T(8,128)(2,1)} %bitcast.7), calls=%async_computation | async-start | bytes 524288 | tf_op jit(solution)/shard_map/all_to_all | solution.py:120
  72.9 5.6 %copy-start.3 = (s32[128,8]{0,1:T(8,128)S(1)}, s32[128,8]{0,1:T(8,128)}, u32[]{:S(2)}) copy-start(s32[128,8]{0,1:T(8,128)} %param.6) | copy-start | bytes 12292
  72.9 39.1 %all-to-all-start.1 = ((bf16[8,8,128,128]{3,2,1,0:T(8,128)(2,1)}), bf16[8,8,128,128]{3,2,1,0:T(8,128)(2,1)}, u32[]{:S(2)}, u32[]{:S(2)}) async-start(bf16[8,8,128,128]{3,2,1,0:T(8,128)(2,1)} %broadcast_in_dim.6), calls=%async_computation.1 | async-start | bytes 4194304 | tf_op jit(solution)/shard_map/all_to_all | solution.py:118
  124.0 1.6 copy-start
  155.3 77.0 %all-to-all-start.2 = ((bf16[8,8,128,128]{3,2,1,0:T(8,128)(2,1)}), bf16[8,8,128,128]{3,2,1,0:T(8,128)(2,1)S(1)}, u32[]{:S(2)}, u32[]{:S(2)}) async-start(bf16[8,8,128,128]{3,2,1,0:T(8,128)(2,1)} %get-tuple-element.23), calls=%async_computation.2 | async-start | bytes 4194304 | tf_op jit(solution)/shard_map/all_to_all | solution.py:153
  161.6 51.7 %collective-permute-start.6 = (bf16[8,128,128]{2,1,0:T(8,128)(2,1)S(1)}, bf16[8,128,128]{2,1,0:T(8,128)(2,1)}, u32[]{:S(2)}, u32[]{:S(2)}) collective-permute-start(bf16[8,128,128]{2,1,0:T(8,128)(2,1)S(1)} %get-tuple-element.26), channel_id=1, source_target_pairs={{0,7},{1,0},{2,1},{3,2},{4,3},{5,4},{6,5},{7,6},{8,15},{9,8},{10,9... | collective-permute-start | bytes 786440 | tf_op jit(solution)/shard_map/ppermute | solution.py:161
  166.5 46.8 %collective-permute-start.5 = (bf16[8,128,128]{2,1,0:T(8,128)(2,1)S(1)}, bf16[8,128,128]{2,1,0:T(8,128)(2,1)}, u32[]{:S(2)}, u32[]{:S(2)}) collective-permute-start(bf16[8,128,128]{2,1,0:T(8,128)(2,1)S(1)} %get-tuple-element.27), channel_id=1, source_target_pairs={{0,6},{1,7},{2,0},{3,1},{4,2},{5,3},{6,4},{7,5},{8,14},{9,15},{10,... | collective-permute-start | bytes 786440 | tf_op jit(solution)/shard_map/ppermute | solution.py:161
  167.0 46.5 %collective-permute-start.4 = (bf16[8,128,128]{2,1,0:T(8,128)(2,1)}, bf16[8,128,128]{2,1,0:T(8,128)(2,1)}, u32[]{:S(2)}, u32[]{:S(2)}) collective-permute-start(bf16[8,128,128]{2,1,0:T(8,128)(2,1)} %get-tuple-element.28), channel_id=1, source_target_pairs={{0,5},{1,6},{2,7},{3,0},{4,1},{5,2},{6,3},{7,4},{8,13},{9,14},{10,... | collective-permute-start | bytes 786440 | tf_op jit(solution)/shard_map/ppermute | solution.py:161
  167.3 46.2 %collective-permute-start.3 = (bf16[8,128,128]{2,1,0:T(8,128)(2,1)}, bf16[8,128,128]{2,1,0:T(8,128)(2,1)}, u32[]{:S(2)}, u32[]{:S(2)}) collective-permute-start(bf16[8,128,128]{2,1,0:T(8,128)(2,1)} %get-tuple-element.29), channel_id=1, source_target_pairs={{0,4},{1,5},{2,6},{3,7},{4,0},{5,1},{6,2},{7,3},{8,12},{9,13},{10,... | collective-permute-start | bytes 786440 | tf_op jit(solution)/shard_map/ppermute | solution.py:161
  169.7 43.8 %collective-permute-start.2 = (bf16[8,128,128]{2,1,0:T(8,128)(2,1)}, bf16[8,128,128]{2,1,0:T(8,128)(2,1)}, u32[]{:S(2)}, u32[]{:S(2)}) collective-permute-start(bf16[8,128,128]{2,1,0:T(8,128)(2,1)} %get-tuple-element.30), channel_id=1, source_target_pairs={{0,3},{1,4},{2,5},{3,6},{4,7},{5,0},{6,1},{7,2},{8,11},{9,12},{10,... | collective-permute-start | bytes 786440 | tf_op jit(solution)/shard_map/ppermute | solution.py:161
  213.3 10.0 %collective-permute-start.1 = (bf16[8,128,128]{2,1,0:T(8,128)(2,1)}, bf16[8,128,128]{2,1,0:T(8,128)(2,1)}, u32[]{:S(2)}, u32[]{:S(2)}) collective-permute-start(bf16[8,128,128]{2,1,0:T(8,128)(2,1)} %get-tuple-element.31), channel_id=1, source_target_pairs={{0,2},{1,3},{2,4},{3,5},{4,6},{5,7},{6,0},{7,1},{8,10},{9,11},{10,... | collective-permute-start | bytes 786440 | tf_op jit(solution)/shard_map/ppermute | solution.py:161
  213.3 17.1 %collective-permute-start = (bf16[8,128,128]{2,1,0:T(8,128)(2,1)}, bf16[8,128,128]{2,1,0:T(8,128)(2,1)}, u32[]{:S(2)}, u32[]{:S(2)}) collective-permute-start(bf16[8,128,128]{2,1,0:T(8,128)(2,1)} %get-tuple-element.25), channel_id=1, source_target_pairs={{0,1},{1,2},{2,3},{3,4},{4,5},{5,6},{6,7},{7,0},{8,9},{9,10},{10,1... | collective-permute-start | bytes 786440 | tf_op jit(solution)/shard_map/ppermute | solution.py:161
  237.0 13.8 %all-to-all-start.4 = ((f32[8,128,192]{1,2,0:T(8,128)}), f32[8,128,192]{1,2,0:T(8,128)S(1)}, u32[]{:S(2)}, u32[]{:S(2)}) async-start(f32[8,128,192]{1,2,0:T(8,128)} %bitcast.64), calls=%async_computation.4 | async-start | bytes 1572864 | tf_op jit(solution)/shard_map/all_to_all | solution.py:181
  240.9 60.7 %all-gather.12.cloned.1.call-start = ((), (), s32[]{:S(2)}) async-start(), calls=%async_computation.8 | async-start | bytes 1671168 | tf_op jit(solution)/shard_map/all_gather | solution.py:184
  241.0 56.9 %collective-permute-start.7 = (bf16[1024,1536]{1,0:T(8,128)(2,1)}, bf16[1024,1536]{1,0:T(8,128)(2,1)}, u32[]{:S(2)}, u32[]{:S(2)}) collective-permute-start(bf16[1024,1536]{1,0:T(8,128)(2,1)} %all-gather.10.cloned.1.call-done), channel_id=1, source_target_pairs={{0,8},{8,0},{16,24},{24,16},{32,40},{40,32},{48,56},{56,48},{64,72... | collective-permute-start | bytes 9437192 | tf_op jit(solution)/shard_map/ppermute | solution.py:99
  257.9 27.0 %all-to-all-start.3 = ((bf16[16,2,16384]{2,1,0:T(2,128)(2,1)}), bf16[16,2,16384]{2,1,0:T(2,128)(2,1)}, u32[]{:S(2)}, u32[]{:S(2)}) async-start(bf16[16,2,16384]{2,1,0:T(2,128)(2,1)} %reshape.100), calls=%async_computation.3 | async-start | bytes 2097152 | tf_op jit(solution)/shard_map/all_to_all | solution.py:167
Sparse Core Ops, SparseCore 0:
  9.7 43.8 all-gather.5
  58.3 65.5 all-gather.7
  126.3 99.2 all-gather.9
  251.7 39.9 all-gather.11

commit v14 on v11

--- a/solution.py
+++ b/solution.py
@@ -171,9 +171,9 @@
     head_part = head_part.reshape(zero_count, -1, 3 * head_cols)
     head_part = lax.all_to_all(head_part, "zero", split_axis=0, concat_axis=0, tiled=True)
     own_rows = jnp.sum(head_part, axis=0)
-    own_rows = own_rows.reshape(1, -1, 3, head_cols)
-    gathered = lax.all_gather(own_rows, "seq", axis=0, tiled=True)
-    weight_gradient = gathered.transpose(1, 2, 0, 3).reshape(-1, 3 * seq_count * head_cols)
+    own_rows = own_rows.reshape(-1, 3, head_cols)
+    gathered = lax.all_gather(own_rows, "seq", axis=2, tiled=False)
+    weight_gradient = gathered.reshape(-1, 3 * seq_count * head_cols)
     return (attended, token_gradient, weight_gradient)
 
 

time: 287 us -> 287 us (level)
  no operation moved by 1% of the time
where the time goes in v14:
time: 287 us; the launch traced here: 286 us
  waiting for transfers between devices  91.5 us (32%)
  blocking collectives  88.8 us (31%)
  Pallas kernels  25 us (9%)
  starting transfers between devices  24 us (8%)
  local copies, waits for them, and re-layouts  21.1 us (7%)
  matrix products  17.7 us (6%)
  between operations  14 us (5%)
  other arithmetic  4.31 us (2%)
    all_to_all x1, blocking collectives, on_device(): lax.all_to_all(group_sums, 'zero', split_axis=0, concat_axis=0, tiled=True)  60 us
    all_gather x1, blocking collectives, on_device(): head_w = lax.all_gather(head_w, 'zero', axis=0, tiled=True)  28.7 us
    all_to_all x1, waiting for transfers between devices, on_device(): kv_b = lax.all_to_all(kv_b, 'zero', split_axis=0, concat_axis=0, tiled=True)  27.3 us
    pallas_call x1, Pallas kernels, block_attention(): pl.pallas_call(functools.partial(_attn_kernel, scale=scale), grid_spec=gr...  25 us
    all_to_all x1, waiting for transfers between devices, on_device(): lax.all_to_all(outgoing, 'seq', split_axis=0, concat_axis=2, tiled=True)  17.5 us
    all_gather x1, waiting for transfers between devices, on_device(): group_tokens = lax.all_gather(tokens, 'seq', axis=0, tiled=True)  15.3 us
    all_gather x1, waiting for transfers between devices, on_device(): kv_a = lax.all_gather(kv_local[:split], 'zero', axis=0, tiled=True)  12.3 us
    unnamed x14, local copies, waits for them, and re-layouts  10.7 us
  transfers between devices with their start and end apart: 9, of which 7 were waited for; matrix products, arithmetic and copies ran while one was open for 12% of the time, Pallas kernels for 9%

profile of v14, /device:TPU:1, one launch (start us, length us, event | category | flops | bytes accessed | tf_op | source)
XLA Modules:
  0.0 286.5 jit_solution(10311000212920682627)
XLA Ops:
  7.2 0.0 all-gather.6.cloned.1.call-start
  7.2 0.7 all-gather.6.cloned.1.call-update
  7.9 0.0 all-gather.8.cloned.1.call-start
  7.9 1.5 copy.26
  9.5 28.7 %all-gather = bf16[1024,3,1,64]{0,3,2,1:T(8,128)(2,1)S(1)} all-gather(bf16[128,3,1,64]{0,3,2,1:T(8,128)(2,1)S(1)} %constant_dynamic-slice_fusion.1), channel_id=2, replica_groups=mesh['seq'=16,'zero'=8] {'zero'}, dimensions={0}, use_global_device_ids=true | all-gather | bytes 442368 | tf_op jit(solution)/shard_map/all_gather | solution.py:103
  38.2 15.3 %all-gather.6.cloned.1.call-done = bf16[2048,1024]{1,0:T(8,128)(2,1)} async-done(((bf16[128,1024]{1,0:T(8,128)(2,1)}), bf16[2048,1024]{1,0:T(8,128)(2,1)}) %all-gather.6.cloned.1.call-update) | async-done | bytes 4194320 | tf_op jit(solution)/shard_map/all_gather | solution.py:100
  53.6 0.0 copy-start.2
  53.6 3.7 %fusion = bf16[2048,128]{0,1:T(8,128)(2,1)S(1)} fusion(bf16[1024,128]{0,1:T(8,128)(2,1)S(1)} %bitcast.62, bf16[2048,1024]{1,0:T(8,128)(2,1)} %all-gather.6.cloned.1.call-done), kind=kOutput, calls=%fused_computation.2 | convolution fusion | flops 537133056 | bytes 4980736 | tf_op jit(solution)/shard_map/td,dc->tc/dot_general | solution.py:104
  57.3 0.8 copy.40
  58.2 0.0 all-gather.8.cloned.1.call-update
  58.2 0.0 copy-done.2
  58.2 0.8 copy.28
  59.1 3.6 %all-to-all-start = ((bf16[128,16,64]{0,2,1:T(8,128)(2,1)}), bf16[128,16,64]{0,2,1:T(8,128)(2,1)S(1)}, u32[]{:S(2)}, u32[]{:S(2)}) async-start(bf16[128,16,64]{0,2,1:T(8,128)(2,1)} %bitcast.7), calls=%async_computation | async-start | bytes 524288 | tf_op jit(solution)/shard_map/all_to_all | solution.py:120
  62.7 0.2 copy.41
  62.8 7.2 %all-to-all-done = bf16[128,16,64]{0,2,1:T(8,128)(2,1)S(1)} async-done(((bf16[128,16,64]{0,2,1:T(8,128)(2,1)}), bf16[128,16,64]{0,2,1:T(8,128)(2,1)S(1)}, u32[]{:S(2)}, u32[]{:S(2)}) %all-to-all-start) | async-done | bytes 262176 | tf_op jit(solution)/shard_map/all_to_all | solution.py:120
  70.0 0.0 copy-start.1
  70.0 1.9 broadcast_in_dim.6
  71.9 0.0 copy-start.3
  71.9 5.4 %all-to-all-start.1 = ((bf16[8,8,128,128]{3,2,1,0:T(8,128)(2,1)}), bf16[8,8,128,128]{3,2,1,0:T(8,128)(2,1)}, u32[]{:S(2)}, u32[]{:S(2)}) async-start(bf16[8,8,128,128]{3,2,1,0:T(8,128)(2,1)} %broadcast_in_dim.6), calls=%async_computation.1 | async-start | bytes 4194304 | tf_op jit(solution)/shard_map/all_to_all | solution.py:118
  77.3 0.0 all-gather.10.cloned.1.call-start
  77.4 0.0 copy-done.1
  77.4 0.8 constant_dynamic-slice_fusion
  78.2 0.0 all-gather.10.cloned.1.call-update
  78.2 0.0 copy-done.3
  78.2 0.1 copy.25
  78.4 0.6 gather_fusion
  79.0 3.6 %convolution_convert_fusion.1 = bf16[2048,64]{0,1:T(8,128)(2,1)S(1)} fusion(bf16[2048,1024]{1,0:T(8,128)(2,1)} %all-gather.6.cloned.1.call-done, bf16[1024,3,64]{0,2,1:T(8,128)(2,1)S(1)} %bitcast.60), kind=kOutput, calls=%fused_computation.3 | convolution fusion | flops 268566528 | bytes 4587520 | tf_op jit(solution)/shard_map/td,dc->tc/dot_general | solution.py:111
  82.5 0.3 copy.27
  82.8 0.3 copy.29
  83.1 27.3 %all-to-all-done.1 = bf16[8,8,128,128]{3,2,1,0:T(8,128)(2,1)} async-done(((bf16[8,8,128,128]{3,2,1,0:T(8,128)(2,1)}), bf16[8,8,128,128]{3,2,1,0:T(8,128)(2,1)}, u32[]{:S(2)}, u32[]{:S(2)}) %all-to-all-start.1) | async-done | bytes 2097184 | tf_op jit(solution)/shard_map/all_to_all | solution.py:118
  110.5 12.3 %all-gather.8.cloned.1.call-done.ka_ref = bf16[64,128,128]{2,1,0:T(8,128)(2,1)} async-done(((bf16[8,128,128]{2,1,0:T(8,128)(2,1)}), bf16[64,128,128]{2,1,0:T(8,128)(2,1)}) %all-gather.8.cloned.1.call-update) | async-done | bytes 2097168 | tf_op jit(solution)/shard_map/all_gather | solution.py:116
  122.8 0.0 copy-start
  122.8 1.6 copy-done
  124.4 25.0 %shard_map.67 = (bf16[16,128,64]{2,1,0:T(8,128)(2,1)S(1)}, bf16[16,128,64]{2,1,0:T(8,128)(2,1)S(1)}, bf16[128,128,128]{2,1,0:T(8,128)(2,1)}) custom-call(s32[16,8]{1,0:T(8,128)S(1)} %get-tuple-element.22.slots_ref, s32[16,8]{1,0:T(8,128)S(1)} %add_select_fusion.4.a_ids_ref, s32[16,8]{1,0:T(8,128)S(1)} %get-tuple-element.21.b_ids_ref, ...), custom_call_target="tpu_custom_call" | custom-call | tf_op jit(solution)/shard_map/pallas_call | solution.py:72
  149.4 60.0 %all_to_all.48 = bf16[8,2048,128]{2,1,0:T(8,128)(2,1)} all-to-all(bf16[8,2048,128]{2,1,0:T(8,128)(2,1)} %bitcast.55), channel_id=1, replica_groups=mesh['seq'=16,'zero'=8] {'zero'}, dimensions={0} | all-to-all | bytes 8388608 | tf_op jit(solution)/shard_map/all_to_all | solution.py:153
  209.4 3.1 %reduce_sum.21 = bf16[2048,128]{1,0:T(8,128)(2,1)S(1)} reduce(bf16[8,2048,128]{2,1,0:T(8,128)(2,1)} %all_to_all.48, bf16[]{:T(256)} %constant.123.clone.1), dimensions={0}, to_apply=%region_0.1 | reduce | flops 1835008 | bytes 4718594 | tf_op jit(solution)/shard_map/reduce_sum | solution.py:154
  212.5 3.6 %convolution_bitcast_fusion = f32[24,8,8,128]{3,2,1,0:T(8,128)S(1)} fusion(bf16[2048,1024]{1,0:T(8,128)(2,1)} %all-gather.6.cloned.1.call-done, bf16[2048,128]{1,0:T(8,128)(2,1)S(1)} %reduce_sum.21, bf16[2048,64]{1,0:T(8,128)(2,1)S(1)} %bitcast.48), kind=kOutput, calls=%fused_computation.4 | convolution fusion | flops 806879232 | bytes 5767168 | tf_op jit(solution)/shard_map/td,tc->dc/dot_general | solution.py:168
  216.1 0.9 copy.45
  217.0 8.1 %all-to-all-start.4 = ((f32[8,128,192]{1,2,0:T(8,128)}), f32[8,128,192]{1,2,0:T(8,128)S(1)}, u32[]{:S(2)}, u32[]{:S(2)}) async-start(f32[8,128,192]{1,2,0:T(8,128)} %bitcast.44), calls=%async_computation.4 | async-start | bytes 1572864 | tf_op jit(solution)/shard_map/all_to_all | solution.py:172
  225.1 0.0 all-gather.12.cloned.1.call-start
  225.2 3.9 %all-gather.10.cloned.1.call-done = bf16[1024,1536]{1,0:T(8,128)(2,1)} async-done(((bf16[128,1536]{1,0:T(8,128)(2,1)}), bf16[1024,1536]{1,0:T(8,128)(2,1)}) %all-gather.10.cloned.1.call-update) | async-done | bytes 3145744 | tf_op jit(solution)/shard_map/all_gather | solution.py:98
  229.1 1.0 collective-permute-start
  230.1 7.2 %all-to-all-done.4 = f32[8,128,192]{1,2,0:T(8,128)S(1)} async-done(((f32[8,128,192]{1,2,0:T(8,128)}), f32[8,128,192]{1,2,0:T(8,128)S(1)}, u32[]{:S(2)}, u32[]{:S(2)}) %all-to-all-start.4) | async-done | bytes 786464 | tf_op jit(solution)/shard_map/all_to_all | solution.py:172
  237.3 0.7 reduce_sum.22
  238.0 0.0 all-gather.12.cloned.1.call-update
  238.0 0.5 pad_maximum_fusion
  238.5 0.6 copy.32
  239.1 1.4 copy.33
  240.5 2.2 reshape.90
  242.8 5.8 %all-to-all-start.3 = ((bf16[16,2,16384]{2,1,0:T(2,128)(2,1)}), bf16[16,2,16384]{2,1,0:T(2,128)(2,1)S(1)}, u32[]{:S(2)}, u32[]{:S(2)}) async-start(bf16[16,2,16384]{2,1,0:T(2,128)(2,1)} %reshape.90), calls=%async_computation.3 | async-start | bytes 2097152 | tf_op jit(solution)/shard_map/all_to_all | solution.py:158
  248.5 17.5 %all-to-all-done.3 = bf16[16,2,16384]{2,1,0:T(2,128)(2,1)S(1)} async-done(((bf16[16,2,16384]{2,1,0:T(2,128)(2,1)}), bf16[16,2,16384]{2,1,0:T(2,128)(2,1)S(1)}, u32[]{:S(2)}, u32[]{:S(2)}) %all-to-all-start.3) | async-done | bytes 1048608 | tf_op jit(solution)/shard_map/all_to_all | solution.py:158
  266.0 1.3 reshape.91
  267.4 1.4 copy.42
  268.8 0.1 slice.37
  269.0 0.2 copy.36
  269.2 0.1 copy.35
  269.2 0.9 copy.38
  270.1 3.1 %fusion.6 = f32[128,1024]{1,0:T(8,128)S(1)} fusion(bf16[1024,1536]{1,0:T(8,128)(2,1)} %all-gather.10.cloned.1.call-done, bf16[128,3072]{0,1:T(8,128)(2,1)S(1)} %bitcast.56, s32[]{:T(128)S(6)} %select_n.75), kind=kOutput, calls=%fused_computation.13 | convolution fusion | flops 402653184 | bytes 4063236 | tf_op jit(solution)/shard_map/tc,dc->td/dot_general | solution.py:164
  273.2 0.0 collective-permute-done
  273.2 3.8 %fusion.1 = bf16[128,1024]{1,0:T(8,128)(2,1)} fusion(f32[128,1024]{1,0:T(8,128)S(1)} %fusion.6, bf16[1024,1536]{1,0:T(8,128)(2,1)} %collective-permute-done, bf16[128,3072]{0,1:T(8,128)(2,1)S(1)} %bitcast.57, s32[]{:T(128)S(6)} %select_n.76), kind=kOutput, calls=%fused_computation.6 | convolution fusion | flops 402915328 | bytes 4325380 | tf_op jit(solution)/shard_map/tc,dc->td/dot_general | solution.py:165
  276.9 0.0 all-gather.12.cloned.1.call-done
  276.9 3.0 %copy.39 = f32[128,3072]{1,0:T(8,128)} copy(f32[128,3072]{0,1:T(8,128)} %bitcast.58) | data formatting | bytes 3145728
  (8 shorter events, 0.1 us)
Async XLA Ops:
  7.2 46.4 %all-gather.6.cloned.1.call-start = ((), (), s32[]{:S(2)}) async-start(), calls=%async_computation.5 | async-start | bytes 4456448 | tf_op jit(solution)/shard_map/all_gather | solution.py:100
  7.9 114.9 %all-gather.8.cloned.1.call-start = ((), (), s32[]{:S(2)}) async-start(), calls=%async_computation.6 | async-start | bytes 2359296 | tf_op jit(solution)/shard_map/all_gather | solution.py:116
  53.6 4.7 %copy-start.2 = (bf16[128,1024]{1,0:T(8,128)(2,1)S(1)}, bf16[128,1024]{1,0:T(8,128)(2,1)}, u32[]{:S(2)}) copy-start(bf16[128,1024]{1,0:T(8,128)(2,1)} %param.7) | copy-start | bytes 786436
  59.1 11.0 %all-to-all-start = ((bf16[128,16,64]{0,2,1:T(8,128)(2,1)}), bf16[128,16,64]{0,2,1:T(8,128)(2,1)S(1)}, u32[]{:S(2)}, u32[]{:S(2)}) async-start(bf16[128,16,64]{0,2,1:T(8,128)(2,1)} %bitcast.7), calls=%async_computation | async-start | bytes 524288 | tf_op jit(solution)/shard_map/all_to_all | solution.py:120
  70.0 7.3 %copy-start.1 = (bf16[128,3072]{1,0:T(8,128)(2,1)S(1)}, bf16[128,3072]{1,0:T(8,128)(2,1)}, u32[]{:S(2)}) copy-start(bf16[128,3072]{1,0:T(8,128)(2,1)} %param.5) | copy-start | bytes 2359300
  71.9 6.3 %copy-start.3 = (s32[128,8]{0,1:T(8,128)S(1)}, s32[128,8]{0,1:T(8,128)}, u32[]{:S(2)}) copy-start(s32[128,8]{0,1:T(8,128)} %param.6) | copy-start | bytes 12292
  71.9 38.6 %all-to-all-start.1 = ((bf16[8,8,128,128]{3,2,1,0:T(8,128)(2,1)}), bf16[8,8,128,128]{3,2,1,0:T(8,128)(2,1)}, u32[]{:S(2)}, u32[]{:S(2)}) async-start(bf16[8,8,128,128]{3,2,1,0:T(8,128)(2,1)} %broadcast_in_dim.6), calls=%async_computation.1 | async-start | bytes 4194304 | tf_op jit(solution)/shard_map/all_to_all | solution.py:118
  77.3 151.8 %all-gather.10.cloned.1.call-start = ((), (), s32[]{:S(2)}) async-start(), calls=%async_computation.7 | async-start | bytes 3538944 | tf_op jit(solution)/shard_map/all_gather | solution.py:98
  122.8 1.6 copy-start
  217.0 20.2 %all-to-all-start.4 = ((f32[8,128,192]{1,2,0:T(8,128)}), f32[8,128,192]{1,2,0:T(8,128)S(1)}, u32[]{:S(2)}, u32[]{:S(2)}) async-start(f32[8,128,192]{1,2,0:T(8,128)} %bitcast.44), calls=%async_computation.4 | async-start | bytes 1572864 | tf_op jit(solution)/shard_map/all_to_all | solution.py:172
  225.1 51.8 %all-gather.12.cloned.1.call-start = ((), (), s32[]{:S(2)}) async-start(), calls=%async_computation.8 | async-start | bytes 1671168 | tf_op jit(solution)/shard_map/all_gather | solution.py:175
  229.1 44.0 %collective-permute-start = (bf16[1024,1536]{1,0:T(8,128)(2,1)}, bf16[1024,1536]{1,0:T(8,128)(2,1)}, u32[]{:S(2)}, u32[]{:S(2)}) collective-permute-start(bf16[1024,1536]{1,0:T(8,128)(2,1)} %all-gather.10.cloned.1.call-done), channel_id=1, source_target_pairs={{0,8},{8,0},{16,24},{24,16},{32,40},{40,32},{48,56},{56,48},{64,72... | collective-permute-start | bytes 9437192 | tf_op jit(solution)/shard_map/ppermute | solution.py:99
  242.8 23.3 %all-to-all-start.3 = ((bf16[16,2,16384]{2,1,0:T(2,128)(2,1)}), bf16[16,2,16384]{2,1,0:T(2,128)(2,1)S(1)}, u32[]{:S(2)}, u32[]{:S(2)}) async-start(bf16[16,2,16384]{2,1,0:T(2,128)(2,1)} %reshape.90), calls=%async_computation.3 | async-start | bytes 2097152 | tf_op jit(solution)/shard_map/all_to_all | solution.py:158
Sparse Core Ops, SparseCore 0:
  9.7 43.8 all-gather.5
  58.3 64.4 all-gather.7
  125.1 103.9 all-gather.9
  238.1 38.1 all-gather.11

commit v15 on v11

--- a/solution.py
+++ b/solution.py
@@ -30,10 +30,10 @@
     vals = jnp.concatenate([b[:, HEAD:] for b in blocks], axis=0)
     nt = (((1,), (1,)), ((), ()))
     tn = (((0,), (0,)), ((), ()))
-    scores = lax.dot_general(q, keys, nt, preferred_element_type=jnp.float32) * scale
+    scores = lax.dot_general(q * scale, keys, nt, preferred_element_type=jnp.float32)
     row_max = jnp.max(scores, axis=-1, keepdims=True)
     exponent = jnp.exp(scores - row_max)
-    prob_full = exponent / jnp.sum(exponent, axis=-1, keepdims=True)
+    prob_full = exponent * (1.0 / jnp.sum(exponent, axis=-1, keepdims=True))
     prob_low = prob_full.astype(jnp.bfloat16)
     out_ref[0] = jnp.dot(prob_low, vals, preferred_element_type=jnp.float32).astype(out_ref.dtype)
     prob_grad = lax.dot_general(up, vals, nt, preferred_element_type=jnp.float32)

time: 287 us -> 288 us (level)
  no operation moved by 1% of the time
where the time goes in v15:
time: 288 us; the launch traced here: 287 us
  waiting for transfers between devices  92 us (32%)
  blocking collectives  88 us (31%)
  Pallas kernels  24.8 us (9%)
  starting transfers between devices  24.7 us (9%)
  local copies, waits for them, and re-layouts  21.2 us (7%)
  matrix products  17.7 us (6%)
  between operations  14 us (5%)
  other arithmetic  4.28 us (1%)
    all_to_all x1, blocking collectives, on_device(): lax.all_to_all(group_sums, 'zero', split_axis=0, concat_axis=0, tiled=True)  59.2 us
    all_gather x1, blocking collectives, on_device(): head_w = lax.all_gather(head_w, 'zero', axis=0, tiled=True)  28.7 us
    all_to_all x1, waiting for transfers between devices, on_device(): kv_b = lax.all_to_all(kv_b, 'zero', split_axis=0, concat_axis=0, tiled=True)  27.3 us
    pallas_call x1, Pallas kernels, block_attention(): pl.pallas_call(functools.partial(_attn_kernel, scale=scale), grid_spec=gr...  24.8 us
    all_to_all x1, waiting for transfers between devices, on_device(): lax.all_to_all(outgoing, 'seq', split_axis=0, concat_axis=2, tiled=True)  18.1 us
    all_gather x1, waiting for transfers between devices, on_device(): group_tokens = lax.all_gather(tokens, 'seq', axis=0, tiled=True)  15.3 us
    all_gather x1, waiting for transfers between devices, on_device(): kv_a = lax.all_gather(kv_local[:split], 'zero', axis=0, tiled=True)  12.3 us
    unnamed x14, local copies, waits for them, and re-layouts  9.25 us
  transfers between devices with their start and end apart: 9, of which 7 were waited for; matrix products, arithmetic and copies ran while one was open for 12% of the time, Pallas kernels for 9%

profile of v15, /device:TPU:1, one launch (start us, length us, event | category | flops | bytes accessed | tf_op | source)
XLA Modules:
  0.0 286.8 jit_solution(3538689673759778212)
XLA Ops:
  7.2 0.0 all-gather.6.cloned.1.call-start
  7.2 0.7 all-gather.6.cloned.1.call-update
  7.9 0.0 all-gather.8.cloned.1.call-start
  7.9 1.5 copy.27
  9.5 28.7 %all-gather = bf16[1024,3,1,64]{0,3,2,1:T(8,128)(2,1)S(1)} all-gather(bf16[128,3,1,64]{0,3,2,1:T(8,128)(2,1)S(1)} %constant_dynamic-slice_fusion.1), channel_id=2, replica_groups=mesh['seq'=16,'zero'=8] {'zero'}, dimensions={0}, use_global_device_ids=true | all-gather | bytes 442368 | tf_op jit(solution)/shard_map/all_gather | solution.py:103
  38.2 15.3 %all-gather.6.cloned.1.call-done = bf16[2048,1024]{1,0:T(8,128)(2,1)} async-done(((bf16[128,1024]{1,0:T(8,128)(2,1)}), bf16[2048,1024]{1,0:T(8,128)(2,1)}) %all-gather.6.cloned.1.call-update) | async-done | bytes 4194320 | tf_op jit(solution)/shard_map/all_gather | solution.py:100
  53.6 0.0 copy-start.2
  53.6 3.7 %fusion = bf16[2048,128]{0,1:T(8,128)(2,1)S(1)} fusion(bf16[1024,128]{0,1:T(8,128)(2,1)S(1)} %bitcast.64, bf16[2048,1024]{1,0:T(8,128)(2,1)} %all-gather.6.cloned.1.call-done), kind=kOutput, calls=%fused_computation.2 | convolution fusion | flops 537133056 | bytes 4980736 | tf_op jit(solution)/shard_map/td,dc->tc/dot_general | solution.py:104
  57.3 0.8 copy.42
  58.2 0.0 all-gather.8.cloned.1.call-update
  58.2 0.0 copy-done.2
  58.2 0.8 copy.29
  59.1 3.6 %all-to-all-start = ((bf16[128,16,64]{0,2,1:T(8,128)(2,1)}), bf16[128,16,64]{0,2,1:T(8,128)(2,1)S(1)}, u32[]{:S(2)}, u32[]{:S(2)}) async-start(bf16[128,16,64]{0,2,1:T(8,128)(2,1)} %bitcast.7), calls=%async_computation | async-start | bytes 524288 | tf_op jit(solution)/shard_map/all_to_all | solution.py:120
  62.7 0.2 copy.43
  62.8 7.2 %all-to-all-done = bf16[128,16,64]{0,2,1:T(8,128)(2,1)S(1)} async-done(((bf16[128,16,64]{0,2,1:T(8,128)(2,1)}), bf16[128,16,64]{0,2,1:T(8,128)(2,1)S(1)}, u32[]{:S(2)}, u32[]{:S(2)}) %all-to-all-start) | async-done | bytes 262176 | tf_op jit(solution)/shard_map/all_to_all | solution.py:120
  70.0 0.0 copy-start.1
  70.0 1.9 broadcast_in_dim.6
  71.9 0.0 copy-start.3
  71.9 5.4 %all-to-all-start.1 = ((bf16[8,8,128,128]{3,2,1,0:T(8,128)(2,1)}), bf16[8,8,128,128]{3,2,1,0:T(8,128)(2,1)}, u32[]{:S(2)}, u32[]{:S(2)}) async-start(bf16[8,8,128,128]{3,2,1,0:T(8,128)(2,1)} %broadcast_in_dim.6), calls=%async_computation.1 | async-start | bytes 4194304 | tf_op jit(solution)/shard_map/all_to_all | solution.py:118
  77.3 0.0 all-gather.10.cloned.1.call-start
  77.4 0.0 copy-done.1
  77.4 0.8 constant_dynamic-slice_fusion
  78.2 0.0 all-gather.10.cloned.1.call-update
  78.2 0.0 copy-done.3
  78.2 0.1 copy.26
  78.4 0.6 gather_fusion
  79.0 3.6 %convolution_convert_fusion.1 = bf16[2048,64]{0,1:T(8,128)(2,1)S(1)} fusion(bf16[2048,1024]{1,0:T(8,128)(2,1)} %all-gather.6.cloned.1.call-done, bf16[1024,3,64]{0,2,1:T(8,128)(2,1)S(1)} %bitcast.62), kind=kOutput, calls=%fused_computation.3 | convolution fusion | flops 268566528 | bytes 4587520 | tf_op jit(solution)/shard_map/td,dc->tc/dot_general | solution.py:111
  82.5 0.3 copy.28
  82.8 0.3 copy.30
  83.1 27.3 %all-to-all-done.1 = bf16[8,8,128,128]{3,2,1,0:T(8,128)(2,1)} async-done(((bf16[8,8,128,128]{3,2,1,0:T(8,128)(2,1)}), bf16[8,8,128,128]{3,2,1,0:T(8,128)(2,1)}, u32[]{:S(2)}, u32[]{:S(2)}) %all-to-all-start.1) | async-done | bytes 2097184 | tf_op jit(solution)/shard_map/all_to_all | solution.py:118
  110.5 12.3 %all-gather.8.cloned.1.call-done.ka_ref = bf16[64,128,128]{2,1,0:T(8,128)(2,1)} async-done(((bf16[8,128,128]{2,1,0:T(8,128)(2,1)}), bf16[64,128,128]{2,1,0:T(8,128)(2,1)}) %all-gather.8.cloned.1.call-update) | async-done | bytes 2097168 | tf_op jit(solution)/shard_map/all_gather | solution.py:116
  122.8 0.0 copy-start
  122.8 1.6 copy-done
  124.4 24.8 %shard_map.67 = (bf16[16,128,64]{2,1,0:T(8,128)(2,1)S(1)}, bf16[16,128,64]{2,1,0:T(8,128)(2,1)S(1)}, bf16[128,128,128]{2,1,0:T(8,128)(2,1)}) custom-call(s32[16,8]{1,0:T(8,128)S(1)} %get-tuple-element.22.slots_ref, s32[16,8]{1,0:T(8,128)S(1)} %add_select_fusion.4.a_ids_ref, s32[16,8]{1,0:T(8,128)S(1)} %get-tuple-element.21.b_ids_ref, ...), custom_call_target="tpu_custom_call" | custom-call | tf_op jit(solution)/shard_map/pallas_call | solution.py:72
  149.2 59.2 %all_to_all.48 = bf16[8,2048,128]{2,1,0:T(8,128)(2,1)} all-to-all(bf16[8,2048,128]{2,1,0:T(8,128)(2,1)} %bitcast.58), channel_id=1, replica_groups=mesh['seq'=16,'zero'=8] {'zero'}, dimensions={0} | all-to-all | bytes 8388608 | tf_op jit(solution)/shard_map/all_to_all | solution.py:153
  208.4 3.1 %reduce_sum.21 = bf16[2048,128]{1,0:T(8,128)(2,1)S(1)} reduce(bf16[8,2048,128]{2,1,0:T(8,128)(2,1)} %all_to_all.48, bf16[]{:T(256)} %constant.123.clone.1), dimensions={0}, to_apply=%region_0.1 | reduce | flops 1835008 | bytes 4718594 | tf_op jit(solution)/shard_map/reduce_sum | solution.py:154
  211.5 3.6 %convolution_bitcast_fusion = f32[24,8,8,128]{3,2,1,0:T(8,128)S(1)} fusion(bf16[2048,1024]{1,0:T(8,128)(2,1)} %all-gather.6.cloned.1.call-done, bf16[2048,128]{1,0:T(8,128)(2,1)S(1)} %reduce_sum.21, bf16[2048,64]{1,0:T(8,128)(2,1)S(1)} %bitcast.50), kind=kOutput, calls=%fused_computation.4 | convolution fusion | flops 806879232 | bytes 5767168 | tf_op jit(solution)/shard_map/td,tc->dc/dot_general | solution.py:168
  215.1 0.9 copy.47
  216.0 8.7 %all-to-all-start.4 = ((f32[8,128,192]{1,2,0:T(8,128)}), f32[8,128,192]{1,2,0:T(8,128)S(1)}, u32[]{:S(2)}, u32[]{:S(2)}) async-start(f32[8,128,192]{1,2,0:T(8,128)} %bitcast.46), calls=%async_computation.4 | async-start | bytes 1572864 | tf_op jit(solution)/shard_map/all_to_all | solution.py:172
  224.7 0.0 all-gather.12.cloned.1.call-start
  224.8 4.1 %all-gather.10.cloned.1.call-done = bf16[1024,1536]{1,0:T(8,128)(2,1)} async-done(((bf16[128,1536]{1,0:T(8,128)(2,1)}), bf16[1024,1536]{1,0:T(8,128)(2,1)}) %all-gather.10.cloned.1.call-update) | async-done | bytes 3145744 | tf_op jit(solution)/shard_map/all_gather | solution.py:98
  228.9 1.1 collective-permute-start
  230.0 6.9 %all-to-all-done.4 = f32[8,128,192]{1,2,0:T(8,128)S(1)} async-done(((f32[8,128,192]{1,2,0:T(8,128)}), f32[8,128,192]{1,2,0:T(8,128)S(1)}, u32[]{:S(2)}, u32[]{:S(2)}) %all-to-all-start.4) | async-done | bytes 786464 | tf_op jit(solution)/shard_map/all_to_all | solution.py:172
  236.9 0.7 reduce_sum.22
  237.6 0.0 all-gather.12.cloned.1.call-update
  237.6 0.5 pad_maximum_fusion
  238.1 0.6 copy.33
  238.8 1.4 copy.34
  240.2 2.2 reshape.94
  242.4 5.7 %all-to-all-start.3 = ((bf16[16,2,16384]{2,1,0:T(2,128)(2,1)}), bf16[16,2,16384]{2,1,0:T(2,128)(2,1)S(1)}, u32[]{:S(2)}, u32[]{:S(2)}) async-start(bf16[16,2,16384]{2,1,0:T(2,128)(2,1)} %reshape.94), calls=%async_computation.3 | async-start | bytes 2097152 | tf_op jit(solution)/shard_map/all_to_all | solution.py:158
  248.1 18.1 %all-to-all-done.3 = bf16[16,2,16384]{2,1,0:T(2,128)(2,1)S(1)} async-done(((bf16[16,2,16384]{2,1,0:T(2,128)(2,1)}), bf16[16,2,16384]{2,1,0:T(2,128)(2,1)S(1)}, u32[]{:S(2)}, u32[]{:S(2)}) %all-to-all-start.3) | async-done | bytes 1048608 | tf_op jit(solution)/shard_map/all_to_all | solution.py:158
  266.2 1.3 reshape.95
  267.6 1.4 copy.44
  269.0 0.1 slice.37
  269.1 0.2 copy.37
  269.3 0.1 copy.36
  269.4 0.9 copy.40
  270.3 3.1 %fusion.6 = f32[128,1024]{1,0:T(8,128)S(1)} fusion(bf16[1024,1536]{1,0:T(8,128)(2,1)} %all-gather.10.cloned.1.call-done, bf16[128,3072]{0,1:T(8,128)(2,1)S(1)} %bitcast.59, s32[]{:T(128)S(6)} %select_n.75), kind=kOutput, calls=%fused_computation.13 | convolution fusion | flops 402653184 | bytes 4063236 | tf_op jit(solution)/shard_map/tc,dc->td/dot_general | solution.py:164
  273.3 0.0 collective-permute-done
  273.3 3.8 %fusion.1 = bf16[128,1024]{1,0:T(8,128)(2,1)} fusion(f32[128,1024]{1,0:T(8,128)S(1)} %fusion.6, bf16[1024,1536]{1,0:T(8,128)(2,1)} %collective-permute-done, bf16[128,3072]{0,1:T(8,128)(2,1)S(1)} %bitcast.60, s32[]{:T(128)S(6)} %select_n.76), kind=kOutput, calls=%fused_computation.6 | convolution fusion | flops 402915328 | bytes 4325380 | tf_op jit(solution)/shard_map/tc,dc->td/dot_general | solution.py:165
  277.1 0.0 all-gather.12.cloned.1.call-done
  277.1 1.5 copy.39
  278.6 1.6 copy.41
  (8 shorter events, 0.1 us)
Async XLA Ops:
  7.2 46.4 %all-gather.6.cloned.1.call-start = ((), (), s32[]{:S(2)}) async-start(), calls=%async_computation.5 | async-start | bytes 4456448 | tf_op jit(solution)/shard_map/all_gather | solution.py:100
  7.9 114.9 %all-gather.8.cloned.1.call-start = ((), (), s32[]{:S(2)}) async-start(), calls=%async_computation.6 | async-start | bytes 2359296 | tf_op jit(solution)/shard_map/all_gather | solution.py:116
  53.6 4.7 %copy-start.2 = (bf16[128,1024]{1,0:T(8,128)(2,1)S(1)}, bf16[128,1024]{1,0:T(8,128)(2,1)}, u32[]{:S(2)}) copy-start(bf16[128,1024]{1,0:T(8,128)(2,1)} %param.7) | copy-start | bytes 786436
  59.1 11.0 %all-to-all-start = ((bf16[128,16,64]{0,2,1:T(8,128)(2,1)}), bf16[128,16,64]{0,2,1:T(8,128)(2,1)S(1)}, u32[]{:S(2)}, u32[]{:S(2)}) async-start(bf16[128,16,64]{0,2,1:T(8,128)(2,1)} %bitcast.7), calls=%async_computation | async-start | bytes 524288 | tf_op jit(solution)/shard_map/all_to_all | solution.py:120
  70.0 7.3 %copy-start.1 = (bf16[128,3072]{1,0:T(8,128)(2,1)S(1)}, bf16[128,3072]{1,0:T(8,128)(2,1)}, u32[]{:S(2)}) copy-start(bf16[128,3072]{1,0:T(8,128)(2,1)} %param.5) | copy-start | bytes 2359300
  71.9 6.3 %copy-start.3 = (s32[128,8]{0,1:T(8,128)S(1)}, s32[128,8]{0,1:T(8,128)}, u32[]{:S(2)}) copy-start(s32[128,8]{0,1:T(8,128)} %param.6) | copy-start | bytes 12292
  71.9 38.6 %all-to-all-start.1 = ((bf16[8,8,128,128]{3,2,1,0:T(8,128)(2,1)}), bf16[8,8,128,128]{3,2,1,0:T(8,128)(2,1)}, u32[]{:S(2)}, u32[]{:S(2)}) async-start(bf16[8,8,128,128]{3,2,1,0:T(8,128)(2,1)} %broadcast_in_dim.6), calls=%async_computation.1 | async-start | bytes 4194304 | tf_op jit(solution)/shard_map/all_to_all | solution.py:118
  77.3 151.6 %all-gather.10.cloned.1.call-start = ((), (), s32[]{:S(2)}) async-start(), calls=%async_computation.7 | async-start | bytes 3538944 | tf_op jit(solution)/shard_map/all_gather | solution.py:98
  122.8 1.6 copy-start
  216.0 20.9 %all-to-all-start.4 = ((f32[8,128,192]{1,2,0:T(8,128)}), f32[8,128,192]{1,2,0:T(8,128)S(1)}, u32[]{:S(2)}, u32[]{:S(2)}) async-start(f32[8,128,192]{1,2,0:T(8,128)} %bitcast.46), calls=%async_computation.4 | async-start | bytes 1572864 | tf_op jit(solution)/shard_map/all_to_all | solution.py:172
  224.7 52.4 %all-gather.12.cloned.1.call-start = ((), (), s32[]{:S(2)}) async-start(), calls=%async_computation.8 | async-start | bytes 1671168 | tf_op jit(solution)/shard_map/all_gather | solution.py:175
  228.9 44.4 %collective-permute-start = (bf16[1024,1536]{1,0:T(8,128)(2,1)}, bf16[1024,1536]{1,0:T(8,128)(2,1)}, u32[]{:S(2)}, u32[]{:S(2)}) collective-permute-start(bf16[1024,1536]{1,0:T(8,128)(2,1)} %all-gather.10.cloned.1.call-done), channel_id=1, source_target_pairs={{0,8},{8,0},{16,24},{24,16},{32,40},{40,32},{48,56},{56,48},{64,72... | collective-permute-start | bytes 9437192 | tf_op jit(solution)/shard_map/ppermute | solution.py:99
  242.4 23.8 %all-to-all-start.3 = ((bf16[16,2,16384]{2,1,0:T(2,128)(2,1)}), bf16[16,2,16384]{2,1,0:T(2,128)(2,1)S(1)}, u32[]{:S(2)}, u32[]{:S(2)}) async-start(bf16[16,2,16384]{2,1,0:T(2,128)(2,1)} %reshape.94), calls=%async_computation.3 | async-start | bytes 2097152 | tf_op jit(solution)/shard_map/all_to_all | solution.py:158
Sparse Core Ops, SparseCore 0:
  9.7 43.8 all-gather.5
  58.3 64.4 all-gather.7
  125.1 103.7 all-gather.9
  237.7 37.7 all-gather.11

commit v16 on v15

--- a/solution.py
+++ b/solution.py
@@ -10,6 +10,7 @@
 HEAD = 64
 BLOCK = 128
 NBK = 8
+ROWS_PER_STEP = 2
 
 
 def _attn_kernel(slots_ref, a_ids_ref, b_ids_ref, q_ref, up_ref, ka_ref, kb_ref, out_ref, qg_ref, kvg_ref, acc_ref, *, scale):
@@ -19,32 +20,34 @@
     def _():
         acc_ref[...] = jnp.zeros(acc_ref.shape, acc_ref.dtype)
 
-    q = q_ref[0]
-    up = up_ref[0]
-    ids = [slots_ref[i, j] for j in range(NBK)]
-    blocks = [
-        jnp.where(a_ids_ref[i, j] >= 0, ka_ref[jnp.maximum(a_ids_ref[i, j], 0)], kb_ref[b_ids_ref[i, j]])
-        for j in range(NBK)
-    ]
-    keys = jnp.concatenate([b[:, :HEAD] for b in blocks], axis=0)
-    vals = jnp.concatenate([b[:, HEAD:] for b in blocks], axis=0)
-    nt = (((1,), (1,)), ((), ()))
-    tn = (((0,), (0,)), ((), ()))
-    scores = lax.dot_general(q * scale, keys, nt, preferred_element_type=jnp.float32)
-    row_max = jnp.max(scores, axis=-1, keepdims=True)
-    exponent = jnp.exp(scores - row_max)
-    prob_full = exponent * (1.0 / jnp.sum(exponent, axis=-1, keepdims=True))
-    prob_low = prob_full.astype(jnp.bfloat16)
-    out_ref[0] = jnp.dot(prob_low, vals, preferred_element_type=jnp.float32).astype(out_ref.dtype)
-    prob_grad = lax.dot_general(up, vals, nt, preferred_element_type=jnp.float32)
-    row_delta = jnp.sum(prob_full * prob_grad, axis=-1, keepdims=True)
-    score_grad = (prob_full * (prob_grad - row_delta) * scale).astype(jnp.bfloat16)
-    qg_ref[0] = jnp.dot(score_grad, keys, preferred_element_type=jnp.float32).astype(qg_ref.dtype)
-    key_terms = lax.dot_general(score_grad, q, tn, preferred_element_type=jnp.float32)
-    value_terms = lax.dot_general(prob_low, up, tn, preferred_element_type=jnp.float32)
-    terms = jnp.concatenate([key_terms, value_terms], axis=1)
-    for j in range(NBK):
-        acc_ref[ids[j]] += terms[j * BLOCK:(j + 1) * BLOCK]
+    for r in range(ROWS_PER_STEP):
+        row = i * ROWS_PER_STEP + r
+        q = q_ref[r]
+        up = up_ref[r]
+        ids = [slots_ref[row, j] for j in range(NBK)]
+        blocks = [
+            jnp.where(a_ids_ref[row, j] >= 0, ka_ref[jnp.maximum(a_ids_ref[row, j], 0)], kb_ref[b_ids_ref[row, j]])
+            for j in range(NBK)
+        ]
+        keys = jnp.concatenate([b[:, :HEAD] for b in blocks], axis=0)
+        vals = jnp.concatenate([b[:, HEAD:] for b in blocks], axis=0)
+        nt = (((1,), (1,)), ((), ()))
+        tn = (((0,), (0,)), ((), ()))
+        scores = lax.dot_general(q, keys, nt, preferred_element_type=jnp.float32) * scale
+        row_max = jnp.max(scores, axis=-1, keepdims=True)
+        exponent = jnp.exp(scores - row_max)
+        prob_full = exponent / jnp.sum(exponent, axis=-1, keepdims=True)
+        prob_low = prob_full.astype(jnp.bfloat16)
+        out_ref[r] = jnp.dot(prob_low, vals, preferred_element_type=jnp.float32).astype(out_ref.dtype)
+        prob_grad = lax.dot_general(up, vals, nt, preferred_element_type=jnp.float32)
+        row_delta = jnp.sum(prob_full * prob_grad, axis=-1, keepdims=True)
+        score_grad = (prob_full * (prob_grad - row_delta) * scale).astype(jnp.bfloat16)
+        qg_ref[r] = jnp.dot(score_grad, keys, preferred_element_type=jnp.float32).astype(qg_ref.dtype)
+        key_terms = lax.dot_general(score_grad, q, tn, preferred_element_type=jnp.float32)
+        value_terms = lax.dot_general(prob_low, up, tn, preferred_element_type=jnp.float32)
+        terms = jnp.concatenate([key_terms, value_terms], axis=1)
+        for j in range(NBK):
+            acc_ref[ids[j]] += terms[j * BLOCK:(j + 1) * BLOCK]
 
     @pl.when(i == pl.num_programs(0) - 1)
     def _():
@@ -54,12 +57,12 @@
 def block_attention(slots, a_ids, b_ids, queries, upstream, kv_a, kv_b, scale):
     rows = queries.shape[0]
     slot_count = 2 * kv_a.shape[0]
-    row_spec = pl.BlockSpec((1, BLOCK, HEAD), lambda i, s, a, b: (i, 0, 0))
+    row_spec = pl.BlockSpec((ROWS_PER_STEP, BLOCK, HEAD), lambda i, s, a, b: (i, 0, 0))
     half_spec = pl.BlockSpec((slot_count // 2, BLOCK, 2 * HEAD), lambda i, s, a, b: (0, 0, 0))
     full_spec = pl.BlockSpec((slot_count, BLOCK, 2 * HEAD), lambda i, s, a, b: (0, 0, 0))
     grid_spec = pltpu.PrefetchScalarGridSpec(
         num_scalar_prefetch=3,
-        grid=(rows,),
+        grid=(rows // ROWS_PER_STEP,),
         in_specs=[row_spec, row_spec, half_spec, half_spec],
         out_specs=[row_spec, row_spec, full_spec],
         scratch_shapes=[pltpu.VMEM((slot_count, BLOCK, 2 * HEAD), jnp.float32)],

time: 288 us -> 287 us (level)
  transfers between devices with their start and end apart: 9 -> 9, of which waited for: 7 -> 7; matrix products, arithmetic and copies ran while one was open for 12% -> 12% of each run, Pallas kernels for 9% -> 8%
where the time goes in v16:
time: 287 us; the launch traced here: 286 us
  waiting for transfers between devices  91.4 us (32%)
  blocking collectives  87.3 us (30%)
  starting transfers between devices  25.9 us (9%)
  Pallas kernels  24.1 us (8%)
  local copies, waits for them, and re-layouts  21.2 us (7%)
  matrix products  17.7 us (6%)
  between operations  14 us (5%)
  other arithmetic  4.28 us (1%)
    all_to_all x1, blocking collectives, on_device(): lax.all_to_all(group_sums, 'zero', split_axis=0, concat_axis=0, tiled=True)  58.6 us
    all_gather x1, blocking collectives, on_device(): head_w = lax.all_gather(head_w, 'zero', axis=0, tiled=True)  28.7 us
    all_to_all x1, waiting for transfers between devices, on_device(): kv_b = lax.all_to_all(kv_b, 'zero', split_axis=0, concat_axis=0, tiled=True)  27.3 us
    pallas_call x1, Pallas kernels, block_attention(): pl.pallas_call(functools.partial(_attn_kernel, scale=scale), grid_spec=gr...  24.1 us
    all_to_all x1, waiting for transfers between devices, on_device(): lax.all_to_all(outgoing, 'seq', split_axis=0, concat_axis=2, tiled=True)  18.4 us
    all_gather x1, waiting for transfers between devices, on_device(): group_tokens = lax.all_gather(tokens, 'seq', axis=0, tiled=True)  15.3 us
    all_gather x1, waiting for transfers between devices, on_device(): kv_a = lax.all_gather(kv_local[:split], 'zero', axis=0, tiled=True)  12.3 us
    unnamed x14, local copies, waits for them, and re-layouts  9.25 us
  transfers between devices with their start and end apart: 9, of which 7 were waited for; matrix products, arithmetic and copies ran while one was open for 12% of the time, Pallas kernels for 8%

profile of v16, /device:TPU:1, one launch (start us, length us, event | category | flops | bytes accessed | tf_op | source)
XLA Modules:
  0.0 285.9 jit_solution(7635567765613617682)
XLA Ops:
  7.2 0.0 all-gather.6.cloned.1.call-start
  7.2 0.7 all-gather.6.cloned.1.call-update
  7.9 0.0 all-gather.8.cloned.1.call-start
  7.9 1.5 copy.27
  9.5 28.7 %all-gather = bf16[1024,3,1,64]{0,3,2,1:T(8,128)(2,1)S(1)} all-gather(bf16[128,3,1,64]{0,3,2,1:T(8,128)(2,1)S(1)} %constant_dynamic-slice_fusion.1), channel_id=2, replica_groups=mesh['seq'=16,'zero'=8] {'zero'}, dimensions={0}, use_global_device_ids=true | all-gather | bytes 442368 | tf_op jit(solution)/shard_map/all_gather | solution.py:106
  38.2 15.3 %all-gather.6.cloned.1.call-done = bf16[2048,1024]{1,0:T(8,128)(2,1)} async-done(((bf16[128,1024]{1,0:T(8,128)(2,1)}), bf16[2048,1024]{1,0:T(8,128)(2,1)}) %all-gather.6.cloned.1.call-update) | async-done | bytes 4194320 | tf_op jit(solution)/shard_map/all_gather | solution.py:103
  53.6 0.0 copy-start.2
  53.6 3.7 %fusion = bf16[2048,128]{0,1:T(8,128)(2,1)S(1)} fusion(bf16[1024,128]{0,1:T(8,128)(2,1)S(1)} %bitcast.64, bf16[2048,1024]{1,0:T(8,128)(2,1)} %all-gather.6.cloned.1.call-done), kind=kOutput, calls=%fused_computation.2 | convolution fusion | flops 537133056 | bytes 4980736 | tf_op jit(solution)/shard_map/td,dc->tc/dot_general | solution.py:107
  57.3 0.8 copy.42
  58.2 0.0 all-gather.8.cloned.1.call-update
  58.2 0.0 copy-done.2
  58.2 0.8 copy.29
  59.1 3.6 %all-to-all-start = ((bf16[128,16,64]{0,2,1:T(8,128)(2,1)}), bf16[128,16,64]{0,2,1:T(8,128)(2,1)S(1)}, u32[]{:S(2)}, u32[]{:S(2)}) async-start(bf16[128,16,64]{0,2,1:T(8,128)(2,1)} %bitcast.7), calls=%async_computation | async-start | bytes 524288 | tf_op jit(solution)/shard_map/all_to_all | solution.py:123
  62.7 0.2 copy.43
  62.8 7.2 %all-to-all-done = bf16[128,16,64]{0,2,1:T(8,128)(2,1)S(1)} async-done(((bf16[128,16,64]{0,2,1:T(8,128)(2,1)}), bf16[128,16,64]{0,2,1:T(8,128)(2,1)S(1)}, u32[]{:S(2)}, u32[]{:S(2)}) %all-to-all-start) | async-done | bytes 262176 | tf_op jit(solution)/shard_map/all_to_all | solution.py:123
  70.0 0.0 copy-start.1
  70.0 1.9 broadcast_in_dim.6
  71.9 0.0 copy-start.3
  71.9 5.4 %all-to-all-start.1 = ((bf16[8,8,128,128]{3,2,1,0:T(8,128)(2,1)}), bf16[8,8,128,128]{3,2,1,0:T(8,128)(2,1)}, u32[]{:S(2)}, u32[]{:S(2)}) async-start(bf16[8,8,128,128]{3,2,1,0:T(8,128)(2,1)} %broadcast_in_dim.6), calls=%async_computation.1 | async-start | bytes 4194304 | tf_op jit(solution)/shard_map/all_to_all | solution.py:121
  77.3 0.0 all-gather.10.cloned.1.call-start
  77.4 0.0 copy-done.1
  77.4 0.8 constant_dynamic-slice_fusion
  78.2 0.0 all-gather.10.cloned.1.call-update
  78.2 0.0 copy-done.3
  78.2 0.1 copy.26
  78.4 0.6 gather_fusion
  79.0 3.6 %convolution_convert_fusion.1 = bf16[2048,64]{0,1:T(8,128)(2,1)S(1)} fusion(bf16[2048,1024]{1,0:T(8,128)(2,1)} %all-gather.6.cloned.1.call-done, bf16[1024,3,64]{0,2,1:T(8,128)(2,1)S(1)} %bitcast.62), kind=kOutput, calls=%fused_computation.3 | convolution fusion | flops 268566528 | bytes 4587520 | tf_op jit(solution)/shard_map/td,dc->tc/dot_general | solution.py:114
  82.5 0.3 copy.28
  82.8 0.3 copy.30
  83.1 27.3 %all-to-all-done.1 = bf16[8,8,128,128]{3,2,1,0:T(8,128)(2,1)} async-done(((bf16[8,8,128,128]{3,2,1,0:T(8,128)(2,1)}), bf16[8,8,128,128]{3,2,1,0:T(8,128)(2,1)}, u32[]{:S(2)}, u32[]{:S(2)}) %all-to-all-start.1) | async-done | bytes 2097184 | tf_op jit(solution)/shard_map/all_to_all | solution.py:121
  110.5 12.3 %all-gather.8.cloned.1.call-done.ka_ref = bf16[64,128,128]{2,1,0:T(8,128)(2,1)} async-done(((bf16[8,128,128]{2,1,0:T(8,128)(2,1)}), bf16[64,128,128]{2,1,0:T(8,128)(2,1)}) %all-gather.8.cloned.1.call-update) | async-done | bytes 2097168 | tf_op jit(solution)/shard_map/all_gather | solution.py:119
  122.8 0.0 copy-start
  122.8 1.6 copy-done
  124.4 24.1 %shard_map.67 = (bf16[16,128,64]{2,1,0:T(8,128)(2,1)S(1)}, bf16[16,128,64]{2,1,0:T(8,128)(2,1)S(1)}, bf16[128,128,128]{2,1,0:T(8,128)(2,1)}) custom-call(s32[16,8]{1,0:T(8,128)S(1)} %get-tuple-element.22.slots_ref, s32[16,8]{1,0:T(8,128)S(1)} %add_select_fusion.4.a_ids_ref, s32[16,8]{1,0:T(8,128)S(1)} %get-tuple-element.21.b_ids_ref, ...), custom_call_target="tpu_custom_call" | custom-call | tf_op jit(solution)/shard_map/pallas_call | solution.py:75
  148.5 58.6 %all_to_all.48 = bf16[8,2048,128]{2,1,0:T(8,128)(2,1)} all-to-all(bf16[8,2048,128]{2,1,0:T(8,128)(2,1)} %bitcast.58), channel_id=1, replica_groups=mesh['seq'=16,'zero'=8] {'zero'}, dimensions={0} | all-to-all | bytes 8388608 | tf_op jit(solution)/shard_map/all_to_all | solution.py:156
  207.1 3.1 %reduce_sum.21 = bf16[2048,128]{1,0:T(8,128)(2,1)S(1)} reduce(bf16[8,2048,128]{2,1,0:T(8,128)(2,1)} %all_to_all.48, bf16[]{:T(256)} %constant.123.clone.1), dimensions={0}, to_apply=%region_0.1 | reduce | flops 1835008 | bytes 4718594 | tf_op jit(solution)/shard_map/reduce_sum | solution.py:157
  210.1 3.6 %convolution_bitcast_fusion = f32[24,8,8,128]{3,2,1,0:T(8,128)S(1)} fusion(bf16[2048,1024]{1,0:T(8,128)(2,1)} %all-gather.6.cloned.1.call-done, bf16[2048,128]{1,0:T(8,128)(2,1)S(1)} %reduce_sum.21, bf16[2048,64]{1,0:T(8,128)(2,1)S(1)} %bitcast.50), kind=kOutput, calls=%fused_computation.4 | convolution fusion | flops 806879232 | bytes 5767168 | tf_op jit(solution)/shard_map/td,tc->dc/dot_general | solution.py:171
  213.7 0.9 copy.47
  214.6 8.7 %all-to-all-start.4 = ((f32[8,128,192]{1,2,0:T(8,128)}), f32[8,128,192]{1,2,0:T(8,128)S(1)}, u32[]{:S(2)}, u32[]{:S(2)}) async-start(f32[8,128,192]{1,2,0:T(8,128)} %bitcast.46), calls=%async_computation.4 | async-start | bytes 1572864 | tf_op jit(solution)/shard_map/all_to_all | solution.py:175
  223.3 0.0 all-gather.12.cloned.1.call-start
  223.4 5.0 %all-gather.10.cloned.1.call-done = bf16[1024,1536]{1,0:T(8,128)(2,1)} async-done(((bf16[128,1536]{1,0:T(8,128)(2,1)}), bf16[1024,1536]{1,0:T(8,128)(2,1)}) %all-gather.10.cloned.1.call-update) | async-done | bytes 3145744 | tf_op jit(solution)/shard_map/all_gather | solution.py:101
  228.4 1.5 collective-permute-start
  229.9 5.1 %all-to-all-done.4 = f32[8,128,192]{1,2,0:T(8,128)S(1)} async-done(((f32[8,128,192]{1,2,0:T(8,128)}), f32[8,128,192]{1,2,0:T(8,128)S(1)}, u32[]{:S(2)}, u32[]{:S(2)}) %all-to-all-start.4) | async-done | bytes 786464 | tf_op jit(solution)/shard_map/all_to_all | solution.py:175
  235.0 0.7 reduce_sum.22
  235.6 0.0 all-gather.12.cloned.1.call-update
  235.7 0.5 pad_maximum_fusion
  236.2 0.6 copy.33
  236.8 1.4 copy.34
  238.2 2.2 reshape.94
  240.5 6.5 %all-to-all-start.3 = ((bf16[16,2,16384]{2,1,0:T(2,128)(2,1)}), bf16[16,2,16384]{2,1,0:T(2,128)(2,1)S(1)}, u32[]{:S(2)}, u32[]{:S(2)}) async-start(bf16[16,2,16384]{2,1,0:T(2,128)(2,1)} %reshape.94), calls=%async_computation.3 | async-start | bytes 2097152 | tf_op jit(solution)/shard_map/all_to_all | solution.py:161
  247.0 18.4 %all-to-all-done.3 = bf16[16,2,16384]{2,1,0:T(2,128)(2,1)S(1)} async-done(((bf16[16,2,16384]{2,1,0:T(2,128)(2,1)}), bf16[16,2,16384]{2,1,0:T(2,128)(2,1)S(1)}, u32[]{:S(2)}, u32[]{:S(2)}) %all-to-all-start.3) | async-done | bytes 1048608 | tf_op jit(solution)/shard_map/all_to_all | solution.py:161
  265.3 1.3 reshape.95
  266.6 1.4 copy.44
  268.1 0.1 slice.37
  268.2 0.2 copy.37
  268.4 0.1 copy.36
  268.5 0.9 copy.40
  269.4 3.1 %fusion.6 = f32[128,1024]{1,0:T(8,128)S(1)} fusion(bf16[1024,1536]{1,0:T(8,128)(2,1)} %all-gather.10.cloned.1.call-done, bf16[128,3072]{0,1:T(8,128)(2,1)S(1)} %bitcast.59, s32[]{:T(128)S(6)} %select_n.75), kind=kOutput, calls=%fused_computation.13 | convolution fusion | flops 402653184 | bytes 4063236 | tf_op jit(solution)/shard_map/tc,dc->td/dot_general | solution.py:167
  272.4 0.0 collective-permute-done
  272.4 3.8 %fusion.1 = bf16[128,1024]{1,0:T(8,128)(2,1)} fusion(f32[128,1024]{1,0:T(8,128)S(1)} %fusion.6, bf16[1024,1536]{1,0:T(8,128)(2,1)} %collective-permute-done, bf16[128,3072]{0,1:T(8,128)(2,1)S(1)} %bitcast.60, s32[]{:T(128)S(6)} %select_n.76), kind=kOutput, calls=%fused_computation.6 | convolution fusion | flops 402915328 | bytes 4325380 | tf_op jit(solution)/shard_map/tc,dc->td/dot_general | solution.py:168
  276.2 0.0 all-gather.12.cloned.1.call-done
  276.2 1.5 copy.39
  277.7 1.6 copy.41
  (8 shorter events, 0.1 us)
Async XLA Ops:
  7.2 46.4 %all-gather.6.cloned.1.call-start = ((), (), s32[]{:S(2)}) async-start(), calls=%async_computation.5 | async-start | bytes 4456448 | tf_op jit(solution)/shard_map/all_gather | solution.py:103
  7.9 114.9 %all-gather.8.cloned.1.call-start = ((), (), s32[]{:S(2)}) async-start(), calls=%async_computation.6 | async-start | bytes 2359296 | tf_op jit(solution)/shard_map/all_gather | solution.py:119
  53.6 4.7 %copy-start.2 = (bf16[128,1024]{1,0:T(8,128)(2,1)S(1)}, bf16[128,1024]{1,0:T(8,128)(2,1)}, u32[]{:S(2)}) copy-start(bf16[128,1024]{1,0:T(8,128)(2,1)} %param.7) | copy-start | bytes 786436
  59.1 11.0 %all-to-all-start = ((bf16[128,16,64]{0,2,1:T(8,128)(2,1)}), bf16[128,16,64]{0,2,1:T(8,128)(2,1)S(1)}, u32[]{:S(2)}, u32[]{:S(2)}) async-start(bf16[128,16,64]{0,2,1:T(8,128)(2,1)} %bitcast.7), calls=%async_computation | async-start | bytes 524288 | tf_op jit(solution)/shard_map/all_to_all | solution.py:123
  70.0 7.3 %copy-start.1 = (bf16[128,3072]{1,0:T(8,128)(2,1)S(1)}, bf16[128,3072]{1,0:T(8,128)(2,1)}, u32[]{:S(2)}) copy-start(bf16[128,3072]{1,0:T(8,128)(2,1)} %param.5) | copy-start | bytes 2359300
  71.9 6.3 %copy-start.3 = (s32[128,8]{0,1:T(8,128)S(1)}, s32[128,8]{0,1:T(8,128)}, u32[]{:S(2)}) copy-start(s32[128,8]{0,1:T(8,128)} %param.6) | copy-start | bytes 12292
  71.9 38.6 %all-to-all-start.1 = ((bf16[8,8,128,128]{3,2,1,0:T(8,128)(2,1)}), bf16[8,8,128,128]{3,2,1,0:T(8,128)(2,1)}, u32[]{:S(2)}, u32[]{:S(2)}) async-start(bf16[8,8,128,128]{3,2,1,0:T(8,128)(2,1)} %broadcast_in_dim.6), calls=%async_computation.1 | async-start | bytes 4194304 | tf_op jit(solution)/shard_map/all_to_all | solution.py:121
  77.3 151.0 %all-gather.10.cloned.1.call-start = ((), (), s32[]{:S(2)}) async-start(), calls=%async_computation.7 | async-start | bytes 3538944 | tf_op jit(solution)/shard_map/all_gather | solution.py:101
  122.8 1.6 copy-start
  214.6 20.3 %all-to-all-start.4 = ((f32[8,128,192]{1,2,0:T(8,128)}), f32[8,128,192]{1,2,0:T(8,128)S(1)}, u32[]{:S(2)}, u32[]{:S(2)}) async-start(f32[8,128,192]{1,2,0:T(8,128)} %bitcast.46), calls=%async_computation.4 | async-start | bytes 1572864 | tf_op jit(solution)/shard_map/all_to_all | solution.py:175
  223.3 52.9 %all-gather.12.cloned.1.call-start = ((), (), s32[]{:S(2)}) async-start(), calls=%async_computation.8 | async-start | bytes 1671168 | tf_op jit(solution)/shard_map/all_gather | solution.py:178
  228.4 44.1 %collective-permute-start = (bf16[1024,1536]{1,0:T(8,128)(2,1)}, bf16[1024,1536]{1,0:T(8,128)(2,1)}, u32[]{:S(2)}, u32[]{:S(2)}) collective-permute-start(bf16[1024,1536]{1,0:T(8,128)(2,1)} %all-gather.10.cloned.1.call-done), channel_id=1, source_target_pairs={{0,8},{8,0},{16,24},{24,16},{32,40},{40,32},{48,56},{56,48},{64,72... | collective-permute-start | bytes 9437192 | tf_op jit(solution)/shard_map/ppermute | solution.py:102
  240.5 24.9 %all-to-all-start.3 = ((bf16[16,2,16384]{2,1,0:T(2,128)(2,1)}), bf16[16,2,16384]{2,1,0:T(2,128)(2,1)S(1)}, u32[]{:S(2)}, u32[]{:S(2)}) async-start(bf16[16,2,16384]{2,1,0:T(2,128)(2,1)} %reshape.94), calls=%async_computation.3 | async-start | bytes 2097152 | tf_op jit(solution)/shard_map/all_to_all | solution.py:161
Sparse Core Ops, SparseCore 0:
  9.7 43.8 all-gather.5
  58.3 64.4 all-gather.7
  125.1 103.2 all-gather.9
  235.8 38.4 all-gather.11

commit v17 on v16

--- a/solution.py
+++ b/solution.py
@@ -56,9 +56,9 @@
 
 def block_attention(slots, a_ids, b_ids, queries, upstream, kv_a, kv_b, scale):
     rows = queries.shape[0]
-    slot_count = 2 * kv_a.shape[0]
+    slot_count = kv_b.shape[0]
     row_spec = pl.BlockSpec((ROWS_PER_STEP, BLOCK, HEAD), lambda i, s, a, b: (i, 0, 0))
-    half_spec = pl.BlockSpec((slot_count // 2, BLOCK, 2 * HEAD), lambda i, s, a, b: (0, 0, 0))
+    half_spec = pl.BlockSpec((kv_a.shape[0], BLOCK, 2 * HEAD), lambda i, s, a, b: (0, 0, 0))
     full_spec = pl.BlockSpec((slot_count, BLOCK, 2 * HEAD), lambda i, s, a, b: (0, 0, 0))
     grid_spec = pltpu.PrefetchScalarGridSpec(
         num_scalar_prefetch=3,
@@ -115,11 +115,11 @@
         "td,dc->tc", group_tokens, head_w[:, 0], preferred_element_type=jnp.float32
     ).astype(jnp.bfloat16)
     kv_local = kv_local.reshape(local_blocks, BLOCK, 2 * head_cols)
-    split = local_blocks // 2
-    kv_a = lax.all_gather(kv_local[:split], "zero", axis=0, tiled=True)
+    split = 0
     kv_b = jnp.broadcast_to(kv_local[split:], (zero_count,) + kv_local[split:].shape)
     kv_b = lax.all_to_all(kv_b, "zero", split_axis=0, concat_axis=0, tiled=True)
     kv_b = kv_b.reshape(-1, BLOCK, 2 * head_cols)
+    kv_a = kv_b
     incoming = lax.all_to_all(
         upstream.reshape(tok_rows, seq_count, head_cols),
         "seq",

time: 287 us -> 303 us (1.056)
  waiting for transfers between devices: 91.4 us -> 110 us
  blocking collectives: 87.3 us -> 81.2 us
    all_to_all x1, waiting for transfers between devices: 27.3 us -> 62.9 us  [on_device(): kv_b = lax.all_to_all(kv_b, 'zero', split_axis=0, concat_axis=0, tiled=True)]
    all_gather x1 -> x0, waiting for transfers between devices: 12.3 us -> none  [on_device(): kv_a = lax.all_gather(kv_local[:split], 'zero', axis=0, tiled=True)]
    all_to_all x1, blocking collectives: 58.6 us -> 52.3 us  [on_device(): lax.all_to_all(group_sums, 'zero', split_axis=0, concat_axis=0, tiled=True)]
    all_to_all x1, starting transfers between devices: 8.67 us -> 3.55 us  [on_device(): lax.all_to_all(head_part, 'zero', split_axis=0, concat_axis=0, tiled=True)]
    all_gather x1, waiting for transfers between devices: 4.99 us -> 0.03 us  [on_device(): w_mine = lax.all_gather(w_mine, 'zero', axis=0, tiled=True)]
    all_to_all x1, starting transfers between devices: 6.5 us -> 10.2 us  [on_device(): lax.all_to_all(outgoing, 'seq', split_axis=0, concat_axis=2, tiled=True)]
    unnamed x14 -> x12, local copies, waits for them, and re-layouts: 9.25 us -> 7.66 us
  transfers between devices with their start and end apart: 9 -> 8, of which waited for: 7 -> 5; matrix products, arithmetic and copies ran while one was open for 12% -> 10% of each run, Pallas kernels for 8% -> 9%
where the time goes in v17:
time: 303 us; the launch traced here: 302 us
  waiting for transfers between devices  110 us (36%)
  blocking collectives  81.2 us (27%)
  starting transfers between devices  27.1 us (9%)
  Pallas kernels  26 us (9%)
  local copies, waits for them, and re-layouts  20 us (7%)
  matrix products  17.7 us (6%)
  between operations  15.7 us (5%)
  other arithmetic  4.27 us (1%)
    all_to_all x1, waiting for transfers between devices, on_device(): kv_b = lax.all_to_all(kv_b, 'zero', split_axis=0, concat_axis=0, tiled=True)  62.9 us
    all_to_all x1, blocking collectives, on_device(): lax.all_to_all(group_sums, 'zero', split_axis=0, concat_axis=0, tiled=True)  52.3 us
    all_gather x1, blocking collectives, on_device(): head_w = lax.all_gather(head_w, 'zero', axis=0, tiled=True)  28.9 us
    pallas_call x1, Pallas kernels, block_attention(): pl.pallas_call(functools.partial(_attn_kernel, scale=scale), grid_spec=gr...  26 us
    all_to_all x1, waiting for transfers between devices, on_device(): lax.all_to_all(outgoing, 'seq', split_axis=0, concat_axis=2, tiled=True)  18.2 us
    all_gather x1, waiting for transfers between devices, on_device(): group_tokens = lax.all_gather(tokens, 'seq', axis=0, tiled=True)  15.2 us
    all_to_all x1, starting transfers between devices, on_device(): lax.all_to_all(outgoing, 'seq', split_axis=0, concat_axis=2, tiled=True)  10.2 us
    unnamed x12, local copies, waits for them, and re-layouts  7.66 us
  transfers between devices with their start and end apart: 8, of which 5 were waited for; matrix products, arithmetic and copies ran while one was open for 10% of the time, Pallas kernels for 9%

profile of v17, /device:TPU:1, one launch (start us, length us, event | category | flops | bytes accessed | tf_op | source)
XLA Modules:
  0.0 301.9 jit_solution(16399381630072065299)
XLA Ops:
  8.0 0.0 all-gather.5.cloned.1.call-start
  8.0 0.7 all-gather.5.cloned.1.call-update
  8.7 1.5 copy.25
  10.2 0.0 copy-start.1
  10.3 28.9 %all-gather = bf16[1024,3,1,64]{0,3,2,1:T(8,128)(2,1)S(1)} all-gather(bf16[128,3,1,64]{0,3,2,1:T(8,128)(2,1)S(1)} %constant_dynamic-slice_fusion.1), channel_id=2, replica_groups=mesh['seq'=16,'zero'=8] {'zero'}, dimensions={0}, use_global_device_ids=true | all-gather | bytes 442368 | tf_op jit(solution)/shard_map/all_gather | solution.py:106
  39.2 15.2 %all-gather.5.cloned.1.call-done = bf16[2048,1024]{1,0:T(8,128)(2,1)} async-done(((bf16[128,1024]{1,0:T(8,128)(2,1)}), bf16[2048,1024]{1,0:T(8,128)(2,1)}) %all-gather.5.cloned.1.call-update) | async-done | bytes 4194320 | tf_op jit(solution)/shard_map/all_gather | solution.py:103
  54.4 3.7 %fusion = bf16[2048,128]{0,1:T(8,128)(2,1)S(1)} fusion(bf16[1024,128]{0,1:T(8,128)(2,1)S(1)} %bitcast.63, bf16[2048,1024]{1,0:T(8,128)(2,1)} %all-gather.5.cloned.1.call-done), kind=kOutput, calls=%fused_computation.2 | convolution fusion | flops 537133056 | bytes 4980736 | tf_op jit(solution)/shard_map/td,dc->tc/dot_general | solution.py:107
  58.1 0.0 copy-done.1
  58.1 0.8 copy.27
  58.9 3.6 %all-to-all-start = ((bf16[128,16,64]{0,2,1:T(8,128)(2,1)}), bf16[128,16,64]{0,2,1:T(8,128)(2,1)S(1)}, u32[]{:S(2)}, u32[]{:S(2)}) async-start(bf16[128,16,64]{0,2,1:T(8,128)(2,1)} %bitcast.7), calls=%async_computation | async-start | bytes 524288 | tf_op jit(solution)/shard_map/all_to_all | solution.py:123
  62.5 0.3 copy.39
  62.8 7.0 %all-to-all-done = bf16[128,16,64]{0,2,1:T(8,128)(2,1)S(1)} async-done(((bf16[128,16,64]{0,2,1:T(8,128)(2,1)}), bf16[128,16,64]{0,2,1:T(8,128)(2,1)S(1)}, u32[]{:S(2)}, u32[]{:S(2)}) %all-to-all-start) | async-done | bytes 262176 | tf_op jit(solution)/shard_map/all_to_all | solution.py:123
  69.8 3.0 broadcast_in_dim.6
  72.8 0.0 copy-start
  72.8 0.0 copy-start.2
  72.8 5.7 %all-to-all-start.1 = ((bf16[8,16,128,128]{3,2,1,0:T(8,128)(2,1)}), bf16[8,16,128,128]{3,2,1,0:T(8,128)(2,1)}, u32[]{:S(2)}, u32[]{:S(2)}) async-start(bf16[8,16,128,128]{3,2,1,0:T(8,128)(2,1)} %broadcast_in_dim.6), calls=%async_computation.1 | async-start | bytes 8388608 | tf_op jit(solution)/shard_map/all_to_all | solution.py:120
  78.5 0.0 all-gather.7.cloned.1.call-start
  78.6 0.0 copy-done
  78.6 0.8 constant_dynamic-slice_fusion
  79.4 0.0 all-gather.7.cloned.1.call-update
  79.4 0.0 copy-done.2
  79.4 0.1 copy.24
  79.6 0.6 gather_fusion
  80.2 3.6 %convolution_convert_fusion.1 = bf16[2048,64]{0,1:T(8,128)(2,1)S(1)} fusion(bf16[2048,1024]{1,0:T(8,128)(2,1)} %all-gather.5.cloned.1.call-done, bf16[1024,3,64]{0,2,1:T(8,128)(2,1)S(1)} %bitcast.62), kind=kOutput, calls=%fused_computation.3 | convolution fusion | flops 268566528 | bytes 4587520 | tf_op jit(solution)/shard_map/td,dc->tc/dot_general | solution.py:114
  83.8 0.3 copy.26
  84.0 0.3 copy.28
  84.3 62.9 %all-to-all-done.1 = bf16[8,16,128,128]{3,2,1,0:T(8,128)(2,1)} async-done(((bf16[8,16,128,128]{3,2,1,0:T(8,128)(2,1)}), bf16[8,16,128,128]{3,2,1,0:T(8,128)(2,1)}, u32[]{:S(2)}, u32[]{:S(2)}) %all-to-all-start.1) | async-done | bytes 4194336 | tf_op jit(solution)/shard_map/all_to_all | solution.py:120
  147.2 26.0 %shard_map.67 = (bf16[16,128,64]{2,1,0:T(8,128)(2,1)S(1)}, bf16[16,128,64]{2,1,0:T(8,128)(2,1)S(1)}, bf16[128,128,128]{2,1,0:T(8,128)(2,1)}) custom-call(s32[16,8]{1,0:T(8,128)S(1)} %get-tuple-element.22.slots_ref, s32[16,8]{1,0:T(8,128)S(1)} %compare_select_fusion.a_ids_ref, s32[16,8]{1,0:T(8,128)S(1)} %get-tuple-element.21.b_ids_ref, ...), custom_call_target="tpu_custom_call" | custom-call | tf_op jit(solution)/shard_map/pallas_call | solution.py:75
  173.2 52.3 %all_to_all.48 = bf16[8,2048,128]{2,1,0:T(8,128)(2,1)} all-to-all(bf16[8,2048,128]{2,1,0:T(8,128)(2,1)} %bitcast.57), channel_id=1, replica_groups=mesh['seq'=16,'zero'=8] {'zero'}, dimensions={0} | all-to-all | bytes 8388608 | tf_op jit(solution)/shard_map/all_to_all | solution.py:156
  225.5 3.1 %reduce_sum.21 = bf16[2048,128]{1,0:T(8,128)(2,1)S(1)} reduce(bf16[8,2048,128]{2,1,0:T(8,128)(2,1)} %all_to_all.48, bf16[]{:T(256)} %constant.120.clone.1), dimensions={0}, to_apply=%region_0.1 | reduce | flops 1835008 | bytes 4718594 | tf_op jit(solution)/shard_map/reduce_sum | solution.py:157
  228.6 3.6 %convolution_bitcast_fusion = f32[24,8,8,128]{3,2,1,0:T(8,128)S(1)} fusion(bf16[2048,1024]{1,0:T(8,128)(2,1)} %all-gather.5.cloned.1.call-done, bf16[2048,128]{1,0:T(8,128)(2,1)S(1)} %reduce_sum.21, bf16[2048,64]{1,0:T(8,128)(2,1)S(1)} %bitcast.49), kind=kOutput, calls=%fused_computation.4 | convolution fusion | flops 806879232 | bytes 5767168 | tf_op jit(solution)/shard_map/td,tc->dc/dot_general | solution.py:171
  232.2 0.9 copy.43
  233.1 3.5 %all-to-all-start.4 = ((f32[8,128,192]{1,2,0:T(8,128)}), f32[8,128,192]{1,2,0:T(8,128)S(1)}, u32[]{:S(2)}, u32[]{:S(2)}) async-start(f32[8,128,192]{1,2,0:T(8,128)} %bitcast.45), calls=%async_computation.4 | async-start | bytes 1572864 | tf_op jit(solution)/shard_map/all_to_all | solution.py:175
  236.7 0.0 all-gather.9.cloned.1.call-start
  236.7 0.0 all-gather.7.cloned.1.call-done
  236.7 4.0 %collective-permute-start = (bf16[1024,1536]{1,0:T(8,128)(2,1)}, bf16[1024,1536]{1,0:T(8,128)(2,1)}, u32[]{:S(2)}, u32[]{:S(2)}) collective-permute-start(bf16[1024,1536]{1,0:T(8,128)(2,1)} %all-gather.7.cloned.1.call-done), channel_id=1, source_target_pairs={{0,8},{8,0},{16,24},{24,16},{32,40},{40,32},{48,56},{56,48},{64,72... | collective-permute-start | bytes 9437192 | tf_op jit(solution)/shard_map/ppermute | solution.py:102
  240.7 5.8 %all-to-all-done.4 = f32[8,128,192]{1,2,0:T(8,128)S(1)} async-done(((f32[8,128,192]{1,2,0:T(8,128)}), f32[8,128,192]{1,2,0:T(8,128)S(1)}, u32[]{:S(2)}, u32[]{:S(2)}) %all-to-all-start.4) | async-done | bytes 786464 | tf_op jit(solution)/shard_map/all_to_all | solution.py:175
  246.5 0.7 reduce_sum.22
  247.2 0.0 all-gather.9.cloned.1.call-update
  247.2 0.5 pad_maximum_fusion
  247.7 0.6 copy.30
  248.4 1.4 copy.31
  249.8 2.2 reshape.95
  252.0 10.2 %all-to-all-start.3 = ((bf16[16,2,16384]{2,1,0:T(2,128)(2,1)}), bf16[16,2,16384]{2,1,0:T(2,128)(2,1)S(1)}, u32[]{:S(2)}, u32[]{:S(2)}) async-start(bf16[16,2,16384]{2,1,0:T(2,128)(2,1)} %reshape.95), calls=%async_computation.3 | async-start | bytes 2097152 | tf_op jit(solution)/shard_map/all_to_all | solution.py:161
  262.2 18.2 %all-to-all-done.3 = bf16[16,2,16384]{2,1,0:T(2,128)(2,1)S(1)} async-done(((bf16[16,2,16384]{2,1,0:T(2,128)(2,1)}), bf16[16,2,16384]{2,1,0:T(2,128)(2,1)S(1)}, u32[]{:S(2)}, u32[]{:S(2)}) %all-to-all-start.3) | async-done | bytes 1048608 | tf_op jit(solution)/shard_map/all_to_all | solution.py:161
  280.4 1.3 reshape.96
  281.7 1.4 copy.40
  283.1 0.1 slice.21
  283.3 0.2 copy.34
  283.5 0.1 copy.33
  283.6 0.9 copy.37
  284.4 3.1 %fusion.6 = f32[128,1024]{1,0:T(8,128)S(1)} fusion(bf16[1024,1536]{1,0:T(8,128)(2,1)} %all-gather.7.cloned.1.call-done, bf16[128,3072]{0,1:T(8,128)(2,1)S(1)} %bitcast.58, s32[]{:T(128)S(6)} %select_n.75), kind=kOutput, calls=%fused_computation.13 | convolution fusion | flops 402653184 | bytes 4063236 | tf_op jit(solution)/shard_map/tc,dc->td/dot_general | solution.py:167
  287.5 0.0 collective-permute-done
  287.5 3.8 %fusion.1 = bf16[128,1024]{1,0:T(8,128)(2,1)} fusion(f32[128,1024]{1,0:T(8,128)S(1)} %fusion.6, bf16[1024,1536]{1,0:T(8,128)(2,1)} %collective-permute-done, bf16[128,3072]{0,1:T(8,128)(2,1)S(1)} %bitcast.59, s32[]{:T(128)S(6)} %select_n.76), kind=kOutput, calls=%fused_computation.6 | convolution fusion | flops 402915328 | bytes 4325380 | tf_op jit(solution)/shard_map/tc,dc->td/dot_general | solution.py:168
  291.3 0.0 all-gather.9.cloned.1.call-done
  291.3 1.5 copy.36
  292.8 1.6 copy.38
  (7 shorter events, 0.1 us)
Async XLA Ops:
  8.0 46.4 %all-gather.5.cloned.1.call-start = ((), (), s32[]{:S(2)}) async-start(), calls=%async_computation.5 | async-start | bytes 4456448 | tf_op jit(solution)/shard_map/all_gather | solution.py:103
  10.2 47.8 %copy-start.1 = (bf16[128,1024]{1,0:T(8,128)(2,1)S(1)}, bf16[128,1024]{1,0:T(8,128)(2,1)}, u32[]{:S(2)}) copy-start(bf16[128,1024]{1,0:T(8,128)(2,1)} %param.7) | copy-start | bytes 786436
  58.9 10.9 %all-to-all-start = ((bf16[128,16,64]{0,2,1:T(8,128)(2,1)}), bf16[128,16,64]{0,2,1:T(8,128)(2,1)S(1)}, u32[]{:S(2)}, u32[]{:S(2)}) async-start(bf16[128,16,64]{0,2,1:T(8,128)(2,1)} %bitcast.7), calls=%async_computation | async-start | bytes 524288 | tf_op jit(solution)/shard_map/all_to_all | solution.py:123
  72.8 5.8 %copy-start = (bf16[128,3072]{1,0:T(8,128)(2,1)S(1)}, bf16[128,3072]{1,0:T(8,128)(2,1)}, u32[]{:S(2)}) copy-start(bf16[128,3072]{1,0:T(8,128)(2,1)} %param.5) | copy-start | bytes 2359300
  72.8 6.6 %copy-start.2 = (s32[128,8]{0,1:T(8,128)S(1)}, s32[128,8]{0,1:T(8,128)}, u32[]{:S(2)}) copy-start(s32[128,8]{0,1:T(8,128)} %param.6) | copy-start | bytes 12292
  72.8 74.4 %all-to-all-start.1 = ((bf16[8,16,128,128]{3,2,1,0:T(8,128)(2,1)}), bf16[8,16,128,128]{3,2,1,0:T(8,128)(2,1)}, u32[]{:S(2)}, u32[]{:S(2)}) async-start(bf16[8,16,128,128]{3,2,1,0:T(8,128)(2,1)} %broadcast_in_dim.6), calls=%async_computation.1 | async-start | bytes 8388608 | tf_op jit(solution)/shard_map/all_to_all | solution.py:120
  78.5 158.2 %all-gather.7.cloned.1.call-start = ((), (), s32[]{:S(2)}) async-start(), calls=%async_computation.6 | async-start | bytes 3538944 | tf_op jit(solution)/shard_map/all_gather | solution.py:101
  233.1 13.4 %all-to-all-start.4 = ((f32[8,128,192]{1,2,0:T(8,128)}), f32[8,128,192]{1,2,0:T(8,128)S(1)}, u32[]{:S(2)}, u32[]{:S(2)}) async-start(f32[8,128,192]{1,2,0:T(8,128)} %bitcast.45), calls=%async_computation.4 | async-start | bytes 1572864 | tf_op jit(solution)/shard_map/all_to_all | solution.py:175
  236.7 54.6 %all-gather.9.cloned.1.call-start = ((), (), s32[]{:S(2)}) async-start(), calls=%async_computation.7 | async-start | bytes 1671168 | tf_op jit(solution)/shard_map/all_gather | solution.py:178
  236.7 50.8 %collective-permute-start = (bf16[1024,1536]{1,0:T(8,128)(2,1)}, bf16[1024,1536]{1,0:T(8,128)(2,1)}, u32[]{:S(2)}, u32[]{:S(2)}) collective-permute-start(bf16[1024,1536]{1,0:T(8,128)(2,1)} %all-gather.7.cloned.1.call-done), channel_id=1, source_target_pairs={{0,8},{8,0},{16,24},{24,16},{32,40},{40,32},{48,56},{56,48},{64,72... | collective-permute-start | bytes 9437192 | tf_op jit(solution)/shard_map/ppermute | solution.py:102
  252.0 28.4 %all-to-all-start.3 = ((bf16[16,2,16384]{2,1,0:T(2,128)(2,1)}), bf16[16,2,16384]{2,1,0:T(2,128)(2,1)S(1)}, u32[]{:S(2)}, u32[]{:S(2)}) async-start(bf16[16,2,16384]{2,1,0:T(2,128)(2,1)} %reshape.95), calls=%async_computation.3 | async-start | bytes 2097152 | tf_op jit(solution)/shard_map/all_to_all | solution.py:161
Sparse Core Ops, SparseCore 0:
  10.5 43.8 all-gather.4
  247.3 42.2 all-gather.8
Sparse Core Ops, SparseCore 1:
  81.4 76.6 all-gather.6

commit v18 on v16

--- a/solution.py
+++ b/solution.py
@@ -10,7 +10,7 @@
 HEAD = 64
 BLOCK = 128
 NBK = 8
-ROWS_PER_STEP = 2
+ROWS_PER_STEP = 4
 
 
 def _attn_kernel(slots_ref, a_ids_ref, b_ids_ref, q_ref, up_ref, ka_ref, kb_ref, out_ref, qg_ref, kvg_ref, acc_ref, *, scale):

time: 287 us -> 285 us (level)
  no operation moved by 1% of the time
where the time goes in v18:
time: 285 us
  waiting for transfers between devices  91.3 us (32%)
  blocking collectives  87.5 us (31%)
  starting transfers between devices  25.7 us (9%)
  Pallas kernels  22.9 us (8%)
  local copies, waits for them, and re-layouts  21.2 us (7%)
  matrix products  17.7 us (6%)
  between operations  14 us (5%)
  other arithmetic  4.28 us (2%)
    all_to_all x1, blocking collectives, on_device(): lax.all_to_all(group_sums, 'zero', split_axis=0, concat_axis=0, tiled=True)  58.8 us
    all_gather x1, blocking collectives, on_device(): head_w = lax.all_gather(head_w, 'zero', axis=0, tiled=True)  28.7 us
    all_to_all x1, waiting for transfers between devices, on_device(): kv_b = lax.all_to_all(kv_b, 'zero', split_axis=0, concat_axis=0, tiled=True)  27.3 us
    pallas_call x1, Pallas kernels, block_attention(): pl.pallas_call(functools.partial(_attn_kernel, scale=scale), grid_spec=gr...  22.9 us
    all_to_all x1, waiting for transfers between devices, on_device(): lax.all_to_all(outgoing, 'seq', split_axis=0, concat_axis=2, tiled=True)  18.3 us
    all_gather x1, waiting for transfers between devices, on_device(): group_tokens = lax.all_gather(tokens, 'seq', axis=0, tiled=True)  15.3 us
    all_gather x1, waiting for transfers between devices, on_device(): kv_a = lax.all_gather(kv_local[:split], 'zero', axis=0, tiled=True)  12.3 us
    unnamed x14, local copies, waits for them, and re-layouts  9.25 us
  transfers between devices with their start and end apart: 9, of which 7 were waited for; matrix products, arithmetic and copies ran while one was open for 12% of the time, Pallas kernels for 8%

profile of v18, /device:TPU:1, one launch (start us, length us, event | category | flops | bytes accessed | tf_op | source)
XLA Modules:
  0.0 284.6 jit_solution(18385366597385363847)
XLA Ops:
  7.2 0.0 all-gather.6.cloned.1.call-start
  7.2 0.7 all-gather.6.cloned.1.call-update
  7.9 0.0 all-gather.8.cloned.1.call-start
  7.9 1.5 copy.27
  9.5 28.7 %all-gather = bf16[1024,3,1,64]{0,3,2,1:T(8,128)(2,1)S(1)} all-gather(bf16[128,3,1,64]{0,3,2,1:T(8,128)(2,1)S(1)} %constant_dynamic-slice_fusion.1), channel_id=2, replica_groups=mesh['seq'=16,'zero'=8] {'zero'}, dimensions={0}, use_global_device_ids=true | all-gather | bytes 442368 | tf_op jit(solution)/shard_map/all_gather | solution.py:106
  38.2 15.3 %all-gather.6.cloned.1.call-done = bf16[2048,1024]{1,0:T(8,128)(2,1)} async-done(((bf16[128,1024]{1,0:T(8,128)(2,1)}), bf16[2048,1024]{1,0:T(8,128)(2,1)}) %all-gather.6.cloned.1.call-update) | async-done | bytes 4194320 | tf_op jit(solution)/shard_map/all_gather | solution.py:103
  53.6 0.0 copy-start.2
  53.6 3.7 %fusion = bf16[2048,128]{0,1:T(8,128)(2,1)S(1)} fusion(bf16[1024,128]{0,1:T(8,128)(2,1)S(1)} %bitcast.64, bf16[2048,1024]{1,0:T(8,128)(2,1)} %all-gather.6.cloned.1.call-done), kind=kOutput, calls=%fused_computation.2 | convolution fusion | flops 537133056 | bytes 4980736 | tf_op jit(solution)/shard_map/td,dc->tc/dot_general | solution.py:107
  57.3 0.8 copy.42
  58.2 0.0 all-gather.8.cloned.1.call-update
  58.2 0.0 copy-done.2
  58.2 0.8 copy.29
  59.1 3.6 %all-to-all-start = ((bf16[128,16,64]{0,2,1:T(8,128)(2,1)}), bf16[128,16,64]{0,2,1:T(8,128)(2,1)S(1)}, u32[]{:S(2)}, u32[]{:S(2)}) async-start(bf16[128,16,64]{0,2,1:T(8,128)(2,1)} %bitcast.7), calls=%async_computation | async-start | bytes 524288 | tf_op jit(solution)/shard_map/all_to_all | solution.py:123
  62.7 0.2 copy.43
  62.8 7.2 %all-to-all-done = bf16[128,16,64]{0,2,1:T(8,128)(2,1)S(1)} async-done(((bf16[128,16,64]{0,2,1:T(8,128)(2,1)}), bf16[128,16,64]{0,2,1:T(8,128)(2,1)S(1)}, u32[]{:S(2)}, u32[]{:S(2)}) %all-to-all-start) | async-done | bytes 262176 | tf_op jit(solution)/shard_map/all_to_all | solution.py:123
  70.0 0.0 copy-start.1
  70.0 1.9 broadcast_in_dim.6
  71.9 0.0 copy-start.3
  71.9 5.4 %all-to-all-start.1 = ((bf16[8,8,128,128]{3,2,1,0:T(8,128)(2,1)}), bf16[8,8,128,128]{3,2,1,0:T(8,128)(2,1)}, u32[]{:S(2)}, u32[]{:S(2)}) async-start(bf16[8,8,128,128]{3,2,1,0:T(8,128)(2,1)} %broadcast_in_dim.6), calls=%async_computation.1 | async-start | bytes 4194304 | tf_op jit(solution)/shard_map/all_to_all | solution.py:121
  77.3 0.0 all-gather.10.cloned.1.call-start
  77.4 0.0 copy-done.1
  77.4 0.8 constant_dynamic-slice_fusion
  78.2 0.0 all-gather.10.cloned.1.call-update
  78.2 0.0 copy-done.3
  78.2 0.1 copy.26
  78.4 0.6 gather_fusion
  79.0 3.6 %convolution_convert_fusion.1 = bf16[2048,64]{0,1:T(8,128)(2,1)S(1)} fusion(bf16[2048,1024]{1,0:T(8,128)(2,1)} %all-gather.6.cloned.1.call-done, bf16[1024,3,64]{0,2,1:T(8,128)(2,1)S(1)} %bitcast.62), kind=kOutput, calls=%fused_computation.3 | convolution fusion | flops 268566528 | bytes 4587520 | tf_op jit(solution)/shard_map/td,dc->tc/dot_general | solution.py:114
  82.5 0.3 copy.28
  82.8 0.3 copy.30
  83.1 27.3 %all-to-all-done.1 = bf16[8,8,128,128]{3,2,1,0:T(8,128)(2,1)} async-done(((bf16[8,8,128,128]{3,2,1,0:T(8,128)(2,1)}), bf16[8,8,128,128]{3,2,1,0:T(8,128)(2,1)}, u32[]{:S(2)}, u32[]{:S(2)}) %all-to-all-start.1) | async-done | bytes 2097184 | tf_op jit(solution)/shard_map/all_to_all | solution.py:121
  110.5 12.3 %all-gather.8.cloned.1.call-done.ka_ref = bf16[64,128,128]{2,1,0:T(8,128)(2,1)} async-done(((bf16[8,128,128]{2,1,0:T(8,128)(2,1)}), bf16[64,128,128]{2,1,0:T(8,128)(2,1)}) %all-gather.8.cloned.1.call-update) | async-done | bytes 2097168 | tf_op jit(solution)/shard_map/all_gather | solution.py:119
  122.8 0.0 copy-start
  122.8 1.6 copy-done
  124.4 22.9 %shard_map.67 = (bf16[16,128,64]{2,1,0:T(8,128)(2,1)S(1)}, bf16[16,128,64]{2,1,0:T(8,128)(2,1)S(1)}, bf16[128,128,128]{2,1,0:T(8,128)(2,1)}) custom-call(s32[16,8]{1,0:T(8,128)S(1)} %get-tuple-element.22.slots_ref, s32[16,8]{1,0:T(8,128)S(1)} %add_select_fusion.4.a_ids_ref, s32[16,8]{1,0:T(8,128)S(1)} %get-tuple-element.21.b_ids_ref, ...), custom_call_target="tpu_custom_call" | custom-call | tf_op jit(solution)/shard_map/pallas_call | solution.py:75
  147.2 58.8 %all_to_all.48 = bf16[8,2048,128]{2,1,0:T(8,128)(2,1)} all-to-all(bf16[8,2048,128]{2,1,0:T(8,128)(2,1)} %bitcast.58), channel_id=1, replica_groups=mesh['seq'=16,'zero'=8] {'zero'}, dimensions={0} | all-to-all | bytes 8388608 | tf_op jit(solution)/shard_map/all_to_all | solution.py:156
  206.0 3.1 %reduce_sum.21 = bf16[2048,128]{1,0:T(8,128)(2,1)S(1)} reduce(bf16[8,2048,128]{2,1,0:T(8,128)(2,1)} %all_to_all.48, bf16[]{:T(256)} %constant.123.clone.1), dimensions={0}, to_apply=%region_0.1 | reduce | flops 1835008 | bytes 4718594 | tf_op jit(solution)/shard_map/reduce_sum | solution.py:157
  209.1 3.6 %convolution_bitcast_fusion = f32[24,8,8,128]{3,2,1,0:T(8,128)S(1)} fusion(bf16[2048,1024]{1,0:T(8,128)(2,1)} %all-gather.6.cloned.1.call-done, bf16[2048,128]{1,0:T(8,128)(2,1)S(1)} %reduce_sum.21, bf16[2048,64]{1,0:T(8,128)(2,1)S(1)} %bitcast.50), kind=kOutput, calls=%fused_computation.4 | convolution fusion | flops 806879232 | bytes 5767168 | tf_op jit(solution)/shard_map/td,tc->dc/dot_general | solution.py:171
  212.7 0.9 copy.47
  213.6 8.5 %all-to-all-start.4 = ((f32[8,128,192]{1,2,0:T(8,128)}), f32[8,128,192]{1,2,0:T(8,128)S(1)}, u32[]{:S(2)}, u32[]{:S(2)}) async-start(f32[8,128,192]{1,2,0:T(8,128)} %bitcast.46), calls=%async_computation.4 | async-start | bytes 1572864 | tf_op jit(solution)/shard_map/all_to_all | solution.py:175
  222.1 0.0 all-gather.12.cloned.1.call-start
  222.1 5.0 %all-gather.10.cloned.1.call-done = bf16[1024,1536]{1,0:T(8,128)(2,1)} async-done(((bf16[128,1536]{1,0:T(8,128)(2,1)}), bf16[1024,1536]{1,0:T(8,128)(2,1)}) %all-gather.10.cloned.1.call-update) | async-done | bytes 3145744 | tf_op jit(solution)/shard_map/all_gather | solution.py:101
  227.1 1.5 collective-permute-start
  228.6 5.1 %all-to-all-done.4 = f32[8,128,192]{1,2,0:T(8,128)S(1)} async-done(((f32[8,128,192]{1,2,0:T(8,128)}), f32[8,128,192]{1,2,0:T(8,128)S(1)}, u32[]{:S(2)}, u32[]{:S(2)}) %all-to-all-start.4) | async-done | bytes 786464 | tf_op jit(solution)/shard_map/all_to_all | solution.py:175
  233.7 0.7 reduce_sum.22
  234.4 0.0 all-gather.12.cloned.1.call-update
  234.4 0.5 pad_maximum_fusion
  234.9 0.6 copy.33
  235.6 1.4 copy.34
  237.0 2.2 reshape.94
  239.2 6.5 %all-to-all-start.3 = ((bf16[16,2,16384]{2,1,0:T(2,128)(2,1)}), bf16[16,2,16384]{2,1,0:T(2,128)(2,1)S(1)}, u32[]{:S(2)}, u32[]{:S(2)}) async-start(bf16[16,2,16384]{2,1,0:T(2,128)(2,1)} %reshape.94), calls=%async_computation.3 | async-start | bytes 2097152 | tf_op jit(solution)/shard_map/all_to_all | solution.py:161
  245.7 18.3 %all-to-all-done.3 = bf16[16,2,16384]{2,1,0:T(2,128)(2,1)S(1)} async-done(((bf16[16,2,16384]{2,1,0:T(2,128)(2,1)}), bf16[16,2,16384]{2,1,0:T(2,128)(2,1)S(1)}, u32[]{:S(2)}, u32[]{:S(2)}) %all-to-all-start.3) | async-done | bytes 1048608 | tf_op jit(solution)/shard_map/all_to_all | solution.py:161
  264.1 1.3 reshape.95
  265.4 1.4 copy.44
  266.8 0.1 slice.37
  267.0 0.2 copy.37
  267.2 0.1 copy.36
  267.3 0.9 copy.40
  268.1 3.0 %fusion.6 = f32[128,1024]{1,0:T(8,128)S(1)} fusion(bf16[1024,1536]{1,0:T(8,128)(2,1)} %all-gather.10.cloned.1.call-done, bf16[128,3072]{0,1:T(8,128)(2,1)S(1)} %bitcast.59, s32[]{:T(128)S(6)} %select_n.75), kind=kOutput, calls=%fused_computation.13 | convolution fusion | flops 402653184 | bytes 4063236 | tf_op jit(solution)/shard_map/tc,dc->td/dot_general | solution.py:167
  271.2 0.0 collective-permute-done
  271.2 3.8 %fusion.1 = bf16[128,1024]{1,0:T(8,128)(2,1)} fusion(f32[128,1024]{1,0:T(8,128)S(1)} %fusion.6, bf16[1024,1536]{1,0:T(8,128)(2,1)} %collective-permute-done, bf16[128,3072]{0,1:T(8,128)(2,1)S(1)} %bitcast.60, s32[]{:T(128)S(6)} %select_n.76), kind=kOutput, calls=%fused_computation.6 | convolution fusion | flops 402915328 | bytes 4325380 | tf_op jit(solution)/shard_map/tc,dc->td/dot_general | solution.py:168
  274.9 0.0 all-gather.12.cloned.1.call-done
  275.0 1.5 copy.39
  276.5 1.6 copy.41
  (8 shorter events, 0.1 us)
Async XLA Ops:
  7.2 46.4 %all-gather.6.cloned.1.call-start = ((), (), s32[]{:S(2)}) async-start(), calls=%async_computation.5 | async-start | bytes 4456448 | tf_op jit(solution)/shard_map/all_gather | solution.py:103
  7.9 114.9 %all-gather.8.cloned.1.call-start = ((), (), s32[]{:S(2)}) async-start(), calls=%async_computation.6 | async-start | bytes 2359296 | tf_op jit(solution)/shard_map/all_gather | solution.py:119
  53.6 4.7 %copy-start.2 = (bf16[128,1024]{1,0:T(8,128)(2,1)S(1)}, bf16[128,1024]{1,0:T(8,128)(2,1)}, u32[]{:S(2)}) copy-start(bf16[128,1024]{1,0:T(8,128)(2,1)} %param.7) | copy-start | bytes 786436
  59.1 11.0 %all-to-all-start = ((bf16[128,16,64]{0,2,1:T(8,128)(2,1)}), bf16[128,16,64]{0,2,1:T(8,128)(2,1)S(1)}, u32[]{:S(2)}, u32[]{:S(2)}) async-start(bf16[128,16,64]{0,2,1:T(8,128)(2,1)} %bitcast.7), calls=%async_computation | async-start | bytes 524288 | tf_op jit(solution)/shard_map/all_to_all | solution.py:123
  70.0 7.3 %copy-start.1 = (bf16[128,3072]{1,0:T(8,128)(2,1)S(1)}, bf16[128,3072]{1,0:T(8,128)(2,1)}, u32[]{:S(2)}) copy-start(bf16[128,3072]{1,0:T(8,128)(2,1)} %param.5) | copy-start | bytes 2359300
  71.9 6.3 %copy-start.3 = (s32[128,8]{0,1:T(8,128)S(1)}, s32[128,8]{0,1:T(8,128)}, u32[]{:S(2)}) copy-start(s32[128,8]{0,1:T(8,128)} %param.6) | copy-start | bytes 12292
  71.9 38.6 %all-to-all-start.1 = ((bf16[8,8,128,128]{3,2,1,0:T(8,128)(2,1)}), bf16[8,8,128,128]{3,2,1,0:T(8,128)(2,1)}, u32[]{:S(2)}, u32[]{:S(2)}) async-start(bf16[8,8,128,128]{3,2,1,0:T(8,128)(2,1)} %broadcast_in_dim.6), calls=%async_computation.1 | async-start | bytes 4194304 | tf_op jit(solution)/shard_map/all_to_all | solution.py:121
  77.3 149.8 %all-gather.10.cloned.1.call-start = ((), (), s32[]{:S(2)}) async-start(), calls=%async_computation.7 | async-start | bytes 3538944 | tf_op jit(solution)/shard_map/all_gather | solution.py:101
  122.8 1.6 copy-start
  213.6 20.1 %all-to-all-start.4 = ((f32[8,128,192]{1,2,0:T(8,128)}), f32[8,128,192]{1,2,0:T(8,128)S(1)}, u32[]{:S(2)}, u32[]{:S(2)}) async-start(f32[8,128,192]{1,2,0:T(8,128)} %bitcast.46), calls=%async_computation.4 | async-start | bytes 1572864 | tf_op jit(solution)/shard_map/all_to_all | solution.py:175
  222.1 52.9 %all-gather.12.cloned.1.call-start = ((), (), s32[]{:S(2)}) async-start(), calls=%async_computation.8 | async-start | bytes 1671168 | tf_op jit(solution)/shard_map/all_gather | solution.py:178
  227.1 44.1 %collective-permute-start = (bf16[1024,1536]{1,0:T(8,128)(2,1)}, bf16[1024,1536]{1,0:T(8,128)(2,1)}, u32[]{:S(2)}, u32[]{:S(2)}) collective-permute-start(bf16[1024,1536]{1,0:T(8,128)(2,1)} %all-gather.10.cloned.1.call-done), channel_id=1, source_target_pairs={{0,8},{8,0},{16,24},{24,16},{32,40},{40,32},{48,56},{56,48},{64,72... | collective-permute-start | bytes 9437192 | tf_op jit(solution)/shard_map/ppermute | solution.py:102
  239.2 24.8 %all-to-all-start.3 = ((bf16[16,2,16384]{2,1,0:T(2,128)(2,1)}), bf16[16,2,16384]{2,1,0:T(2,128)(2,1)S(1)}, u32[]{:S(2)}, u32[]{:S(2)}) async-start(bf16[16,2,16384]{2,1,0:T(2,128)(2,1)} %reshape.94), calls=%async_computation.3 | async-start | bytes 2097152 | tf_op jit(solution)/shard_map/all_to_all | solution.py:161
Sparse Core Ops, SparseCore 0:
  9.7 43.8 all-gather.5
  58.3 64.4 all-gather.7
  125.1 101.9 all-gather.9
  234.5 38.3 all-gather.11

commit v19 on v16

--- a/solution.py
+++ b/solution.py
@@ -167,13 +167,18 @@
         jnp.einsum("tc,dc->td", g_mine, w_mine, preferred_element_type=jnp.float32)
         + jnp.einsum("tc,dc->td", g_other, w_other, preferred_element_type=jnp.float32)
     ).astype(jnp.bfloat16)
-    head_grads = local_grads
-    head_part = jnp.einsum(
-        "td,tc->dc", group_tokens, head_grads, preferred_element_type=jnp.float32
+    part_q = jnp.einsum(
+        "td,tc->dc",
+        group_tokens,
+        query_grads.reshape(-1, head_cols),
+        preferred_element_type=jnp.float32,
     )
-    head_part = head_part.reshape(zero_count, -1, 3 * head_cols)
-    head_part = lax.all_to_all(head_part, "zero", split_axis=0, concat_axis=0, tiled=True)
-    own_rows = jnp.sum(head_part, axis=0)
+    part_q = part_q.reshape(zero_count, -1, head_cols)
+    part_q = lax.all_to_all(part_q, "zero", split_axis=0, concat_axis=0, tiled=True)
+    part_kv = jnp.einsum("td,tc->dc", group_tokens, kv_sum, preferred_element_type=jnp.float32)
+    part_kv = part_kv.reshape(zero_count, -1, 2 * head_cols)
+    part_kv = lax.all_to_all(part_kv, "zero", split_axis=0, concat_axis=0, tiled=True)
+    own_rows = jnp.concatenate([jnp.sum(part_q, axis=0), jnp.sum(part_kv, axis=0)], axis=1)
     own_rows = own_rows.reshape(1, -1, 3, head_cols)
     gathered = lax.all_gather(own_rows, "seq", axis=0, tiled=True)
     weight_gradient = gathered.transpose(1, 2, 0, 3).reshape(-1, 3 * seq_count * head_cols)

time: 287 us -> 299 us (1.042)
  blocking collectives: 87.3 us -> 28.7 us
  waiting for transfers between devices: 91.4 us -> 136 us
  starting transfers between devices: 25.9 us -> 38.9 us
  local copies, waits for them, and re-layouts: 21.2 us -> 28.6 us
  matrix products: 17.7 us -> 22.7 us
    all_to_all x1 -> x0, blocking collectives: 58.6 us -> none  [on_device(): lax.all_to_all(group_sums, 'zero', split_axis=0, concat_axis=0, tiled=True)]
    all_to_all x1 -> x3, waiting for transfers between devices: 5.09 us -> 54.6 us  [the longest x1 49.6 us: on_device(): lax.all_to_all(group_sums, 'zero', split_axis=0, concat_axis=0, tiled=True)]
    all_to_all x1 -> x3, starting transfers between devices: 8.67 us -> 16.2 us  [the longest x1 6.3 us: on_device(): lax.all_to_all(part_q, 'zero', split_axis=0, concat_axis=0, tiled=True)]
    dot_general x0 -> x1, local copies, waits for them, and re-layouts: none -> 6.59 us  [on_device(): jnp.einsum('td,tc->dc', group_tokens, query_grads.reshape(-1, head_cols),...]
    all_gather x1, waiting for transfers between devices: 4.99 us -> 0.02 us  [on_device(): w_mine = lax.all_gather(w_mine, 'zero', axis=0, tiled=True)]
    dot_general x1 -> x2, matrix products: 3.59 us -> 8.55 us  [the longest x1 4.29 us: on_device(): jnp.einsum('td,tc->dc', group_tokens, query_grads.reshape(-1, head_cols),...]
    ppermute x1, starting transfers between devices: 1.5 us -> 4.62 us  [on_device(): w_other = lax.ppermute(w_mine, 'seq', pair)]
  transfers between devices with their start and end apart: 9 -> 11, of which waited for: 7 -> 8; matrix products, arithmetic and copies ran while one was open for 12% -> 16% of each run, Pallas kernels for 8% -> 8%
where the time goes in v19:
time: 299 us; the launch traced here: 298 us
  waiting for transfers between devices  136 us (45%)
  starting transfers between devices  38.9 us (13%)
  blocking collectives  28.7 us (10%)
  local copies, waits for them, and re-layouts  28.6 us (10%)
  Pallas kernels  24.1 us (8%)
  matrix products  22.7 us (8%)
  between operations  14 us (5%)
  other arithmetic  4.75 us (2%)
    all_to_all x1, waiting for transfers between devices, on_device(): lax.all_to_all(group_sums, 'zero', split_axis=0, concat_axis=0, tiled=True)  49.6 us
    all_gather x1, blocking collectives, on_device(): head_w = lax.all_gather(head_w, 'zero', axis=0, tiled=True)  28.7 us
    all_to_all x1, waiting for transfers between devices, on_device(): kv_b = lax.all_to_all(kv_b, 'zero', split_axis=0, concat_axis=0, tiled=True)  27.3 us
    pallas_call x1, Pallas kernels, block_attention(): pl.pallas_call(functools.partial(_attn_kernel, scale=scale), grid_spec=gr...  24.1 us
    all_to_all x1, waiting for transfers between devices, on_device(): lax.all_to_all(outgoing, 'seq', split_axis=0, concat_axis=2, tiled=True)  18.2 us
    all_gather x1, waiting for transfers between devices, on_device(): group_tokens = lax.all_gather(tokens, 'seq', axis=0, tiled=True)  15.3 us
    all_gather x1, waiting for transfers between devices, on_device(): kv_a = lax.all_gather(kv_local[:split], 'zero', axis=0, tiled=True)  12.3 us
    unnamed x14, local copies, waits for them, and re-layouts  9.25 us
  transfers between devices with their start and end apart: 11, of which 8 were waited for; matrix products, arithmetic and copies ran while one was open for 16% of the time, Pallas kernels for 8%

profile of v19, /device:TPU:1, one launch (start us, length us, event | category | flops | bytes accessed | tf_op | source)
XLA Modules:
  0.0 297.5 jit_solution(6183934559118321964)
XLA Ops:
  7.2 0.0 all-gather.6.cloned.1.call-start
  7.2 0.7 all-gather.6.cloned.1.call-update
  7.9 0.0 all-gather.8.cloned.1.call-start
  7.9 1.5 copy.52
  9.5 28.7 %all-gather = bf16[1024,3,1,64]{0,3,2,1:T(8,128)(2,1)S(1)} all-gather(bf16[128,3,1,64]{0,3,2,1:T(8,128)(2,1)S(1)} %constant_dynamic-slice_fusion.1), channel_id=2, replica_groups=mesh['seq'=16,'zero'=8] {'zero'}, dimensions={0}, use_global_device_ids=true | all-gather | bytes 442368 | tf_op jit(solution)/shard_map/all_gather | solution.py:106
  38.2 15.3 %all-gather.6.cloned.1.call-done = bf16[2048,1024]{1,0:T(8,128)(2,1)} async-done(((bf16[128,1024]{1,0:T(8,128)(2,1)}), bf16[2048,1024]{1,0:T(8,128)(2,1)}) %all-gather.6.cloned.1.call-update) | async-done | bytes 4194320 | tf_op jit(solution)/shard_map/all_gather | solution.py:103
  53.6 3.7 %fusion = bf16[2048,128]{0,1:T(8,128)(2,1)S(1)} fusion(bf16[1024,128]{0,1:T(8,128)(2,1)S(1)} %bitcast.71, bf16[2048,1024]{1,0:T(8,128)(2,1)} %all-gather.6.cloned.1.call-done), kind=kOutput, calls=%fused_computation.2 | convolution fusion | flops 537133056 | bytes 4980736 | tf_op jit(solution)/shard_map/td,dc->tc/dot_general | solution.py:107
  57.3 0.8 copy.72
  58.2 0.0 all-gather.8.cloned.1.call-update
  58.2 0.0 copy-done.2
  58.2 0.8 copy.54
  59.1 3.6 %all-to-all-start = ((bf16[128,16,64]{0,2,1:T(8,128)(2,1)}), bf16[128,16,64]{0,2,1:T(8,128)(2,1)S(1)}, u32[]{:S(2)}, u32[]{:S(2)}) async-start(bf16[128,16,64]{0,2,1:T(8,128)(2,1)} %bitcast.7), calls=%async_computation | async-start | bytes 524288 | tf_op jit(solution)/shard_map/all_to_all | solution.py:123
  62.7 0.2 copy.73
  62.8 7.2 %all-to-all-done = bf16[128,16,64]{0,2,1:T(8,128)(2,1)S(1)} async-done(((bf16[128,16,64]{0,2,1:T(8,128)(2,1)}), bf16[128,16,64]{0,2,1:T(8,128)(2,1)S(1)}, u32[]{:S(2)}, u32[]{:S(2)}) %all-to-all-start) | async-done | bytes 262176 | tf_op jit(solution)/shard_map/all_to_all | solution.py:123
  70.0 1.9 broadcast_in_dim.6
  71.9 5.4 %all-to-all-start.1 = ((bf16[8,8,128,128]{3,2,1,0:T(8,128)(2,1)}), bf16[8,8,128,128]{3,2,1,0:T(8,128)(2,1)}, u32[]{:S(2)}, u32[]{:S(2)}) async-start(bf16[8,8,128,128]{3,2,1,0:T(8,128)(2,1)} %broadcast_in_dim.6), calls=%async_computation.1 | async-start | bytes 4194304 | tf_op jit(solution)/shard_map/all_to_all | solution.py:121
  77.4 0.0 all-gather.10.cloned.1.call-start
  77.4 0.0 copy-done.1
  77.4 0.8 constant_dynamic-slice_fusion
  78.2 0.0 all-gather.10.cloned.1.call-update
  78.2 0.0 copy-done.3
  78.2 0.1 copy.51
  78.4 0.6 gather_fusion
  79.0 3.6 %convolution_convert_fusion.1 = bf16[2048,64]{0,1:T(8,128)(2,1)S(1)} fusion(bf16[2048,1024]{1,0:T(8,128)(2,1)} %all-gather.6.cloned.1.call-done, bf16[1024,3,64]{0,2,1:T(8,128)(2,1)S(1)} %bitcast.69), kind=kOutput, calls=%fused_computation.3 | convolution fusion | flops 268566528 | bytes 4587520 | tf_op jit(solution)/shard_map/td,dc->tc/dot_general | solution.py:114
  82.6 0.3 copy.53
  82.8 0.3 copy.55
  83.1 27.3 %all-to-all-done.1 = bf16[8,8,128,128]{3,2,1,0:T(8,128)(2,1)} async-done(((bf16[8,8,128,128]{3,2,1,0:T(8,128)(2,1)}), bf16[8,8,128,128]{3,2,1,0:T(8,128)(2,1)}, u32[]{:S(2)}, u32[]{:S(2)}) %all-to-all-start.1) | async-done | bytes 2097184 | tf_op jit(solution)/shard_map/all_to_all | solution.py:121
  110.5 12.3 %all-gather.8.cloned.1.call-done.ka_ref = bf16[64,128,128]{2,1,0:T(8,128)(2,1)} async-done(((bf16[8,128,128]{2,1,0:T(8,128)(2,1)}), bf16[64,128,128]{2,1,0:T(8,128)(2,1)}) %all-gather.8.cloned.1.call-update) | async-done | bytes 2097168 | tf_op jit(solution)/shard_map/all_gather | solution.py:119
  122.8 1.6 copy-done
  124.4 24.1 %shard_map.67 = (bf16[16,128,64]{2,1,0:T(8,128)(2,1)S(1)}, bf16[16,128,64]{2,1,0:T(8,128)(2,1)S(1)}, bf16[128,128,128]{2,1,0:T(8,128)(2,1)}) custom-call(s32[16,8]{1,0:T(8,128)S(1)} %get-tuple-element.25.slots_ref, s32[16,8]{1,0:T(8,128)S(1)} %add_select_fusion.4.a_ids_ref, s32[16,8]{1,0:T(8,128)S(1)} %get-tuple-element.24.b_ids_ref, ...), custom_call_target="tpu_custom_call" | custom-call | tf_op jit(solution)/shard_map/pallas_call | solution.py:75
  148.5 4.6 %all-to-all-start.2 = ((bf16[8,2048,128]{2,1,0:T(8,128)(2,1)}), bf16[8,2048,128]{2,1,0:T(8,128)(2,1)}, u32[]{:S(2)}, u32[]{:S(2)}) async-start(bf16[8,2048,128]{2,1,0:T(8,128)(2,1)} %bitcast.65), calls=%async_computation.2 | async-start | bytes 8388608 | tf_op jit(solution)/shard_map/all_to_all | solution.py:156
  153.1 6.6 %copy.76 = bf16[1024,2048]{1,0:T(8,128)(2,1)} copy(bf16[1024,2048]{0,1:T(8,128)(2,1)} %bitcast.56) | data formatting | bytes 8388608 | tf_op jit(solution)/shard_map/td,tc->dc/dot_general | solution.py:170
  159.7 4.3 %fusion.21 = f32[8,128,64]{1,2,0:T(8,128)} fusion(bf16[8,128,2048]{2,1,0:T(8,128)(2,1)} %bitcast.57, bf16[2048,64,1]{1,0,2:T(8,128)(2,1)S(1)} %bitcast.51), kind=kOutput, calls=%fused_computation.45 | convolution fusion | flops 268435456 | bytes 4718592 | tf_op jit(solution)/shard_map/td,tc->dc/dot_general | solution.py:170
  164.0 49.6 %all-to-all-done.2 = bf16[8,2048,128]{2,1,0:T(8,128)(2,1)} async-done(((bf16[8,2048,128]{2,1,0:T(8,128)(2,1)}), bf16[8,2048,128]{2,1,0:T(8,128)(2,1)}, u32[]{:S(2)}, u32[]{:S(2)}) %all-to-all-start.2) | async-done | bytes 4194336 | tf_op jit(solution)/shard_map/all_to_all | solution.py:156
  213.6 6.3 %all-to-all-start.4 = ((f32[8,128,64]{1,2,0:T(8,128)}), f32[8,128,64]{1,2,0:T(8,128)S(1)}, u32[]{:S(2)}, u32[]{:S(2)}) async-start(f32[8,128,64]{1,2,0:T(8,128)} %fusion.21), calls=%async_computation.4 | async-start | bytes 524288 | tf_op jit(solution)/shard_map/all_to_all | solution.py:177
  219.9 3.1 %reduce_sum.30 = bf16[2048,128]{1,0:T(8,128)(2,1)S(1)} reduce(bf16[8,2048,128]{2,1,0:T(8,128)(2,1)} %all-to-all-done.2, bf16[]{:T(256)} %constant.123.clone.1), dimensions={0}, to_apply=%region_0.1 | reduce | flops 1835008 | bytes 4718594 | tf_op jit(solution)/shard_map/reduce_sum | solution.py:157
  223.0 4.3 %fusion.2 = f32[8,128,128]{2,1,0:T(8,128)} fusion(bf16[8,128,2048]{2,1,0:T(8,128)(2,1)} %bitcast.58, bf16[2048,128]{1,0:T(8,128)(2,1)S(1)} %reduce_sum.30), kind=kOutput, calls=%fused_computation.7 | convolution fusion | flops 536870912 | bytes 5242880 | tf_op jit(solution)/shard_map/td,tc->dc/dot_general | solution.py:178
  227.3 1.3 all-to-all-done.4
  228.6 5.3 %all-to-all-start.5 = ((f32[8,128,128]{2,1,0:T(8,128)}), f32[8,128,128]{2,1,0:T(8,128)S(1)}, u32[]{:S(2)}, u32[]{:S(2)}) async-start(f32[8,128,128]{2,1,0:T(8,128)} %fusion.2), calls=%async_computation.5 | async-start | bytes 1048576 | tf_op jit(solution)/shard_map/all_to_all | solution.py:180
  233.9 0.0 all-gather.12.cloned.1.call-start
  233.9 0.0 all-gather.10.cloned.1.call-done
  233.9 4.6 %collective-permute-start = (bf16[1024,1536]{1,0:T(8,128)(2,1)}, bf16[1024,1536]{1,0:T(8,128)(2,1)}, u32[]{:S(2)}, u32[]{:S(2)}) collective-permute-start(bf16[1024,1536]{1,0:T(8,128)(2,1)} %all-gather.10.cloned.1.call-done), channel_id=1, source_target_pairs={{0,8},{8,0},{16,24},{24,16},{32,40},{40,32},{48,56},{56,48},{64,72... | collective-permute-start | bytes 9437192 | tf_op jit(solution)/shard_map/ppermute | solution.py:102
  238.6 0.1 copy.66
  238.7 3.7 %all-to-all-done.5 = f32[8,128,128]{2,1,0:T(8,128)S(1)} async-done(((f32[8,128,128]{2,1,0:T(8,128)}), f32[8,128,128]{2,1,0:T(8,128)S(1)}, u32[]{:S(2)}, u32[]{:S(2)}) %all-to-all-start.5) | async-done | bytes 524320 | tf_op jit(solution)/shard_map/all_to_all | solution.py:180
  242.4 0.1 pad_maximum_fusion.1
  242.5 0.7 copy.67
  243.3 0.0 all-gather.12.cloned.1.call-update
  243.3 1.4 pad_maximum_fusion
  244.7 1.5 copy.58
  246.2 1.4 copy.59
  247.6 2.2 reshape.97
  249.9 9.0 %all-to-all-start.3 = ((bf16[16,2,16384]{2,1,0:T(2,128)(2,1)}), bf16[16,2,16384]{2,1,0:T(2,128)(2,1)S(1)}, u32[]{:S(2)}, u32[]{:S(2)}) async-start(bf16[16,2,16384]{2,1,0:T(2,128)(2,1)} %reshape.97), calls=%async_computation.3 | async-start | bytes 2097152 | tf_op jit(solution)/shard_map/all_to_all | solution.py:161
  258.8 18.2 %all-to-all-done.3 = bf16[16,2,16384]{2,1,0:T(2,128)(2,1)S(1)} async-done(((bf16[16,2,16384]{2,1,0:T(2,128)(2,1)}), bf16[16,2,16384]{2,1,0:T(2,128)(2,1)S(1)}, u32[]{:S(2)}, u32[]{:S(2)}) %all-to-all-start.3) | async-done | bytes 1048608 | tf_op jit(solution)/shard_map/all_to_all | solution.py:161
  277.0 1.3 reshape.98
  278.3 1.4 copy.74
  279.7 0.1 slice.37
  279.9 0.2 copy.62
  280.1 0.1 copy.61
  280.2 0.9 copy.69
  281.0 3.0 %fusion.5 = f32[128,1024]{1,0:T(8,128)S(1)} fusion(bf16[1024,1536]{1,0:T(8,128)(2,1)} %all-gather.10.cloned.1.call-done, bf16[128,3072]{0,1:T(8,128)(2,1)S(1)} %bitcast.66, s32[]{:T(128)S(6)} %select_n.75), kind=kOutput, calls=%fused_computation.10 | convolution fusion | flops 402653184 | bytes 4063236 | tf_op jit(solution)/shard_map/tc,dc->td/dot_general | solution.py:167
  284.1 0.0 collective-permute-done
  284.1 3.8 %fusion.1 = bf16[128,1024]{1,0:T(8,128)(2,1)} fusion(f32[128,1024]{1,0:T(8,128)S(1)} %fusion.5, bf16[1024,1536]{1,0:T(8,128)(2,1)} %collective-permute-done, bf16[128,3072]{0,1:T(8,128)(2,1)S(1)} %bitcast.67, s32[]{:T(128)S(6)} %select_n.76), kind=kOutput, calls=%fused_computation.5 | convolution fusion | flops 402915328 | bytes 4325380 | tf_op jit(solution)/shard_map/tc,dc->td/dot_general | solution.py:168
  287.9 1.5 copy.68
  289.4 1.6 copy.70
  (15 shorter events, 0.2 us)
Async XLA Ops:
  7.2 46.4 %all-gather.6.cloned.1.call-start = ((), (), s32[]{:S(2)}) async-start(), calls=%async_computation.6 | async-start | bytes 4456448 | tf_op jit(solution)/shard_map/all_gather | solution.py:103
  7.9 114.9 %all-gather.8.cloned.1.call-start = ((), (), s32[]{:S(2)}) async-start(), calls=%async_computation.7 | async-start | bytes 2359296 | tf_op jit(solution)/shard_map/all_gather | solution.py:119
  53.6 4.7 %copy-start.2 = (bf16[128,1024]{1,0:T(8,128)(2,1)S(1)}, bf16[128,1024]{1,0:T(8,128)(2,1)}, u32[]{:S(2)}) copy-start(bf16[128,1024]{1,0:T(8,128)(2,1)} %param.7) | copy-start | bytes 786436
  59.1 11.0 %all-to-all-start = ((bf16[128,16,64]{0,2,1:T(8,128)(2,1)}), bf16[128,16,64]{0,2,1:T(8,128)(2,1)S(1)}, u32[]{:S(2)}, u32[]{:S(2)}) async-start(bf16[128,16,64]{0,2,1:T(8,128)(2,1)} %bitcast.7), calls=%async_computation | async-start | bytes 524288 | tf_op jit(solution)/shard_map/all_to_all | solution.py:123
  70.0 7.4 %copy-start.1 = (bf16[128,3072]{1,0:T(8,128)(2,1)S(1)}, bf16[128,3072]{1,0:T(8,128)(2,1)}, u32[]{:S(2)}) copy-start(bf16[128,3072]{1,0:T(8,128)(2,1)} %param.5) | copy-start | bytes 2359300
  71.9 6.3 %copy-start.3 = (s32[128,8]{0,1:T(8,128)S(1)}, s32[128,8]{0,1:T(8,128)}, u32[]{:S(2)}) copy-start(s32[128,8]{0,1:T(8,128)} %param.6) | copy-start | bytes 12292
  71.9 38.6 %all-to-all-start.1 = ((bf16[8,8,128,128]{3,2,1,0:T(8,128)(2,1)}), bf16[8,8,128,128]{3,2,1,0:T(8,128)(2,1)}, u32[]{:S(2)}, u32[]{:S(2)}) async-start(bf16[8,8,128,128]{3,2,1,0:T(8,128)(2,1)} %broadcast_in_dim.6), calls=%async_computation.1 | async-start | bytes 4194304 | tf_op jit(solution)/shard_map/all_to_all | solution.py:121
  77.4 156.6 %all-gather.10.cloned.1.call-start = ((), (), s32[]{:S(2)}) async-start(), calls=%async_computation.8 | async-start | bytes 3538944 | tf_op jit(solution)/shard_map/all_gather | solution.py:101
  122.8 1.6 copy-start
  148.5 65.1 %all-to-all-start.2 = ((bf16[8,2048,128]{2,1,0:T(8,128)(2,1)}), bf16[8,2048,128]{2,1,0:T(8,128)(2,1)}, u32[]{:S(2)}, u32[]{:S(2)}) async-start(bf16[8,2048,128]{2,1,0:T(8,128)(2,1)} %bitcast.65), calls=%async_computation.2 | async-start | bytes 8388608 | tf_op jit(solution)/shard_map/all_to_all | solution.py:156
  213.6 15.0 %all-to-all-start.4 = ((f32[8,128,64]{1,2,0:T(8,128)}), f32[8,128,64]{1,2,0:T(8,128)S(1)}, u32[]{:S(2)}, u32[]{:S(2)}) async-start(f32[8,128,64]{1,2,0:T(8,128)} %fusion.21), calls=%async_computation.4 | async-start | bytes 524288 | tf_op jit(solution)/shard_map/all_to_all | solution.py:177
  228.6 13.8 %all-to-all-start.5 = ((f32[8,128,128]{2,1,0:T(8,128)}), f32[8,128,128]{2,1,0:T(8,128)S(1)}, u32[]{:S(2)}, u32[]{:S(2)}) async-start(f32[8,128,128]{2,1,0:T(8,128)} %fusion.2), calls=%async_computation.5 | async-start | bytes 1048576 | tf_op jit(solution)/shard_map/all_to_all | solution.py:180
  233.9 54.0 %all-gather.12.cloned.1.call-start = ((), (), s32[]{:S(2)}) async-start(), calls=%async_computation.9 | async-start | bytes 1671168 | tf_op jit(solution)/shard_map/all_gather | solution.py:183
  233.9 50.2 %collective-permute-start = (bf16[1024,1536]{1,0:T(8,128)(2,1)}, bf16[1024,1536]{1,0:T(8,128)(2,1)}, u32[]{:S(2)}, u32[]{:S(2)}) collective-permute-start(bf16[1024,1536]{1,0:T(8,128)(2,1)} %all-gather.10.cloned.1.call-done), channel_id=1, source_target_pairs={{0,8},{8,0},{16,24},{24,16},{32,40},{40,32},{48,56},{56,48},{64,72... | collective-permute-start | bytes 9437192 | tf_op jit(solution)/shard_map/ppermute | solution.py:102
  249.9 27.1 %all-to-all-start.3 = ((bf16[16,2,16384]{2,1,0:T(2,128)(2,1)}), bf16[16,2,16384]{2,1,0:T(2,128)(2,1)S(1)}, u32[]{:S(2)}, u32[]{:S(2)}) async-start(bf16[16,2,16384]{2,1,0:T(2,128)(2,1)} %reshape.97), calls=%async_computation.3 | async-start | bytes 2097152 | tf_op jit(solution)/shard_map/all_to_all | solution.py:161
Sparse Core Ops, SparseCore 0:
  9.7 43.8 all-gather.5
  58.3 64.4 all-gather.7
  125.1 105.0 all-gather.9
  243.4 42.0 all-gather.11
